TPU v7x, 32 devices: a whole 2x2x4 slice. The times are simulated.
32 devices in a mesh: seq: 8 (over y, x, core), head: 4 (over z).
Axes of the slice: x: 2, y: 2, z: 4, core: 2. Of those that a mesh axis runs over, the one named last changes fastest.
Arguments:
- queries: bfloat16 [4096, 64, 128], P(('seq', 'head')), may hold values from -36 to 36
- keys: bfloat16 [4096, 8, 128], P(('seq', 'head')), may hold values from -6 to 6
- values: bfloat16 [4096, 8, 128], P(('seq', 'head')), may hold values from -6 to 6
- output_gradient: bfloat16 [4096, 64, 128], P(('seq', 'head')), may hold values from -6 to 6
- global_blocks: int32 [2], replicated, may hold values from 0 to 31, as said below
- random_blocks: int32 [32, 3], replicated, may hold values from 0 to 31, as said below
Outputs:
- out: bfloat16 [4096, 64, 128], P(('seq', 'head'))
- grad_queries: bfloat16 [4096, 64, 128], P(('seq', 'head'))
- grad_keys: bfloat16 [4096, 8, 128], P(('seq', 'head'))
- grad_values: bfloat16 [4096, 8, 128], P(('seq', 'head'))
Inputs may be any that keep to these rules, and one draw needn't show every extreme that they name: `global_blocks`: the two blocks differ; one of them is the last block, 31. `random_blocks`: call 4 consecutive blocks starting at a multiple of 4 a group. The entries listed by a group's query blocks never lie in that group's own blocks, and at most 2 of them lie in any one other group; in every group some other group is hit exactly 2 times.
All inputs are finite; a program needn't handle non-finite values.
Results may differ from a plain program's by a relative error of at most 0.035.
Values may be sent and summed in bfloat16 or wider, within the bound.
No kernel may reach another device: no remote copies, remote signals or barrier semaphores. Data moves between devices by JAX's collectives and lax.ppermute only.
A program may use at most 128 MiB of HBM per device.

v0:
```python
import math

import jax
import jax.numpy as jnp
from jax import lax
from jax.sharding import PartitionSpec as P

BLOCK_TOKENS = 128


def padded(shard, sides, width):
    for axis, dim in sides:
        count, length = (lax.axis_size(axis), shard.shape[dim])
        up = [(i, (i + 1) % count) for i in range(count - 1)]
        down = [(j, i) for i, j in up]
        last = lax.slice_in_dim(shard, length - width, length, axis=dim)
        leading = lax.slice_in_dim(shard, 0, width, axis=dim)
        before = lax.ppermute(last, axis, up)
        after = lax.ppermute(leading, axis, down)
        shard = jnp.concatenate([before, shard, after], axis=dim)
    return shard


def from_root(block, axis, owner):
    block = jnp.where(lax.axis_index(axis) == owner, block, jnp.zeros_like(block))
    return lax.psum(block, axis)


def per_device(queries, keys, values, output_gradient, global_blocks, random_blocks):
    query_loc, key_loc, value_loc, grad_loc = (
        lax.all_to_all(queries, "head", split_axis=1, concat_axis=0, tiled=True),
        lax.all_to_all(keys, "head", split_axis=1, concat_axis=0, tiled=True),
        lax.all_to_all(values, "head", split_axis=1, concat_axis=0, tiled=True),
        lax.all_to_all(output_gradient, "head", split_axis=1, concat_axis=0, tiled=True),
    )
    shard_len, heads_q, head_width = query_loc.shape
    heads_kv = key_loc.shape[1]
    heads_per_group = heads_q // heads_kv
    kv_width = heads_kv * head_width
    blocks = shard_len // BLOCK_TOKENS
    seq_count = lax.axis_size("seq")
    own_index = lax.axis_index("seq")
    block_total_count = seq_count * blocks
    capacity = (3 * blocks + seq_count - 2) // (seq_count - 1)
    entry_count = 3 * blocks
    score_scale = 1.0 / math.sqrt(head_width)
    kv_pair = jnp.stack(
        [key_loc.reshape(shard_len, kv_width), value_loc.reshape(shard_len, kv_width)]
    )
    extended = padded(kv_pair, (("seq", 1),), BLOCK_TOKENS)
    kv_tiles = kv_pair.reshape(2, blocks, BLOCK_TOKENS, kv_width).transpose(1, 0, 2, 3)
    global_owner = global_blocks // blocks
    global_offset = global_blocks % blocks
    own_global = (jnp.arange(blocks)[None, :] == global_offset[:, None]) & (
        global_owner == own_index
    )[:, None]
    received_rows = []
    for global_slot in range(2):
        candidate = lax.dynamic_index_in_dim(
            kv_tiles, global_offset[global_slot], 0, keepdims=False
        )
        received_rows.append(from_root(candidate, "seq", global_owner[global_slot]))
    global_tiles = jnp.stack(received_rows)
    all_entries = (
        random_blocks.reshape(seq_count, blocks, 3)
        .transpose(0, 2, 1)
        .reshape(seq_count, entry_count)
    )
    all_owner = all_entries // blocks
    entry_ids = jnp.arange(entry_count)
    entry_earlier = entry_ids[None, :] < entry_ids[:, None]
    all_rank = jnp.sum(
        (all_owner[:, :, None] == all_owner[:, None, :]) & entry_earlier[None], axis=2
    )
    my_entries = lax.dynamic_index_in_dim(all_entries, own_index, 0, keepdims=False)
    my_owner = lax.dynamic_index_in_dim(all_owner, own_index, 0, keepdims=False)
    my_rank = lax.dynamic_index_in_dim(all_rank, own_index, 0, keepdims=False)
    my_slot = my_owner * capacity + my_rank
    owned_here = (all_owner == own_index)[:, :, None] & (
        all_rank[:, :, None] == jnp.arange(capacity)[None, None, :]
    )
    offset_match = (all_entries % blocks)[:, :, None] == jnp.arange(blocks)[None, None, :]
    selector = jnp.einsum(
        "tec,teo->tco",
        owned_here.astype(jnp.bfloat16),
        offset_match.astype(jnp.bfloat16),
        preferred_element_type=jnp.float32,
    ).astype(jnp.bfloat16)
    everything = lax.all_gather(kv_pair, "seq", axis=1, tiled=True)
    tiled_all = everything.reshape(2, block_total_count, BLOCK_TOKENS, kv_width)
    random_tiles = jnp.take(tiled_all, my_entries, axis=1).transpose(1, 0, 2, 3)
    random_by_block = random_tiles.reshape(3, blocks, 2, BLOCK_TOKENS, kv_width).transpose(
        1, 0, 2, 3, 4
    )
    block_ids = own_index * blocks + jnp.arange(blocks)
    listed = jnp.concatenate(
        [
            jnp.stack([block_ids - 1, block_ids, block_ids + 1], axis=1),
            jnp.broadcast_to(global_blocks[None, :], (blocks, 2)),
            my_entries.reshape(3, blocks).T,
        ],
        axis=1,
    )
    inside = (listed >= 0) & (listed < block_total_count)
    tile_ids = jnp.arange(8)
    tile_earlier = tile_ids[None, :] < tile_ids[:, None]
    repeat = jnp.any((listed[:, :, None] == listed[:, None, :]) & tile_earlier[None], axis=2)
    live = inside & jnp.logical_not(repeat)

    def attend(unused_state, inputs):
        query_blk, grad_blk, random_blk, live_row, position = inputs
        near_tiles = lax.dynamic_slice_in_dim(
            extended, position * BLOCK_TOKENS, 3 * BLOCK_TOKENS, 1
        )
        near_tiles = near_tiles.reshape(2, 3, BLOCK_TOKENS, kv_width).transpose(1, 0, 2, 3)
        all_tiles = jnp.concatenate([near_tiles, global_tiles, random_blk], axis=0)
        key_t = all_tiles[:, 0].reshape(8, BLOCK_TOKENS, heads_kv, head_width)
        value_t = all_tiles[:, 1].reshape(8, BLOCK_TOKENS, heads_kv, head_width)
        query_grid = query_blk.reshape(BLOCK_TOKENS, heads_kv, heads_per_group, head_width)
        grad_grid = grad_blk.reshape(BLOCK_TOKENS, heads_kv, heads_per_group, head_width)
        scores = (
            jnp.einsum("qkgd,tbkd->kgqtb", query_grid, key_t, preferred_element_type=jnp.float32)
            * score_scale
        )
        scores = jnp.where(live_row[None, None, None, :, None], scores, -jnp.inf)
        row_max = jnp.max(scores, axis=(3, 4), keepdims=True)
        expo = jnp.exp(scores - row_max)
        attn_prob = expo / jnp.sum(expo, axis=(3, 4), keepdims=True)
        prob_low = attn_prob.astype(jnp.bfloat16)
        attended = jnp.einsum(
            "kgqtb,tbkd->qkgd", prob_low, value_t, preferred_element_type=jnp.float32
        )
        out_low = attended.astype(jnp.bfloat16)
        row_delta = jnp.sum(grad_grid.astype(jnp.float32) * out_low.astype(jnp.float32), axis=-1)
        grad_prob = jnp.einsum(
            "qkgd,tbkd->kgqtb", grad_grid, value_t, preferred_element_type=jnp.float32
        )
        grad_score = attn_prob * (
            grad_prob - jnp.transpose(row_delta, (1, 2, 0))[:, :, :, None, None]
        )
        score_low = grad_score.astype(jnp.bfloat16)
        query_grad = (
            jnp.einsum("kgqtb,tbkd->qkgd", score_low, key_t, preferred_element_type=jnp.float32)
            * score_scale
        )
        key_grad = (
            jnp.einsum(
                "kgqtb,qkgd->tbkd", score_low, query_grid, preferred_element_type=jnp.float32
            )
            * score_scale
        )
        value_grad = jnp.einsum(
            "kgqtb,qkgd->tbkd", prob_low, grad_grid, preferred_element_type=jnp.float32
        )
        tile_terms = jnp.stack(
            [
                key_grad.reshape(8, BLOCK_TOKENS, kv_width),
                value_grad.reshape(8, BLOCK_TOKENS, kv_width),
            ],
            axis=1,
        )
        return (
            unused_state,
            (
                out_low.reshape(BLOCK_TOKENS, heads_q, head_width),
                query_grad.astype(jnp.bfloat16).reshape(BLOCK_TOKENS, heads_q, head_width),
                tile_terms,
            ),
        )

    unused_final, (output_block_rows, query_gradient_rows, tile_grads) = lax.scan(
        attend,
        0,
        (
            query_loc.reshape(blocks, BLOCK_TOKENS, heads_q, head_width),
            grad_loc.reshape(blocks, BLOCK_TOKENS, heads_q, head_width),
            random_by_block,
            live,
            jnp.arange(blocks),
        ),
    )
    pad_spec_low = ((0, 2), (0, 0), (0, 0), (0, 0))
    pad_spec_mid = ((1, 1), (0, 0), (0, 0), (0, 0))
    pad_spec_high = ((2, 0), (0, 0), (0, 0), (0, 0))
    window_sum = (
        jnp.pad(tile_grads[:, 0], pad_spec_low)
        + jnp.pad(tile_grads[:, 1], pad_spec_mid)
        + jnp.pad(tile_grads[:, 2], pad_spec_high)
    )
    rims = jnp.concatenate([window_sum[0], window_sum[blocks + 1]], axis=1)
    returned_rims = padded(rims.astype(jnp.bfloat16), (("seq", 1),), BLOCK_TOKENS).astype(
        rims.dtype
    )
    interior = window_sum[1 : blocks + 1]
    interior = (
        interior.at[0]
        .add(returned_rims[:, :BLOCK_TOKENS])
        .at[blocks - 1]
        .add(returned_rims[:, 3 * BLOCK_TOKENS :])
    )
    global_terms = jnp.sum(tile_grads[:, 3:5], axis=0)
    global_total = lax.psum(global_terms.astype(jnp.bfloat16), "seq").astype(jnp.float32)
    own_weight = own_global.astype(jnp.float32)[:, :, None, None, None]
    interior = interior + jnp.sum(own_weight * global_total[:, None], axis=0)
    random_terms = (
        tile_grads[:, 5:8]
        .transpose(1, 0, 2, 3, 4)
        .reshape(entry_count, 2, BLOCK_TOKENS, kv_width)
        .astype(jnp.bfloat16)
    )
    slot_onehot = (my_slot[:, None] == jnp.arange(seq_count * capacity)[None, :]).astype(
        jnp.bfloat16
    )
    back_buffer = jnp.einsum(
        "es,exbw->sxbw", slot_onehot, random_terms, preferred_element_type=jnp.float32
    ).astype(jnp.bfloat16)
    returned_terms = lax.all_to_all(back_buffer, "seq", split_axis=0, concat_axis=0, tiled=True)
    interior = interior + jnp.einsum(
        "tco,tcxbw->oxbw",
        selector,
        returned_terms.reshape(seq_count, capacity, 2, BLOCK_TOKENS, kv_width),
        preferred_element_type=jnp.float32,
    )
    kv_grad = interior.transpose(1, 0, 2, 3).reshape(2, shard_len, kv_width).astype(jnp.bfloat16)
    out_all = output_block_rows.reshape(shard_len, heads_q, head_width)
    query_grad_all = query_gradient_rows.reshape(shard_len, heads_q, head_width)
    key_grad_all = kv_grad[0].reshape(shard_len, heads_kv, head_width)
    value_grad_all = kv_grad[1].reshape(shard_len, heads_kv, head_width)
    return (
        lax.all_to_all(out_all, "head", split_axis=0, concat_axis=1, tiled=True),
        lax.all_to_all(query_grad_all, "head", split_axis=0, concat_axis=1, tiled=True),
        lax.all_to_all(key_grad_all, "head", split_axis=0, concat_axis=1, tiled=True),
        lax.all_to_all(value_grad_all, "head", split_axis=0, concat_axis=1, tiled=True),
    )


def solution(mesh):
    placed = (
        P(("seq", "head"), None, None),
        P(("seq", "head"), None, None),
        P(("seq", "head"), None, None),
        P(("seq", "head"), None, None),
        P(),
        P(),
    )
    return jax.shard_map(
        per_device,
        mesh=mesh,
        in_specs=placed,
        out_specs=(
            P(("seq", "head"), None, None),
            P(("seq", "head"), None, None),
            P(("seq", "head"), None, None),
            P(("seq", "head"), None, None),
        ),
        check_vma=False,
    )
```

profile of v0, /device:TPU:4, one launch (start us, length us, event | category | flops | bytes accessed | tf_op | source)
XLA Modules:
  0.0 491.2 jit_solution(17608688807124787782)
XLA Ops:
  7.2 1.7 copy.314
  8.9 4.9 all-to-all-start
  13.7 1.7 copy.316
  15.4 7.2 %all-to-all-done = bf16[128,8,128]{2,0,1:T(8,128)(2,1)S(1)} async-done(((bf16[128,8,128]{2,0,1:T(8,128)(2,1)}), bf16[128,8,128]{2,0,1:T(8,128)(2,1)S(1)}, u32[]{:S(2)}, u32[]{:S(2)}) %all-to-all-start) | async-done | bytes 262176 | tf_op jit(solution)/shard_map/all_to_all | solution.py:32
  22.6 3.4 all-to-all-start.1
  26.6 6.5 %all-to-all-done.1 = bf16[128,8,128]{2,0,1:T(8,128)(2,1)S(1)} async-done(((bf16[128,8,128]{2,0,1:T(8,128)(2,1)}), bf16[128,8,128]{2,0,1:T(8,128)(2,1)S(1)}, u32[]{:S(2)}, u32[]{:S(2)}) %all-to-all-start.1) | async-done | bytes 262176 | tf_op jit(solution)/shard_map/all_to_all | solution.py:33
  34.4 2.7 copy.323
  37.0 3.7 all-to-all-start.3
  44.0 4.3 copy.322
  48.9 37.3 %all-to-all-done.3 = bf16[128,64,128]{2,0,1:T(8,128)(2,1)S(1)} async-done(((bf16[128,64,128]{2,0,1:T(8,128)(2,1)}), bf16[128,64,128]{2,0,1:T(8,128)(2,1)S(1)}, u32[]{:S(2)}, u32[]{:S(2)}) %all-to-all-start.3) | async-done | bytes 2097184 | tf_op jit(solution)/shard_map/all_to_all | solution.py:34
  86.2 4.5 all-to-all-start.2
  98.1 1.9 collective-permute-start
  100.0 4.5 collective-permute-start.1
  105.5 1.6 collective-permute-done.1
  108.0 2.7 copy.324
  110.6 2.9 gather_fusion
  114.9 44.3 %all-reduce.9.cloned.1.call-done = (bf16[1,2,128,256]{3,2,1,0:T(8,128)(2,1)}, bf16[1,2,128,256]{3,2,0,1:T(8,128)(2,1)}) async-done(((bf16[1,2,128,256]{3,2,1,0:T(8,128)(2,1)}, bf16[1,2,128,256]{3,2,0,1:T(8,128)(2,1)}), (bf16[1,2,128,256]{3,2,1,0:T(8,128)(2,1)}, bf16[1,2,128,256]{3,2,0,1:T(8,128)(2,1)})) %all-reduce.9.cloned.1.call-update) | async-done | bytes 262160 | tf_op jit(solution)/shard_map/psum | solution.py:26
  159.2 105.5 %while.16 = (s32[]{:T(128)}, bf16[4,128,16,128]{3,2,1,0:T(8,128)(2,1)}, bf16[4,128,16,128]{3,2,1,0:T(8,128)(2,1)}, f32[4,8,2,128,256]{3,4,1,2,0:T(8,128)}, s32[4...) while((s32[]{:T(128)}, ...), condition=%wide.region_7.8_spmd, body=%wide.region_3.7_spmd.sunk | while | flops 3265259520 | bytes 89202968 | solution.py:171
  166.5 1.9 bitcast_reduce_fusion.2
  168.4 1.7 fusion.113
  170.1 2.2 fusion.114
  172.3 1.6 multiply_reduce_fusion.3
  175.4 3.2 fusion.115
  179.4 1.5 fusion.117
  192.8 1.9 bitcast_reduce_fusion.2
  194.8 1.7 fusion.113
  196.5 2.2 fusion.114
  198.6 1.6 multiply_reduce_fusion.3
  201.8 3.2 fusion.115
  205.8 1.5 fusion.117
  219.2 1.9 bitcast_reduce_fusion.2
  221.1 1.7 fusion.113
  222.8 2.2 fusion.114
  225.0 1.6 multiply_reduce_fusion.3
  228.1 3.2 fusion.115
  232.1 1.5 fusion.117
  245.5 1.9 bitcast_reduce_fusion.2
  247.5 1.7 fusion.113
  249.2 2.2 fusion.114
  251.3 1.6 multiply_reduce_fusion.3
  254.5 3.2 fusion.115
  263.2 1.5 fusion.118
  264.7 9.1 %copy.331 = f32[4,8,2,128,256]{4,3,2,0,1:T(8,128)} copy(f32[4,8,2,128,256]{3,4,1,2,0:T(8,128)} %get-tuple-element.94) | data formatting | bytes 16777216 | tf_op jit(solution)/shard_map/while | solution.py:171
  273.8 2.1 slice.167
  277.0 2.1 copy.347
  279.1 4.8 all-to-all-start.6
  284.1 2.2 slice_bitcast_fusion.2
  287.8 2.0 collective-permute-start.2
  289.8 4.4 collective-permute-start.3
  294.3 2.5 slice_reduce_fusion
  298.1 14.2 %collective-permute-done.2 = bf16[2,128,256]{2,1,0:T(8,128)(2,1)S(1)} collective-permute-done((bf16[2,128,256]{2,1,0:T(8,128)(2,1)S(1)}, bf16[2,128,256]{2,1,0:T(8,128)(2,1)S(1)}, u32[]{:S(2)}, u32[]{:S(2)}) %collective-permute-start.2) | collective-permute-done | bytes 131104 | tf_op jit(solution)/shard_map/ppermute | solution.py:18
  314.7 3.8 scatter-add.9
  318.4 32.7 %all-reduce.7.cloned.1.call-done = bf16[2,2,128,256]{2,3,0,1:T(8,128)(2,1)} async-done(((bf16[2,2,128,256]{2,3,0,1:T(8,128)(2,1)}), bf16[2,2,128,256]{2,3,0,1:T(8,128)(2,1)}) %all-reduce.7.cloned.1.call-update) | async-done | bytes 262160 | tf_op jit(solution)/shard_map/psum | solution.py:202
  351.1 1.9 copy.336
  353.0 2.4 multiply_reduce_fusion.1
  355.4 3.1 fusion.50
  359.6 4.6 all-to-all-start.8
  364.3 7.9 %all-to-all-done.8 = bf16[512,2,128]{2,1,0:T(2,128)(2,1)S(1)} async-done(((bf16[512,2,128]{2,1,0:T(2,128)(2,1)}), bf16[512,2,128]{2,1,0:T(2,128)(2,1)S(1)}, u32[]{:S(2)}, u32[]{:S(2)}) %all-to-all-start.8) | async-done | bytes 262176 | tf_op jit(solution)/shard_map/all_to_all | solution.py:233
  372.1 10.2 %all_to_all.137 = bf16[512,2,128]{2,1,0:T(2,128)(2,1)S(1)} all-to-all(bf16[512,2,128]{2,1,0:T(2,128)(2,1)S(1)} %reshape_squeeze.6), channel_id=1, replica_groups=mesh['seq'=8,'head'=4] {'head'}, dimensions={0} | all-to-all | bytes 524288 | tf_op jit(solution)/shard_map/all_to_all | solution.py:232
  382.3 49.6 %all_to_all.138 = bf16[512,16,128]{2,1,0:T(8,128)(2,1)} all-to-all(bf16[512,16,128]{2,1,0:T(8,128)(2,1)S(1)} %bitcast.276), channel_id=1, replica_groups=mesh['seq'=8,'head'=4] {'head'}, dimensions={0} | all-to-all | bytes 4194304 | tf_op jit(solution)/shard_map/all_to_all | solution.py:231
  431.9 3.6 all-to-all-start.4
  437.4 2.0 copy.330
  439.4 43.2 %all-to-all-done.4 = bf16[512,16,128]{2,1,0:T(8,128)(2,1)S(1)} async-done(((bf16[512,16,128]{2,1,0:T(8,128)(2,1)}), bf16[512,16,128]{2,1,0:T(8,128)(2,1)S(1)}, u32[]{:S(2)}, u32[]{:S(2)}) %all-to-all-start.4) | async-done | bytes 2097184 | tf_op jit(solution)/shard_map/all_to_all | solution.py:230
  482.6 2.0 copy.328
  (185 shorter events, 74.2 us)
Async XLA Ops:
  8.9 13.8 %all-to-all-start = ((bf16[128,8,128]{2,0,1:T(8,128)(2,1)}), bf16[128,8,128]{2,0,1:T(8,128)(2,1)S(1)}, u32[]{:S(2)}, u32[]{:S(2)}) async-start(bf16[128,8,128]{2,0,1:T(8,128)(2,1)} %copy.314), calls=%async_computation | async-start | bytes 524288 | tf_op jit(solution)/shard_map/all_to_all | solution.py:32
  15.4 18.9 %copy-start.3 = (bf16[128,64,128]{2,1,0:T(8,128)(2,1)S(1)}, bf16[128,64,128]{2,1,0:T(8,128)(2,1)}, u32[]{:S(2)}) copy-start(bf16[128,64,128]{2,1,0:T(8,128)(2,1)} %param.15) | copy-start | bytes 6291460
  22.6 10.4 %all-to-all-start.1 = ((bf16[128,8,128]{2,0,1:T(8,128)(2,1)}), bf16[128,8,128]{2,0,1:T(8,128)(2,1)S(1)}, u32[]{:S(2)}, u32[]{:S(2)}) async-start(bf16[128,8,128]{2,0,1:T(8,128)(2,1)} %copy.316), calls=%async_computation.1 | async-start | bytes 524288 | tf_op jit(solution)/shard_map/all_to_all | solution.py:33
  26.1 84.6 %all-gather.2.cloned.1.call-start = ((), (), s32[]{:S(2)}) async-start(), calls=%async_computation.9 | async-start | bytes 4718592 | tf_op jit(solution)/shard_map/all_gather | solution.py:89
  33.5 0.8 copy-start.1
  37.0 3.8 copy-start.14
  37.0 49.2 %all-to-all-start.3 = ((bf16[128,64,128]{2,0,1:T(8,128)(2,1)}), bf16[128,64,128]{2,0,1:T(8,128)(2,1)S(1)}, u32[]{:S(2)}, u32[]{:S(2)}) async-start(bf16[128,64,128]{2,0,1:T(8,128)(2,1)} %copy.323), calls=%async_computation.3 | async-start | bytes 4194304 | tf_op jit(solution)/shard_map/all_to_all | solution.py:34
  40.8 7.5 %copy-start.9 = (s32[2]{0:T(128)}, s32[2]{0:T(128)S(1)}, u32[]{:S(2)}) copy-start(s32[2]{0:T(128)S(1)} %and_select_fusion) | copy-start | bytes 28
  48.9 43.6 %copy-start.13 = (s32[32,3]{0,1:T(4,128)S(1)}, s32[32,3]{0,1:T(4,128)}, u32[]{:S(2)}) copy-start(s32[32,3]{0,1:T(4,128)} %param.17) | copy-start | bytes 1156
  48.9 48.5 %copy-start.2 = (bf16[2,512,256]{2,1,0:T(8,128)(2,1)S(1)}, bf16[2,512,256]{2,1,0:T(8,128)(2,1)}, u32[]{:S(2)}) copy-start(bf16[2,512,256]{2,1,0:T(8,128)(2,1)} %copy-done.1) | copy-start | bytes 1572868
  86.2 73.0 %all-to-all-start.2 = ((bf16[128,64,128]{2,0,1:T(8,128)(2,1)}), bf16[128,64,128]{2,0,1:T(8,128)(2,1)}, u32[]{:S(2)}, u32[]{:S(2)}) async-start(bf16[128,64,128]{2,0,1:T(8,128)(2,1)} %copy.322), calls=%async_computation.2 | async-start | bytes 4194304 | tf_op jit(solution)/shard_map/all_to_all | solution.py:31
  90.7 68.5 %all-reduce.9.cloned.1.call-start = ((), (), s32[]{:S(2)}) async-start(), calls=%async_computation.11 | async-start | bytes 524288 | tf_op jit(solution)/shard_map/psum | solution.py:26
  94.2 2.2 copy-start.7
  98.1 7.4 %collective-permute-start = (bf16[2,128,256]{2,1,0:T(8,128)(2,1)}, bf16[2,128,256]{2,1,0:T(8,128)(2,1)S(1)}, u32[]{:S(2)}, u32[]{:S(2)}) collective-permute-start(bf16[2,128,256]{2,1,0:T(8,128)(2,1)} %get-tuple-element.248), channel_id=1, source_target_pairs={{0,4},{4,8},{8,12},{12,16},{16,20},{20,24},{24,28},{1,5},{5,9},{9,... | collective-permute-start | bytes 393224 | tf_op jit(solution)/shard_map/ppermute | solution.py:18
  100.0 7.0 %collective-permute-start.1 = (bf16[2,128,256]{2,1,0:T(8,128)(2,1)S(1)}, bf16[2,128,256]{2,1,0:T(8,128)(2,1)S(1)}, u32[]{:S(2)}, u32[]{:S(2)}) collective-permute-start(bf16[2,128,256]{2,1,0:T(8,128)(2,1)S(1)} %get-tuple-element.249), channel_id=1, source_target_pairs={{4,0},{8,4},{12,8},{16,12},{20,16},{24,20},{28,24},{5,1},{9,5},{13... | collective-permute-start | bytes 393224 | tf_op jit(solution)/shard_map/ppermute | solution.py:19
  273.8 2.1 copy-start.12
  279.1 4.8 copy-start.10
  279.1 4.8 copy-start.15
  279.1 4.9 copy-start.8
  279.1 4.9 copy-start.11
  279.1 4.9 copy-start.16
  279.1 76.3 %all-to-all-start.6 = ((bf16[16,2,128,256]{3,2,1,0:T(8,128)(2,1)}), bf16[16,2,128,256]{3,2,1,0:T(8,128)(2,1)S(1)}, u32[]{:S(2)}, u32[]{:S(2)}) async-start(bf16[16,2,128,256]{3,2,1,0:T(8,128)(2,1)} %copy.347), calls=%async_computation.6 | async-start | bytes 4194304 | tf_op jit(solution)/shard_map/all_to_all | solution.py:217
  283.9 67.3 %all-reduce.7.cloned.1.call-start = ((), (), s32[]{:S(2)}) async-start(), calls=%async_computation.10 | async-start | bytes 524288 | tf_op jit(solution)/shard_map/psum | solution.py:202
  287.8 24.5 %collective-permute-start.2 = (bf16[2,128,256]{2,1,0:T(8,128)(2,1)S(1)}, bf16[2,128,256]{2,1,0:T(8,128)(2,1)S(1)}, u32[]{:S(2)}, u32[]{:S(2)}) collective-permute-start(bf16[2,128,256]{2,1,0:T(8,128)(2,1)S(1)} %get-tuple-element.242), channel_id=1, source_target_pairs={{0,4},{4,8},{8,12},{12,16},{16,20},{20,24},{24,28},{1,5},{5,9},{9,... | collective-permute-start | bytes 393224 | tf_op jit(solution)/shard_map/ppermute | solution.py:18
  289.8 22.5 %collective-permute-start.3 = (bf16[2,128,256]{2,1,0:T(8,128)(2,1)S(1)}, bf16[2,128,256]{2,1,0:T(8,128)(2,1)S(1)}, u32[]{:S(2)}, u32[]{:S(2)}) collective-permute-start(bf16[2,128,256]{2,1,0:T(8,128)(2,1)S(1)} %get-tuple-element.243), channel_id=1, source_target_pairs={{4,0},{8,4},{12,8},{16,12},{20,16},{24,20},{28,24},{5,1},{9,5},{13... | collective-permute-start | bytes 393224 | tf_op jit(solution)/shard_map/ppermute | solution.py:19
  312.3 1.0 copy-start.5
  313.4 0.9 copy-start.6
  358.5 23.8 %copy-start.4 = (bf16[4,128,16,128]{3,2,1,0:T(8,128)(2,1)S(1)}, bf16[4,128,16,128]{3,2,1,0:T(8,128)(2,1)}, u32[]{:S(2)}) copy-start(bf16[4,128,16,128]{3,2,1,0:T(8,128)(2,1)} %get-tuple-element.93) | copy-start | bytes 6291460
  359.6 12.6 %all-to-all-start.8 = ((bf16[512,2,128]{2,1,0:T(2,128)(2,1)}), bf16[512,2,128]{2,1,0:T(2,128)(2,1)S(1)}, u32[]{:S(2)}, u32[]{:S(2)}) async-start(bf16[512,2,128]{2,1,0:T(2,128)(2,1)} %reshape_squeeze.7), calls=%async_computation.8 | async-start | bytes 524288 | tf_op jit(solution)/shard_map/all_to_all | solution.py:233
  431.9 50.7 %all-to-all-start.4 = ((bf16[512,16,128]{2,1,0:T(8,128)(2,1)}), bf16[512,16,128]{2,1,0:T(8,128)(2,1)S(1)}, u32[]{:S(2)}, u32[]{:S(2)}) async-start(bf16[512,16,128]{2,1,0:T(8,128)(2,1)} %bitcast.277), calls=%async_computation.4 | async-start | bytes 4194304 | tf_op jit(solution)/shard_map/all_to_all | solution.py:230
  435.5 1.9 copy-start
Sparse Core Ops, SparseCore 0:
  34.5 35.9 all-gather.1
  105.5 53.6 all-reduce.8
  296.9 54.2 all-reduce.6
where the time goes:
time: 497 us; the launch traced here: 491 us
  waiting for transfers between devices  195 us (39%)
  local copies, waits for them, and re-layouts  85.5 us (17%)
  blocking collectives  59.8 us (12%)
  matrix products  46.3 us (9%)
  starting transfers between devices  42.5 us (9%)
  other arithmetic  39.6 us (8%)
  between operations  19.3 us (4%)
    all_to_all x1, blocking collectives, per_device(): lax.all_to_all(query_grad_all, 'head', split_axis=0, concat_axis=1, tiled...  49.6 us
    psum x1, waiting for transfers between devices, from_root(): return lax.psum(block, axis)  44.3 us
    all_to_all x1, waiting for transfers between devices, per_device(): lax.all_to_all(out_all, 'head', split_axis=0, concat_axis=1, tiled=True)  43.2 us
    all_to_all x1, waiting for transfers between devices, per_device(): lax.all_to_all(output_gradient, 'head', split_axis=1, concat_axis=0, tile...  37.3 us
    psum x1, waiting for transfers between devices, per_device(): lax.psum(global_terms.astype(jnp.bfloat16), 'seq').astype(jnp.float32)  32.7 us
    ppermute x2, waiting for transfers between devices, padded(): before = lax.ppermute(last, axis, up)  14.3 us
    unnamed x42, local copies, waits for them, and re-layouts  13.2 us
    dot_general x4, matrix products, attend(): jnp.einsum('qkgd,tbkd->kgqtb', grad_grid, value_t, preferred_element_type...  13 us
  transfers between devices with their start and end apart: 14, of which 10 were waited for; matrix products, arithmetic and copies ran while one was open for 9% of the time, Pallas kernels for 0%

commit v1 on v0

--- a/solution.py
+++ b/solution.py
@@ -24,6 +24,19 @@
 def from_root(block, axis, owner):
     block = jnp.where(lax.axis_index(axis) == owner, block, jnp.zeros_like(block))
     return lax.psum(block, axis)
+
+
+def tree_sum(part, axis):
+    count = lax.axis_size(axis)
+    if count & (count - 1):
+        return lax.psum(part.astype(jnp.bfloat16), axis).astype(jnp.float32)
+    stride = 1
+    while stride < count:
+        pairs = [(i, i ^ stride) for i in range(count)]
+        other = lax.ppermute(part.astype(jnp.bfloat16), axis, pairs)
+        part = part + other.astype(jnp.float32)
+        stride *= 2
+    return part
 
 
 def per_device(queries, keys, values, output_gradient, global_blocks, random_blocks):
@@ -54,13 +67,6 @@
     own_global = (jnp.arange(blocks)[None, :] == global_offset[:, None]) & (
         global_owner == own_index
     )[:, None]
-    received_rows = []
-    for global_slot in range(2):
-        candidate = lax.dynamic_index_in_dim(
-            kv_tiles, global_offset[global_slot], 0, keepdims=False
-        )
-        received_rows.append(from_root(candidate, "seq", global_owner[global_slot]))
-    global_tiles = jnp.stack(received_rows)
     all_entries = (
         random_blocks.reshape(seq_count, blocks, 3)
         .transpose(0, 2, 1)
@@ -89,6 +95,7 @@
     everything = lax.all_gather(kv_pair, "seq", axis=1, tiled=True)
     tiled_all = everything.reshape(2, block_total_count, BLOCK_TOKENS, kv_width)
     random_tiles = jnp.take(tiled_all, my_entries, axis=1).transpose(1, 0, 2, 3)
+    global_tiles = jnp.take(tiled_all, global_blocks, axis=1).transpose(1, 0, 2, 3)
     random_by_block = random_tiles.reshape(3, blocks, 2, BLOCK_TOKENS, kv_width).transpose(
         1, 0, 2, 3, 4
     )
@@ -199,7 +206,7 @@
         .add(returned_rims[:, 3 * BLOCK_TOKENS :])
     )
     global_terms = jnp.sum(tile_grads[:, 3:5], axis=0)
-    global_total = lax.psum(global_terms.astype(jnp.bfloat16), "seq").astype(jnp.float32)
+    global_total = tree_sum(global_terms, "seq")
     own_weight = own_global.astype(jnp.float32)[:, :, None, None, None]
     interior = interior + jnp.sum(own_weight * global_total[:, None], axis=0)
     random_terms = (

time: 497 us -> 452 us (0.909)
  waiting for transfers between devices: 195 us -> 156 us
  other arithmetic: 39.6 us -> 34.4 us
    psum x2 -> x0, waiting for transfers between devices: 77 us -> none  [the longest x1 44.3 us: from_root(): return lax.psum(block, axis)]
    all_to_all x1, waiting for transfers between devices: 0.01 us -> 26.4 us  [per_device(): lax.all_to_all(queries, 'head', split_axis=1, concat_axis=0, tiled=True)]
    unnamed x42 -> x35, local copies, waits for them, and re-layouts: 13.2 us -> 13 us
  transfers between devices with their start and end apart: 14 -> 15, of which waited for: 10 -> 10; matrix products, arithmetic and copies ran while one was open for 9% -> 10% of each run, Pallas kernels for 0% -> 0%
where the time goes in v1:
time: 452 us; the launch traced here: 448 us
  waiting for transfers between devices  156 us (35%)
  local copies, waits for them, and re-layouts  88.8 us (20%)
  blocking collectives  61 us (13%)
  matrix products  46.6 us (10%)
  starting transfers between devices  43.5 us (10%)
  other arithmetic  34.4 us (8%)
  between operations  14.5 us (3%)
    all_to_all x1, blocking collectives, per_device(): lax.all_to_all(query_grad_all, 'head', split_axis=0, concat_axis=1, tiled...  50.4 us
    all_to_all x1, waiting for transfers between devices, per_device(): lax.all_to_all(out_all, 'head', split_axis=0, concat_axis=1, tiled=True)  43.4 us
    all_to_all x1, waiting for transfers between devices, per_device(): lax.all_to_all(output_gradient, 'head', split_axis=1, concat_axis=0, tile...  39.3 us
    all_to_all x1, waiting for transfers between devices, per_device(): lax.all_to_all(queries, 'head', split_axis=1, concat_axis=0, tiled=True)  26.4 us
    ppermute x2, waiting for transfers between devices, padded(): before = lax.ppermute(last, axis, up)  17.9 us
    unnamed x35, local copies, waits for them, and re-layouts  13 us
    dot_general x4, matrix products, attend(): jnp.einsum('qkgd,tbkd->kgqtb', grad_grid, value_t, preferred_element_type...  13 us
    dynamic_update_slice x12, local copies, waits for them, and re-layouts, per_device(): lax.scan(attend, 0, (query_loc.reshape(blocks, BLOCK_TOKENS, heads_q, hea...  12.2 us
  transfers between devices with their start and end apart: 15, of which 10 were waited for; matrix products, arithmetic and copies ran while one was open for 10% of the time, Pallas kernels for 0%

profile of v1, /device:TPU:4, one launch (start us, length us, event | category | flops | bytes accessed | tf_op | source)
XLA Modules:
  0.0 447.7 jit_solution(14881411618664810077)
XLA Ops:
  7.2 1.7 copy.305
  8.9 4.9 %all-to-all-start = ((bf16[128,8,128]{2,0,1:T(8,128)(2,1)}), bf16[128,8,128]{2,0,1:T(8,128)(2,1)S(1)}, u32[]{:S(2)}, u32[]{:S(2)}) async-start(bf16[128,8,128]{2,0,1:T(8,128)(2,1)} %copy.305), calls=%async_computation | async-start | bytes 524288 | tf_op jit(solution)/shard_map/all_to_all | solution.py:45
  13.7 1.7 copy.307
  15.4 7.2 %all-to-all-done = bf16[128,8,128]{2,0,1:T(8,128)(2,1)S(1)} async-done(((bf16[128,8,128]{2,0,1:T(8,128)(2,1)}), bf16[128,8,128]{2,0,1:T(8,128)(2,1)S(1)}, u32[]{:S(2)}, u32[]{:S(2)}) %all-to-all-start) | async-done | bytes 262176 | tf_op jit(solution)/shard_map/all_to_all | solution.py:45
  22.6 3.4 all-to-all-start.1
  26.6 6.5 %all-to-all-done.1 = bf16[128,8,128]{2,0,1:T(8,128)(2,1)S(1)} async-done(((bf16[128,8,128]{2,0,1:T(8,128)(2,1)}), bf16[128,8,128]{2,0,1:T(8,128)(2,1)S(1)}, u32[]{:S(2)}, u32[]{:S(2)}) %all-to-all-start.1) | async-done | bytes 262176 | tf_op jit(solution)/shard_map/all_to_all | solution.py:46
  34.4 2.7 copy.312
  37.1 3.7 all-to-all-start.3
  42.6 4.3 copy.311
  46.9 39.3 %all-to-all-done.3 = bf16[128,64,128]{2,0,1:T(8,128)(2,1)S(1)} async-done(((bf16[128,64,128]{2,0,1:T(8,128)(2,1)}), bf16[128,64,128]{2,0,1:T(8,128)(2,1)S(1)}, u32[]{:S(2)}, u32[]{:S(2)}) %all-to-all-start.3) | async-done | bytes 2097184 | tf_op jit(solution)/shard_map/all_to_all | solution.py:47
  86.2 4.5 %all-to-all-start.2 = ((bf16[128,64,128]{2,0,1:T(8,128)(2,1)}), bf16[128,64,128]{2,0,1:T(8,128)(2,1)}, u32[]{:S(2)}, u32[]{:S(2)}) async-start(bf16[128,64,128]{2,0,1:T(8,128)(2,1)} %copy.311), calls=%async_computation.2 | async-start | bytes 4194304 | tf_op jit(solution)/shard_map/all_to_all | solution.py:44
  92.5 1.9 collective-permute-start
  94.4 4.5 %collective-permute-start.1 = (bf16[2,128,256]{2,1,0:T(8,128)(2,1)S(1)}, bf16[2,128,256]{2,1,0:T(8,128)(2,1)S(1)}, u32[]{:S(2)}, u32[]{:S(2)}) collective-permute-start(bf16[2,128,256]{2,1,0:T(8,128)(2,1)S(1)} %get-tuple-element.229), channel_id=1, source_target_pairs={{4,0},{8,4},{12,8},{16,12},{20,16},{24,20},{28,24},{5,1},{9,5},{13... | collective-permute-start | bytes 393224 | tf_op jit(solution)/shard_map/ppermute | solution.py:19
  99.6 1.8 collective-permute-done.1
  102.4 2.6 copy.313
  105.0 2.7 gather_fusion.1
  107.7 2.8 gather_fusion
  112.1 26.4 %all-to-all-done.2 = bf16[128,64,128]{2,0,1:T(8,128)(2,1)} async-done(((bf16[128,64,128]{2,0,1:T(8,128)(2,1)}), bf16[128,64,128]{2,0,1:T(8,128)(2,1)}, u32[]{:S(2)}, u32[]{:S(2)}) %all-to-all-start.2) | async-done | bytes 2097184 | tf_op jit(solution)/shard_map/all_to_all | solution.py:44
  138.6 102.0 %while.16 = (s32[]{:T(128)}, bf16[4,128,16,128]{3,2,1,0:T(8,128)(2,1)}, bf16[4,128,16,128]{3,2,1,0:T(8,128)(2,1)}, f32[4,8,2,128,256]{3,4,1,2,0:T(8,128)}, s32[4...) while((s32[]{:T(128)}, ...), condition=%wide.region_5.6_spmd, body=%wide.region_1.5_spmd.sunk | while | flops 3264735232 | bytes 89202960 | solution.py:178
  144.9 1.9 bitcast_reduce_fusion.2
  146.8 1.7 fusion.114
  148.5 2.2 fusion.115
  150.7 1.6 multiply_reduce_fusion.3
  153.9 3.2 fusion.116
  157.9 1.5 fusion.118
  170.3 1.9 bitcast_reduce_fusion.2
  172.3 1.7 fusion.114
  174.0 2.2 fusion.115
  176.2 1.6 multiply_reduce_fusion.3
  179.3 3.2 fusion.116
  195.8 1.9 bitcast_reduce_fusion.2
  197.7 1.7 fusion.114
  199.4 2.2 fusion.115
  201.6 1.6 multiply_reduce_fusion.3
  204.8 3.2 fusion.116
  221.3 1.9 bitcast_reduce_fusion.2
  223.2 1.7 fusion.114
  224.9 2.2 fusion.115
  227.1 1.6 multiply_reduce_fusion.3
  230.3 3.2 fusion.116
  238.9 1.6 fusion.119
  240.5 1.8 slice_reduce_fusion
  242.3 9.3 %copy.320 = f32[4,8,2,128,256]{4,3,2,0,1:T(8,128)} copy(f32[4,8,2,128,256]{3,4,1,2,0:T(8,128)} %get-tuple-element.89) | data formatting | bytes 16777216 | tf_op jit(solution)/shard_map/while | solution.py:178
  251.6 2.1 slice.153
  253.7 3.6 slice_bitcast_fusion.2
  258.5 2.1 copy.336
  260.6 4.3 all-to-all-start.6
  264.9 2.2 fusion.76
  267.1 2.0 collective-permute-start.2
  269.1 4.4 collective-permute-start.3
  274.5 17.7 %collective-permute-done.2 = bf16[2,128,256]{2,1,0:T(8,128)(2,1)S(1)} collective-permute-done((bf16[2,128,256]{2,1,0:T(8,128)(2,1)S(1)}, bf16[2,128,256]{2,1,0:T(8,128)(2,1)S(1)}, u32[]{:S(2)}, u32[]{:S(2)}) %collective-permute-start.2) | collective-permute-done | bytes 131104 | tf_op jit(solution)/shard_map/ppermute | solution.py:18
  292.3 4.8 %collective-permute-done.5 = bf16[2,2,128,256]{2,3,0,1:T(8,128)(2,1)S(1)} collective-permute-done((bf16[2,2,128,256]{2,3,0,1:T(8,128)(2,1)S(1)}, bf16[2,2,128,256]{2,3,0,1:T(8,128)(2,1)S(1)}, u32[]{:S(2)}, u32[]{:S(2)}) %collective-permute-start.5) | collective-permute-done | bytes 262176 | tf_op jit(solution)/shard_map/ppermute | solution.py:36
  297.1 2.0 collective-permute-start.6
  299.2 1.6 copy.324
  301.2 6.7 %scatter-add.9 = f32[4,2,128,256]{3,0,2,1:T(4,128)} dynamic-update-slice(f32[4,2,128,256]{3,0,2,1:T(4,128)} %copy.324, f32[1,2,128,256]{3,0,2,1:T(1,128)S(1)} %copy_add_fusion.1, s32[]{:T(128)} %constant.183.clone.1, s32[]{:T(128)} %constant.170.clone.1, s32[]{:T(128)} %constant.170.clone.1, s32[]{:T(128)} %constant.170.clone.1) | dynamic-update-slice | bytes 524292 | tf_op jit(solution)/shard_map/scatter-add | solution.py:206
  310.5 3.4 fusion.50
  315.0 3.4 all-to-all-start.8
  318.5 8.4 %all-to-all-done.8 = bf16[512,2,128]{2,1,0:T(2,128)(2,1)S(1)} async-done(((bf16[512,2,128]{2,1,0:T(2,128)(2,1)}), bf16[512,2,128]{2,1,0:T(2,128)(2,1)S(1)}, u32[]{:S(2)}, u32[]{:S(2)}) %all-to-all-start.8) | async-done | bytes 262176 | tf_op jit(solution)/shard_map/all_to_all | solution.py:240
  326.9 10.7 %all_to_all.137 = bf16[512,2,128]{2,1,0:T(2,128)(2,1)S(1)} all-to-all(bf16[512,2,128]{2,1,0:T(2,128)(2,1)S(1)} %reshape_squeeze.6), channel_id=1, replica_groups=mesh['seq'=8,'head'=4] {'head'}, dimensions={0} | all-to-all | bytes 524288 | tf_op jit(solution)/shard_map/all_to_all | solution.py:239
  337.6 50.4 %all_to_all.138 = bf16[512,16,128]{2,1,0:T(8,128)(2,1)} all-to-all(bf16[512,16,128]{2,1,0:T(8,128)(2,1)S(1)} %bitcast.266), channel_id=1, replica_groups=mesh['seq'=8,'head'=4] {'head'}, dimensions={0} | all-to-all | bytes 4194304 | tf_op jit(solution)/shard_map/all_to_all | solution.py:238
  388.0 3.6 all-to-all-start.4
  393.5 2.0 copy.319
  395.5 43.4 %all-to-all-done.4 = bf16[512,16,128]{2,1,0:T(8,128)(2,1)S(1)} async-done(((bf16[512,16,128]{2,1,0:T(8,128)(2,1)}), bf16[512,16,128]{2,1,0:T(8,128)(2,1)S(1)}, u32[]{:S(2)}, u32[]{:S(2)}) %all-to-all-start.4) | async-done | bytes 2097184 | tf_op jit(solution)/shard_map/all_to_all | solution.py:237
  438.9 2.0 copy.317
  (179 shorter events, 69.7 us)
Async XLA Ops:
  8.9 13.8 %all-to-all-start = ((bf16[128,8,128]{2,0,1:T(8,128)(2,1)}), bf16[128,8,128]{2,0,1:T(8,128)(2,1)S(1)}, u32[]{:S(2)}, u32[]{:S(2)}) async-start(bf16[128,8,128]{2,0,1:T(8,128)(2,1)} %copy.305), calls=%async_computation | async-start | bytes 524288 | tf_op jit(solution)/shard_map/all_to_all | solution.py:45
  15.4 19.0 %copy-start.3 = (bf16[128,64,128]{2,1,0:T(8,128)(2,1)S(1)}, bf16[128,64,128]{2,1,0:T(8,128)(2,1)}, u32[]{:S(2)}) copy-start(bf16[128,64,128]{2,1,0:T(8,128)(2,1)} %param.15) | copy-start | bytes 6291460
  22.6 10.4 %all-to-all-start.1 = ((bf16[128,8,128]{2,0,1:T(8,128)(2,1)}), bf16[128,8,128]{2,0,1:T(8,128)(2,1)S(1)}, u32[]{:S(2)}, u32[]{:S(2)}) async-start(bf16[128,8,128]{2,0,1:T(8,128)(2,1)} %copy.307), calls=%async_computation.1 | async-start | bytes 524288 | tf_op jit(solution)/shard_map/all_to_all | solution.py:46
  26.1 78.9 %all-gather.2.cloned.1.call-start = ((), (), s32[]{:S(2)}) async-start(), calls=%async_computation.9 | async-start | bytes 4718592 | tf_op jit(solution)/shard_map/all_gather | solution.py:95
  33.5 0.8 copy-start.1
  37.0 3.8 copy-start.11
  37.1 49.2 %all-to-all-start.3 = ((bf16[128,64,128]{2,0,1:T(8,128)(2,1)}), bf16[128,64,128]{2,0,1:T(8,128)(2,1)S(1)}, u32[]{:S(2)}, u32[]{:S(2)}) async-start(bf16[128,64,128]{2,0,1:T(8,128)(2,1)} %copy.312), calls=%async_computation.3 | async-start | bytes 4194304 | tf_op jit(solution)/shard_map/all_to_all | solution.py:47
  42.6 56.4 %copy-start.6 = (s32[8,12]{1,0:T(8,128)}, s32[8,12]{1,0:T(8,128)S(1)}, u32[]{:S(2)}) copy-start(s32[8,12]{1,0:T(8,128)S(1)} %copy.332) | copy-start | bytes 1156
  46.9 43.9 %copy-start.12 = (s32[2]{0:T(128)S(1)}, s32[2]{0:T(128)}, u32[]{:S(2)}) copy-start(s32[2]{0:T(128)} %param.16) | copy-start | bytes 28
  46.9 45.5 %copy-start.2 = (bf16[2,512,256]{2,1,0:T(8,128)(2,1)S(1)}, bf16[2,512,256]{2,1,0:T(8,128)(2,1)}, u32[]{:S(2)}) copy-start(bf16[2,512,256]{2,1,0:T(8,128)(2,1)} %copy-done.1) | copy-start | bytes 1572868
  86.2 52.3 %all-to-all-start.2 = ((bf16[128,64,128]{2,0,1:T(8,128)(2,1)}), bf16[128,64,128]{2,0,1:T(8,128)(2,1)}, u32[]{:S(2)}, u32[]{:S(2)}) async-start(bf16[128,64,128]{2,0,1:T(8,128)(2,1)} %copy.311), calls=%async_computation.2 | async-start | bytes 4194304 | tf_op jit(solution)/shard_map/all_to_all | solution.py:44
  92.5 7.2 %collective-permute-start = (bf16[2,128,256]{2,1,0:T(8,128)(2,1)S(1)}, bf16[2,128,256]{2,1,0:T(8,128)(2,1)S(1)}, u32[]{:S(2)}, u32[]{:S(2)}) collective-permute-start(bf16[2,128,256]{2,1,0:T(8,128)(2,1)S(1)} %get-tuple-element.228), channel_id=1, source_target_pairs={{0,4},{4,8},{8,12},{12,16},{16,20},{20,24},{24,28},{1,5},{5,9},{9,... | collective-permute-start | bytes 393224 | tf_op jit(solution)/shard_map/ppermute | solution.py:18
  94.4 7.0 %collective-permute-start.1 = (bf16[2,128,256]{2,1,0:T(8,128)(2,1)S(1)}, bf16[2,128,256]{2,1,0:T(8,128)(2,1)S(1)}, u32[]{:S(2)}, u32[]{:S(2)}) collective-permute-start(bf16[2,128,256]{2,1,0:T(8,128)(2,1)S(1)} %get-tuple-element.229), channel_id=1, source_target_pairs={{4,0},{8,4},{12,8},{16,12},{20,16},{24,20},{28,24},{5,1},{9,5},{13... | collective-permute-start | bytes 393224 | tf_op jit(solution)/shard_map/ppermute | solution.py:19
  253.7 3.7 copy-start.10
  257.4 16.2 %collective-permute-start.4 = (bf16[2,2,128,256]{2,3,0,1:T(8,128)(2,1)S(1)}, bf16[2,2,128,256]{2,3,0,1:T(8,128)(2,1)S(1)}, u32[]{:S(2)}, u32[]{:S(2)}) collective-permute-start(bf16[2,2,128,256]{2,3,0,1:T(8,128)(2,1)S(1)} %convert_element_type.87), channel_id=1, source_target_pairs={{0,4},{4,0},{8,12},{12,8},{16,20},{20,16},{24,28},{28,24},{1,5},{5... | collective-permute-start | bytes 786440 | tf_op jit(solution)/shard_map/ppermute | solution.py:36
  260.6 50.0 %all-to-all-start.6 = ((bf16[16,2,128,256]{3,2,1,0:T(8,128)(2,1)}), bf16[16,2,128,256]{3,2,1,0:T(8,128)(2,1)S(1)}, u32[]{:S(2)}, u32[]{:S(2)}) async-start(bf16[16,2,128,256]{3,2,1,0:T(8,128)(2,1)} %copy.336), calls=%async_computation.6 | async-start | bytes 4194304 | tf_op jit(solution)/shard_map/all_to_all | solution.py:224
  264.9 9.4 %copy-start.7 = (s32[8,12]{1,0:T(8,128)S(1)}, s32[8,12]{1,0:T(8,128)}, u32[]{:S(2)}) copy-start(s32[8,12]{1,0:T(8,128)} %copy-done.6) | copy-start | bytes 1156
  264.9 9.4 %copy-start.8 = (s32[8,12]{1,0:T(8,128)S(1)}, s32[8,12]{1,0:T(8,128)}, u32[]{:S(2)}) copy-start(s32[8,12]{1,0:T(8,128)} %add_select_fusion) | copy-start | bytes 1156
  264.9 9.4 %copy-start.13 = (pred[8,12]{1,0:T(8,128)(4,1)S(1)}, pred[8,12]{1,0:T(8,128)(4,1)}, u32[]{:S(2)}) copy-start(pred[8,12]{1,0:T(8,128)(4,1)} %get-tuple-element.209) | copy-start | bytes 292
  267.1 25.2 %collective-permute-start.2 = (bf16[2,128,256]{2,1,0:T(8,128)(2,1)S(1)}, bf16[2,128,256]{2,1,0:T(8,128)(2,1)S(1)}, u32[]{:S(2)}, u32[]{:S(2)}) collective-permute-start(bf16[2,128,256]{2,1,0:T(8,128)(2,1)S(1)} %get-tuple-element.224), channel_id=1, source_target_pairs={{0,4},{4,8},{8,12},{12,16},{16,20},{20,24},{24,28},{1,5},{5,9},{9,... | collective-permute-start | bytes 393224 | tf_op jit(solution)/shard_map/ppermute | solution.py:18
  269.1 23.1 %collective-permute-start.3 = (bf16[2,128,256]{2,1,0:T(8,128)(2,1)S(1)}, bf16[2,128,256]{2,1,0:T(8,128)(2,1)S(1)}, u32[]{:S(2)}, u32[]{:S(2)}) collective-permute-start(bf16[2,128,256]{2,1,0:T(8,128)(2,1)S(1)} %get-tuple-element.225), channel_id=1, source_target_pairs={{4,0},{8,4},{12,8},{16,12},{20,16},{24,20},{28,24},{5,1},{9,5},{13... | collective-permute-start | bytes 393224 | tf_op jit(solution)/shard_map/ppermute | solution.py:19
  273.6 23.4 %collective-permute-start.5 = (bf16[2,2,128,256]{2,3,0,1:T(8,128)(2,1)S(1)}, bf16[2,2,128,256]{2,3,0,1:T(8,128)(2,1)S(1)}, u32[]{:S(2)}, u32[]{:S(2)}) collective-permute-start(bf16[2,2,128,256]{2,3,0,1:T(8,128)(2,1)S(1)} %fusion.54), channel_id=1, source_target_pairs={{0,8},{4,12},{8,0},{12,4},{16,24},{20,28},{24,16},{28,20},{1,9},{5... | collective-permute-start | bytes 786440 | tf_op jit(solution)/shard_map/ppermute | solution.py:36
  297.0 2.1 copy-start.5
  297.1 10.8 %collective-permute-start.6 = (bf16[2,2,128,256]{2,3,0,1:T(8,128)(2,1)S(1)}, bf16[2,2,128,256]{2,3,0,1:T(8,128)(2,1)}, u32[]{:S(2)}, u32[]{:S(2)}) collective-permute-start(bf16[2,2,128,256]{2,3,0,1:T(8,128)(2,1)S(1)} %fusion.57), channel_id=1, source_target_pairs={{0,16},{4,20},{8,24},{12,28},{16,0},{20,4},{24,8},{28,12},{1,17},{... | collective-permute-start | bytes 786440 | tf_op jit(solution)/shard_map/ppermute | solution.py:36
  300.9 8.4 %copy-start.9 = (f32[2,4]{1,0:T(2,128)S(1)}, f32[2,4]{1,0:T(2,128)}, u32[]{:S(2)}) copy-start(f32[2,4]{1,0:T(2,128)} %and_convert_fusion) | copy-start | bytes 100
  314.0 23.6 %copy-start.4 = (bf16[4,128,16,128]{3,2,1,0:T(8,128)(2,1)S(1)}, bf16[4,128,16,128]{3,2,1,0:T(8,128)(2,1)}, u32[]{:S(2)}) copy-start(bf16[4,128,16,128]{3,2,1,0:T(8,128)(2,1)} %get-tuple-element.88) | copy-start | bytes 6291460
  315.0 12.0 %all-to-all-start.8 = ((bf16[512,2,128]{2,1,0:T(2,128)(2,1)}), bf16[512,2,128]{2,1,0:T(2,128)(2,1)S(1)}, u32[]{:S(2)}, u32[]{:S(2)}) async-start(bf16[512,2,128]{2,1,0:T(2,128)(2,1)} %reshape_squeeze.7), calls=%async_computation.8 | async-start | bytes 524288 | tf_op jit(solution)/shard_map/all_to_all | solution.py:240
  388.0 50.9 %all-to-all-start.4 = ((bf16[512,16,128]{2,1,0:T(8,128)(2,1)}), bf16[512,16,128]{2,1,0:T(8,128)(2,1)S(1)}, u32[]{:S(2)}, u32[]{:S(2)}) async-start(bf16[512,16,128]{2,1,0:T(8,128)(2,1)} %bitcast.267), calls=%async_computation.4 | async-start | bytes 4194304 | tf_op jit(solution)/shard_map/all_to_all | solution.py:237
  391.6 1.9 copy-start
Sparse Core Ops, SparseCore 0:
  34.5 35.9 all-gather.1

commit v2 on v1

--- a/solution.py
+++ b/solution.py
@@ -39,13 +39,36 @@
     return part
 
 
-def per_device(queries, keys, values, output_gradient, global_blocks, random_blocks):
+def head_exchange(array, split_axis, concat_axis):
+    count = lax.axis_size("head")
+    own = lax.axis_index("head")
+    piece = array.shape[split_axis] // count
+    received = []
+    for shift in range(count):
+        target = (own + shift) % count
+        part = lax.dynamic_slice_in_dim(array, target * piece, piece, split_axis)
+        if shift:
+            pairs = [(i, (i + shift) % count) for i in range(count)]
+            part = lax.ppermute(part, "head", pairs)
+        received.append(part)
+    order = (own - jnp.arange(count)) % count
+    stacked = jnp.take(jnp.stack(received), order, axis=0)
+    stacked = jnp.moveaxis(stacked, 0, concat_axis)
+    shape = list(array.shape)
+    shape[split_axis] = piece
+    shape[concat_axis] *= count
+    return stacked.reshape(shape)
+
+
+def per_chunk(queries, keys, values, output_gradient, global_blocks, random_blocks, gate):
     query_loc, key_loc, value_loc, grad_loc = (
         lax.all_to_all(queries, "head", split_axis=1, concat_axis=0, tiled=True),
         lax.all_to_all(keys, "head", split_axis=1, concat_axis=0, tiled=True),
         lax.all_to_all(values, "head", split_axis=1, concat_axis=0, tiled=True),
         lax.all_to_all(output_gradient, "head", split_axis=1, concat_axis=0, tiled=True),
     )
+    if gate is not None:
+        (query_loc, grad_loc), gate = lax.optimization_barrier(((query_loc, grad_loc), gate))
     shard_len, heads_q, head_width = query_loc.shape
     heads_kv = key_loc.shape[1]
     heads_per_group = heads_q // heads_kv
@@ -233,12 +256,42 @@
     query_grad_all = query_gradient_rows.reshape(shard_len, heads_q, head_width)
     key_grad_all = kv_grad[0].reshape(shard_len, heads_kv, head_width)
     value_grad_all = kv_grad[1].reshape(shard_len, heads_kv, head_width)
-    return (
-        lax.all_to_all(out_all, "head", split_axis=0, concat_axis=1, tiled=True),
-        lax.all_to_all(query_grad_all, "head", split_axis=0, concat_axis=1, tiled=True),
-        lax.all_to_all(key_grad_all, "head", split_axis=0, concat_axis=1, tiled=True),
-        lax.all_to_all(value_grad_all, "head", split_axis=0, concat_axis=1, tiled=True),
-    )
+    return (out_all, query_grad_all, key_grad_all, value_grad_all), gate
+
+
+def head_part(array, chunks, chunk):
+    tokens, heads, width = array.shape
+    lanes = chunks * lax.axis_size("head")
+    grid = array.reshape(tokens, lanes // chunks, chunks, heads // lanes, width)
+    return grid[:, :, chunk].reshape(tokens, heads // chunks, width)
+
+
+def head_join(parts):
+    tokens, heads, width = parts[0].shape
+    lanes = lax.axis_size("head")
+    grid = jnp.stack([p.reshape(tokens, lanes, heads // lanes, width) for p in parts], axis=2)
+    return grid.reshape(tokens, heads * len(parts), width)
+
+
+def per_device(queries, keys, values, output_gradient, global_blocks, random_blocks):
+    chunks = max(1, keys.shape[1] // lax.axis_size("head"))
+    results = []
+    gate = None
+    for chunk in range(chunks):
+        local, passed = per_chunk(
+            head_part(queries, chunks, chunk),
+            head_part(keys, chunks, chunk),
+            head_part(values, chunks, chunk),
+            head_part(output_gradient, chunks, chunk),
+            global_blocks,
+            random_blocks,
+            gate,
+        )
+        if passed is not None:
+            results.append(tuple(head_exchange(x, 0, 1) for x in passed))
+        gate = local
+    results.append(tuple(head_exchange(x, 0, 1) for x in gate))
+    return tuple(head_join([r[i] for r in results]) for i in range(4))
 
 
 def solution(mesh):

time: 452 us -> 601 us (1.33)
  starting transfers between devices: 43.5 us -> 126 us
  local copies, waits for them, and re-layouts: 88.8 us -> 168 us
  blocking collectives: 61 us -> 8.43 us
  waiting for transfers between devices: 156 us -> 115 us
  matrix products: 46.6 us -> 86.2 us
  other arithmetic: 34.4 us -> 67.2 us
    all_to_all x7 -> x9, waiting for transfers between devices: 131 us -> 64.8 us  [the longest x2 33.8 us: per_chunk(): lax.all_to_all(queries, 'head', split_axis=1, concat_axis=0, tiled=True)]
    ppermute x0 -> x24, starting transfers between devices: none -> 58.4 us  [head_exchange(): part = lax.ppermute(part, 'head', pairs)]
    all_to_all x2 -> x1, blocking collectives: 61 us -> 8.43 us  [per_chunk(): lax.all_to_all(values, 'head', split_axis=1, concat_axis=0, tiled=True)]
    another operation x6 -> x30, local copies, waits for them, and re-layouts: 1.21 us -> 44.4 us  [the longest x1 0.77 us: per_device(): value_grad_all = kv_grad[1].reshape(shard_len, heads_kv, head_width)]
    ppermute x0 -> x24, waiting for transfers between devices: none -> 35 us  [head_exchange(): part = lax.ppermute(part, 'head', pairs)]
    another operation x3 -> x28, other arithmetic: 2.18 us -> 22.8 us
    ppermute x2 -> x4, waiting for transfers between devices: 17.9 us -> 0.01 us  [padded(): before = lax.ppermute(last, axis, up)]
    dot_general x4 -> x8, matrix products: 13 us -> 28.4 us  [attend(): jnp.einsum('qkgd,tbkd->kgqtb', grad_grid, value_t, preferred_element_type...]
  transfers between devices with their start and end apart: 15 -> 49, of which waited for: 10 -> 16; matrix products, arithmetic and copies ran while one was open for 10% -> 15% of each run, Pallas kernels for 0% -> 0%
where the time goes in v2:
time: 601 us; the launch traced here: 591 us
  local copies, waits for them, and re-layouts  168 us (28%)
  starting transfers between devices  126 us (21%)
  waiting for transfers between devices  115 us (19%)
  matrix products  86.2 us (14%)
  other arithmetic  67.2 us (11%)
  between operations  15.5 us (3%)
  blocking collectives  8.43 us (1%)
  loops' own time  6.06 us (1%)
    ppermute x24, starting transfers between devices, head_exchange(): part = lax.ppermute(part, 'head', pairs)  58.4 us
    another operation x20, local copies, waits for them, and re-layouts  35.9 us
    ppermute x24, waiting for transfers between devices, head_exchange(): part = lax.ppermute(part, 'head', pairs)  35 us
    all_to_all x2, waiting for transfers between devices, per_chunk(): lax.all_to_all(queries, 'head', split_axis=1, concat_axis=0, tiled=True)  33.8 us
    dot_general x8, matrix products, attend(): jnp.einsum('qkgd,tbkd->kgqtb', grad_grid, value_t, preferred_element_type...  28.4 us
    dot_general x8, matrix products, attend(): jnp.einsum('kgqtb,qkgd->tbkd', prob_low, grad_grid, preferred_element_typ...  17.2 us
    all_to_all x2, waiting for transfers between devices, per_chunk(): lax.all_to_all(output_gradient, 'head', split_axis=1, concat_axis=0, tile...  17.1 us
    dynamic_slice x24, local copies, waits for them, and re-layouts, per_chunk(): lax.scan(attend, 0, (query_loc.reshape(blocks, BLOCK_TOKENS, heads_q, hea...  16.8 us
  transfers between devices with their start and end apart: 49, of which 16 were waited for; matrix products, arithmetic and copies ran while one was open for 15% of the time, Pallas kernels for 0%

profile of v2, /device:TPU:4, one launch (start us, length us, event | category | flops | bytes accessed | tf_op | source)
XLA Modules:
  0.0 591.4 jit_solution(5233339170795102321)
XLA Ops:
  9.5 4.9 all-to-all-start.2
  15.9 4.5 all-to-all-done.2
  20.4 8.4 %all_to_all.136 = bf16[128,4,128]{2,0,1:T(8,128)(2,1)S(1)} all-to-all(bf16[128,4,128]{2,0,1:T(8,128)(2,1)S(1)} %bitcast.819), channel_id=1, replica_groups=mesh['seq'=8,'head'=4] {'head'}, dimensions={1} | all-to-all | bytes 262144 | tf_op jit(solution)/shard_map/all_to_all | solution.py:67
  30.3 3.3 all-to-all-start.7
  34.3 5.2 all-to-all-done.7
  39.5 4.0 all-to-all-start.8
  45.3 4.2 all-to-all-done.8
  49.5 4.2 all-to-all-start.4
  55.4 20.1 %all-to-all-done.4 = bf16[128,32,128]{2,0,1:T(8,128)(2,1)} async-done(((bf16[128,32,128]{2,0,1:T(8,128)(2,1)}), bf16[128,32,128]{2,0,1:T(8,128)(2,1)}, u32[]{:S(2)}, u32[]{:S(2)}) %all-to-all-start.4) | async-done | bytes 1048608 | tf_op jit(solution)/shard_map/all_to_all | solution.py:65
  75.6 3.5 all-to-all-start
  89.1 13.7 %all-to-all-done = bf16[128,32,128]{2,0,1:T(8,128)(2,1)S(1)} async-done(((bf16[128,32,128]{2,0,1:T(8,128)(2,1)}), bf16[128,32,128]{2,0,1:T(8,128)(2,1)S(1)}, u32[]{:S(2)}, u32[]{:S(2)}) %all-to-all-start) | async-done | bytes 1048608 | tf_op jit(solution)/shard_map/all_to_all | solution.py:65
  102.8 3.5 all-to-all-start.1
  114.5 17.1 %all-to-all-done.1 = bf16[128,32,128]{2,0,1:T(8,128)(2,1)S(1)} async-done(((bf16[128,32,128]{2,0,1:T(8,128)(2,1)}), bf16[128,32,128]{2,0,1:T(8,128)(2,1)S(1)}, u32[]{:S(2)}, u32[]{:S(2)}) %all-to-all-start.1) | async-done | bytes 1048608 | tf_op jit(solution)/shard_map/all_to_all | solution.py:68
  131.5 4.3 all-to-all-start.5
  138.9 4.5 collective-permute-start.1
  146.2 4.7 collective-permute-start.11
  157.8 2.3 gather_fusion
  160.1 2.3 gather_fusion.3
  168.9 2.5 broadcast.440.clone
  173.7 89.8 %while.32 = (s32[]{:T(128)}, bf16[4,128,8,128]{3,2,1,0:T(8,128)(2,1)}, bf16[4,128,8,128]{3,2,1,0:T(8,128)(2,1)}, f32[4,8,2,128,128]{3,4,1,2,0:T(8,128)}, s32[4]{...) while((s32[]{:T(128)}, ...), condition=%wide.region_5.8_spmd, body=%wide.region_1.7_spmd.sunk | while | flops 1632367616 | bytes 61382416 | solution.py:201
  181.3 2.8 copy.654
  187.9 3.6 fusion.183
  203.7 2.8 copy.654
  210.4 3.5 fusion.183
  226.2 2.8 copy.654
  232.8 3.6 fusion.183
  248.6 2.8 copy.654
  255.2 3.6 fusion.183
  264.7 5.4 copy.496
  273.7 2.3 collective-permute-start.2
  276.0 4.5 collective-permute-start.3
  282.6 6.4 %all-to-all-start.6 = ((bf16[16,2,128,128]{3,2,1,0:T(8,128)(2,1)}), bf16[16,2,128,128]{3,2,1,0:T(8,128)(2,1)S(1)}, u32[]{:S(2)}, u32[]{:S(2)}) async-start(bf16[16,2,128,128]{3,2,1,0:T(8,128)(2,1)} %copy.513), calls=%async_computation.6 | async-start | bytes 2097152 | tf_op jit(solution)/shard_map/all_to_all | solution.py:247
  289.7 3.1 scatter-add.15
  292.8 11.7 %collective-permute-done.6 = bf16[2,2,128,128]{2,3,0,1:T(8,128)(2,1)S(1)} collective-permute-done((bf16[2,2,128,128]{2,3,0,1:T(8,128)(2,1)S(1)}, bf16[2,2,128,128]{2,3,0,1:T(8,128)(2,1)S(1)}, u32[]{:S(2)}, u32[]{:S(2)}) %collective-permute-start.6) | collective-permute-done | bytes 131104 | tf_op jit(solution)/shard_map/ppermute | solution.py:36
  307.3 2.5 broadcast.440
  312.1 109.1 %while.33 = (s32[]{:T(128)}, bf16[4,128,8,128]{3,2,1,0:T(8,128)(2,1)}, bf16[4,128,8,128]{3,2,1,0:T(8,128)(2,1)}, f32[4,8,2,128,128]{3,4,1,2,0:T(8,128)}, s32[4]{...) while((s32[]{:T(128)}, ...), condition=%wide.region_13.17_spmd, body=%wide.region_9.16_spmd.sunk | while | flops 1632367616 | bytes 79207432 | solution.py:201
  324.0 3.6 fusion.196
  330.5 2.8 copy.663
  351.2 3.6 fusion.196
  357.8 2.8 copy.663
  378.5 3.6 fusion.196
  385.0 2.8 copy.663
  405.8 3.6 fusion.196
  412.3 2.8 copy.663
  422.5 5.4 copy.529
  439.5 2.7 collective-permute-start.24
  444.1 6.4 %all-to-all-start.9 = ((bf16[16,2,128,128]{3,2,1,0:T(8,128)(2,1)}), bf16[16,2,128,128]{3,2,1,0:T(8,128)(2,1)}, u32[]{:S(2)}, u32[]{:S(2)}) async-start(bf16[16,2,128,128]{3,2,1,0:T(8,128)(2,1)} %copy.538), calls=%async_computation.9 | async-start | bytes 2097152 | tf_op jit(solution)/shard_map/all_to_all | solution.py:247
  456.1 2.3 collective-permute-start.34
  460.5 2.5 collective-permute-start.25
  466.2 2.8 collective-permute-start.9
  470.5 3.1 scatter-add.19
  474.9 2.9 collective-permute-start.20
  478.5 7.1 %collective-permute-done.8 = bf16[128,8,128]{2,1,0:T(8,128)(2,1)} collective-permute-done((bf16[128,8,128]{2,1,0:T(8,128)(2,1)S(1)}, bf16[128,8,128]{2,1,0:T(8,128)(2,1)}, u32[]{:S(2)}, u32[]{:S(2)}) %collective-permute-start.8) | collective-permute-done | bytes 262176 | tf_op jit(solution)/shard_map/ppermute | solution.py:52
  485.6 14.3 %collective-permute-start.12 = (bf16[128,8,128]{2,1,0:T(8,128)(2,1)}, bf16[128,8,128]{2,1,0:T(8,128)(2,1)}, u32[]{:S(2)}, u32[]{:S(2)}) collective-permute-start(bf16[128,8,128]{2,1,0:T(8,128)(2,1)} %get-tuple-element.457), channel_id=1, source_target_pairs={{0,1},{1,2},{2,3},{3,0},{4,5},{5,6},{6,7},{7,4},{8,9},{9,10},{10,1... | collective-permute-start | bytes 786440 | tf_op jit(solution)/shard_map/ppermute | solution.py:52
  499.9 3.8 collective-permute-start.13
  506.7 11.5 %collective-permute-done.19 = bf16[128,8,128]{2,1,0:T(8,128)(2,1)S(1)} collective-permute-done((bf16[128,8,128]{2,1,0:T(8,128)(2,1)}, bf16[128,8,128]{2,1,0:T(8,128)(2,1)S(1)}, u32[]{:S(2)}, u32[]{:S(2)}) %collective-permute-start.19) | collective-permute-done | bytes 262176 | tf_op jit(solution)/shard_map/ppermute | solution.py:52
  518.1 4.6 collective-permute-start.15
  528.1 3.3 collective-permute-start.16
  533.6 7.1 %collective-permute-done.13 = bf16[128,8,128]{2,1,0:T(8,128)(2,1)} collective-permute-done((bf16[128,8,128]{2,1,0:T(8,128)(2,1)}, bf16[128,8,128]{2,1,0:T(8,128)(2,1)}, u32[]{:S(2)}, u32[]{:S(2)}) %collective-permute-start.13) | collective-permute-done | bytes 262176 | tf_op jit(solution)/shard_map/ppermute | solution.py:52
  540.7 2.3 pad_maximum_fusion.5
  545.0 6.9 %collective-permute-done.16 = bf16[128,8,128]{2,1,0:T(8,128)(2,1)} collective-permute-done((bf16[128,8,128]{2,1,0:T(8,128)(2,1)}, bf16[128,8,128]{2,1,0:T(8,128)(2,1)}, u32[]{:S(2)}, u32[]{:S(2)}) %collective-permute-start.16) | collective-permute-done | bytes 262176 | tf_op jit(solution)/shard_map/ppermute | solution.py:52
  552.0 2.3 pad_maximum_fusion.6
  554.2 2.9 gather_fusion.6
  566.8 5.5 collective-permute-start.35
  (466 shorter events, 266.2 us)
Async XLA Ops:
  7.2 36.3 %copy-start.9 = (bf16[128,64,128]{2,1,0:T(8,128)(2,1)S(1)}, bf16[128,64,128]{2,1,0:T(8,128)(2,1)}, u32[]{:S(2)}) copy-start(bf16[128,64,128]{2,1,0:T(8,128)(2,1)} %param.26) | copy-start | bytes 6291460
  9.5 10.9 %all-to-all-start.2 = ((bf16[128,4,128]{2,0,1:T(8,128)(2,1)}), bf16[128,4,128]{2,0,1:T(8,128)(2,1)S(1)}, u32[]{:S(2)}, u32[]{:S(2)}) async-start(bf16[128,4,128]{2,0,1:T(8,128)(2,1)} %bitcast.637), calls=%async_computation.2 | async-start | bytes 262144 | tf_op jit(solution)/shard_map/all_to_all | solution.py:66
  14.4 143.4 %all-gather.3.cloned.1.call-start = ((), (), s32[]{:S(2)}) async-start(), calls=%async_computation.10 | async-start | bytes 2359296 | tf_op jit(solution)/shard_map/all_gather | solution.py:118
  30.3 9.2 %all-to-all-start.7 = ((bf16[128,4,128]{2,0,1:T(8,128)(2,1)}), bf16[128,4,128]{2,0,1:T(8,128)(2,1)S(1)}, u32[]{:S(2)}, u32[]{:S(2)}) async-start(bf16[128,4,128]{2,0,1:T(8,128)(2,1)} %bitcast.635), calls=%async_computation.7 | async-start | bytes 262144 | tf_op jit(solution)/shard_map/all_to_all | solution.py:66
  39.5 104.0 %copy-start.10 = (bf16[128,4,128]{2,0,1:T(8,128)(2,1)}, bf16[128,4,128]{2,0,1:T(8,128)(2,1)S(1)}, u32[]{:S(2)}) copy-start(bf16[128,4,128]{2,0,1:T(8,128)(2,1)S(1)} %all-to-all-done.7) | copy-start | bytes 393220
  39.5 9.9 %all-to-all-start.8 = ((bf16[128,4,128]{2,0,1:T(8,128)(2,1)}), bf16[128,4,128]{2,0,1:T(8,128)(2,1)}, u32[]{:S(2)}, u32[]{:S(2)}) async-start(bf16[128,4,128]{2,0,1:T(8,128)(2,1)} %bitcast.634), calls=%async_computation.8 | async-start | bytes 262144 | tf_op jit(solution)/shard_map/all_to_all | solution.py:67
  49.5 26.1 %all-to-all-start.4 = ((bf16[128,32,128]{2,0,1:T(8,128)(2,1)}), bf16[128,32,128]{2,0,1:T(8,128)(2,1)}, u32[]{:S(2)}, u32[]{:S(2)}) async-start(bf16[128,32,128]{2,0,1:T(8,128)(2,1)} %bitcast.135), calls=%async_computation.4 | async-start | bytes 2097152 | tf_op jit(solution)/shard_map/all_to_all | solution.py:65
  75.6 27.2 %all-to-all-start = ((bf16[128,32,128]{2,0,1:T(8,128)(2,1)}), bf16[128,32,128]{2,0,1:T(8,128)(2,1)S(1)}, u32[]{:S(2)}, u32[]{:S(2)}) async-start(bf16[128,32,128]{2,0,1:T(8,128)(2,1)} %bitcast.105), calls=%async_computation | async-start | bytes 2097152 | tf_op jit(solution)/shard_map/all_to_all | solution.py:65
  79.1 81.0 %all-gather.5.cloned.1.call-start = ((), (), s32[]{:S(2)}) async-start(), calls=%async_computation.11 | async-start | bytes 2359296 | tf_op jit(solution)/shard_map/all_gather | solution.py:118
  102.8 28.8 %all-to-all-start.1 = ((bf16[128,32,128]{2,0,1:T(8,128)(2,1)}), bf16[128,32,128]{2,0,1:T(8,128)(2,1)S(1)}, u32[]{:S(2)}, u32[]{:S(2)}) async-start(bf16[128,32,128]{2,0,1:T(8,128)(2,1)} %bitcast.111), calls=%async_computation.1 | async-start | bytes 2097152 | tf_op jit(solution)/shard_map/all_to_all | solution.py:68
  131.5 37.3 %all-to-all-start.5 = ((bf16[128,32,128]{0,2,1:T(8,128)(2,1)}), bf16[128,32,128]{0,2,1:T(8,128)(2,1)}, u32[]{:S(2)}, u32[]{:S(2)}) async-start(bf16[128,32,128]{0,2,1:T(8,128)(2,1)} %bitcast.138), calls=%async_computation.5 | async-start | bytes 2097152 | tf_op jit(solution)/shard_map/all_to_all | solution.py:68
  136.4 168.3 %copy-start.26 = (f32[2,4]{1,0:T(2,128)}, f32[2,4]{1,0:T(2,128)S(1)}, u32[]{:S(2)}) copy-start(f32[2,4]{1,0:T(2,128)S(1)} %and_convert_fusion) | copy-start | bytes 100
  137.0 13.9 %collective-permute-start = (bf16[2,128,128]{2,1,0:T(8,128)(2,1)S(1)}, bf16[2,128,128]{2,1,0:T(8,128)(2,1)S(1)}, u32[]{:S(2)}, u32[]{:S(2)}) collective-permute-start(bf16[2,128,128]{2,1,0:T(8,128)(2,1)S(1)} %get-tuple-element.466), channel_id=1, source_target_pairs={{0,4},{4,8},{8,12},{12,16},{16,20},{20,24},{24,28},{1,5},{5,9},{9,... | collective-permute-start | bytes 196616 | tf_op jit(solution)/shard_map/ppermute | solution.py:18
  138.9 12.0 %collective-permute-start.1 = (bf16[2,128,128]{2,1,0:T(8,128)(2,1)S(1)}, bf16[2,128,128]{2,1,0:T(8,128)(2,1)S(1)}, u32[]{:S(2)}, u32[]{:S(2)}) collective-permute-start(bf16[2,128,128]{2,1,0:T(8,128)(2,1)S(1)} %get-tuple-element.467), channel_id=1, source_target_pairs={{4,0},{8,4},{12,8},{16,12},{20,16},{24,20},{28,24},{5,1},{9,5},{13... | collective-permute-start | bytes 196616 | tf_op jit(solution)/shard_map/ppermute | solution.py:19
  144.3 6.7 %collective-permute-start.10 = (bf16[2,128,128]{2,1,0:T(8,128)(2,1)S(1)}, bf16[2,128,128]{2,1,0:T(8,128)(2,1)S(1)}, u32[]{:S(2)}, u32[]{:S(2)}) collective-permute-start(bf16[2,128,128]{2,1,0:T(8,128)(2,1)S(1)} %get-tuple-element.472), channel_id=1, source_target_pairs={{0,4},{4,8},{8,12},{12,16},{16,20},{20,24},{24,28},{1,5},{5,9},{9,... | collective-permute-start | bytes 196616 | tf_op jit(solution)/shard_map/ppermute | solution.py:18
  146.2 6.4 %collective-permute-start.11 = (bf16[2,128,128]{2,1,0:T(8,128)(2,1)S(1)}, bf16[2,128,128]{2,1,0:T(8,128)(2,1)S(1)}, u32[]{:S(2)}, u32[]{:S(2)}) collective-permute-start(bf16[2,128,128]{2,1,0:T(8,128)(2,1)S(1)} %get-tuple-element.473), channel_id=1, source_target_pairs={{4,0},{8,4},{12,8},{16,12},{20,16},{24,20},{28,24},{5,1},{9,5},{13... | collective-permute-start | bytes 196616 | tf_op jit(solution)/shard_map/ppermute | solution.py:19
  273.2 7.3 %collective-permute-start.4 = (bf16[2,2,128,128]{2,3,0,1:T(8,128)(2,1)S(1)}, bf16[2,2,128,128]{2,3,0,1:T(8,128)(2,1)S(1)}, u32[]{:S(2)}, u32[]{:S(2)}) collective-permute-start(bf16[2,2,128,128]{2,3,0,1:T(8,128)(2,1)S(1)} %convert_element_type.193), channel_id=1, source_target_pairs={{0,4},{4,0},{8,12},{12,8},{16,20},{20,16},{24,28},{28,24},{1,5},{5... | collective-permute-start | bytes 393224 | tf_op jit(solution)/shard_map/ppermute | solution.py:36
  273.7 15.2 %copy-start.15 = (bf16[2,2,128,128]{3,2,1,0:T(8,128)(2,1)S(1)}, bf16[2,2,128,128]{3,2,1,0:T(8,128)(2,1)}, u32[]{:S(2)}) copy-start(bf16[2,2,128,128]{3,2,1,0:T(8,128)(2,1)} %get-tuple-element.503) | copy-start | bytes 393220
  273.7 15.4 %collective-permute-start.2 = (bf16[2,128,128]{2,1,0:T(8,128)(2,1)S(1)}, bf16[2,128,128]{2,1,0:T(8,128)(2,1)S(1)}, u32[]{:S(2)}, u32[]{:S(2)}) collective-permute-start(bf16[2,128,128]{2,1,0:T(8,128)(2,1)S(1)} %get-tuple-element.460), channel_id=1, source_target_pairs={{0,4},{4,8},{8,12},{12,16},{16,20},{20,24},{24,28},{1,5},{5,9},{9,... | collective-permute-start | bytes 196616 | tf_op jit(solution)/shard_map/ppermute | solution.py:18
  276.0 13.2 %collective-permute-start.3 = (bf16[2,128,128]{2,1,0:T(8,128)(2,1)S(1)}, bf16[2,128,128]{2,1,0:T(8,128)(2,1)S(1)}, u32[]{:S(2)}, u32[]{:S(2)}) collective-permute-start(bf16[2,128,128]{2,1,0:T(8,128)(2,1)S(1)} %get-tuple-element.461), channel_id=1, source_target_pairs={{4,0},{8,4},{12,8},{16,12},{20,16},{24,20},{28,24},{5,1},{9,5},{13... | collective-permute-start | bytes 196616 | tf_op jit(solution)/shard_map/ppermute | solution.py:19
  280.6 8.4 %collective-permute-start.5 = (bf16[2,2,128,128]{2,3,0,1:T(8,128)(2,1)S(1)}, bf16[2,2,128,128]{2,3,0,1:T(8,128)(2,1)S(1)}, u32[]{:S(2)}, u32[]{:S(2)}) collective-permute-start(bf16[2,2,128,128]{2,3,0,1:T(8,128)(2,1)S(1)} %fusion.89), channel_id=1, source_target_pairs={{0,8},{4,12},{8,0},{12,4},{16,24},{20,28},{24,16},{28,20},{1,9},{5... | collective-permute-start | bytes 393224 | tf_op jit(solution)/shard_map/ppermute | solution.py:36
  282.6 22.3 %all-to-all-start.6 = ((bf16[16,2,128,128]{3,2,1,0:T(8,128)(2,1)}), bf16[16,2,128,128]{3,2,1,0:T(8,128)(2,1)S(1)}, u32[]{:S(2)}, u32[]{:S(2)}) async-start(bf16[16,2,128,128]{3,2,1,0:T(8,128)(2,1)} %copy.513), calls=%async_computation.6 | async-start | bytes 2097152 | tf_op jit(solution)/shard_map/all_to_all | solution.py:247
  289.0 15.5 %collective-permute-start.6 = (bf16[2,2,128,128]{2,3,0,1:T(8,128)(2,1)S(1)}, bf16[2,2,128,128]{2,3,0,1:T(8,128)(2,1)S(1)}, u32[]{:S(2)}, u32[]{:S(2)}) collective-permute-start(bf16[2,2,128,128]{2,3,0,1:T(8,128)(2,1)S(1)} %fusion.99), channel_id=1, source_target_pairs={{0,16},{4,20},{8,24},{12,28},{16,0},{20,4},{24,8},{28,12},{1,17},{... | collective-permute-start | bytes 393224 | tf_op jit(solution)/shard_map/ppermute | solution.py:36
  428.0 14.2 %copy-start.29 = (s32[12]{0:T(128)S(1)}, s32[12]{0:T(128)}, u32[]{:S(2)}) copy-start(s32[12]{0:T(128)} %fusion.129) | copy-start | bytes 148
  431.7 22.8 %collective-permute-start.21 = (bf16[128,1,128]{2,0,1:T(8,128)(2,1)}, bf16[128,1,128]{2,0,1:T(8,128)(2,1)}, u32[]{:S(2)}, u32[]{:S(2)}) collective-permute-start(bf16[128,1,128]{2,0,1:T(8,128)(2,1)} %get-tuple-element.485), channel_id=1, source_target_pairs={{0,1},{1,2},{2,3},{3,0},{4,5},{5,6},{6,7},{7,4},{8,9},{9,10},{10,1... | collective-permute-start | bytes 98312 | tf_op jit(solution)/shard_map/ppermute | solution.py:52
  433.7 21.5 %collective-permute-start.22 = (bf16[128,1,128]{2,0,1:T(8,128)(2,1)}, bf16[128,1,128]{2,0,1:T(8,128)(2,1)}, u32[]{:S(2)}, u32[]{:S(2)}) collective-permute-start(bf16[128,1,128]{2,0,1:T(8,128)(2,1)} %get-tuple-element.484), channel_id=1, source_target_pairs={{0,2},{1,3},{2,0},{3,1},{4,6},{5,7},{6,4},{7,5},{8,10},{9,11},{10,... | collective-permute-start | bytes 98312 | tf_op jit(solution)/shard_map/ppermute | solution.py:52
  435.6 20.5 %collective-permute-start.23 = (bf16[128,1,128]{2,0,1:T(8,128)(2,1)}, bf16[128,1,128]{2,0,1:T(8,128)(2,1)}, u32[]{:S(2)}, u32[]{:S(2)}) collective-permute-start(bf16[128,1,128]{2,0,1:T(8,128)(2,1)} %get-tuple-element.483), channel_id=1, source_target_pairs={{0,3},{1,0},{2,1},{3,2},{4,7},{5,4},{6,5},{7,6},{8,11},{9,8},{10,9... | collective-permute-start | bytes 98312 | tf_op jit(solution)/shard_map/ppermute | solution.py:52
  437.8 35.7 %collective-permute-start.26 = (bf16[2,2,128,128]{2,3,0,1:T(8,128)(2,1)}, bf16[2,2,128,128]{2,3,0,1:T(8,128)(2,1)S(1)}, u32[]{:S(2)}, u32[]{:S(2)}) collective-permute-start(bf16[2,2,128,128]{2,3,0,1:T(8,128)(2,1)} %convert_element_type.207), channel_id=1, source_target_pairs={{0,4},{4,0},{8,12},{12,8},{16,20},{20,16},{24,28},{28,24},{1,5},{5... | collective-permute-start | bytes 393224 | tf_op jit(solution)/shard_map/ppermute | solution.py:36
  437.8 12.7 %copy-start.6 = (bf16[4,128,8,128]{3,2,1,0:T(8,128)(2,1)S(1)}, bf16[4,128,8,128]{3,2,1,0:T(8,128)(2,1)}, u32[]{:S(2)}) copy-start(bf16[4,128,8,128]{3,2,1,0:T(8,128)(2,1)} %get-tuple-element.180) | copy-start | bytes 3145732
  439.5 26.7 %collective-permute-start.24 = (bf16[2,128,128]{2,1,0:T(8,128)(2,1)}, bf16[2,128,128]{2,1,0:T(8,128)(2,1)}, u32[]{:S(2)}, u32[]{:S(2)}) collective-permute-start(bf16[2,128,128]{2,1,0:T(8,128)(2,1)} %get-tuple-element.458), channel_id=1, source_target_pairs={{0,4},{4,8},{8,12},{12,16},{16,20},{20,24},{24,28},{1,5},{5,9},{9,... | collective-permute-start | bytes 196616 | tf_op jit(solution)/shard_map/ppermute | solution.py:18
  444.1 120.4 %all-to-all-start.9 = ((bf16[16,2,128,128]{3,2,1,0:T(8,128)(2,1)}), bf16[16,2,128,128]{3,2,1,0:T(8,128)(2,1)}, u32[]{:S(2)}, u32[]{:S(2)}) async-start(bf16[16,2,128,128]{3,2,1,0:T(8,128)(2,1)} %copy.538), calls=%async_computation.9 | async-start | bytes 2097152 | tf_op jit(solution)/shard_map/all_to_all | solution.py:247
  452.5 10.6 %copy-start.22 = (bf16[128,8,128]{2,1,0:T(8,128)(2,1)S(1)}, bf16[128,8,128]{2,1,0:T(8,128)(2,1)}, u32[]{:S(2)}) copy-start(bf16[128,8,128]{2,1,0:T(8,128)(2,1)} %get-tuple-element.453) | copy-start | bytes 786436
  452.5 11.2 %copy-start.21 = (bf16[128,8,128]{2,1,0:T(8,128)(2,1)S(1)}, bf16[128,8,128]{2,1,0:T(8,128)(2,1)}, u32[]{:S(2)}) copy-start(bf16[128,8,128]{2,1,0:T(8,128)(2,1)} %get-tuple-element.452) | copy-start | bytes 786436
  452.5 13.7 %copy-start.20 = (bf16[128,8,128]{2,1,0:T(8,128)(2,1)S(1)}, bf16[128,8,128]{2,1,0:T(8,128)(2,1)}, u32[]{:S(2)}) copy-start(bf16[128,8,128]{2,1,0:T(8,128)(2,1)} %get-tuple-element.451) | copy-start | bytes 786436
  453.5 50.2 %copy-start.13 = (bf16[1,128,8,128]{3,2,1,0:T(8,128)(2,1)S(1)}, bf16[1,128,8,128]{3,2,1,0:T(8,128)(2,1)}, u32[]{:S(2)}) copy-start(bf16[1,128,8,128]{3,2,1,0:T(8,128)(2,1)} %get-tuple-element.450) | copy-start | bytes 786436
  454.5 6.0 %collective-permute-start.32 = (bf16[128,1,128]{2,0,1:T(8,128)(2,1)S(1)}, bf16[128,1,128]{2,0,1:T(8,128)(2,1)S(1)}, u32[]{:S(2)}, u32[]{:S(2)}) collective-permute-start(bf16[128,1,128]{2,0,1:T(8,128)(2,1)S(1)} %get-tuple-element.477), channel_id=1, source_target_pairs={{0,1},{1,2},{2,3},{3,0},{4,5},{5,6},{6,7},{7,4},{8,9},{9,10},{10,1... | collective-permute-start | bytes 98312 | tf_op jit(solution)/shard_map/ppermute | solution.py:52
  455.2 7.9 %collective-permute-start.33 = (bf16[128,1,128]{2,0,1:T(8,128)(2,1)S(1)}, bf16[128,1,128]{2,0,1:T(8,128)(2,1)S(1)}, u32[]{:S(2)}, u32[]{:S(2)}) collective-permute-start(bf16[128,1,128]{2,0,1:T(8,128)(2,1)S(1)} %get-tuple-element.476), channel_id=1, source_target_pairs={{0,2},{1,3},{2,0},{3,1},{4,6},{5,7},{6,4},{7,5},{8,10},{9,11},{10,... | collective-permute-start | bytes 98312 | tf_op jit(solution)/shard_map/ppermute | solution.py:52
  456.1 7.5 %collective-permute-start.34 = (bf16[128,1,128]{2,0,1:T(8,128)(2,1)S(1)}, bf16[128,1,128]{2,0,1:T(8,128)(2,1)S(1)}, u32[]{:S(2)}, u32[]{:S(2)}) collective-permute-start(bf16[128,1,128]{2,0,1:T(8,128)(2,1)S(1)} %get-tuple-element.475), channel_id=1, source_target_pairs={{0,3},{1,0},{2,1},{3,2},{4,7},{5,4},{6,5},{7,6},{8,11},{9,8},{10,9... | collective-permute-start | bytes 98312 | tf_op jit(solution)/shard_map/ppermute | solution.py:52
  460.5 8.5 %collective-permute-start.25 = (bf16[2,128,128]{2,1,0:T(8,128)(2,1)S(1)}, bf16[2,128,128]{2,1,0:T(8,128)(2,1)S(1)}, u32[]{:S(2)}, u32[]{:S(2)}) collective-permute-start(bf16[2,128,128]{2,1,0:T(8,128)(2,1)S(1)} %copy-done.14), channel_id=1, source_target_pairs={{4,0},{8,4},{12,8},{16,12},{20,16},{24,20},{28,24},{5,1},{9,5},{13... | collective-permute-start | bytes 196616 | tf_op jit(solution)/shard_map/ppermute | solution.py:19
  463.1 11.8 %collective-permute-start.7 = (bf16[128,8,128]{2,1,0:T(8,128)(2,1)S(1)}, bf16[128,8,128]{2,1,0:T(8,128)(2,1)S(1)}, u32[]{:S(2)}, u32[]{:S(2)}) collective-permute-start(bf16[128,8,128]{2,1,0:T(8,128)(2,1)S(1)} %copy-done.22), channel_id=1, source_target_pairs={{0,1},{1,2},{2,3},{3,0},{4,5},{5,6},{6,7},{7,4},{8,9},{9,10},{10,1... | collective-permute-start | bytes 786440 | tf_op jit(solution)/shard_map/ppermute | solution.py:52
  463.6 21.9 %collective-permute-start.8 = (bf16[128,8,128]{2,1,0:T(8,128)(2,1)S(1)}, bf16[128,8,128]{2,1,0:T(8,128)(2,1)}, u32[]{:S(2)}, u32[]{:S(2)}) collective-permute-start(bf16[128,8,128]{2,1,0:T(8,128)(2,1)S(1)} %copy-done.21), channel_id=1, source_target_pairs={{0,2},{1,3},{2,0},{3,1},{4,6},{5,7},{6,4},{7,5},{8,10},{9,11},{10,... | collective-permute-start | bytes 786440 | tf_op jit(solution)/shard_map/ppermute | solution.py:52
  466.2 33.7 %collective-permute-start.9 = (bf16[128,8,128]{2,1,0:T(8,128)(2,1)S(1)}, bf16[128,8,128]{2,1,0:T(8,128)(2,1)}, u32[]{:S(2)}, u32[]{:S(2)}) collective-permute-start(bf16[128,8,128]{2,1,0:T(8,128)(2,1)S(1)} %copy-done.20), channel_id=1, source_target_pairs={{0,3},{1,0},{2,1},{3,2},{4,7},{5,4},{6,5},{7,6},{8,11},{9,8},{10,9... | collective-permute-start | bytes 786440 | tf_op jit(solution)/shard_map/ppermute | solution.py:52
  469.0 35.9 %collective-permute-start.18 = (bf16[128,8,128]{2,1,0:T(8,128)(2,1)}, bf16[128,8,128]{2,1,0:T(8,128)(2,1)}, u32[]{:S(2)}, u32[]{:S(2)}) collective-permute-start(bf16[128,8,128]{2,1,0:T(8,128)(2,1)} %get-tuple-element.449), channel_id=1, source_target_pairs={{0,1},{1,2},{2,3},{3,0},{4,5},{5,6},{6,7},{7,4},{8,9},{9,10},{10,1... | collective-permute-start | bytes 786440 | tf_op jit(solution)/shard_map/ppermute | solution.py:52
  473.5 50.4 %copy-start.11 = (f32[4,2,128,128]{3,0,2,1:T(4,128)}, f32[4,2,128,128]{3,0,2,1:T(4,128)S(1)}, u32[]{:S(2)}) copy-start(f32[4,2,128,128]{3,0,2,1:T(4,128)S(1)} %scatter-add.19) | copy-start | bytes 1572868
  473.5 44.6 %collective-permute-start.19 = (bf16[128,8,128]{2,1,0:T(8,128)(2,1)}, bf16[128,8,128]{2,1,0:T(8,128)(2,1)S(1)}, u32[]{:S(2)}, u32[]{:S(2)}) collective-permute-start(bf16[128,8,128]{2,1,0:T(8,128)(2,1)} %get-tuple-element.448), channel_id=1, source_target_pairs={{0,2},{1,3},{2,0},{3,1},{4,6},{5,7},{6,4},{7,5},{8,10},{9,11},{10,... | collective-permute-start | bytes 786440 | tf_op jit(solution)/shard_map/ppermute | solution.py:52
  474.9 28.8 %copy-start.23 = (bf16[128,8,128]{2,1,0:T(8,128)(2,1)}, bf16[128,8,128]{2,1,0:T(8,128)(2,1)S(1)}, u32[]{:S(2)}) copy-start(bf16[128,8,128]{2,1,0:T(8,128)(2,1)S(1)} %collective-permute-done.7) | copy-start | bytes 786436
  474.9 47.9 %collective-permute-start.20 = (bf16[128,8,128]{2,1,0:T(8,128)(2,1)S(1)}, bf16[128,8,128]{2,1,0:T(8,128)(2,1)S(1)}, u32[]{:S(2)}, u32[]{:S(2)}) collective-permute-start(bf16[128,8,128]{2,1,0:T(8,128)(2,1)S(1)} %get-tuple-element.447), channel_id=1, source_target_pairs={{0,3},{1,0},{2,1},{3,2},{4,7},{5,4},{6,5},{7,6},{8,11},{9,8},{10,9... | collective-permute-start | bytes 786440 | tf_op jit(solution)/shard_map/ppermute | solution.py:52
  485.6 45.8 %collective-permute-start.12 = (bf16[128,8,128]{2,1,0:T(8,128)(2,1)}, bf16[128,8,128]{2,1,0:T(8,128)(2,1)}, u32[]{:S(2)}, u32[]{:S(2)}) collective-permute-start(bf16[128,8,128]{2,1,0:T(8,128)(2,1)} %get-tuple-element.457), channel_id=1, source_target_pairs={{0,1},{1,2},{2,3},{3,0},{4,5},{5,6},{6,7},{7,4},{8,9},{9,10},{10,1... | collective-permute-start | bytes 786440 | tf_op jit(solution)/shard_map/ppermute | solution.py:52
  499.9 40.8 %collective-permute-start.13 = (bf16[128,8,128]{2,1,0:T(8,128)(2,1)}, bf16[128,8,128]{2,1,0:T(8,128)(2,1)}, u32[]{:S(2)}, u32[]{:S(2)}) collective-permute-start(bf16[128,8,128]{2,1,0:T(8,128)(2,1)} %get-tuple-element.456), channel_id=1, source_target_pairs={{0,2},{1,3},{2,0},{3,1},{4,6},{5,7},{6,4},{7,5},{8,10},{9,11},{10,... | collective-permute-start | bytes 786440 | tf_op jit(solution)/shard_map/ppermute | solution.py:52
  504.9 35.8 %collective-permute-start.14 = (bf16[128,8,128]{2,1,0:T(8,128)(2,1)}, bf16[128,8,128]{2,1,0:T(8,128)(2,1)}, u32[]{:S(2)}, u32[]{:S(2)}) collective-permute-start(bf16[128,8,128]{2,1,0:T(8,128)(2,1)} %get-tuple-element.455), channel_id=1, source_target_pairs={{0,3},{1,0},{2,1},{3,2},{4,7},{5,4},{6,5},{7,6},{8,11},{9,8},{10,9... | collective-permute-start | bytes 786440 | tf_op jit(solution)/shard_map/ppermute | solution.py:52
  518.1 26.9 %collective-permute-start.15 = (bf16[128,8,128]{2,1,0:T(8,128)(2,1)}, bf16[128,8,128]{2,1,0:T(8,128)(2,1)}, u32[]{:S(2)}, u32[]{:S(2)}) collective-permute-start(bf16[128,8,128]{2,1,0:T(8,128)(2,1)} %get-tuple-element.445), channel_id=1, source_target_pairs={{0,1},{1,2},{2,3},{3,0},{4,5},{5,6},{6,7},{7,4},{8,9},{9,10},{10,1... | collective-permute-start | bytes 786440 | tf_op jit(solution)/shard_map/ppermute | solution.py:52
  522.8 5.3 collective-permute-start.27
  528.1 23.9 %collective-permute-start.16 = (bf16[128,8,128]{2,1,0:T(8,128)(2,1)}, bf16[128,8,128]{2,1,0:T(8,128)(2,1)}, u32[]{:S(2)}, u32[]{:S(2)}) collective-permute-start(bf16[128,8,128]{2,1,0:T(8,128)(2,1)} %get-tuple-element.444), channel_id=1, source_target_pairs={{0,2},{1,3},{2,0},{3,1},{4,6},{5,7},{6,4},{7,5},{8,10},{9,11},{10,... | collective-permute-start | bytes 786440 | tf_op jit(solution)/shard_map/ppermute | solution.py:52
  531.3 20.6 %collective-permute-start.17 = (bf16[128,8,128]{2,1,0:T(8,128)(2,1)}, bf16[128,8,128]{2,1,0:T(8,128)(2,1)}, u32[]{:S(2)}, u32[]{:S(2)}) collective-permute-start(bf16[128,8,128]{2,1,0:T(8,128)(2,1)} %get-tuple-element.443), channel_id=1, source_target_pairs={{0,3},{1,0},{2,1},{3,2},{4,7},{5,4},{6,5},{7,6},{8,11},{9,8},{10,9... | collective-permute-start | bytes 786440 | tf_op jit(solution)/shard_map/ppermute | solution.py:52
  540.7 22.3 %collective-permute-start.28 = (bf16[2,2,128,128]{2,3,0,1:T(8,128)(2,1)}, bf16[2,2,128,128]{2,3,0,1:T(8,128)(2,1)}, u32[]{:S(2)}, u32[]{:S(2)}) collective-permute-start(bf16[2,2,128,128]{2,3,0,1:T(8,128)(2,1)} %fusion.100), channel_id=1, source_target_pairs={{0,16},{4,20},{8,24},{12,28},{16,0},{20,4},{24,8},{28,12},{1,17},{... | collective-permute-start | bytes 393224 | tf_op jit(solution)/shard_map/ppermute | solution.py:36
  540.7 16.4 %copy-start.30 = (pred[4]{0:T(512)(128)(4,1)S(1)}, pred[4]{0:T(512)(128)(4,1)}, u32[]{:S(2)}) copy-start(pred[4]{0:T(512)(128)(4,1)} %compare_and_fusion.2) | copy-start | bytes 16
  563.0 19.2 %copy-start.18 = (bf16[4,128,128]{2,1,0:T(8,128)(2,1)S(1)}, bf16[4,128,128]{2,1,0:T(8,128)(2,1)}, u32[]{:S(2)}) copy-start(bf16[4,128,128]{2,1,0:T(8,128)(2,1)} %gather_fusion.8) | copy-start | bytes 393220
  563.0 19.2 %copy-start.19 = (bf16[4,128,128]{2,1,0:T(8,128)(2,1)S(1)}, bf16[4,128,128]{2,1,0:T(8,128)(2,1)}, u32[]{:S(2)}) copy-start(bf16[4,128,128]{2,1,0:T(8,128)(2,1)} %gather_fusion.10) | copy-start | bytes 393220
  566.8 10.5 %collective-permute-start.35 = (bf16[128,1,128]{2,0,1:T(8,128)(2,1)S(1)}, bf16[128,1,128]{2,0,1:T(8,128)(2,1)S(1)}, u32[]{:S(2)}, u32[]{:S(2)}) collective-permute-start(bf16[128,1,128]{2,0,1:T(8,128)(2,1)S(1)} %get-tuple-element.481), channel_id=1, source_target_pairs={{0,1},{1,2},{2,3},{3,0},{4,5},{5,6},{6,7},{7,4},{8,9},{9,10},{10,1... | collective-permute-start | bytes 98312 | tf_op jit(solution)/shard_map/ppermute | solution.py:52
  572.3 6.4 %collective-permute-start.36 = (bf16[128,1,128]{2,0,1:T(8,128)(2,1)S(1)}, bf16[128,1,128]{2,0,1:T(8,128)(2,1)S(1)}, u32[]{:S(2)}, u32[]{:S(2)}) collective-permute-start(bf16[128,1,128]{2,0,1:T(8,128)(2,1)S(1)} %get-tuple-element.480), channel_id=1, source_target_pairs={{0,2},{1,3},{2,0},{3,1},{4,6},{5,7},{6,4},{7,5},{8,10},{9,11},{10,... | collective-permute-start | bytes 98312 | tf_op jit(solution)/shard_map/ppermute | solution.py:52
  574.0 4.6 collective-permute-start.37
  574.8 5.8 collective-permute-start.29
  576.1 5.2 collective-permute-start.30
  577.3 4.2 collective-permute-start.31
  (38 other events, 163.6 us)
Sparse Core Ops, SparseCore 0:
  29.7 26.7 all-gather.2
  82.6 29.0 all-gather.4

commit v3 on v1

--- a/solution.py
+++ b/solution.py
@@ -1,11 +1,57 @@
+import functools
 import math
 
 import jax
 import jax.numpy as jnp
 from jax import lax
+from jax.experimental import pallas as pl
 from jax.sharding import PartitionSpec as P
 
 BLOCK_TOKENS = 128
+
+
+def attention_kernel(q_ref, k_ref, v_ref, do_ref, bias_ref, out_ref, dq_ref, dk_ref, dv_ref, *, scale):
+    q = q_ref[...]
+    k = k_ref[...]
+    v = v_ref[...]
+    do = do_ref[...]
+    rows_by_cols = (((1,), (1,)), ((), ()))
+    over_rows = (((0,), (0,)), ((), ()))
+    s = lax.dot_general(q, k, rows_by_cols, preferred_element_type=jnp.float32) * scale
+    s = s + bias_ref[...]
+    e = jnp.exp(s - jnp.max(s, axis=1, keepdims=True))
+    p = e / jnp.sum(e, axis=1, keepdims=True)
+    p_low = p.astype(jnp.bfloat16)
+    o_low = jnp.dot(p_low, v, preferred_element_type=jnp.float32).astype(jnp.bfloat16)
+    out_ref[...] = o_low
+    delta = jnp.sum(do.astype(jnp.float32) * o_low.astype(jnp.float32), axis=1, keepdims=True)
+    dp = lax.dot_general(do, v, rows_by_cols, preferred_element_type=jnp.float32)
+    ds_low = (p * (dp - delta)).astype(jnp.bfloat16)
+    dq = jnp.dot(ds_low, k, preferred_element_type=jnp.float32) * scale
+    dq_ref[...] = dq.astype(jnp.bfloat16)
+    dk_ref[...] = lax.dot_general(ds_low, q, over_rows, preferred_element_type=jnp.float32) * scale
+    dv_ref[...] = lax.dot_general(p_low, do, over_rows, preferred_element_type=jnp.float32)
+
+
+def attention_call(q, k, v, do, bias, scale, interpret=False):
+    blocks, heads_kv, rows, width = q.shape
+    keys_n = k.shape[2]
+    q_spec = pl.BlockSpec((None, None, rows, width), lambda j, h: (j, h, 0, 0))
+    k_spec = pl.BlockSpec((None, None, keys_n, width), lambda j, h: (j, h, 0, 0))
+    b_spec = pl.BlockSpec((None, 1, keys_n), lambda j, h: (j, 0, 0))
+    return pl.pallas_call(
+        functools.partial(attention_kernel, scale=scale),
+        grid=(blocks, heads_kv),
+        in_specs=[q_spec, k_spec, k_spec, q_spec, b_spec],
+        out_specs=[q_spec, q_spec, k_spec, k_spec],
+        out_shape=[
+            jax.ShapeDtypeStruct(q.shape, jnp.bfloat16),
+            jax.ShapeDtypeStruct(q.shape, jnp.bfloat16),
+            jax.ShapeDtypeStruct(k.shape, jnp.float32),
+            jax.ShapeDtypeStruct(k.shape, jnp.float32),
+        ],
+        interpret=interpret,
+    )(q, k, v, do, bias)
 
 
 def padded(shard, sides, width):
@@ -114,78 +160,49 @@
     repeat = jnp.any((listed[:, :, None] == listed[:, None, :]) & tile_earlier[None], axis=2)
     live = inside & jnp.logical_not(repeat)
 
-    def attend(unused_state, inputs):
-        query_blk, grad_blk, random_blk, live_row, position = inputs
-        near_tiles = lax.dynamic_slice_in_dim(
-            extended, position * BLOCK_TOKENS, 3 * BLOCK_TOKENS, 1
+    tiles_per_block = []
+    for position in range(blocks):
+        near_tiles = lax.slice_in_dim(
+            extended, position * BLOCK_TOKENS, (position + 3) * BLOCK_TOKENS, axis=1
         )
         near_tiles = near_tiles.reshape(2, 3, BLOCK_TOKENS, kv_width).transpose(1, 0, 2, 3)
-        all_tiles = jnp.concatenate([near_tiles, global_tiles, random_blk], axis=0)
-        key_t = all_tiles[:, 0].reshape(8, BLOCK_TOKENS, heads_kv, head_width)
-        value_t = all_tiles[:, 1].reshape(8, BLOCK_TOKENS, heads_kv, head_width)
-        query_grid = query_blk.reshape(BLOCK_TOKENS, heads_kv, heads_per_group, head_width)
-        grad_grid = grad_blk.reshape(BLOCK_TOKENS, heads_kv, heads_per_group, head_width)
-        scores = (
-            jnp.einsum("qkgd,tbkd->kgqtb", query_grid, key_t, preferred_element_type=jnp.float32)
-            * score_scale
+        tiles_per_block.append(
+            jnp.concatenate([near_tiles, global_tiles, random_by_block[position]], axis=0)
         )
-        scores = jnp.where(live_row[None, None, None, :, None], scores, -jnp.inf)
-        row_max = jnp.max(scores, axis=(3, 4), keepdims=True)
-        expo = jnp.exp(scores - row_max)
-        attn_prob = expo / jnp.sum(expo, axis=(3, 4), keepdims=True)
-        prob_low = attn_prob.astype(jnp.bfloat16)
-        attended = jnp.einsum(
-            "kgqtb,tbkd->qkgd", prob_low, value_t, preferred_element_type=jnp.float32
-        )
-        out_low = attended.astype(jnp.bfloat16)
-        row_delta = jnp.sum(grad_grid.astype(jnp.float32) * out_low.astype(jnp.float32), axis=-1)
-        grad_prob = jnp.einsum(
-            "qkgd,tbkd->kgqtb", grad_grid, value_t, preferred_element_type=jnp.float32
-        )
-        grad_score = attn_prob * (
-            grad_prob - jnp.transpose(row_delta, (1, 2, 0))[:, :, :, None, None]
-        )
-        score_low = grad_score.astype(jnp.bfloat16)
-        query_grad = (
-            jnp.einsum("kgqtb,tbkd->qkgd", score_low, key_t, preferred_element_type=jnp.float32)
-            * score_scale
-        )
-        key_grad = (
-            jnp.einsum(
-                "kgqtb,qkgd->tbkd", score_low, query_grid, preferred_element_type=jnp.float32
-            )
-            * score_scale
-        )
-        value_grad = jnp.einsum(
-            "kgqtb,qkgd->tbkd", prob_low, grad_grid, preferred_element_type=jnp.float32
-        )
-        tile_terms = jnp.stack(
-            [
-                key_grad.reshape(8, BLOCK_TOKENS, kv_width),
-                value_grad.reshape(8, BLOCK_TOKENS, kv_width),
-            ],
-            axis=1,
-        )
-        return (
-            unused_state,
-            (
-                out_low.reshape(BLOCK_TOKENS, heads_q, head_width),
-                query_grad.astype(jnp.bfloat16).reshape(BLOCK_TOKENS, heads_q, head_width),
-                tile_terms,
-            ),
-        )
-
-    unused_final, (output_block_rows, query_gradient_rows, tile_grads) = lax.scan(
-        attend,
-        0,
-        (
-            query_loc.reshape(blocks, BLOCK_TOKENS, heads_q, head_width),
-            grad_loc.reshape(blocks, BLOCK_TOKENS, heads_q, head_width),
-            random_by_block,
-            live,
-            jnp.arange(blocks),
-        ),
-    )
+    all_tiles = jnp.stack(tiles_per_block)
+    tile_count = all_tiles.shape[1]
+    key_rows = tile_count * BLOCK_TOKENS
+
+    def key_major(part):
+        grid = part.reshape(blocks, tile_count, BLOCK_TOKENS, heads_kv, head_width)
+        return grid.transpose(0, 3, 1, 2, 4).reshape(blocks, heads_kv, key_rows, head_width)
+
+    def query_major(part):
+        grid = part.reshape(blocks, BLOCK_TOKENS, heads_kv, heads_per_group, head_width)
+        grid = grid.transpose(0, 2, 3, 1, 4)
+        return grid.reshape(blocks, heads_kv, heads_per_group * BLOCK_TOKENS, head_width)
+
+    def query_back(part):
+        grid = part.reshape(blocks, heads_kv, heads_per_group, BLOCK_TOKENS, head_width)
+        return grid.transpose(0, 3, 1, 2, 4).reshape(blocks, BLOCK_TOKENS, heads_q, head_width)
+
+    def key_back(part):
+        grid = part.reshape(blocks, heads_kv, tile_count, BLOCK_TOKENS, head_width)
+        return grid.transpose(0, 2, 3, 1, 4).reshape(blocks, tile_count, BLOCK_TOKENS, kv_width)
+
+    bias = jnp.where(live, 0.0, -jnp.inf).astype(jnp.float32)
+    bias = jnp.repeat(bias, BLOCK_TOKENS, axis=1).reshape(blocks, 1, key_rows)
+    out_q, grad_q, grad_k, grad_v = attention_call(
+        query_major(query_loc),
+        key_major(all_tiles[:, :, 0]),
+        key_major(all_tiles[:, :, 1]),
+        query_major(grad_loc),
+        bias,
+        score_scale,
+    )
+    output_block_rows = query_back(out_q)
+    query_gradient_rows = query_back(grad_q)
+    tile_grads = jnp.stack([key_back(grad_k), key_back(grad_v)], axis=2)
     pad_spec_low = ((0, 2), (0, 0), (0, 0), (0, 0))
     pad_spec_mid = ((1, 1), (0, 0), (0, 0), (0, 0))
     pad_spec_high = ((2, 0), (0, 0), (0, 0), (0, 0))

time: 452 us -> 421 us (0.931)
  blocking collectives: 61 us -> 0 us
  Pallas kernels: 0 us -> 43.3 us
  matrix products: 46.6 us -> 4.61 us
  waiting for transfers between devices: 156 us -> 193 us
  other arithmetic: 34.4 us -> 9.67 us
  local copies, waits for them, and re-layouts: 88.8 us -> 101 us
  starting transfers between devices: 43.5 us -> 51.5 us
    all_to_all x2 -> x0, blocking collectives: 61 us -> none  [the longest x1 50.4 us: per_device(): lax.all_to_all(query_grad_all, 'head', split_axis=0, concat_axis=1, tiled...]
    all_to_all x0 -> x2, waiting for transfers between devices: none -> 45.5 us  [the longest x1 41.2 us: per_device(): lax.all_to_all(query_grad_all, 'head', split_axis=0, concat_axis=1, tiled...]
    pallas_call x0 -> x1, Pallas kernels: none -> 43.3 us  [attention_call(): pl.pallas_call(functools.partial(attention_kernel, scale=scale), grid=(bl...]
    dot_general x24 -> x0, matrix products: 42 us -> none  [the longest x4 13 us: attend(): jnp.einsum('qkgd,tbkd->kgqtb', grad_grid, value_t, preferred_element_type...]
    all_to_all x1, waiting for transfers between devices: 39.3 us -> 17 us  [per_device(): lax.all_to_all(output_gradient, 'head', split_axis=1, concat_axis=0, tile...]
    transpose x4 -> x6, local copies, waits for them, and re-layouts: 0.28 us -> 18.2 us  [the longest x2 12.8 us: key_back(): grid.transpose(0, 2, 3, 1, 4)]
    another operation x1 -> x4, local copies, waits for them, and re-layouts: 0.02 us -> 17.5 us  [the longest x3 17.5 us: per_device(): tile_grads = jnp.stack([key_back(grad_k), key_back(grad_v)], axis=2)]
    dynamic_slice x16 -> x0, local copies, waits for them, and re-layouts: 15.3 us -> none  [the longest x12 11.2 us: per_device(): lax.scan(attend, 0, (query_loc.reshape(blocks, BLOCK_TOKENS, heads_q, hea...]
  transfers between devices with their start and end apart: 15 -> 17, of which waited for: 10 -> 12; matrix products, arithmetic and copies ran while one was open for 10% -> 15% of each run, Pallas kernels for 0% -> 0%
where the time goes in v3:
time: 421 us; the launch traced here: 417 us
  waiting for transfers between devices  193 us (46%)
  local copies, waits for them, and re-layouts  101 us (24%)
  starting transfers between devices  51.5 us (12%)
  Pallas kernels  43.3 us (10%)
  between operations  14.6 us (3%)
  other arithmetic  9.67 us (2%)
  matrix products  4.61 us (1%)
    all_to_all x1, waiting for transfers between devices, per_device(): lax.all_to_all(out_all, 'head', split_axis=0, concat_axis=1, tiled=True)  43.9 us
    pallas_call x1, Pallas kernels, attention_call(): pl.pallas_call(functools.partial(attention_kernel, scale=scale), grid=(bl...  43.3 us
    all_to_all x1, waiting for transfers between devices, per_device(): lax.all_to_all(query_grad_all, 'head', split_axis=0, concat_axis=1, tiled...  41.2 us
    all_to_all x1, waiting for transfers between devices, per_device(): lax.all_to_all(queries, 'head', split_axis=1, concat_axis=0, tiled=True)  39.7 us
    ppermute x2, waiting for transfers between devices, padded(): before = lax.ppermute(last, axis, up)  18.3 us
    unnamed x24, local copies, waits for them, and re-layouts  17.9 us
    another operation x3, local copies, waits for them, and re-layouts, per_device(): tile_grads = jnp.stack([key_back(grad_k), key_back(grad_v)], axis=2)  17.5 us
    all_to_all x1, waiting for transfers between devices, per_device(): lax.all_to_all(output_gradient, 'head', split_axis=1, concat_axis=0, tile...  17 us
  transfers between devices with their start and end apart: 17, of which 12 were waited for; matrix products, arithmetic and copies ran while one was open for 15% of the time, Pallas kernels for 0%

profile of v3, /device:TPU:4, one launch (start us, length us, event | category | flops | bytes accessed | tf_op | source)
XLA Modules:
  0.0 417.4 jit_solution(13404673811117907644)
XLA Ops:
  7.2 1.7 copy.242
  8.9 4.9 %all-to-all-start.1 = ((bf16[128,8,128]{2,0,1:T(8,128)(2,1)}), bf16[128,8,128]{2,0,1:T(8,128)(2,1)S(1)}, u32[]{:S(2)}, u32[]{:S(2)}) async-start(bf16[128,8,128]{2,0,1:T(8,128)(2,1)} %copy.242), calls=%async_computation.1 | async-start | bytes 524288 | tf_op jit(solution)/shard_map/all_to_all | solution.py:91
  13.7 1.7 copy.244
  15.4 7.2 %all-to-all-done.1 = bf16[128,8,128]{2,0,1:T(8,128)(2,1)S(1)} async-done(((bf16[128,8,128]{2,0,1:T(8,128)(2,1)}), bf16[128,8,128]{2,0,1:T(8,128)(2,1)S(1)}, u32[]{:S(2)}, u32[]{:S(2)}) %all-to-all-start.1) | async-done | bytes 262176 | tf_op jit(solution)/shard_map/all_to_all | solution.py:91
  22.6 3.4 all-to-all-start.2
  26.6 6.5 %all-to-all-done.2 = bf16[128,8,128]{2,0,1:T(8,128)(2,1)S(1)} async-done(((bf16[128,8,128]{2,0,1:T(8,128)(2,1)}), bf16[128,8,128]{2,0,1:T(8,128)(2,1)S(1)}, u32[]{:S(2)}, u32[]{:S(2)}) %all-to-all-start.2) | async-done | bytes 262176 | tf_op jit(solution)/shard_map/all_to_all | solution.py:92
  33.5 0.8 copy-done
  34.4 2.7 copy.241
  37.0 3.7 all-to-all-start
  41.5 4.4 %copy.258 = bf16[128,64,128]{2,0,1:T(8,128)(2,1)} copy(bf16[128,64,128]{2,1,0:T(8,128)(2,1)} %param.13) | data formatting | bytes 4194304 | tf_op args[3]
  46.5 39.7 %all-to-all-done = bf16[128,64,128]{2,0,1:T(8,128)(2,1)S(1)} async-done(((bf16[128,64,128]{2,0,1:T(8,128)(2,1)}), bf16[128,64,128]{2,0,1:T(8,128)(2,1)S(1)}, u32[]{:S(2)}, u32[]{:S(2)}) %all-to-all-start) | async-done | bytes 2097184 | tf_op jit(solution)/shard_map/all_to_all | solution.py:90
  86.2 4.5 %all-to-all-start.3 = ((bf16[128,64,128]{2,0,1:T(8,128)(2,1)}), bf16[128,64,128]{2,0,1:T(8,128)(2,1)}, u32[]{:S(2)}, u32[]{:S(2)}) async-start(bf16[128,64,128]{2,0,1:T(8,128)(2,1)} %copy.258), calls=%async_computation.3 | async-start | bytes 4194304 | tf_op jit(solution)/shard_map/all_to_all | solution.py:93
  91.1 1.9 collective-permute-start
  93.1 4.7 %collective-permute-start.1 = (bf16[2,128,256]{2,1,0:T(8,128)(2,1)S(1)}, bf16[2,128,256]{2,1,0:T(8,128)(2,1)S(1)}, u32[]{:S(2)}, u32[]{:S(2)}) collective-permute-start(bf16[2,128,256]{2,1,0:T(8,128)(2,1)S(1)} %get-tuple-element.78), channel_id=1, source_target_pairs={{4,0},{8,4},{12,8},{16,12},{20,16},{24,20},{28,24},{5,1},{9,5},{13... | collective-permute-start | bytes 393224 | tf_op jit(solution)/shard_map/ppermute | solution.py:65
  98.3 1.8 collective-permute-done.1
  100.4 2.8 gather_fusion
  103.2 2.8 gather_fusion.1
  107.5 2.6 fusion.51
  110.1 3.0 copy.256
  113.1 2.7 copy.257
  115.8 3.0 copy.254
  118.8 2.6 copy.255
  121.4 17.0 %all-to-all-done.3 = bf16[128,64,128]{2,0,1:T(8,128)(2,1)} async-done(((bf16[128,64,128]{2,0,1:T(8,128)(2,1)}), bf16[128,64,128]{2,0,1:T(8,128)(2,1)}, u32[]{:S(2)}, u32[]{:S(2)}) %all-to-all-start.3) | async-done | bytes 2097184 | tf_op jit(solution)/shard_map/all_to_all | solution.py:93
  139.2 43.3 %shard_map.93 = (bf16[4,2,1024,128]{3,2,1,0:T(8,128)(2,1)}, bf16[4,2,1024,128]{3,2,1,0:T(8,128)(2,1)}, f32[4,2,1024,128]{3,2,1,0:T(8,128)}, f32[4,2,1024,128]{3,2,1,0:T(8,128)}) custom-call(bf16[4,2,1024,128]{3,2,1,0:T(8,128)(2,1)} %bitcast.168, bf16[4,2,1024,128]{3,2,1,0:T(8,128)(2,1)} %bitcast.170, bf16[4,2,1024,128]{3,2,1,0:T(8,128)(2,1)} %bitcast.169, ...), custom_call_target="tpu_custom_call" | custom-call | tf_op jit(solution)/shard_map/pallas_call | solution.py:42
  182.5 7.6 %copy.264 = f32[4,8,128,2,128]{4,3,2,0,1:T(2,128)} copy(f32[4,8,128,2,128]{4,2,1,3,0:T(8,128)} %bitcast.173) | data formatting | bytes 8388608 | tf_op jit(solution)/shard_map/transpose | solution.py:191
  190.0 6.4 %stack_reshape.14 = f32[4,8,1,128,256]{4,3,2,0,1:T(8,128)} reshape(f32[4,8,128,2,128]{4,3,2,0,1:T(2,128)} %copy.264) | data formatting | bytes 8388608 | tf_op jit(solution)/shard_map/stack;reshape | solution.py:205
  196.4 4.8 %constant_dynamic-update-slice_fusion.3 = f32[4,8,2,128,256]{4,3,2,0,1:T(8,128)} fusion(f32[4,8,1,128,256]{4,3,2,0,1:T(8,128)} %stack_reshape.14), kind=kLoop, calls=%fused_computation.70 | loop fusion | bytes 8388608
  201.2 5.2 %copy.265 = f32[4,8,128,2,128]{4,3,2,0,1:T(2,128)} copy(f32[4,8,128,2,128]{4,2,1,3,0:T(8,128)S(1)} %bitcast.172) | data formatting | bytes 8388608 | tf_op jit(solution)/shard_map/transpose | solution.py:191
  206.4 6.5 %stack_reshape.15 = f32[4,8,1,128,256]{4,3,2,0,1:T(8,128)} reshape(f32[4,8,128,2,128]{4,3,2,0,1:T(2,128)} %copy.265) | data formatting | bytes 8388608 | tf_op jit(solution)/shard_map/stack;reshape | solution.py:205
  212.9 4.6 %constant_dynamic-update-slice_fusion.2 = f32[4,8,2,128,256]{4,3,2,0,1:T(8,128)} fusion(f32[4,8,2,128,256]{4,3,2,0,1:T(8,128)} %constant_dynamic-update-slice_fusion.3, f32[4,8,1,128,256]{4,3,2,0,1:T(8,128)} %stack_reshape.15), kind=kLoop, calls=%fused_computation.69 | loop fusion | bytes 8388608 | tf_op jit(solution)/shard_map/stack | solution.py:205
  217.5 1.8 slice_reduce_fusion
  219.3 2.1 slice.200
  221.4 3.6 slice_bitcast_fusion.2
  225.1 1.0 fusion.4
  226.1 2.0 copy.277
  228.2 4.3 %all-to-all-start.6 = ((bf16[16,2,128,256]{3,2,1,0:T(8,128)(2,1)}), bf16[16,2,128,256]{3,2,1,0:T(8,128)(2,1)S(1)}, u32[]{:S(2)}, u32[]{:S(2)}) async-start(bf16[16,2,128,256]{3,2,1,0:T(8,128)(2,1)} %copy.277), calls=%async_computation.6 | async-start | bytes 4194304 | tf_op jit(solution)/shard_map/all_to_all | solution.py:241
  232.5 2.2 fusion.50
  234.7 2.0 collective-permute-start.2
  236.7 4.4 %collective-permute-start.3 = (bf16[2,128,256]{2,1,0:T(8,128)(2,1)S(1)}, bf16[2,128,256]{2,1,0:T(8,128)(2,1)S(1)}, u32[]{:S(2)}, u32[]{:S(2)}) collective-permute-start(bf16[2,128,256]{2,1,0:T(8,128)(2,1)S(1)} %get-tuple-element.70), channel_id=1, source_target_pairs={{4,0},{8,4},{12,8},{16,12},{20,16},{24,20},{28,24},{5,1},{9,5},{13... | collective-permute-start | bytes 393224 | tf_op jit(solution)/shard_map/ppermute | solution.py:65
  242.1 17.8 %collective-permute-done.2 = bf16[2,128,256]{2,1,0:T(8,128)(2,1)S(1)} collective-permute-done((bf16[2,128,256]{2,1,0:T(8,128)(2,1)S(1)}, bf16[2,128,256]{2,1,0:T(8,128)(2,1)S(1)}, u32[]{:S(2)}, u32[]{:S(2)}) %collective-permute-start.2) | collective-permute-done | bytes 131104 | tf_op jit(solution)/shard_map/ppermute | solution.py:64
  259.9 4.8 %collective-permute-done.5 = bf16[2,2,128,256]{3,2,1,0:T(8,128)(2,1)S(1)} collective-permute-done((bf16[2,2,128,256]{3,2,1,0:T(8,128)(2,1)S(1)}, bf16[2,2,128,256]{3,2,1,0:T(8,128)(2,1)S(1)}, u32[]{:S(2)}, u32[]{:S(2)}) %collective-permute-start.5) | collective-permute-done | bytes 262176 | tf_op jit(solution)/shard_map/ppermute | solution.py:82
  264.7 0.8 fusion.31
  265.5 2.0 collective-permute-start.6
  267.5 1.6 copy.267
  269.5 7.0 %scatter-add.9 = f32[4,2,128,256]{3,0,2,1:T(4,128)} dynamic-update-slice(f32[4,2,128,256]{3,0,2,1:T(4,128)} %copy.267, f32[1,2,128,256]{3,0,2,1:T(1,128)S(1)} %copy_add_fusion.1, s32[]{:T(128)} %constant.151.clone.1, s32[]{:T(128)} %constant.138.clone.1, s32[]{:T(128)} %constant.138.clone.1, s32[]{:T(128)} %constant.138.clone.1) | dynamic-update-slice | bytes 524292 | tf_op jit(solution)/shard_map/scatter-add | solution.py:223
  276.5 1.1 convert_add_fusion
  277.5 1.2 multiply_reduce_fusion
  278.8 3.4 fusion.16
  282.4 0.8 reshape_squeeze.15
  283.2 3.4 all-to-all-start.8
  286.7 0.8 reshape_squeeze.14
  287.4 7.7 %all-to-all-done.8 = bf16[512,2,128]{2,1,0:T(2,128)(2,1)S(1)} async-done(((bf16[512,2,128]{2,1,0:T(2,128)(2,1)}), bf16[512,2,128]{2,1,0:T(2,128)(2,1)S(1)}, u32[]{:S(2)}, u32[]{:S(2)}) %all-to-all-start.8) | async-done | bytes 262176 | tf_op jit(solution)/shard_map/all_to_all | solution.py:257
  295.2 3.4 all-to-all-start.7
  298.6 2.7 copy.262
  301.3 4.4 %all-to-all-done.7 = bf16[512,2,128]{2,1,0:T(2,128)(2,1)S(1)} async-done(((bf16[512,2,128]{2,1,0:T(2,128)(2,1)}), bf16[512,2,128]{2,1,0:T(2,128)(2,1)S(1)}, u32[]{:S(2)}, u32[]{:S(2)}) %all-to-all-start.7) | async-done | bytes 262176 | tf_op jit(solution)/shard_map/all_to_all | solution.py:256
  305.6 3.6 all-to-all-start.5
  309.2 4.3 %copy.260 = bf16[4,2,8,128,128]{4,2,1,3,0:T(8,128)(2,1)} copy(bf16[4,2,8,128,128]{4,3,2,1,0:T(8,128)(2,1)} %bitcast.174) | data formatting | bytes 4194304 | tf_op jit(solution)/shard_map/reshape | solution.py:186
  313.5 41.2 %all-to-all-done.5 = bf16[512,16,128]{2,1,0:T(8,128)(2,1)S(1)} async-done(((bf16[512,16,128]{2,1,0:T(8,128)(2,1)}), bf16[512,16,128]{2,1,0:T(8,128)(2,1)S(1)}, u32[]{:S(2)}, u32[]{:S(2)}) %all-to-all-start.5) | async-done | bytes 2097184 | tf_op jit(solution)/shard_map/all_to_all | solution.py:255
  354.7 4.4 %all-to-all-start.4 = ((bf16[512,16,128]{2,1,0:T(8,128)(2,1)}), bf16[512,16,128]{2,1,0:T(8,128)(2,1)}, u32[]{:S(2)}, u32[]{:S(2)}) async-start(bf16[512,16,128]{2,1,0:T(8,128)(2,1)} %bitcast.164), calls=%async_computation.4 | async-start | bytes 4194304 | tf_op jit(solution)/shard_map/all_to_all | solution.py:254
  359.2 0.9 copy.287
  360.2 0.9 copy.286
  361.0 2.0 copy.263
  363.0 43.9 %all-to-all-done.4 = bf16[512,16,128]{2,1,0:T(8,128)(2,1)} async-done(((bf16[512,16,128]{2,1,0:T(8,128)(2,1)}), bf16[512,16,128]{2,1,0:T(8,128)(2,1)}, u32[]{:S(2)}, u32[]{:S(2)}) %all-to-all-start.4) | async-done | bytes 2097184 | tf_op jit(solution)/shard_map/all_to_all | solution.py:254
  407.0 3.6 copy.261
  (84 shorter events, 7.3 us)
Async XLA Ops:
  8.9 13.8 %all-to-all-start.1 = ((bf16[128,8,128]{2,0,1:T(8,128)(2,1)}), bf16[128,8,128]{2,0,1:T(8,128)(2,1)S(1)}, u32[]{:S(2)}, u32[]{:S(2)}) async-start(bf16[128,8,128]{2,0,1:T(8,128)(2,1)} %copy.242), calls=%async_computation.1 | async-start | bytes 524288 | tf_op jit(solution)/shard_map/all_to_all | solution.py:91
  15.4 18.9 %copy-start.4 = (bf16[128,64,128]{2,1,0:T(8,128)(2,1)S(1)}, bf16[128,64,128]{2,1,0:T(8,128)(2,1)}, u32[]{:S(2)}) copy-start(bf16[128,64,128]{2,1,0:T(8,128)(2,1)} %param.10) | copy-start | bytes 6291460
  22.6 10.4 %all-to-all-start.2 = ((bf16[128,8,128]{2,0,1:T(8,128)(2,1)}), bf16[128,8,128]{2,0,1:T(8,128)(2,1)S(1)}, u32[]{:S(2)}, u32[]{:S(2)}) async-start(bf16[128,8,128]{2,0,1:T(8,128)(2,1)} %copy.244), calls=%async_computation.2 | async-start | bytes 524288 | tf_op jit(solution)/shard_map/all_to_all | solution.py:92
  26.1 74.3 %all-gather.2.cloned.1.call-start = ((), (), s32[]{:S(2)}) async-start(), calls=%async_computation.9 | async-start | bytes 4718592 | tf_op jit(solution)/shard_map/all_gather | solution.py:141
  33.5 0.8 copy-start
  37.0 3.8 copy-start.6
  37.0 49.2 %all-to-all-start = ((bf16[128,64,128]{2,0,1:T(8,128)(2,1)}), bf16[128,64,128]{2,0,1:T(8,128)(2,1)S(1)}, u32[]{:S(2)}, u32[]{:S(2)}) async-start(bf16[128,64,128]{2,0,1:T(8,128)(2,1)} %copy.241), calls=%async_computation | async-start | bytes 4194304 | tf_op jit(solution)/shard_map/all_to_all | solution.py:90
  41.5 4.4 %copy-start.7 = (s32[2]{0:T(128)S(1)}, s32[2]{0:T(128)}, u32[]{:S(2)}) copy-start(s32[2]{0:T(128)} %param.14) | copy-start | bytes 28
  46.5 44.6 %copy-start.1 = (bf16[2,512,256]{2,1,0:T(8,128)(2,1)S(1)}, bf16[2,512,256]{2,1,0:T(8,128)(2,1)}, u32[]{:S(2)}) copy-start(bf16[2,512,256]{2,1,0:T(8,128)(2,1)} %copy-done) | copy-start | bytes 1572868
  86.2 4.8 %copy-start.2 = (bf16[128,64,128]{2,0,1:T(8,128)(2,1)}, bf16[128,64,128]{2,0,1:T(8,128)(2,1)S(1)}, u32[]{:S(2)}) copy-start(bf16[128,64,128]{2,0,1:T(8,128)(2,1)S(1)} %all-to-all-done) | copy-start | bytes 6291460
  86.2 52.3 %all-to-all-start.3 = ((bf16[128,64,128]{2,0,1:T(8,128)(2,1)}), bf16[128,64,128]{2,0,1:T(8,128)(2,1)}, u32[]{:S(2)}, u32[]{:S(2)}) async-start(bf16[128,64,128]{2,0,1:T(8,128)(2,1)} %copy.258), calls=%async_computation.3 | async-start | bytes 4194304 | tf_op jit(solution)/shard_map/all_to_all | solution.py:93
  91.1 7.2 %collective-permute-start = (bf16[2,128,256]{2,1,0:T(8,128)(2,1)S(1)}, bf16[2,128,256]{2,1,0:T(8,128)(2,1)S(1)}, u32[]{:S(2)}, u32[]{:S(2)}) collective-permute-start(bf16[2,128,256]{2,1,0:T(8,128)(2,1)S(1)} %get-tuple-element.77), channel_id=1, source_target_pairs={{0,4},{4,8},{8,12},{12,16},{16,20},{20,24},{24,28},{1,5},{5,9},{9,... | collective-permute-start | bytes 393224 | tf_op jit(solution)/shard_map/ppermute | solution.py:64
  93.1 7.0 %collective-permute-start.1 = (bf16[2,128,256]{2,1,0:T(8,128)(2,1)S(1)}, bf16[2,128,256]{2,1,0:T(8,128)(2,1)S(1)}, u32[]{:S(2)}, u32[]{:S(2)}) collective-permute-start(bf16[2,128,256]{2,1,0:T(8,128)(2,1)S(1)} %get-tuple-element.78), channel_id=1, source_target_pairs={{4,0},{8,4},{12,8},{16,12},{20,16},{24,20},{28,24},{5,1},{9,5},{13... | collective-permute-start | bytes 393224 | tf_op jit(solution)/shard_map/ppermute | solution.py:65
  196.4 4.8 %copy-start.3 = (f32[4,2,1024,128]{3,2,1,0:T(8,128)S(1)}, f32[4,2,1024,128]{3,2,1,0:T(8,128)}, u32[]{:S(2)}) copy-start(f32[4,2,1024,128]{3,2,1,0:T(8,128)} %get-tuple-element.35) | copy-start | bytes 12582916
  225.0 16.2 %collective-permute-start.4 = (bf16[2,2,128,256]{3,2,1,0:T(8,128)(2,1)S(1)}, bf16[2,2,128,256]{3,2,1,0:T(8,128)(2,1)S(1)}, u32[]{:S(2)}, u32[]{:S(2)}) collective-permute-start(bf16[2,2,128,256]{3,2,1,0:T(8,128)(2,1)S(1)} %convert_element_type.63), channel_id=1, source_target_pairs={{0,4},{4,0},{8,12},{12,8},{16,20},{20,16},{24,28},{28,24},{1,5},{5... | collective-permute-start | bytes 786440 | tf_op jit(solution)/shard_map/ppermute | solution.py:82
  228.2 50.6 %all-to-all-start.6 = ((bf16[16,2,128,256]{3,2,1,0:T(8,128)(2,1)}), bf16[16,2,128,256]{3,2,1,0:T(8,128)(2,1)S(1)}, u32[]{:S(2)}, u32[]{:S(2)}) async-start(bf16[16,2,128,256]{3,2,1,0:T(8,128)(2,1)} %copy.277), calls=%async_computation.6 | async-start | bytes 4194304 | tf_op jit(solution)/shard_map/all_to_all | solution.py:241
  234.7 25.2 %collective-permute-start.2 = (bf16[2,128,256]{2,1,0:T(8,128)(2,1)S(1)}, bf16[2,128,256]{2,1,0:T(8,128)(2,1)S(1)}, u32[]{:S(2)}, u32[]{:S(2)}) collective-permute-start(bf16[2,128,256]{2,1,0:T(8,128)(2,1)S(1)} %get-tuple-element.69), channel_id=1, source_target_pairs={{0,4},{4,8},{8,12},{12,16},{16,20},{20,24},{24,28},{1,5},{5,9},{9,... | collective-permute-start | bytes 393224 | tf_op jit(solution)/shard_map/ppermute | solution.py:64
  236.7 23.2 %collective-permute-start.3 = (bf16[2,128,256]{2,1,0:T(8,128)(2,1)S(1)}, bf16[2,128,256]{2,1,0:T(8,128)(2,1)S(1)}, u32[]{:S(2)}, u32[]{:S(2)}) collective-permute-start(bf16[2,128,256]{2,1,0:T(8,128)(2,1)S(1)} %get-tuple-element.70), channel_id=1, source_target_pairs={{4,0},{8,4},{12,8},{16,12},{20,16},{24,20},{28,24},{5,1},{9,5},{13... | collective-permute-start | bytes 393224 | tf_op jit(solution)/shard_map/ppermute | solution.py:65
  241.2 23.4 %collective-permute-start.5 = (bf16[2,2,128,256]{3,2,1,0:T(8,128)(2,1)S(1)}, bf16[2,2,128,256]{3,2,1,0:T(8,128)(2,1)S(1)}, u32[]{:S(2)}, u32[]{:S(2)}) collective-permute-start(bf16[2,2,128,256]{3,2,1,0:T(8,128)(2,1)S(1)} %fusion.28), channel_id=1, source_target_pairs={{0,8},{4,12},{8,0},{12,4},{16,24},{20,28},{24,16},{28,20},{1,9},{5... | collective-permute-start | bytes 786440 | tf_op jit(solution)/shard_map/ppermute | solution.py:82
  265.5 11.0 %collective-permute-start.6 = (bf16[2,2,128,256]{3,2,1,0:T(8,128)(2,1)}, bf16[2,2,128,256]{3,2,1,0:T(8,128)(2,1)}, u32[]{:S(2)}, u32[]{:S(2)}) collective-permute-start(bf16[2,2,128,256]{3,2,1,0:T(8,128)(2,1)} %fusion.31), channel_id=1, source_target_pairs={{0,16},{4,20},{8,24},{12,28},{16,0},{20,4},{24,8},{28,12},{1,17},{... | collective-permute-start | bytes 786440 | tf_op jit(solution)/shard_map/ppermute | solution.py:82
  282.2 16.4 %copy-start.5 = (bf16[4,2,1024,128]{3,2,1,0:T(8,128)(2,1)S(1)}, bf16[4,2,1024,128]{3,2,1,0:T(8,128)(2,1)}, u32[]{:S(2)}) copy-start(bf16[4,2,1024,128]{3,2,1,0:T(8,128)(2,1)} %get-tuple-element.33) | copy-start | bytes 6291460
  283.2 12.0 %all-to-all-start.8 = ((bf16[512,2,128]{2,1,0:T(2,128)(2,1)}), bf16[512,2,128]{2,1,0:T(2,128)(2,1)S(1)}, u32[]{:S(2)}, u32[]{:S(2)}) async-start(bf16[512,2,128]{2,1,0:T(2,128)(2,1)} %reshape_squeeze.15), calls=%async_computation.8 | async-start | bytes 524288 | tf_op jit(solution)/shard_map/all_to_all | solution.py:257
  295.2 10.5 %all-to-all-start.7 = ((bf16[512,2,128]{2,1,0:T(2,128)(2,1)}), bf16[512,2,128]{2,1,0:T(2,128)(2,1)S(1)}, u32[]{:S(2)}, u32[]{:S(2)}) async-start(bf16[512,2,128]{2,1,0:T(2,128)(2,1)} %reshape_squeeze.14), calls=%async_computation.7 | async-start | bytes 524288 | tf_op jit(solution)/shard_map/all_to_all | solution.py:256
  305.6 49.1 %all-to-all-start.5 = ((bf16[512,16,128]{2,1,0:T(8,128)(2,1)}), bf16[512,16,128]{2,1,0:T(8,128)(2,1)S(1)}, u32[]{:S(2)}, u32[]{:S(2)}) async-start(bf16[512,16,128]{2,1,0:T(8,128)(2,1)} %bitcast.165), calls=%async_computation.5 | async-start | bytes 4194304 | tf_op jit(solution)/shard_map/all_to_all | solution.py:255
  354.7 52.3 %all-to-all-start.4 = ((bf16[512,16,128]{2,1,0:T(8,128)(2,1)}), bf16[512,16,128]{2,1,0:T(8,128)(2,1)}, u32[]{:S(2)}, u32[]{:S(2)}) async-start(bf16[512,16,128]{2,1,0:T(8,128)(2,1)} %bitcast.164), calls=%async_computation.4 | async-start | bytes 4194304 | tf_op jit(solution)/shard_map/all_to_all | solution.py:254
Sparse Core Ops, SparseCore 0:
  34.5 35.9 all-gather.1

commit v4 on v3

--- a/solution.py
+++ b/solution.py
@@ -10,11 +10,22 @@
 BLOCK_TOKENS = 128
 
 
-def attention_kernel(q_ref, k_ref, v_ref, do_ref, bias_ref, out_ref, dq_ref, dk_ref, dv_ref, *, scale):
-    q = q_ref[...]
-    k = k_ref[...]
-    v = v_ref[...]
-    do = do_ref[...]
+def attention_kernel(q_ref, k_ref, v_ref, do_ref, bias_ref, out_ref, dq_ref, grad_ref, *, scale):
+    group = q_ref.shape[1] // q_ref.shape[0]
+    width = k_ref.shape[-1]
+
+    def rows_of(ref):
+        return jnp.concatenate([ref[:, g * width:(g + 1) * width] for g in range(group)], axis=0)
+
+    def store_rows(ref, value):
+        tokens = ref.shape[0]
+        for g in range(group):
+            ref[:, g * width:(g + 1) * width] = value[g * tokens:(g + 1) * tokens, :]
+
+    q = rows_of(q_ref)
+    do = rows_of(do_ref)
+    k = k_ref[...].reshape(-1, width)
+    v = v_ref[...].reshape(-1, width)
     rows_by_cols = (((1,), (1,)), ((), ()))
     over_rows = (((0,), (0,)), ((), ()))
     s = lax.dot_general(q, k, rows_by_cols, preferred_element_type=jnp.float32) * scale
@@ -23,35 +34,38 @@
     p = e / jnp.sum(e, axis=1, keepdims=True)
     p_low = p.astype(jnp.bfloat16)
     o_low = jnp.dot(p_low, v, preferred_element_type=jnp.float32).astype(jnp.bfloat16)
-    out_ref[...] = o_low
+    store_rows(out_ref, o_low)
     delta = jnp.sum(do.astype(jnp.float32) * o_low.astype(jnp.float32), axis=1, keepdims=True)
     dp = lax.dot_general(do, v, rows_by_cols, preferred_element_type=jnp.float32)
     ds_low = (p * (dp - delta)).astype(jnp.bfloat16)
     dq = jnp.dot(ds_low, k, preferred_element_type=jnp.float32) * scale
-    dq_ref[...] = dq.astype(jnp.bfloat16)
-    dk_ref[...] = lax.dot_general(ds_low, q, over_rows, preferred_element_type=jnp.float32) * scale
-    dv_ref[...] = lax.dot_general(p_low, do, over_rows, preferred_element_type=jnp.float32)
-
-
-def attention_call(q, k, v, do, bias, scale, interpret=False):
-    blocks, heads_kv, rows, width = q.shape
-    keys_n = k.shape[2]
-    q_spec = pl.BlockSpec((None, None, rows, width), lambda j, h: (j, h, 0, 0))
-    k_spec = pl.BlockSpec((None, None, keys_n, width), lambda j, h: (j, h, 0, 0))
-    b_spec = pl.BlockSpec((None, 1, keys_n), lambda j, h: (j, 0, 0))
+    store_rows(dq_ref, dq.astype(jnp.bfloat16))
+    dk = lax.dot_general(ds_low, q, over_rows, preferred_element_type=jnp.float32) * scale
+    dv = lax.dot_general(p_low, do, over_rows, preferred_element_type=jnp.float32)
+    grad_ref[:, 0] = dk.reshape(grad_ref.shape[0], -1, width)
+    grad_ref[:, 1] = dv.reshape(grad_ref.shape[0], -1, width)
+
+
+def attention_call(q, tiles, do, bias, heads_kv, scale):
+    blocks, tokens, q_width = q.shape
+    tile_count, head_width = tiles.shape[1], tiles.shape[-1] // heads_kv
+    rows_width = q_width // heads_kv
+    q_spec = pl.BlockSpec((None, tokens, rows_width), lambda j, h: (j, 0, h))
+    k_spec = pl.BlockSpec((None, tile_count, None, tokens, head_width), lambda j, h: (j, 0, 0, 0, h))
+    v_spec = pl.BlockSpec((None, tile_count, None, tokens, head_width), lambda j, h: (j, 0, 1, 0, h))
+    b_spec = pl.BlockSpec((None, 1, bias.shape[-1]), lambda j, h: (j, 0, 0))
+    g_spec = pl.BlockSpec((None, tile_count, 2, tokens, head_width), lambda j, h: (j, 0, 0, 0, h))
     return pl.pallas_call(
         functools.partial(attention_kernel, scale=scale),
         grid=(blocks, heads_kv),
-        in_specs=[q_spec, k_spec, k_spec, q_spec, b_spec],
-        out_specs=[q_spec, q_spec, k_spec, k_spec],
+        in_specs=[q_spec, k_spec, v_spec, q_spec, b_spec],
+        out_specs=[q_spec, q_spec, g_spec],
         out_shape=[
             jax.ShapeDtypeStruct(q.shape, jnp.bfloat16),
             jax.ShapeDtypeStruct(q.shape, jnp.bfloat16),
-            jax.ShapeDtypeStruct(k.shape, jnp.float32),
-            jax.ShapeDtypeStruct(k.shape, jnp.float32),
+            jax.ShapeDtypeStruct(tiles.shape, jnp.float32),
         ],
-        interpret=interpret,
-    )(q, k, v, do, bias)
+    )(q, tiles, tiles, do, bias)
 
 
 def padded(shard, sides, width):
@@ -171,38 +185,18 @@
         )
     all_tiles = jnp.stack(tiles_per_block)
     tile_count = all_tiles.shape[1]
-    key_rows = tile_count * BLOCK_TOKENS
-
-    def key_major(part):
-        grid = part.reshape(blocks, tile_count, BLOCK_TOKENS, heads_kv, head_width)
-        return grid.transpose(0, 3, 1, 2, 4).reshape(blocks, heads_kv, key_rows, head_width)
-
-    def query_major(part):
-        grid = part.reshape(blocks, BLOCK_TOKENS, heads_kv, heads_per_group, head_width)
-        grid = grid.transpose(0, 2, 3, 1, 4)
-        return grid.reshape(blocks, heads_kv, heads_per_group * BLOCK_TOKENS, head_width)
-
-    def query_back(part):
-        grid = part.reshape(blocks, heads_kv, heads_per_group, BLOCK_TOKENS, head_width)
-        return grid.transpose(0, 3, 1, 2, 4).reshape(blocks, BLOCK_TOKENS, heads_q, head_width)
-
-    def key_back(part):
-        grid = part.reshape(blocks, heads_kv, tile_count, BLOCK_TOKENS, head_width)
-        return grid.transpose(0, 2, 3, 1, 4).reshape(blocks, tile_count, BLOCK_TOKENS, kv_width)
-
     bias = jnp.where(live, 0.0, -jnp.inf).astype(jnp.float32)
-    bias = jnp.repeat(bias, BLOCK_TOKENS, axis=1).reshape(blocks, 1, key_rows)
-    out_q, grad_q, grad_k, grad_v = attention_call(
-        query_major(query_loc),
-        key_major(all_tiles[:, :, 0]),
-        key_major(all_tiles[:, :, 1]),
-        query_major(grad_loc),
+    bias = jnp.repeat(bias, BLOCK_TOKENS, axis=1).reshape(blocks, 1, tile_count * BLOCK_TOKENS)
+    out_q, grad_q, tile_grads = attention_call(
+        query_loc.reshape(blocks, BLOCK_TOKENS, heads_q * head_width),
+        all_tiles,
+        grad_loc.reshape(blocks, BLOCK_TOKENS, heads_q * head_width),
         bias,
+        heads_kv,
         score_scale,
     )
-    output_block_rows = query_back(out_q)
-    query_gradient_rows = query_back(grad_q)
-    tile_grads = jnp.stack([key_back(grad_k), key_back(grad_v)], axis=2)
+    output_block_rows = out_q.reshape(blocks, BLOCK_TOKENS, heads_q, head_width)
+    query_gradient_rows = grad_q.reshape(blocks, BLOCK_TOKENS, heads_q, head_width)
     pad_spec_low = ((0, 2), (0, 0), (0, 0), (0, 0))
     pad_spec_mid = ((1, 1), (0, 0), (0, 0), (0, 0))
     pad_spec_high = ((2, 0), (0, 0), (0, 0), (0, 0))

time: 421 us -> 392 us (0.931)
  local copies, waits for them, and re-layouts: 101 us -> 57.7 us
  waiting for transfers between devices: 193 us -> 208 us
    ppermute x3, waiting for transfers between devices: 4.76 us -> 22.9 us  [tree_sum(): other = lax.ppermute(part.astype(jnp.bfloat16), axis, pairs)]
    transpose x4 -> x0, local copies, waits for them, and re-layouts: 18.1 us -> none  [the longest x2 12.8 us: key_back(): grid.transpose(0, 2, 3, 1, 4)]
    another operation x4 -> x0, local copies, waits for them, and re-layouts: 17.5 us -> none  [the longest x3 17.5 us: per_device(): tile_grads = jnp.stack([key_back(grad_k), key_back(grad_v)], axis=2)]
    ppermute x2, waiting for transfers between devices: 18.3 us -> 1.48 us  [padded(): before = lax.ppermute(last, axis, up)]
    all_to_all x1, waiting for transfers between devices: 17 us -> 30.6 us  [per_device(): lax.all_to_all(output_gradient, 'head', split_axis=1, concat_axis=0, tile...]
    slice x5 -> x0, local copies, waits for them, and re-layouts: 10.7 us -> none  [the longest x2 5.59 us: per_device(): all_tiles[:, :, 1]]
    scatter-add x2 -> x0, local copies, waits for them, and re-layouts: 8.65 us -> none  [per_device(): interior = interior.at[0].add(returned_rims[:, :BLOCK_TOKENS]).at[blocks...]
    all_to_all x0 -> x2, local copies, waits for them, and re-layouts: none -> 5.62 us  [the longest x1 2.95 us: per_device(): lax.all_to_all(output_gradient, 'head', split_axis=1, concat_axis=0, tile...]
  transfers between devices with their start and end apart: 17 -> 17, of which waited for: 12 -> 13; matrix products, arithmetic and copies ran while one was open for 15% -> 11% of each run, Pallas kernels for 0% -> 0%
where the time goes in v4:
time: 392 us; the launch traced here: 389 us
  waiting for transfers between devices  208 us (53%)
  local copies, waits for them, and re-layouts  57.7 us (15%)
  starting transfers between devices  51.6 us (13%)
  Pallas kernels  43.6 us (11%)
  between operations  14.5 us (4%)
  other arithmetic  11.4 us (3%)
    all_to_all x1, waiting for transfers between devices, per_device(): lax.all_to_all(out_all, 'head', split_axis=0, concat_axis=1, tiled=True)  44.1 us
    pallas_call x1, Pallas kernels, attention_call(): pl.pallas_call(functools.partial(attention_kernel, scale=scale), grid=(bl...  43.6 us
    all_to_all x1, waiting for transfers between devices, per_device(): lax.all_to_all(query_grad_all, 'head', split_axis=0, concat_axis=1, tiled...  41.7 us
    all_to_all x1, waiting for transfers between devices, per_device(): lax.all_to_all(queries, 'head', split_axis=1, concat_axis=0, tiled=True)  39.6 us
    all_to_all x1, waiting for transfers between devices, per_device(): lax.all_to_all(output_gradient, 'head', split_axis=1, concat_axis=0, tile...  30.6 us
    ppermute x3, waiting for transfers between devices, tree_sum(): other = lax.ppermute(part.astype(jnp.bfloat16), axis, pairs)  22.9 us
    unnamed x27, local copies, waits for them, and re-layouts  17.7 us
    ppermute x2, starting transfers between devices, padded(): after = lax.ppermute(leading, axis, down)  9.3 us
  transfers between devices with their start and end apart: 17, of which 13 were waited for; matrix products, arithmetic and copies ran while one was open for 11% of the time, Pallas kernels for 0%

profile of v4, /device:TPU:4, one launch (start us, length us, event | category | flops | bytes accessed | tf_op | source)
XLA Modules:
  0.0 389.3 jit_solution(14920418988247340931)
XLA Ops:
  7.2 1.7 copy.157
  8.9 4.9 %all-to-all-start.1 = ((bf16[128,8,128]{2,0,1:T(8,128)(2,1)}), bf16[128,8,128]{2,0,1:T(8,128)(2,1)S(1)}, u32[]{:S(2)}, u32[]{:S(2)}) async-start(bf16[128,8,128]{2,0,1:T(8,128)(2,1)} %copy.157), calls=%async_computation.1 | async-start | bytes 524288 | tf_op jit(solution)/shard_map/all_to_all | solution.py:105
  13.7 1.7 copy.159
  15.4 7.2 %all-to-all-done.1 = bf16[128,8,128]{2,0,1:T(8,128)(2,1)S(1)} async-done(((bf16[128,8,128]{2,0,1:T(8,128)(2,1)}), bf16[128,8,128]{2,0,1:T(8,128)(2,1)S(1)}, u32[]{:S(2)}, u32[]{:S(2)}) %all-to-all-start.1) | async-done | bytes 262176 | tf_op jit(solution)/shard_map/all_to_all | solution.py:105
  22.6 3.4 all-to-all-start.2
  26.6 6.5 %all-to-all-done.2 = bf16[128,8,128]{2,0,1:T(8,128)(2,1)S(1)} async-done(((bf16[128,8,128]{2,0,1:T(8,128)(2,1)}), bf16[128,8,128]{2,0,1:T(8,128)(2,1)S(1)}, u32[]{:S(2)}, u32[]{:S(2)}) %all-to-all-start.2) | async-done | bytes 262176 | tf_op jit(solution)/shard_map/all_to_all | solution.py:106
  33.5 0.8 copy-done
  34.4 2.7 copy.155
  37.1 3.7 all-to-all-start
  42.0 4.5 %copy.167 = bf16[128,64,128]{2,0,1:T(8,128)(2,1)} copy(bf16[128,64,128]{2,1,0:T(8,128)(2,1)} %param.13) | data formatting | bytes 4194304 | tf_op args[3]
  46.7 39.6 %all-to-all-done = bf16[128,64,128]{2,0,1:T(8,128)(2,1)S(1)} async-done(((bf16[128,64,128]{2,0,1:T(8,128)(2,1)}), bf16[128,64,128]{2,0,1:T(8,128)(2,1)S(1)}, u32[]{:S(2)}, u32[]{:S(2)}) %all-to-all-start) | async-done | bytes 2097184 | tf_op jit(solution)/shard_map/all_to_all | solution.py:104
  86.2 4.4 %all-to-all-start.3 = ((bf16[128,64,128]{2,0,1:T(8,128)(2,1)}), bf16[128,64,128]{2,0,1:T(8,128)(2,1)}, u32[]{:S(2)}, u32[]{:S(2)}) async-start(bf16[128,64,128]{2,0,1:T(8,128)(2,1)} %copy.167), calls=%async_computation.3 | async-start | bytes 4194304 | tf_op jit(solution)/shard_map/all_to_all | solution.py:107
  91.1 1.9 collective-permute-start
  93.1 4.5 %collective-permute-start.1 = (bf16[2,128,256]{2,1,0:T(8,128)(2,1)S(1)}, bf16[2,128,256]{2,1,0:T(8,128)(2,1)S(1)}, u32[]{:S(2)}, u32[]{:S(2)}) collective-permute-start(bf16[2,128,256]{2,1,0:T(8,128)(2,1)S(1)} %get-tuple-element.53), channel_id=1, source_target_pairs={{4,0},{8,4},{12,8},{16,12},{20,16},{24,20},{28,24},{5,1},{9,5},{13... | collective-permute-start | bytes 393224 | tf_op jit(solution)/shard_map/ppermute | solution.py:79
  97.8 0.6 collective-permute-done
  98.3 1.8 collective-permute-done.1
  100.3 0.8 copy_bitcast_fusion.5
  101.1 2.7 copy.223
  103.8 4.2 %reshape.350.q_ref = bf16[4,128,2048]{2,1,0:T(8,128)(2,1)} reshape(bf16[4,128,16,128]{3,2,1,0:T(8,128)(2,1)} %bitcast.136) | data formatting | bytes 4194304 | tf_op jit(solution)/shard_map/reshape | solution.py:191
  108.0 30.6 %all-to-all-done.3 = bf16[128,64,128]{2,0,1:T(8,128)(2,1)} async-done(((bf16[128,64,128]{2,0,1:T(8,128)(2,1)}), bf16[128,64,128]{2,0,1:T(8,128)(2,1)}, u32[]{:S(2)}, u32[]{:S(2)}) %all-to-all-start.3) | async-done | bytes 2097184 | tf_op jit(solution)/shard_map/all_to_all | solution.py:107
  138.5 2.9 copy.222
  141.5 2.3 reshape.359.do_ref
  143.8 2.7 gather_fusion
  146.5 2.8 gather_fusion.1
  150.0 0.7 copy-done.7
  151.1 2.3 pad_maximum_fusion.k_ref.v_ref
  153.4 0.7 broadcast_in_dim.42
  154.1 43.6 %shard_map.93 = (bf16[4,128,2048]{2,1,0:T(8,128)(2,1)}, bf16[4,128,2048]{2,1,0:T(8,128)(2,1)}, f32[4,8,2,128,256]{4,3,2,1,0:T(8,128)}) custom-call(bf16[4,128,2048]{2,1,0:T(8,128)(2,1)} %reshape.350.q_ref, bf16[4,8,2,128,256]{4,3,2,1,0:T(8,128)(2,1)} %pad_maximum_fusion.k_ref.v_ref, bf16[4,8,2,128,256]{4,3,2,1,0:T(8,128)(2,1)} %pad_maximum_fusion.k_ref.v_ref, ...), custom_call_target="tpu_custom_call" | custom-call | tf_op jit(solution)/shard_map/pallas_call | solution.py:58
  197.7 1.8 slice_reduce_fusion
  199.5 2.1 fusion.7
  201.6 3.1 slice_bitcast_fusion.1
  204.9 1.0 fusion.4
  206.0 2.0 copy.183
  208.0 4.3 %all-to-all-start.6 = ((bf16[16,2,128,256]{3,2,1,0:T(8,128)(2,1)}), bf16[16,2,128,256]{3,2,1,0:T(8,128)(2,1)S(1)}, u32[]{:S(2)}, u32[]{:S(2)}) async-start(bf16[16,2,128,256]{3,2,1,0:T(8,128)(2,1)} %copy.183), calls=%async_computation.6 | async-start | bytes 4194304 | tf_op jit(solution)/shard_map/all_to_all | solution.py:235
  212.3 1.5 slice_bitcast_fusion.2
  213.9 1.5 collective-permute-start.5
  215.7 1.9 collective-permute-start.2
  217.6 4.8 %collective-permute-start.3 = (bf16[2,128,256]{2,1,0:T(8,128)(2,1)S(1)}, bf16[2,128,256]{2,1,0:T(8,128)(2,1)S(1)}, u32[]{:S(2)}, u32[]{:S(2)}) collective-permute-start(bf16[2,128,256]{2,1,0:T(8,128)(2,1)S(1)} %get-tuple-element.45), channel_id=1, source_target_pairs={{4,0},{8,4},{12,8},{16,12},{20,16},{24,20},{28,24},{5,1},{9,5},{13... | collective-permute-start | bytes 393224 | tf_op jit(solution)/shard_map/ppermute | solution.py:79
  222.4 1.1 slice.168
  223.5 19.6 %collective-permute-done.5 = bf16[2,2,128,256]{3,2,1,0:T(8,128)(2,1)S(1)} collective-permute-done((bf16[2,2,128,256]{3,2,1,0:T(8,128)(2,1)S(1)}, bf16[2,2,128,256]{3,2,1,0:T(8,128)(2,1)S(1)}, u32[]{:S(2)}, u32[]{:S(2)}) %collective-permute-start.5) | collective-permute-done | bytes 262176 | tf_op jit(solution)/shard_map/ppermute | solution.py:96
  243.2 1.2 collective-permute-start.6
  244.4 0.9 collective-permute-done.2
  245.3 0.7 fusion.25
  246.0 1.7 fusion.23
  247.7 3.3 collective-permute-done.6
  251.1 1.2 multiply_reduce_fusion
  252.4 1.3 fusion.8
  253.7 1.5 fusion.21
  255.3 0.8 reshape_squeeze.7
  256.0 3.4 all-to-all-start.8
  259.4 0.8 reshape_squeeze.6
  260.2 7.4 %all-to-all-done.8 = bf16[512,2,128]{2,1,0:T(2,128)(2,1)S(1)} async-done(((bf16[512,2,128]{2,1,0:T(2,128)(2,1)}), bf16[512,2,128]{2,1,0:T(2,128)(2,1)S(1)}, u32[]{:S(2)}, u32[]{:S(2)}) %all-to-all-start.8) | async-done | bytes 262176 | tf_op jit(solution)/shard_map/all_to_all | solution.py:251
  267.6 3.4 all-to-all-start.7
  271.0 1.9 copy.195
  273.0 4.8 %all-to-all-done.7 = bf16[512,2,128]{2,1,0:T(2,128)(2,1)S(1)} async-done(((bf16[512,2,128]{2,1,0:T(2,128)(2,1)}), bf16[512,2,128]{2,1,0:T(2,128)(2,1)S(1)}, u32[]{:S(2)}, u32[]{:S(2)}) %all-to-all-start.7) | async-done | bytes 262176 | tf_op jit(solution)/shard_map/all_to_all | solution.py:250
  277.7 3.6 all-to-all-start.5
  281.4 3.5 copy.194
  284.9 41.7 %all-to-all-done.5 = bf16[512,16,128]{2,1,0:T(8,128)(2,1)S(1)} async-done(((bf16[512,16,128]{2,1,0:T(8,128)(2,1)}), bf16[512,16,128]{2,1,0:T(8,128)(2,1)S(1)}, u32[]{:S(2)}, u32[]{:S(2)}) %all-to-all-start.5) | async-done | bytes 2097184 | tf_op jit(solution)/shard_map/all_to_all | solution.py:249
  326.6 4.4 %all-to-all-start.4 = ((bf16[512,16,128]{2,1,0:T(8,128)(2,1)}), bf16[512,16,128]{2,1,0:T(8,128)(2,1)}, u32[]{:S(2)}, u32[]{:S(2)}) async-start(bf16[512,16,128]{2,1,0:T(8,128)(2,1)} %bitcast.134), calls=%async_computation.4 | async-start | bytes 4194304 | tf_op jit(solution)/shard_map/all_to_all | solution.py:248
  331.1 0.9 copy.188
  332.0 0.9 copy.187
  332.9 2.0 copy.171
  334.8 44.1 %all-to-all-done.4 = bf16[512,16,128]{2,1,0:T(8,128)(2,1)} async-done(((bf16[512,16,128]{2,1,0:T(8,128)(2,1)}), bf16[512,16,128]{2,1,0:T(8,128)(2,1)}, u32[]{:S(2)}, u32[]{:S(2)}) %all-to-all-start.4) | async-done | bytes 2097184 | tf_op jit(solution)/shard_map/all_to_all | solution.py:248
  378.9 3.6 copy.170
  (75 shorter events, 4.8 us)
Async XLA Ops:
  8.9 13.8 %all-to-all-start.1 = ((bf16[128,8,128]{2,0,1:T(8,128)(2,1)}), bf16[128,8,128]{2,0,1:T(8,128)(2,1)S(1)}, u32[]{:S(2)}, u32[]{:S(2)}) async-start(bf16[128,8,128]{2,0,1:T(8,128)(2,1)} %copy.157), calls=%async_computation.1 | async-start | bytes 524288 | tf_op jit(solution)/shard_map/all_to_all | solution.py:105
  15.4 19.0 %copy-start.5 = (bf16[128,64,128]{2,1,0:T(8,128)(2,1)S(1)}, bf16[128,64,128]{2,1,0:T(8,128)(2,1)}, u32[]{:S(2)}) copy-start(bf16[128,64,128]{2,1,0:T(8,128)(2,1)} %param.10) | copy-start | bytes 6291460
  22.6 10.4 %all-to-all-start.2 = ((bf16[128,8,128]{2,0,1:T(8,128)(2,1)}), bf16[128,8,128]{2,0,1:T(8,128)(2,1)S(1)}, u32[]{:S(2)}, u32[]{:S(2)}) async-start(bf16[128,8,128]{2,0,1:T(8,128)(2,1)} %copy.159), calls=%async_computation.2 | async-start | bytes 524288 | tf_op jit(solution)/shard_map/all_to_all | solution.py:106
  26.1 117.7 %all-gather.2.cloned.1.call-start = ((), (), s32[]{:S(2)}) async-start(), calls=%async_computation.9 | async-start | bytes 4718592 | tf_op jit(solution)/shard_map/all_gather | solution.py:155
  33.5 0.8 copy-start
  37.1 3.8 copy-start.8
  37.1 49.2 %all-to-all-start = ((bf16[128,64,128]{2,0,1:T(8,128)(2,1)}), bf16[128,64,128]{2,0,1:T(8,128)(2,1)S(1)}, u32[]{:S(2)}, u32[]{:S(2)}) async-start(bf16[128,64,128]{2,0,1:T(8,128)(2,1)} %copy.155), calls=%async_computation | async-start | bytes 4194304 | tf_op jit(solution)/shard_map/all_to_all | solution.py:104
  42.0 4.6 %copy-start.9 = (s32[2]{0:T(128)S(1)}, s32[2]{0:T(128)}, u32[]{:S(2)}) copy-start(s32[2]{0:T(128)} %param.14) | copy-start | bytes 28
  46.7 44.4 %copy-start.1 = (bf16[2,512,256]{2,1,0:T(8,128)(2,1)S(1)}, bf16[2,512,256]{2,1,0:T(8,128)(2,1)}, u32[]{:S(2)}) copy-start(bf16[2,512,256]{2,1,0:T(8,128)(2,1)} %copy-done) | copy-start | bytes 1572868
  86.2 52.3 %all-to-all-start.3 = ((bf16[128,64,128]{2,0,1:T(8,128)(2,1)}), bf16[128,64,128]{2,0,1:T(8,128)(2,1)}, u32[]{:S(2)}, u32[]{:S(2)}) async-start(bf16[128,64,128]{2,0,1:T(8,128)(2,1)} %copy.167), calls=%async_computation.3 | async-start | bytes 4194304 | tf_op jit(solution)/shard_map/all_to_all | solution.py:107
  91.1 7.2 %collective-permute-start = (bf16[2,128,256]{2,1,0:T(8,128)(2,1)S(1)}, bf16[2,128,256]{2,1,0:T(8,128)(2,1)S(1)}, u32[]{:S(2)}, u32[]{:S(2)}) collective-permute-start(bf16[2,128,256]{2,1,0:T(8,128)(2,1)S(1)} %get-tuple-element.52), channel_id=1, source_target_pairs={{0,4},{4,8},{8,12},{12,16},{16,20},{20,24},{24,28},{1,5},{5,9},{9,... | collective-permute-start | bytes 393224 | tf_op jit(solution)/shard_map/ppermute | solution.py:78
  93.1 7.0 %collective-permute-start.1 = (bf16[2,128,256]{2,1,0:T(8,128)(2,1)S(1)}, bf16[2,128,256]{2,1,0:T(8,128)(2,1)S(1)}, u32[]{:S(2)}, u32[]{:S(2)}) collective-permute-start(bf16[2,128,256]{2,1,0:T(8,128)(2,1)S(1)} %get-tuple-element.53), channel_id=1, source_target_pairs={{4,0},{8,4},{12,8},{16,12},{20,16},{24,20},{28,24},{5,1},{9,5},{13... | collective-permute-start | bytes 393224 | tf_op jit(solution)/shard_map/ppermute | solution.py:79
  149.7 1.0 copy-start.7
  204.7 9.1 %collective-permute-start.4 = (bf16[2,2,128,256]{3,2,1,0:T(8,128)(2,1)S(1)}, bf16[2,2,128,256]{3,2,1,0:T(8,128)(2,1)S(1)}, u32[]{:S(2)}, u32[]{:S(2)}) collective-permute-start(bf16[2,2,128,256]{3,2,1,0:T(8,128)(2,1)S(1)} %convert_element_type.63), channel_id=1, source_target_pairs={{0,4},{4,0},{8,12},{12,8},{16,20},{20,16},{24,28},{28,24},{1,5},{5... | collective-permute-start | bytes 786440 | tf_op jit(solution)/shard_map/ppermute | solution.py:96
  208.0 44.4 %all-to-all-start.6 = ((bf16[16,2,128,256]{3,2,1,0:T(8,128)(2,1)}), bf16[16,2,128,256]{3,2,1,0:T(8,128)(2,1)S(1)}, u32[]{:S(2)}, u32[]{:S(2)}) async-start(bf16[16,2,128,256]{3,2,1,0:T(8,128)(2,1)} %copy.183), calls=%async_computation.6 | async-start | bytes 4194304 | tf_op jit(solution)/shard_map/all_to_all | solution.py:235
  212.3 3.1 copy-start.3
  212.3 3.1 copy-start.4
  213.9 29.2 %collective-permute-start.5 = (bf16[2,2,128,256]{3,2,1,0:T(8,128)(2,1)S(1)}, bf16[2,2,128,256]{3,2,1,0:T(8,128)(2,1)S(1)}, u32[]{:S(2)}, u32[]{:S(2)}) collective-permute-start(bf16[2,2,128,256]{3,2,1,0:T(8,128)(2,1)S(1)} %fusion.22), channel_id=1, source_target_pairs={{0,8},{4,12},{8,0},{12,4},{16,24},{20,28},{24,16},{28,20},{1,9},{5... | collective-permute-start | bytes 786440 | tf_op jit(solution)/shard_map/ppermute | solution.py:96
  215.7 29.6 %collective-permute-start.2 = (bf16[2,128,256]{2,1,0:T(8,128)(2,1)S(1)}, bf16[2,128,256]{2,1,0:T(8,128)(2,1)S(1)}, u32[]{:S(2)}, u32[]{:S(2)}) collective-permute-start(bf16[2,128,256]{2,1,0:T(8,128)(2,1)S(1)} %get-tuple-element.44), channel_id=1, source_target_pairs={{0,4},{4,8},{8,12},{12,16},{16,20},{20,24},{24,28},{1,5},{5,9},{9,... | collective-permute-start | bytes 393224 | tf_op jit(solution)/shard_map/ppermute | solution.py:78
  217.6 27.7 %collective-permute-start.3 = (bf16[2,128,256]{2,1,0:T(8,128)(2,1)S(1)}, bf16[2,128,256]{2,1,0:T(8,128)(2,1)S(1)}, u32[]{:S(2)}, u32[]{:S(2)}) collective-permute-start(bf16[2,128,256]{2,1,0:T(8,128)(2,1)S(1)} %get-tuple-element.45), channel_id=1, source_target_pairs={{4,0},{8,4},{12,8},{16,12},{20,16},{24,20},{28,24},{5,1},{9,5},{13... | collective-permute-start | bytes 393224 | tf_op jit(solution)/shard_map/ppermute | solution.py:79
  243.2 7.8 %collective-permute-start.6 = (bf16[2,2,128,256]{3,2,1,0:T(8,128)(2,1)S(1)}, bf16[2,2,128,256]{3,2,1,0:T(8,128)(2,1)S(1)}, u32[]{:S(2)}, u32[]{:S(2)}) collective-permute-start(bf16[2,2,128,256]{3,2,1,0:T(8,128)(2,1)S(1)} %fusion.26), channel_id=1, source_target_pairs={{0,16},{4,20},{8,24},{12,28},{16,0},{20,4},{24,8},{28,12},{1,17},{... | collective-permute-start | bytes 786440 | tf_op jit(solution)/shard_map/ppermute | solution.py:96
  252.4 1.3 copy-start.2
  255.2 15.8 %copy-start.6 = (bf16[4,128,2048]{2,1,0:T(8,128)(2,1)S(1)}, bf16[4,128,2048]{2,1,0:T(8,128)(2,1)}, u32[]{:S(2)}) copy-start(bf16[4,128,2048]{2,1,0:T(8,128)(2,1)} %get-tuple-element.32) | copy-start | bytes 6291460
  256.0 11.6 %all-to-all-start.8 = ((bf16[512,2,128]{2,1,0:T(2,128)(2,1)}), bf16[512,2,128]{2,1,0:T(2,128)(2,1)S(1)}, u32[]{:S(2)}, u32[]{:S(2)}) async-start(bf16[512,2,128]{2,1,0:T(2,128)(2,1)} %reshape_squeeze.7), calls=%async_computation.8 | async-start | bytes 524288 | tf_op jit(solution)/shard_map/all_to_all | solution.py:251
  267.6 10.2 %all-to-all-start.7 = ((bf16[512,2,128]{2,1,0:T(2,128)(2,1)}), bf16[512,2,128]{2,1,0:T(2,128)(2,1)S(1)}, u32[]{:S(2)}, u32[]{:S(2)}) async-start(bf16[512,2,128]{2,1,0:T(2,128)(2,1)} %reshape_squeeze.6), calls=%async_computation.7 | async-start | bytes 524288 | tf_op jit(solution)/shard_map/all_to_all | solution.py:250
  277.7 48.9 %all-to-all-start.5 = ((bf16[512,16,128]{2,1,0:T(8,128)(2,1)}), bf16[512,16,128]{2,1,0:T(8,128)(2,1)S(1)}, u32[]{:S(2)}, u32[]{:S(2)}) async-start(bf16[512,16,128]{2,1,0:T(8,128)(2,1)} %bitcast.135), calls=%async_computation.5 | async-start | bytes 4194304 | tf_op jit(solution)/shard_map/all_to_all | solution.py:249
  326.6 52.3 %all-to-all-start.4 = ((bf16[512,16,128]{2,1,0:T(8,128)(2,1)}), bf16[512,16,128]{2,1,0:T(8,128)(2,1)}, u32[]{:S(2)}, u32[]{:S(2)}) async-start(bf16[512,16,128]{2,1,0:T(8,128)(2,1)} %bitcast.134), calls=%async_computation.4 | async-start | bytes 4194304 | tf_op jit(solution)/shard_map/all_to_all | solution.py:248
Sparse Core Ops, SparseCore 0:
  34.5 35.9 all-gather.1

commit v5 on v4

--- a/solution.py
+++ b/solution.py
@@ -68,6 +68,27 @@
     )(q, tiles, tiles, do, bias)
 
 
+def exchange(array, axis, split_axis, concat_axis):
+    count = lax.axis_size(axis)
+    own = lax.axis_index(axis)
+    piece = array.shape[split_axis] // count
+    received = []
+    for shift in range(count):
+        target = (own + shift) % count
+        part = lax.dynamic_slice_in_dim(array, target * piece, piece, split_axis)
+        if shift:
+            pairs = [(i, (i + shift) % count) for i in range(count)]
+            part = lax.ppermute(part, axis, pairs)
+        received.append(part)
+    order = (own - jnp.arange(count)) % count
+    stacked = jnp.take(jnp.stack(received), order, axis=0)
+    stacked = jnp.moveaxis(stacked, 0, concat_axis)
+    shape = list(array.shape)
+    shape[split_axis] = piece
+    shape[concat_axis] *= count
+    return stacked.reshape(shape)
+
+
 def padded(shard, sides, width):
     for axis, dim in sides:
         count, length = (lax.axis_size(axis), shard.shape[dim])
@@ -232,7 +253,7 @@
     back_buffer = jnp.einsum(
         "es,exbw->sxbw", slot_onehot, random_terms, preferred_element_type=jnp.float32
     ).astype(jnp.bfloat16)
-    returned_terms = lax.all_to_all(back_buffer, "seq", split_axis=0, concat_axis=0, tiled=True)
+    returned_terms = exchange(back_buffer, "seq", 0, 0)
     interior = interior + jnp.einsum(
         "tco,tcxbw->oxbw",
         selector,
@@ -244,12 +265,12 @@
     query_grad_all = query_gradient_rows.reshape(shard_len, heads_q, head_width)
     key_grad_all = kv_grad[0].reshape(shard_len, heads_kv, head_width)
     value_grad_all = kv_grad[1].reshape(shard_len, heads_kv, head_width)
-    return (
-        lax.all_to_all(out_all, "head", split_axis=0, concat_axis=1, tiled=True),
-        lax.all_to_all(query_grad_all, "head", split_axis=0, concat_axis=1, tiled=True),
-        lax.all_to_all(key_grad_all, "head", split_axis=0, concat_axis=1, tiled=True),
-        lax.all_to_all(value_grad_all, "head", split_axis=0, concat_axis=1, tiled=True),
-    )
+    out_back = lax.all_to_all(out_all, "head", split_axis=0, concat_axis=1, tiled=True)
+    query_back = lax.all_to_all(query_grad_all, "head", split_axis=0, concat_axis=1, tiled=True)
+    (out_back, query_back), kv_grad = lax.optimization_barrier(((out_back, query_back), kv_grad))
+    kv_grad = kv_grad.reshape(2, shard_len, heads_kv, head_width)
+    kv_back = lax.all_to_all(kv_grad, "head", split_axis=1, concat_axis=2, tiled=True)
+    return (out_back, query_back, kv_back[0], kv_back[1])
 
 
 def solution(mesh):

time: 392 us -> 341 us (0.87)
  waiting for transfers between devices: 208 us -> 127 us
  blocking collectives: 0 us -> 16.4 us
  local copies, waits for them, and re-layouts: 57.7 us -> 72.6 us
    all_to_all x1, waiting for transfers between devices: 44.1 us -> 15.4 us  [per_device(): lax.all_to_all(out_all, 'head', split_axis=0, concat_axis=1, tiled=True)]
    all_to_all x1, waiting for transfers between devices: 41.7 us -> 19.9 us  [per_device(): lax.all_to_all(query_grad_all, 'head', split_axis=0, concat_axis=1, tiled...]
    ppermute x3, waiting for transfers between devices: 22.9 us -> 1.79 us  [tree_sum(): other = lax.ppermute(part.astype(jnp.bfloat16), axis, pairs)]
    all_to_all x0 -> x1, blocking collectives: none -> 16.4 us  [per_device(): lax.all_to_all(kv_grad, 'head', split_axis=1, concat_axis=2, tiled=True)]
    all_to_all x3 -> x0, waiting for transfers between devices: 12.2 us -> none  [the longest x1 7.38 us: per_device(): lax.all_to_all(value_grad_all, 'head', split_axis=0, concat_axis=1, tiled...]
    all_to_all x3 -> x0, starting transfers between devices: 11.1 us -> none  [the longest x1 4.32 us: per_device(): lax.all_to_all(back_buffer, 'seq', split_axis=0, concat_axis=0, tiled=True)]
    unnamed x27 -> x32, local copies, waits for them, and re-layouts: 17.7 us -> 27.6 us
    ppermute x0 -> x7, starting transfers between devices: none -> 7.72 us  [exchange(): part = lax.ppermute(part, axis, pairs)]
  transfers between devices with their start and end apart: 17 -> 21, of which waited for: 13 -> 10; matrix products, arithmetic and copies ran while one was open for 11% -> 19% of each run, Pallas kernels for 0% -> 0%
where the time goes in v5:
time: 341 us; the launch traced here: 338 us
  waiting for transfers between devices  127 us (37%)
  local copies, waits for them, and re-layouts  72.6 us (21%)
  starting transfers between devices  48.6 us (14%)
  Pallas kernels  43.6 us (13%)
  blocking collectives  16.4 us (5%)
  between operations  14.7 us (4%)
  other arithmetic  12.7 us (4%)
    pallas_call x1, Pallas kernels, attention_call(): pl.pallas_call(functools.partial(attention_kernel, scale=scale), grid=(bl...  43.6 us
    all_to_all x1, waiting for transfers between devices, per_device(): lax.all_to_all(queries, 'head', split_axis=1, concat_axis=0, tiled=True)  41.5 us
    all_to_all x1, waiting for transfers between devices, per_device(): lax.all_to_all(output_gradient, 'head', split_axis=1, concat_axis=0, tile...  31.1 us
    unnamed x32, local copies, waits for them, and re-layouts  27.6 us
    all_to_all x1, waiting for transfers between devices, per_device(): lax.all_to_all(query_grad_all, 'head', split_axis=0, concat_axis=1, tiled...  19.9 us
    all_to_all x1, blocking collectives, per_device(): lax.all_to_all(kv_grad, 'head', split_axis=1, concat_axis=2, tiled=True)  16.4 us
    all_to_all x1, waiting for transfers between devices, per_device(): lax.all_to_all(out_all, 'head', split_axis=0, concat_axis=1, tiled=True)  15.4 us
    ppermute x2, starting transfers between devices, padded(): after = lax.ppermute(leading, axis, down)  9 us
  transfers between devices with their start and end apart: 21, of which 10 were waited for; matrix products, arithmetic and copies ran while one was open for 19% of the time, Pallas kernels for 0%

profile of v5, /device:TPU:4, one launch (start us, length us, event | category | flops | bytes accessed | tf_op | source)
XLA Modules:
  0.0 338.0 jit_solution(148773777599992634)
XLA Ops:
  7.2 1.7 copy.163
  8.9 4.9 %all-to-all-start.1 = ((bf16[128,8,128]{2,0,1:T(8,128)(2,1)}), bf16[128,8,128]{2,0,1:T(8,128)(2,1)S(1)}, u32[]{:S(2)}, u32[]{:S(2)}) async-start(bf16[128,8,128]{2,0,1:T(8,128)(2,1)} %copy.163), calls=%async_computation.1 | async-start | bytes 524288 | tf_op jit(solution)/shard_map/all_to_all | solution.py:126
  13.7 1.7 copy.165
  15.4 7.2 %all-to-all-done.1 = bf16[128,8,128]{2,0,1:T(8,128)(2,1)S(1)} async-done(((bf16[128,8,128]{2,0,1:T(8,128)(2,1)}), bf16[128,8,128]{2,0,1:T(8,128)(2,1)S(1)}, u32[]{:S(2)}, u32[]{:S(2)}) %all-to-all-start.1) | async-done | bytes 262176 | tf_op jit(solution)/shard_map/all_to_all | solution.py:126
  22.6 3.4 %all-to-all-start.2 = ((bf16[128,8,128]{2,0,1:T(8,128)(2,1)}), bf16[128,8,128]{2,0,1:T(8,128)(2,1)S(1)}, u32[]{:S(2)}, u32[]{:S(2)}) async-start(bf16[128,8,128]{2,0,1:T(8,128)(2,1)} %copy.165), calls=%async_computation.2 | async-start | bytes 524288 | tf_op jit(solution)/shard_map/all_to_all | solution.py:127
  26.6 6.5 %all-to-all-done.2 = bf16[128,8,128]{2,0,1:T(8,128)(2,1)S(1)} async-done(((bf16[128,8,128]{2,0,1:T(8,128)(2,1)}), bf16[128,8,128]{2,0,1:T(8,128)(2,1)S(1)}, u32[]{:S(2)}, u32[]{:S(2)}) %all-to-all-start.2) | async-done | bytes 262176 | tf_op jit(solution)/shard_map/all_to_all | solution.py:127
  34.4 4.3 %copy.161 = bf16[128,64,128]{2,0,1:T(8,128)(2,1)} copy(bf16[128,64,128]{2,1,0:T(8,128)(2,1)} %param.10) | data formatting | bytes 4194304 | tf_op args[0]
  38.7 4.6 %all-to-all-start = ((bf16[128,64,128]{2,0,1:T(8,128)(2,1)}), bf16[128,64,128]{2,0,1:T(8,128)(2,1)}, u32[]{:S(2)}, u32[]{:S(2)}) async-start(bf16[128,64,128]{2,0,1:T(8,128)(2,1)} %copy.161), calls=%async_computation | async-start | bytes 4194304 | tf_op jit(solution)/shard_map/all_to_all | solution.py:125
  43.9 2.7 copy.173
  47.3 41.5 %all-to-all-done = bf16[128,64,128]{2,0,1:T(8,128)(2,1)} async-done(((bf16[128,64,128]{2,0,1:T(8,128)(2,1)}), bf16[128,64,128]{2,0,1:T(8,128)(2,1)}, u32[]{:S(2)}, u32[]{:S(2)}) %all-to-all-start) | async-done | bytes 2097184 | tf_op jit(solution)/shard_map/all_to_all | solution.py:125
  88.8 4.5 %all-to-all-start.3 = ((bf16[128,64,128]{2,0,1:T(8,128)(2,1)}), bf16[128,64,128]{2,0,1:T(8,128)(2,1)}, u32[]{:S(2)}, u32[]{:S(2)}) async-start(bf16[128,64,128]{2,0,1:T(8,128)(2,1)} %copy.173), calls=%async_computation.3 | async-start | bytes 4194304 | tf_op jit(solution)/shard_map/all_to_all | solution.py:128
  93.7 1.9 collective-permute-start
  95.6 4.7 %collective-permute-start.1 = (bf16[2,128,256]{2,1,0:T(8,128)(2,1)S(1)}, bf16[2,128,256]{2,1,0:T(8,128)(2,1)S(1)}, u32[]{:S(2)}, u32[]{:S(2)}) collective-permute-start(bf16[2,128,256]{2,1,0:T(8,128)(2,1)S(1)} %get-tuple-element.82), channel_id=1, source_target_pairs={{4,0},{8,4},{12,8},{16,12},{20,16},{24,20},{28,24},{5,1},{9,5},{13... | collective-permute-start | bytes 393224 | tf_op jit(solution)/shard_map/ppermute | solution.py:100
  100.8 1.8 collective-permute-done.1
  102.8 1.0 copy_bitcast_fusion.3
  103.7 0.9 copy_bitcast_fusion.5
  104.7 2.9 copy.233
  107.6 2.3 reshape.404.q_ref
  109.9 31.1 %all-to-all-done.3 = bf16[128,64,128]{2,0,1:T(8,128)(2,1)} async-done(((bf16[128,64,128]{2,0,1:T(8,128)(2,1)}), bf16[128,64,128]{2,0,1:T(8,128)(2,1)}, u32[]{:S(2)}, u32[]{:S(2)}) %all-to-all-start.3) | async-done | bytes 2097184 | tf_op jit(solution)/shard_map/all_to_all | solution.py:128
  141.0 2.9 copy.232
  144.0 2.3 reshape.413.do_ref
  146.3 2.8 gather_fusion.1
  149.5 0.9 slice_bitcast_fusion.6
  150.3 2.7 gather_fusion
  153.2 1.8 fusion.13
  155.0 2.3 pad_maximum_fusion.k_ref.v_ref
  157.9 43.6 %shard_map.93 = (bf16[4,128,2048]{2,1,0:T(8,128)(2,1)}, bf16[4,128,2048]{2,1,0:T(8,128)(2,1)}, f32[4,8,2,128,256]{4,3,2,1,0:T(8,128)}) custom-call(bf16[4,128,2048]{2,1,0:T(8,128)(2,1)} %reshape.404.q_ref, bf16[4,8,2,128,256]{4,3,2,1,0:T(8,128)(2,1)} %pad_maximum_fusion.k_ref.v_ref, bf16[4,8,2,128,256]{4,3,2,1,0:T(8,128)(2,1)} %pad_maximum_fusion.k_ref.v_ref, ...), custom_call_target="tpu_custom_call" | custom-call | tf_op jit(solution)/shard_map/pallas_call | solution.py:58
  201.6 3.5 %copy.204 = bf16[64,8,16,128]{3,2,1,0:T(8,128)(2,1)} copy(bf16[64,8,16,128]{3,1,2,0:T(8,128)(2,1)} %bitcast.148) | data formatting | bytes 4194304
  205.1 3.6 %all-to-all-start.4 = ((bf16[512,16,128]{2,1,0:T(8,128)(2,1)}), bf16[512,16,128]{2,1,0:T(8,128)(2,1)S(1)}, u32[]{:S(2)}, u32[]{:S(2)}) async-start(bf16[512,16,128]{2,1,0:T(8,128)(2,1)} %bitcast.139), calls=%async_computation.4 | async-start | bytes 4194304 | tf_op jit(solution)/shard_map/all_to_all | solution.py:268
  208.9 1.8 slice_reduce_fusion
  210.8 1.3 slice_bitcast_fusion.2
  212.1 1.7 slice_bitcast_fusion.1
  214.2 2.4 collective-permute-start.2
  216.7 4.3 %collective-permute-start.3 = (bf16[2,128,256]{2,1,0:T(8,128)(2,1)S(1)}, bf16[2,128,256]{2,1,0:T(8,128)(2,1)S(1)}, u32[]{:S(2)}, u32[]{:S(2)}) collective-permute-start(bf16[2,128,256]{2,1,0:T(8,128)(2,1)S(1)} %get-tuple-element.74), channel_id=1, source_target_pairs={{4,0},{8,4},{12,8},{16,12},{20,16},{24,20},{28,24},{5,1},{9,5},{13... | collective-permute-start | bytes 393224 | tf_op jit(solution)/shard_map/ppermute | solution.py:100
  220.9 2.1 fusion.7
  223.2 1.0 fusion.4
  224.2 2.8 constant_dynamic-slice_fusion
  227.8 2.0 copy.205
  229.8 1.0 bitcast_dynamic-update-slice_fusion.7
  230.8 1.3 collective-permute-start.9
  232.1 1.5 collective-permute-start.10
  233.8 0.9 fusion.22
  234.7 1.4 collective-permute-done.7
  236.1 1.0 collective-permute-start.12
  237.1 0.9 bitcast_dynamic-update-slice_fusion.6
  238.0 3.1 collective-permute-start.13
  241.1 15.4 %all-to-all-done.4 = bf16[512,16,128]{2,1,0:T(8,128)(2,1)S(1)} async-done(((bf16[512,16,128]{2,1,0:T(8,128)(2,1)}), bf16[512,16,128]{2,1,0:T(8,128)(2,1)S(1)}, u32[]{:S(2)}, u32[]{:S(2)}) %all-to-all-start.4) | async-done | bytes 2097184 | tf_op jit(solution)/shard_map/all_to_all | solution.py:268
  256.5 4.5 %all-to-all-start.5 = ((bf16[512,16,128]{2,1,0:T(8,128)(2,1)}), bf16[512,16,128]{2,1,0:T(8,128)(2,1)}, u32[]{:S(2)}, u32[]{:S(2)}) async-start(bf16[512,16,128]{2,1,0:T(8,128)(2,1)} %bitcast.140), calls=%async_computation.5 | async-start | bytes 4194304 | tf_op jit(solution)/shard_map/all_to_all | solution.py:269
  260.9 0.9 bitcast_dynamic-update-slice_fusion.5
  261.8 1.5 collective-permute-start.5
  263.3 0.9 bitcast_dynamic-update-slice_fusion.4
  264.2 1.8 bitcast_dynamic-update-slice_fusion.3
  266.0 1.8 bitcast_dynamic-update-slice_fusion.2
  267.9 1.8 bitcast_dynamic-update-slice_fusion.1
  269.7 1.8 bitcast_dynamic-update-slice_fusion
  271.6 7.3 %gather_fusion.2 = bf16[8,2,2,128,256]{4,1,3,2,0:T(2,128)(2,1)} fusion(bf16[8,2,2,128,256]{4,1,3,2,0:T(2,128)(2,1)} %bitcast_dynamic-update-slice_fusion, s32[1024]{0:T(1024)S(1)} %pad_clamp_fusion), kind=kCustom, calls=%fused_computation.2 | custom fusion | bytes 4194336 | tf_op jit(solution)/shard_map/jit(_take)/gather | solution.py:84
  279.5 3.5 %broadcast_select_fusion = bf16[8,2,2,128,256]{4,1,3,2,0:T(2,128)(2,1)S(1)} fusion(bf16[8,2,2,128,256]{4,1,3,2,0:T(2,128)(2,1)} %gather_fusion.2, pred[8]{0:T(512)(128)(4,1)S(1)} %compare_and_fusion.2), kind=kLoop, calls=%fused_computation.4 | loop fusion | flops 1048576 | bytes 4194312 | tf_op jit(solution)/shard_map/jit(_take)/select_n | solution.py:84
  283.0 1.3 fusion.8
  284.3 1.8 collective-permute-done.6
  286.9 2.0 copy.176
  288.9 19.9 %all-to-all-done.5 = bf16[512,16,128]{2,1,0:T(8,128)(2,1)} async-done(((bf16[512,16,128]{2,1,0:T(8,128)(2,1)}), bf16[512,16,128]{2,1,0:T(8,128)(2,1)}, u32[]{:S(2)}, u32[]{:S(2)}) %all-to-all-start.5) | async-done | bytes 2097184 | tf_op jit(solution)/shard_map/all_to_all | solution.py:269
  308.7 3.6 %copy.177 = bf16[4,128,16,128]{3,2,0,1:T(8,128)(2,1)} copy(bf16[4,128,16,128]{3,2,1,0:T(8,128)(2,1)} %bitcast.34) | data formatting | bytes 4194304 | tf_op jit(solution)/shard_map/all_to_all | solution.py:269
  312.8 16.4 %all_to_all.111 = bf16[2,512,2,128]{3,2,0,1:T(2,128)(2,1)S(1)} all-to-all(bf16[2,512,2,128]{3,2,0,1:T(2,128)(2,1)S(1)} %copy.193), channel_id=1, replica_groups=mesh['seq'=8,'head'=4] {'head'}, dimensions={1} | all-to-all | bytes 1048576 | tf_op jit(solution)/shard_map/all_to_all | solution.py:272
  329.4 0.9 copy.197
  (97 shorter events, 9.7 us)
Async XLA Ops:
  8.9 13.8 %all-to-all-start.1 = ((bf16[128,8,128]{2,0,1:T(8,128)(2,1)}), bf16[128,8,128]{2,0,1:T(8,128)(2,1)S(1)}, u32[]{:S(2)}, u32[]{:S(2)}) async-start(bf16[128,8,128]{2,0,1:T(8,128)(2,1)} %copy.163), calls=%async_computation.1 | async-start | bytes 524288 | tf_op jit(solution)/shard_map/all_to_all | solution.py:126
  22.6 10.4 %all-to-all-start.2 = ((bf16[128,8,128]{2,0,1:T(8,128)(2,1)}), bf16[128,8,128]{2,0,1:T(8,128)(2,1)S(1)}, u32[]{:S(2)}, u32[]{:S(2)}) async-start(bf16[128,8,128]{2,0,1:T(8,128)(2,1)} %copy.165), calls=%async_computation.2 | async-start | bytes 524288 | tf_op jit(solution)/shard_map/all_to_all | solution.py:127
  26.1 120.2 %all-gather.2.cloned.1.call-start = ((), (), s32[]{:S(2)}) async-start(), calls=%async_computation.7 | async-start | bytes 4718592 | tf_op jit(solution)/shard_map/all_gather | solution.py:176
  33.5 0.8 copy-start
  38.6 4.6 %copy-start.6 = (s32[32,3]{0,1:T(4,128)S(1)}, s32[32,3]{0,1:T(4,128)}, u32[]{:S(2)}) copy-start(s32[32,3]{0,1:T(4,128)} %param.15) | copy-start | bytes 1156
  38.7 5.3 %copy-start.4 = (bf16[128,64,128]{2,1,0:T(8,128)(2,1)S(1)}, bf16[128,64,128]{2,1,0:T(8,128)(2,1)}, u32[]{:S(2)}) copy-start(bf16[128,64,128]{2,1,0:T(8,128)(2,1)} %param.13) | copy-start | bytes 6291460
  38.7 50.1 %all-to-all-start = ((bf16[128,64,128]{2,0,1:T(8,128)(2,1)}), bf16[128,64,128]{2,0,1:T(8,128)(2,1)}, u32[]{:S(2)}, u32[]{:S(2)}) async-start(bf16[128,64,128]{2,0,1:T(8,128)(2,1)} %copy.161), calls=%async_computation | async-start | bytes 4194304 | tf_op jit(solution)/shard_map/all_to_all | solution.py:125
  43.9 3.2 copy-start.7
  47.3 46.3 %copy-start.1 = (bf16[2,512,256]{2,1,0:T(8,128)(2,1)S(1)}, bf16[2,512,256]{2,1,0:T(8,128)(2,1)}, u32[]{:S(2)}) copy-start(bf16[2,512,256]{2,1,0:T(8,128)(2,1)} %copy-done) | copy-start | bytes 1572868
  88.8 52.3 %all-to-all-start.3 = ((bf16[128,64,128]{2,0,1:T(8,128)(2,1)}), bf16[128,64,128]{2,0,1:T(8,128)(2,1)}, u32[]{:S(2)}, u32[]{:S(2)}) async-start(bf16[128,64,128]{2,0,1:T(8,128)(2,1)} %copy.173), calls=%async_computation.3 | async-start | bytes 4194304 | tf_op jit(solution)/shard_map/all_to_all | solution.py:128
  93.7 7.2 %collective-permute-start = (bf16[2,128,256]{2,1,0:T(8,128)(2,1)S(1)}, bf16[2,128,256]{2,1,0:T(8,128)(2,1)S(1)}, u32[]{:S(2)}, u32[]{:S(2)}) collective-permute-start(bf16[2,128,256]{2,1,0:T(8,128)(2,1)S(1)} %get-tuple-element.81), channel_id=1, source_target_pairs={{0,4},{4,8},{8,12},{12,16},{16,20},{20,24},{24,28},{1,5},{5,9},{9,... | collective-permute-start | bytes 393224 | tf_op jit(solution)/shard_map/ppermute | solution.py:99
  95.6 7.0 %collective-permute-start.1 = (bf16[2,128,256]{2,1,0:T(8,128)(2,1)S(1)}, bf16[2,128,256]{2,1,0:T(8,128)(2,1)S(1)}, u32[]{:S(2)}, u32[]{:S(2)}) collective-permute-start(bf16[2,128,256]{2,1,0:T(8,128)(2,1)S(1)} %get-tuple-element.82), channel_id=1, source_target_pairs={{4,0},{8,4},{12,8},{16,12},{20,16},{24,20},{28,24},{5,1},{9,5},{13... | collective-permute-start | bytes 393224 | tf_op jit(solution)/shard_map/ppermute | solution.py:100
  205.1 51.3 %all-to-all-start.4 = ((bf16[512,16,128]{2,1,0:T(8,128)(2,1)}), bf16[512,16,128]{2,1,0:T(8,128)(2,1)S(1)}, u32[]{:S(2)}, u32[]{:S(2)}) async-start(bf16[512,16,128]{2,1,0:T(8,128)(2,1)} %bitcast.139), calls=%async_computation.4 | async-start | bytes 4194304 | tf_op jit(solution)/shard_map/all_to_all | solution.py:268
  210.7 23.0 %collective-permute-start.4 = (bf16[2,2,128,256]{3,2,1,0:T(8,128)(2,1)S(1)}, bf16[2,2,128,256]{3,2,1,0:T(8,128)(2,1)S(1)}, u32[]{:S(2)}, u32[]{:S(2)}) collective-permute-start(bf16[2,2,128,256]{3,2,1,0:T(8,128)(2,1)S(1)} %convert_element_type.65), channel_id=1, source_target_pairs={{0,4},{4,0},{8,12},{12,8},{16,20},{20,16},{24,28},{28,24},{1,5},{5... | collective-permute-start | bytes 786440 | tf_op jit(solution)/shard_map/ppermute | solution.py:117
  214.2 16.5 %collective-permute-start.2 = (bf16[2,128,256]{2,1,0:T(8,128)(2,1)S(1)}, bf16[2,128,256]{2,1,0:T(8,128)(2,1)S(1)}, u32[]{:S(2)}, u32[]{:S(2)}) collective-permute-start(bf16[2,128,256]{2,1,0:T(8,128)(2,1)S(1)} %get-tuple-element.73), channel_id=1, source_target_pairs={{0,4},{4,8},{8,12},{12,16},{16,20},{20,24},{24,28},{1,5},{5,9},{9,... | collective-permute-start | bytes 393224 | tf_op jit(solution)/shard_map/ppermute | solution.py:99
  216.7 15.5 %collective-permute-start.3 = (bf16[2,128,256]{2,1,0:T(8,128)(2,1)S(1)}, bf16[2,128,256]{2,1,0:T(8,128)(2,1)S(1)}, u32[]{:S(2)}, u32[]{:S(2)}) collective-permute-start(bf16[2,128,256]{2,1,0:T(8,128)(2,1)S(1)} %get-tuple-element.74), channel_id=1, source_target_pairs={{4,0},{8,4},{12,8},{16,12},{20,16},{24,20},{28,24},{5,1},{9,5},{13... | collective-permute-start | bytes 393224 | tf_op jit(solution)/shard_map/ppermute | solution.py:100
  224.2 3.6 %copy-start.5 = (bf16[4,128,2048]{2,1,0:T(8,128)(2,1)S(1)}, bf16[4,128,2048]{2,1,0:T(8,128)(2,1)}, u32[]{:S(2)}) copy-start(bf16[4,128,2048]{2,1,0:T(8,128)(2,1)} %get-tuple-element.35) | copy-start | bytes 6291460
  227.1 9.0 %collective-permute-start.7 = (bf16[2,2,128,256]{3,0,2,1:T(2,128)(2,1)S(1)}, bf16[2,2,128,256]{3,0,2,1:T(2,128)(2,1)S(1)}, u32[]{:S(2)}, u32[]{:S(2)}) collective-permute-start(bf16[2,2,128,256]{3,0,2,1:T(2,128)(2,1)S(1)} %get-tuple-element.68), channel_id=1, source_target_pairs={{0,4},{4,8},{8,12},{12,16},{16,20},{20,24},{24,28},{28,0},{1,5},{5... | collective-permute-start | bytes 786440 | tf_op jit(solution)/shard_map/ppermute | solution.py:81
  227.1 10.8 %collective-permute-start.8 = (bf16[2,2,128,256]{3,0,2,1:T(2,128)(2,1)S(1)}, bf16[2,2,128,256]{3,0,2,1:T(2,128)(2,1)S(1)}, u32[]{:S(2)}, u32[]{:S(2)}) collective-permute-start(bf16[2,2,128,256]{3,0,2,1:T(2,128)(2,1)S(1)} %get-tuple-element.67), channel_id=1, source_target_pairs={{0,8},{4,12},{8,16},{12,20},{16,24},{20,28},{24,0},{28,4},{1,9},{5... | collective-permute-start | bytes 786440 | tf_op jit(solution)/shard_map/ppermute | solution.py:81
  230.8 31.1 %collective-permute-start.9 = (bf16[2,2,128,256]{3,0,2,1:T(2,128)(2,1)}, bf16[2,2,128,256]{3,0,2,1:T(2,128)(2,1)S(1)}, u32[]{:S(2)}, u32[]{:S(2)}) collective-permute-start(bf16[2,2,128,256]{3,0,2,1:T(2,128)(2,1)} %get-tuple-element.66), channel_id=1, source_target_pairs={{0,12},{4,16},{8,20},{12,24},{16,28},{20,0},{24,4},{28,8},{1,13},{... | collective-permute-start | bytes 786440 | tf_op jit(solution)/shard_map/ppermute | solution.py:81
  232.1 32.1 %collective-permute-start.10 = (bf16[2,2,128,256]{3,0,2,1:T(2,128)(2,1)}, bf16[2,2,128,256]{3,0,2,1:T(2,128)(2,1)}, u32[]{:S(2)}, u32[]{:S(2)}) collective-permute-start(bf16[2,2,128,256]{3,0,2,1:T(2,128)(2,1)} %get-tuple-element.65), channel_id=1, source_target_pairs={{0,16},{4,20},{8,24},{12,28},{16,0},{20,4},{24,8},{28,12},{1,17},{... | collective-permute-start | bytes 786440 | tf_op jit(solution)/shard_map/ppermute | solution.py:81
  233.7 4.2 %copy-start.2 = (f32[4,2,128,256]{3,2,1,0:T(8,128)}, f32[4,2,128,256]{3,2,1,0:T(8,128)S(1)}, u32[]{:S(2)}) copy-start(f32[4,2,128,256]{3,2,1,0:T(8,128)S(1)} %fusion.23) | copy-start | bytes 3145732
  233.7 32.3 %collective-permute-start.11 = (bf16[2,2,128,256]{3,0,2,1:T(2,128)(2,1)}, bf16[2,2,128,256]{3,0,2,1:T(2,128)(2,1)}, u32[]{:S(2)}, u32[]{:S(2)}) collective-permute-start(bf16[2,2,128,256]{3,0,2,1:T(2,128)(2,1)} %get-tuple-element.64), channel_id=1, source_target_pairs={{0,20},{4,24},{8,28},{12,0},{16,4},{20,8},{24,12},{28,16},{1,21},{... | collective-permute-start | bytes 786440 | tf_op jit(solution)/shard_map/ppermute | solution.py:81
  236.1 31.8 %collective-permute-start.12 = (bf16[2,2,128,256]{3,0,2,1:T(2,128)(2,1)}, bf16[2,2,128,256]{3,0,2,1:T(2,128)(2,1)}, u32[]{:S(2)}, u32[]{:S(2)}) collective-permute-start(bf16[2,2,128,256]{3,0,2,1:T(2,128)(2,1)} %get-tuple-element.63), channel_id=1, source_target_pairs={{0,24},{4,28},{8,0},{12,4},{16,8},{20,12},{24,16},{28,20},{1,25},{... | collective-permute-start | bytes 786440 | tf_op jit(solution)/shard_map/ppermute | solution.py:81
  238.0 31.8 %collective-permute-start.13 = (bf16[2,2,128,256]{3,0,2,1:T(2,128)(2,1)}, bf16[2,2,128,256]{3,0,2,1:T(2,128)(2,1)}, u32[]{:S(2)}, u32[]{:S(2)}) collective-permute-start(bf16[2,2,128,256]{3,0,2,1:T(2,128)(2,1)} %get-tuple-element.62), channel_id=1, source_target_pairs={{0,28},{4,0},{8,4},{12,8},{16,12},{20,16},{24,20},{28,24},{1,29},{... | collective-permute-start | bytes 786440 | tf_op jit(solution)/shard_map/ppermute | solution.py:81
  256.5 52.3 %all-to-all-start.5 = ((bf16[512,16,128]{2,1,0:T(8,128)(2,1)}), bf16[512,16,128]{2,1,0:T(8,128)(2,1)}, u32[]{:S(2)}, u32[]{:S(2)}) async-start(bf16[512,16,128]{2,1,0:T(8,128)(2,1)} %bitcast.140), calls=%async_computation.5 | async-start | bytes 4194304 | tf_op jit(solution)/shard_map/all_to_all | solution.py:269
  261.8 17.1 %collective-permute-start.5 = (bf16[2,2,128,256]{3,2,1,0:T(8,128)(2,1)}, bf16[2,2,128,256]{3,2,1,0:T(8,128)(2,1)S(1)}, u32[]{:S(2)}, u32[]{:S(2)}) collective-permute-start(bf16[2,2,128,256]{3,2,1,0:T(8,128)(2,1)} %fusion.22), channel_id=1, source_target_pairs={{0,8},{4,12},{8,0},{12,4},{16,24},{20,28},{24,16},{28,20},{1,9},{5... | collective-permute-start | bytes 786440 | tf_op jit(solution)/shard_map/ppermute | solution.py:117
  279.0 7.1 %collective-permute-start.6 = (bf16[2,2,128,256]{3,2,1,0:T(8,128)(2,1)S(1)}, bf16[2,2,128,256]{3,2,1,0:T(8,128)(2,1)S(1)}, u32[]{:S(2)}, u32[]{:S(2)}) collective-permute-start(bf16[2,2,128,256]{3,2,1,0:T(8,128)(2,1)S(1)} %fusion.26), channel_id=1, source_target_pairs={{0,16},{4,20},{8,24},{12,28},{16,0},{20,4},{24,8},{28,12},{1,17},{... | collective-permute-start | bytes 786440 | tf_op jit(solution)/shard_map/ppermute | solution.py:117
  284.3 2.2 copy-start.3
Sparse Core Ops, SparseCore 0:
  34.5 35.9 all-gather.1

commit v6 on v5

--- a/solution.py
+++ b/solution.py
@@ -10,36 +10,52 @@
 BLOCK_TOKENS = 128
 
 
-def attention_kernel(q_ref, k_ref, v_ref, do_ref, bias_ref, out_ref, dq_ref, grad_ref, *, scale):
+def rows_of(ref, group, width):
+    return jnp.concatenate([ref[:, g * width:(g + 1) * width] for g in range(group)], axis=0)
+
+
+def store_rows(ref, value, group, width):
+    tokens = ref.shape[0]
+    for g in range(group):
+        ref[:, g * width:(g + 1) * width] = value[g * tokens:(g + 1) * tokens, :]
+
+
+def softmax_rows(q, k, bias, scale):
+    rows_by_cols = (((1,), (1,)), ((), ()))
+    s = lax.dot_general(q, k, rows_by_cols, preferred_element_type=jnp.float32) * scale
+    s = s + bias
+    e = jnp.exp(s - jnp.max(s, axis=1, keepdims=True))
+    return e / jnp.sum(e, axis=1, keepdims=True)
+
+
+def forward_kernel(q_ref, k_ref, v_ref, bias_ref, out_ref, *, scale):
     group = q_ref.shape[1] // q_ref.shape[0]
     width = k_ref.shape[-1]
-
-    def rows_of(ref):
-        return jnp.concatenate([ref[:, g * width:(g + 1) * width] for g in range(group)], axis=0)
-
-    def store_rows(ref, value):
-        tokens = ref.shape[0]
-        for g in range(group):
-            ref[:, g * width:(g + 1) * width] = value[g * tokens:(g + 1) * tokens, :]
-
-    q = rows_of(q_ref)
-    do = rows_of(do_ref)
+    q = rows_of(q_ref, group, width)
+    k = k_ref[...].reshape(-1, width)
+    v = v_ref[...].reshape(-1, width)
+    p_low = softmax_rows(q, k, bias_ref[...], scale).astype(jnp.bfloat16)
+    o_low = jnp.dot(p_low, v, preferred_element_type=jnp.float32).astype(jnp.bfloat16)
+    store_rows(out_ref, o_low, group, width)
+
+
+def backward_kernel(q_ref, k_ref, v_ref, do_ref, o_ref, bias_ref, dq_ref, grad_ref, *, scale):
+    group = q_ref.shape[1] // q_ref.shape[0]
+    width = k_ref.shape[-1]
+    q = rows_of(q_ref, group, width)
+    do = rows_of(do_ref, group, width)
+    o_low = rows_of(o_ref, group, width)
     k = k_ref[...].reshape(-1, width)
     v = v_ref[...].reshape(-1, width)
     rows_by_cols = (((1,), (1,)), ((), ()))
     over_rows = (((0,), (0,)), ((), ()))
-    s = lax.dot_general(q, k, rows_by_cols, preferred_element_type=jnp.float32) * scale
-    s = s + bias_ref[...]
-    e = jnp.exp(s - jnp.max(s, axis=1, keepdims=True))
-    p = e / jnp.sum(e, axis=1, keepdims=True)
+    p = softmax_rows(q, k, bias_ref[...], scale)
     p_low = p.astype(jnp.bfloat16)
-    o_low = jnp.dot(p_low, v, preferred_element_type=jnp.float32).astype(jnp.bfloat16)
-    store_rows(out_ref, o_low)
     delta = jnp.sum(do.astype(jnp.float32) * o_low.astype(jnp.float32), axis=1, keepdims=True)
     dp = lax.dot_general(do, v, rows_by_cols, preferred_element_type=jnp.float32)
     ds_low = (p * (dp - delta)).astype(jnp.bfloat16)
     dq = jnp.dot(ds_low, k, preferred_element_type=jnp.float32) * scale
-    store_rows(dq_ref, dq.astype(jnp.bfloat16))
+    store_rows(dq_ref, dq.astype(jnp.bfloat16), group, width)
     dk = lax.dot_general(ds_low, q, over_rows, preferred_element_type=jnp.float32) * scale
     dv = lax.dot_general(p_low, do, over_rows, preferred_element_type=jnp.float32)
     grad_ref[:, 0] = dk.reshape(grad_ref.shape[0], -1, width)
@@ -55,17 +71,36 @@
     v_spec = pl.BlockSpec((None, tile_count, None, tokens, head_width), lambda j, h: (j, 0, 1, 0, h))
     b_spec = pl.BlockSpec((None, 1, bias.shape[-1]), lambda j, h: (j, 0, 0))
     g_spec = pl.BlockSpec((None, tile_count, 2, tokens, head_width), lambda j, h: (j, 0, 0, 0, h))
-    return pl.pallas_call(
-        functools.partial(attention_kernel, scale=scale),
+    steps = blocks * heads_kv
+    rows = tokens * (rows_width // head_width)
+    keys_n = tile_count * tokens
+    matmul = 2 * rows * keys_n * head_width * steps
+    moved = 2 * (3 * q.size + 2 * tiles.size) + 4 * tiles.size
+    out = pl.pallas_call(
+        functools.partial(forward_kernel, scale=scale),
+        cost_estimate=pl.CostEstimate(
+            flops=2 * matmul, transcendentals=rows * keys_n * steps, bytes_accessed=moved
+        ),
         grid=(blocks, heads_kv),
-        in_specs=[q_spec, k_spec, v_spec, q_spec, b_spec],
-        out_specs=[q_spec, q_spec, g_spec],
+        in_specs=[q_spec, k_spec, v_spec, b_spec],
+        out_specs=q_spec,
+        out_shape=jax.ShapeDtypeStruct(q.shape, jnp.bfloat16),
+    )(q, tiles, tiles, bias)
+    out, do = lax.optimization_barrier((out, do))
+    grad_q, grads = pl.pallas_call(
+        functools.partial(backward_kernel, scale=scale),
+        cost_estimate=pl.CostEstimate(
+            flops=5 * matmul, transcendentals=rows * keys_n * steps, bytes_accessed=moved
+        ),
+        grid=(blocks, heads_kv),
+        in_specs=[q_spec, k_spec, v_spec, q_spec, q_spec, b_spec],
+        out_specs=[q_spec, g_spec],
         out_shape=[
-            jax.ShapeDtypeStruct(q.shape, jnp.bfloat16),
             jax.ShapeDtypeStruct(q.shape, jnp.bfloat16),
             jax.ShapeDtypeStruct(tiles.shape, jnp.float32),
         ],
-    )(q, tiles, tiles, do, bias)
+    )(q, tiles, tiles, do, out, bias)
+    return out, grad_q, grads
 
 
 def exchange(array, axis, split_axis, concat_axis):
@@ -125,7 +160,7 @@
         lax.all_to_all(queries, "head", split_axis=1, concat_axis=0, tiled=True),
         lax.all_to_all(keys, "head", split_axis=1, concat_axis=0, tiled=True),
         lax.all_to_all(values, "head", split_axis=1, concat_axis=0, tiled=True),
-        lax.all_to_all(output_gradient, "head", split_axis=1, concat_axis=0, tiled=True),
+        output_gradient,
     )
     shard_len, heads_q, head_width = query_loc.shape
     heads_kv = key_loc.shape[1]
@@ -174,6 +209,8 @@
         preferred_element_type=jnp.float32,
     ).astype(jnp.bfloat16)
     everything = lax.all_gather(kv_pair, "seq", axis=1, tiled=True)
+    query_loc, everything, grad_loc = lax.optimization_barrier((query_loc, everything, grad_loc))
+    grad_loc = lax.all_to_all(grad_loc, "head", split_axis=1, concat_axis=0, tiled=True)
     tiled_all = everything.reshape(2, block_total_count, BLOCK_TOKENS, kv_width)
     random_tiles = jnp.take(tiled_all, my_entries, axis=1).transpose(1, 0, 2, 3)
     global_tiles = jnp.take(tiled_all, global_blocks, axis=1).transpose(1, 0, 2, 3)

time: 341 us -> 334 us (0.979)
  waiting for transfers between devices: 127 us -> 99.6 us
  Pallas kernels: 43.6 us -> 62.7 us
    all_to_all x1, waiting for transfers between devices: 31.1 us -> 0.01 us  [per_device(): lax.all_to_all(grad_loc, 'head', split_axis=1, concat_axis=0, tiled=True)]
    pallas_call x1 -> x2, Pallas kernels: 43.6 us -> 62.7 us  [the longest x1 37.4 us: attention_call(): pl.pallas_call(functools.partial(backward_kernel, scale=scale), cost_esti...]
    all_to_all x1, waiting for transfers between devices: 15.4 us -> 21 us  [per_device(): lax.all_to_all(out_all, 'head', split_axis=0, concat_axis=1, tiled=True)]
    all_to_all x1, waiting for transfers between devices: 19.9 us -> 15.3 us  [per_device(): lax.all_to_all(query_grad_all, 'head', split_axis=0, concat_axis=1, tiled...]
    optimization_barrier x0 -> x1, local copies, waits for them, and re-layouts: none -> 4.35 us  [per_device(): lax.optimization_barrier((query_loc, everything, grad_loc))]
    unnamed x32 -> x39, local copies, waits for them, and re-layouts: 27.6 us -> 25.5 us
  transfers between devices with their start and end apart: 21 -> 21, of which waited for: 10 -> 8; matrix products, arithmetic and copies ran while one was open for 19% -> 20% of each run, Pallas kernels for 0% -> 8%
where the time goes in v6:
time: 334 us; the launch traced here: 333 us
  waiting for transfers between devices  99.6 us (30%)
  local copies, waits for them, and re-layouts  75.2 us (23%)
  Pallas kernels  62.7 us (19%)
  starting transfers between devices  48.5 us (15%)
  blocking collectives  16.6 us (5%)
  between operations  14.7 us (4%)
  other arithmetic  12.9 us (4%)
    all_to_all x1, waiting for transfers between devices, per_device(): lax.all_to_all(queries, 'head', split_axis=1, concat_axis=0, tiled=True)  42.7 us
    pallas_call x1, Pallas kernels, attention_call(): pl.pallas_call(functools.partial(backward_kernel, scale=scale), cost_esti...  37.4 us
    unnamed x39, local copies, waits for them, and re-layouts  25.5 us
    pallas_call x1, Pallas kernels, attention_call(): pl.pallas_call(functools.partial(forward_kernel, scale=scale), cost_estim...  25.3 us
    all_to_all x1, waiting for transfers between devices, per_device(): lax.all_to_all(out_all, 'head', split_axis=0, concat_axis=1, tiled=True)  21 us
    all_to_all x1, blocking collectives, per_device(): lax.all_to_all(kv_grad, 'head', split_axis=1, concat_axis=2, tiled=True)  16.6 us
    all_to_all x1, waiting for transfers between devices, per_device(): lax.all_to_all(query_grad_all, 'head', split_axis=0, concat_axis=1, tiled...  15.3 us
    ppermute x2, starting transfers between devices, padded(): after = lax.ppermute(leading, axis, down)  9.48 us
  transfers between devices with their start and end apart: 21, of which 8 were waited for; matrix products, arithmetic and copies ran while one was open for 20% of the time, Pallas kernels for 8%

profile of v6, /device:TPU:4, one launch (start us, length us, event | category | flops | bytes accessed | tf_op | source)
XLA Modules:
  0.0 332.7 jit_solution(10626759175460885700)
XLA Ops:
  7.2 1.7 copy.163
  8.9 4.9 %all-to-all-start.1 = ((bf16[128,8,128]{2,0,1:T(8,128)(2,1)}), bf16[128,8,128]{2,0,1:T(8,128)(2,1)S(1)}, u32[]{:S(2)}, u32[]{:S(2)}) async-start(bf16[128,8,128]{2,0,1:T(8,128)(2,1)} %copy.163), calls=%async_computation.1 | async-start | bytes 524288 | tf_op jit(solution)/shard_map/all_to_all | solution.py:161
  13.7 1.7 copy.165
  15.4 7.2 %all-to-all-done.1 = bf16[128,8,128]{2,0,1:T(8,128)(2,1)S(1)} async-done(((bf16[128,8,128]{2,0,1:T(8,128)(2,1)}), bf16[128,8,128]{2,0,1:T(8,128)(2,1)S(1)}, u32[]{:S(2)}, u32[]{:S(2)}) %all-to-all-start.1) | async-done | bytes 262176 | tf_op jit(solution)/shard_map/all_to_all | solution.py:161
  22.6 3.4 %all-to-all-start.2 = ((bf16[128,8,128]{2,0,1:T(8,128)(2,1)}), bf16[128,8,128]{2,0,1:T(8,128)(2,1)S(1)}, u32[]{:S(2)}, u32[]{:S(2)}) async-start(bf16[128,8,128]{2,0,1:T(8,128)(2,1)} %copy.165), calls=%async_computation.2 | async-start | bytes 524288 | tf_op jit(solution)/shard_map/all_to_all | solution.py:162
  26.6 6.5 %all-to-all-done.2 = bf16[128,8,128]{2,0,1:T(8,128)(2,1)S(1)} async-done(((bf16[128,8,128]{2,0,1:T(8,128)(2,1)}), bf16[128,8,128]{2,0,1:T(8,128)(2,1)S(1)}, u32[]{:S(2)}, u32[]{:S(2)}) %all-to-all-start.2) | async-done | bytes 262176 | tf_op jit(solution)/shard_map/all_to_all | solution.py:162
  33.5 0.8 copy-done
  34.3 4.3 %copy.161 = bf16[128,64,128]{2,0,1:T(8,128)(2,1)} copy(bf16[128,64,128]{2,1,0:T(8,128)(2,1)} %param.10) | data formatting | bytes 4194304 | tf_op args[0]
  38.6 3.8 %all-to-all-start = ((bf16[128,64,128]{2,0,1:T(8,128)(2,1)}), bf16[128,64,128]{2,0,1:T(8,128)(2,1)S(1)}, u32[]{:S(2)}, u32[]{:S(2)}) async-start(bf16[128,64,128]{2,0,1:T(8,128)(2,1)} %copy.161), calls=%async_computation | async-start | bytes 4194304 | tf_op jit(solution)/shard_map/all_to_all | solution.py:160
  45.1 42.7 %all-to-all-done = bf16[128,64,128]{2,0,1:T(8,128)(2,1)S(1)} async-done(((bf16[128,64,128]{2,0,1:T(8,128)(2,1)}), bf16[128,64,128]{2,0,1:T(8,128)(2,1)S(1)}, u32[]{:S(2)}, u32[]{:S(2)}) %all-to-all-start) | async-done | bytes 2097184 | tf_op jit(solution)/shard_map/all_to_all | solution.py:160
  87.8 2.7 copy.162
  90.5 4.3 %copy.174 = bf16[128,64,128]{2,0,1:T(8,128)(2,1)} copy(bf16[128,64,128]{2,1,0:T(8,128)(2,1)} %param.13) | data formatting | bytes 4194304 | tf_op jit(solution)/shard_map/optimization_barrier | solution.py:212
  94.8 4.6 %all-to-all-start.3 = ((bf16[128,64,128]{2,0,1:T(8,128)(2,1)}), bf16[128,64,128]{2,0,1:T(8,128)(2,1)}, u32[]{:S(2)}, u32[]{:S(2)}) async-start(bf16[128,64,128]{2,0,1:T(8,128)(2,1)} %copy.174), calls=%async_computation.3 | async-start | bytes 4194304 | tf_op jit(solution)/shard_map/all_to_all | solution.py:213
  99.5 1.9 collective-permute-start
  101.5 4.7 %collective-permute-start.1 = (bf16[2,128,256]{2,1,0:T(8,128)(2,1)S(1)}, bf16[2,128,256]{2,1,0:T(8,128)(2,1)S(1)}, u32[]{:S(2)}, u32[]{:S(2)}) collective-permute-start(bf16[2,128,256]{2,1,0:T(8,128)(2,1)S(1)} %get-tuple-element.90), channel_id=1, source_target_pairs={{4,0},{8,4},{12,8},{16,12},{20,16},{24,20},{28,24},{5,1},{9,5},{13... | collective-permute-start | bytes 393224 | tf_op jit(solution)/shard_map/ppermute | solution.py:135
  106.9 1.7 collective-permute-done.1
  108.7 0.8 copy_bitcast_fusion.4
  109.5 2.8 gather_fusion.1
  112.6 1.2 copy.232
  113.9 2.7 gather_fusion
  116.6 2.3 reshape.403.q_ref
  119.0 1.5 slice_bitcast_fusion.6
  121.0 2.3 pad_maximum_fusion.k_ref.v_ref
  123.9 25.3 %shard_map.93.o_ref = bf16[4,128,2048]{2,1,0:T(8,128)(2,1)} custom-call(bf16[4,128,2048]{2,1,0:T(8,128)(2,1)} %reshape.403.q_ref, bf16[4,8,2,128,256]{4,3,2,1,0:T(8,128)(2,1)} %pad_maximum_fusion.k_ref.v_ref, bf16[4,8,2,128,256]{4,3,2,1,0:T(8,128)(2,1)} %pad_maximum_fusion.k_ref.v_ref, f32[4,1,1024]{2,1,0:T(1,128)} %bitcast.163), custom_call_target="tpu_custom_call" | custom-call | flops 4294967296 | bytes 23068672 | tf_op jit(solution)/shard_map/pallas_call | solution.py:79
  149.3 2.9 copy.231
  152.2 2.3 reshape.413.do_ref
  154.5 37.4 %shard_map.94 = (bf16[4,128,2048]{2,1,0:T(8,128)(2,1)}, f32[4,8,2,128,256]{4,3,2,1,0:T(8,128)}) custom-call(bf16[4,128,2048]{2,1,0:T(8,128)(2,1)} %reshape.403.q_ref, bf16[4,8,2,128,256]{4,3,2,1,0:T(8,128)(2,1)} %pad_maximum_fusion.k_ref.v_ref, bf16[4,8,2,128,256]{4,3,2,1,0:T(8,128)(2,1)} %pad_maximum_fusion.k_ref.v_ref, ...), custom_call_target="tpu_custom_call" | custom-call | flops 10737418240 | bytes 23068672 | tf_op jit(solution)/shard_map/pallas_call | solution.py:90
  191.9 3.5 %copy.205 = bf16[64,8,16,128]{3,2,1,0:T(8,128)(2,1)} copy(bf16[64,8,16,128]{3,1,2,0:T(8,128)(2,1)} %bitcast.147) | data formatting | bytes 4194304
  195.5 5.0 %all-to-all-start.5 = ((bf16[512,16,128]{2,1,0:T(8,128)(2,1)}), bf16[512,16,128]{2,1,0:T(8,128)(2,1)S(1)}, u32[]{:S(2)}, u32[]{:S(2)}) async-start(bf16[512,16,128]{2,1,0:T(8,128)(2,1)} %bitcast.137), calls=%async_computation.5 | async-start | bytes 4194304 | tf_op jit(solution)/shard_map/all_to_all | solution.py:306
  200.6 1.8 slice_reduce_fusion
  202.4 1.0 collective-permute-start.4
  203.5 1.3 slice_bitcast_fusion.2
  204.8 1.7 slice_bitcast_fusion.1
  206.9 1.9 collective-permute-start.2
  208.8 4.8 %collective-permute-start.3 = (bf16[2,128,256]{2,1,0:T(8,128)(2,1)S(1)}, bf16[2,128,256]{2,1,0:T(8,128)(2,1)S(1)}, u32[]{:S(2)}, u32[]{:S(2)}) collective-permute-start(bf16[2,128,256]{2,1,0:T(8,128)(2,1)S(1)} %get-tuple-element.82), channel_id=1, source_target_pairs={{4,0},{8,4},{12,8},{16,12},{20,16},{24,20},{28,24},{5,1},{9,5},{13... | collective-permute-start | bytes 393224 | tf_op jit(solution)/shard_map/ppermute | solution.py:135
  213.6 2.1 fusion.7
  216.4 1.0 fusion.4
  217.4 2.8 constant_dynamic-slice_fusion
  220.4 2.0 copy.204
  222.4 1.0 bitcast_dynamic-update-slice_fusion.7
  223.4 2.4 collective-permute-start.9
  226.7 0.9 fusion.22
  227.6 1.7 collective-permute-done.7
  229.3 0.9 collective-permute-start.12
  230.3 0.9 bitcast_dynamic-update-slice_fusion.6
  231.2 3.6 %collective-permute-start.13 = (bf16[2,2,128,256]{3,0,2,1:T(2,128)(2,1)}, bf16[2,2,128,256]{3,0,2,1:T(2,128)(2,1)}, u32[]{:S(2)}, u32[]{:S(2)}) collective-permute-start(bf16[2,2,128,256]{3,0,2,1:T(2,128)(2,1)} %get-tuple-element.70), channel_id=1, source_target_pairs={{0,28},{4,0},{8,4},{12,8},{16,12},{20,16},{24,20},{28,24},{1,29},{... | collective-permute-start | bytes 786440 | tf_op jit(solution)/shard_map/ppermute | solution.py:116
  234.8 15.3 %all-to-all-done.5 = bf16[512,16,128]{2,1,0:T(8,128)(2,1)S(1)} async-done(((bf16[512,16,128]{2,1,0:T(8,128)(2,1)}), bf16[512,16,128]{2,1,0:T(8,128)(2,1)S(1)}, u32[]{:S(2)}, u32[]{:S(2)}) %all-to-all-start.5) | async-done | bytes 2097184 | tf_op jit(solution)/shard_map/all_to_all | solution.py:306
  250.1 4.4 %all-to-all-start.4 = ((bf16[512,16,128]{2,1,0:T(8,128)(2,1)}), bf16[512,16,128]{2,1,0:T(8,128)(2,1)}, u32[]{:S(2)}, u32[]{:S(2)}) async-start(bf16[512,16,128]{2,1,0:T(8,128)(2,1)} %bitcast.138), calls=%async_computation.4 | async-start | bytes 4194304 | tf_op jit(solution)/shard_map/all_to_all | solution.py:305
  254.5 0.9 bitcast_dynamic-update-slice_fusion.5
  255.4 0.9 bitcast_dynamic-update-slice_fusion.4
  256.3 1.8 bitcast_dynamic-update-slice_fusion.3
  258.2 1.8 bitcast_dynamic-update-slice_fusion.2
  260.0 1.8 bitcast_dynamic-update-slice_fusion.1
  261.8 1.8 bitcast_dynamic-update-slice_fusion
  263.7 7.3 %gather_fusion.2 = bf16[8,2,2,128,256]{4,1,3,2,0:T(2,128)(2,1)} fusion(bf16[8,2,2,128,256]{4,1,3,2,0:T(2,128)(2,1)} %bitcast_dynamic-update-slice_fusion, s32[1024]{0:T(1024)S(1)} %pad_clamp_fusion), kind=kCustom, calls=%fused_computation.2 | custom fusion | bytes 4194336 | tf_op jit(solution)/shard_map/jit(_take)/gather | solution.py:119
  271.3 3.5 %broadcast_select_fusion = bf16[8,2,2,128,256]{4,1,3,2,0:T(2,128)(2,1)S(1)} fusion(bf16[8,2,2,128,256]{4,1,3,2,0:T(2,128)(2,1)} %gather_fusion.2, pred[8]{0:T(512)(128)(4,1)S(1)} %compare_and_fusion.2), kind=kLoop, calls=%fused_computation.4 | loop fusion | flops 1048576 | bytes 4194312 | tf_op jit(solution)/shard_map/jit(_take)/select_n | solution.py:119
  274.7 1.3 fusion.8
  276.0 3.4 %collective-permute-done.6 = bf16[2,2,128,256]{3,2,1,0:T(8,128)(2,1)S(1)} collective-permute-done((bf16[2,2,128,256]{3,2,1,0:T(8,128)(2,1)S(1)}, bf16[2,2,128,256]{3,2,1,0:T(8,128)(2,1)S(1)}, u32[]{:S(2)}, u32[]{:S(2)}) %collective-permute-start.6) | collective-permute-done | bytes 262176 | tf_op jit(solution)/shard_map/ppermute | solution.py:152
  280.3 2.0 copy.177
  282.3 21.0 %all-to-all-done.4 = bf16[512,16,128]{2,1,0:T(8,128)(2,1)} async-done(((bf16[512,16,128]{2,1,0:T(8,128)(2,1)}), bf16[512,16,128]{2,1,0:T(8,128)(2,1)}, u32[]{:S(2)}, u32[]{:S(2)}) %all-to-all-start.4) | async-done | bytes 2097184 | tf_op jit(solution)/shard_map/all_to_all | solution.py:305
  303.3 3.6 %copy.176 = bf16[4,128,16,128]{3,2,0,1:T(8,128)(2,1)} copy(bf16[4,128,16,128]{3,2,1,0:T(8,128)(2,1)} %bitcast.32) | data formatting | bytes 4194304 | tf_op jit(solution)/shard_map/all_to_all | solution.py:305
  307.4 16.6 %all_to_all.114 = bf16[2,512,2,128]{3,2,0,1:T(2,128)(2,1)S(1)} all-to-all(bf16[2,512,2,128]{3,2,0,1:T(2,128)(2,1)S(1)} %copy.193), channel_id=1, replica_groups=mesh['seq'=8,'head'=4] {'head'}, dimensions={1} | all-to-all | bytes 1048576 | tf_op jit(solution)/shard_map/all_to_all | solution.py:309
  324.1 0.9 copy.197
  325.0 0.9 copy.198
  (106 shorter events, 9.8 us)
Async XLA Ops:
  8.9 13.8 %all-to-all-start.1 = ((bf16[128,8,128]{2,0,1:T(8,128)(2,1)}), bf16[128,8,128]{2,0,1:T(8,128)(2,1)S(1)}, u32[]{:S(2)}, u32[]{:S(2)}) async-start(bf16[128,8,128]{2,0,1:T(8,128)(2,1)} %copy.163), calls=%async_computation.1 | async-start | bytes 524288 | tf_op jit(solution)/shard_map/all_to_all | solution.py:161
  22.6 10.4 %all-to-all-start.2 = ((bf16[128,8,128]{2,0,1:T(8,128)(2,1)}), bf16[128,8,128]{2,0,1:T(8,128)(2,1)S(1)}, u32[]{:S(2)}, u32[]{:S(2)}) async-start(bf16[128,8,128]{2,0,1:T(8,128)(2,1)} %copy.165), calls=%async_computation.2 | async-start | bytes 524288 | tf_op jit(solution)/shard_map/all_to_all | solution.py:162
  26.1 64.4 %all-gather.2.cloned.1.call-start = ((), (), s32[]{:S(2)}) async-start(), calls=%async_computation.7 | async-start | bytes 4718592 | tf_op jit(solution)/shard_map/all_gather | solution.py:211
  33.5 0.8 copy-start
  38.6 3.8 %copy-start.10 = (s32[32,3]{0,1:T(4,128)S(1)}, s32[32,3]{0,1:T(4,128)}, u32[]{:S(2)}) copy-start(s32[32,3]{0,1:T(4,128)} %param.15) | copy-start | bytes 1156
  38.6 4.6 %copy-start.11 = (s32[2]{0:T(128)S(1)}, s32[2]{0:T(128)}, u32[]{:S(2)}) copy-start(s32[2]{0:T(128)} %param.14) | copy-start | bytes 28
  38.6 49.2 %all-to-all-start = ((bf16[128,64,128]{2,0,1:T(8,128)(2,1)}), bf16[128,64,128]{2,0,1:T(8,128)(2,1)S(1)}, u32[]{:S(2)}, u32[]{:S(2)}) async-start(bf16[128,64,128]{2,0,1:T(8,128)(2,1)} %copy.161), calls=%async_computation | async-start | bytes 4194304 | tf_op jit(solution)/shard_map/all_to_all | solution.py:160
  94.8 4.7 %copy-start.1 = (bf16[2,512,256]{2,1,0:T(8,128)(2,1)S(1)}, bf16[2,512,256]{2,1,0:T(8,128)(2,1)}, u32[]{:S(2)}) copy-start(bf16[2,512,256]{2,1,0:T(8,128)(2,1)} %copy-done) | copy-start | bytes 1572868
  94.8 54.4 %all-to-all-start.3 = ((bf16[128,64,128]{2,0,1:T(8,128)(2,1)}), bf16[128,64,128]{2,0,1:T(8,128)(2,1)}, u32[]{:S(2)}, u32[]{:S(2)}) async-start(bf16[128,64,128]{2,0,1:T(8,128)(2,1)} %copy.174), calls=%async_computation.3 | async-start | bytes 4194304 | tf_op jit(solution)/shard_map/all_to_all | solution.py:213
  99.5 7.3 %collective-permute-start = (bf16[2,128,256]{2,1,0:T(8,128)(2,1)S(1)}, bf16[2,128,256]{2,1,0:T(8,128)(2,1)S(1)}, u32[]{:S(2)}, u32[]{:S(2)}) collective-permute-start(bf16[2,128,256]{2,1,0:T(8,128)(2,1)S(1)} %get-tuple-element.89), channel_id=1, source_target_pairs={{0,4},{4,8},{8,12},{12,16},{16,20},{20,24},{24,28},{1,5},{5,9},{9,... | collective-permute-start | bytes 393224 | tf_op jit(solution)/shard_map/ppermute | solution.py:134
  101.5 7.0 %collective-permute-start.1 = (bf16[2,128,256]{2,1,0:T(8,128)(2,1)S(1)}, bf16[2,128,256]{2,1,0:T(8,128)(2,1)S(1)}, u32[]{:S(2)}, u32[]{:S(2)}) collective-permute-start(bf16[2,128,256]{2,1,0:T(8,128)(2,1)S(1)} %get-tuple-element.90), channel_id=1, source_target_pairs={{4,0},{8,4},{12,8},{16,12},{20,16},{24,20},{28,24},{5,1},{9,5},{13... | collective-permute-start | bytes 393224 | tf_op jit(solution)/shard_map/ppermute | solution.py:135
  112.6 4.0 %copy-start.2 = (bf16[4,128,16,128]{3,2,1,0:T(8,128)(2,1)S(1)}, bf16[4,128,16,128]{3,2,1,0:T(8,128)(2,1)}, u32[]{:S(2)}) copy-start(bf16[4,128,16,128]{3,2,1,0:T(8,128)(2,1)} %copy.162) | copy-start | bytes 6291460
  116.6 2.3 copy-start.9
  118.9 1.6 copy-start.6
  195.5 54.6 %all-to-all-start.5 = ((bf16[512,16,128]{2,1,0:T(8,128)(2,1)}), bf16[512,16,128]{2,1,0:T(8,128)(2,1)S(1)}, u32[]{:S(2)}, u32[]{:S(2)}) async-start(bf16[512,16,128]{2,1,0:T(8,128)(2,1)} %bitcast.137), calls=%async_computation.5 | async-start | bytes 4194304 | tf_op jit(solution)/shard_map/all_to_all | solution.py:306
  202.4 24.2 %collective-permute-start.4 = (bf16[2,2,128,256]{3,2,1,0:T(8,128)(2,1)S(1)}, bf16[2,2,128,256]{3,2,1,0:T(8,128)(2,1)S(1)}, u32[]{:S(2)}, u32[]{:S(2)}) collective-permute-start(bf16[2,2,128,256]{3,2,1,0:T(8,128)(2,1)S(1)} %convert_element_type.65), channel_id=1, source_target_pairs={{0,4},{4,0},{8,12},{12,8},{16,20},{20,16},{24,28},{28,24},{1,5},{5... | collective-permute-start | bytes 786440 | tf_op jit(solution)/shard_map/ppermute | solution.py:152
  206.9 16.5 %collective-permute-start.2 = (bf16[2,128,256]{2,1,0:T(8,128)(2,1)S(1)}, bf16[2,128,256]{2,1,0:T(8,128)(2,1)S(1)}, u32[]{:S(2)}, u32[]{:S(2)}) collective-permute-start(bf16[2,128,256]{2,1,0:T(8,128)(2,1)S(1)} %get-tuple-element.81), channel_id=1, source_target_pairs={{0,4},{4,8},{8,12},{12,16},{16,20},{20,24},{24,28},{1,5},{5,9},{9,... | collective-permute-start | bytes 393224 | tf_op jit(solution)/shard_map/ppermute | solution.py:134
  208.8 16.9 %collective-permute-start.3 = (bf16[2,128,256]{2,1,0:T(8,128)(2,1)S(1)}, bf16[2,128,256]{2,1,0:T(8,128)(2,1)S(1)}, u32[]{:S(2)}, u32[]{:S(2)}) collective-permute-start(bf16[2,128,256]{2,1,0:T(8,128)(2,1)S(1)} %get-tuple-element.82), channel_id=1, source_target_pairs={{4,0},{8,4},{12,8},{16,12},{20,16},{24,20},{28,24},{5,1},{9,5},{13... | collective-permute-start | bytes 393224 | tf_op jit(solution)/shard_map/ppermute | solution.py:135
  215.7 0.7 copy-start.8
  217.4 3.0 copy-start.5
  220.3 9.0 %collective-permute-start.7 = (bf16[2,2,128,256]{3,0,2,1:T(2,128)(2,1)S(1)}, bf16[2,2,128,256]{3,0,2,1:T(2,128)(2,1)S(1)}, u32[]{:S(2)}, u32[]{:S(2)}) collective-permute-start(bf16[2,2,128,256]{3,0,2,1:T(2,128)(2,1)S(1)} %get-tuple-element.76), channel_id=1, source_target_pairs={{0,4},{4,8},{8,12},{12,16},{16,20},{20,24},{24,28},{28,0},{1,5},{5... | collective-permute-start | bytes 786440 | tf_op jit(solution)/shard_map/ppermute | solution.py:116
  220.4 10.8 %collective-permute-start.8 = (bf16[2,2,128,256]{3,0,2,1:T(2,128)(2,1)S(1)}, bf16[2,2,128,256]{3,0,2,1:T(2,128)(2,1)S(1)}, u32[]{:S(2)}, u32[]{:S(2)}) collective-permute-start(bf16[2,2,128,256]{3,0,2,1:T(2,128)(2,1)S(1)} %get-tuple-element.75), channel_id=1, source_target_pairs={{0,8},{4,12},{8,16},{12,20},{16,24},{20,28},{24,0},{28,4},{1,9},{5... | collective-permute-start | bytes 786440 | tf_op jit(solution)/shard_map/ppermute | solution.py:116
  223.4 32.0 %collective-permute-start.9 = (bf16[2,2,128,256]{3,0,2,1:T(2,128)(2,1)}, bf16[2,2,128,256]{3,0,2,1:T(2,128)(2,1)S(1)}, u32[]{:S(2)}, u32[]{:S(2)}) collective-permute-start(bf16[2,2,128,256]{3,0,2,1:T(2,128)(2,1)} %get-tuple-element.74), channel_id=1, source_target_pairs={{0,12},{4,16},{8,20},{12,24},{16,28},{20,0},{24,4},{28,8},{1,13},{... | collective-permute-start | bytes 786440 | tf_op jit(solution)/shard_map/ppermute | solution.py:116
  225.8 30.5 %collective-permute-start.10 = (bf16[2,2,128,256]{3,0,2,1:T(2,128)(2,1)}, bf16[2,2,128,256]{3,0,2,1:T(2,128)(2,1)}, u32[]{:S(2)}, u32[]{:S(2)}) collective-permute-start(bf16[2,2,128,256]{3,0,2,1:T(2,128)(2,1)} %get-tuple-element.73), channel_id=1, source_target_pairs={{0,16},{4,20},{8,24},{12,28},{16,0},{20,4},{24,8},{28,12},{1,17},{... | collective-permute-start | bytes 786440 | tf_op jit(solution)/shard_map/ppermute | solution.py:116
  226.6 4.6 %copy-start.3 = (f32[4,2,128,256]{3,2,1,0:T(8,128)}, f32[4,2,128,256]{3,2,1,0:T(8,128)S(1)}, u32[]{:S(2)}) copy-start(f32[4,2,128,256]{3,2,1,0:T(8,128)S(1)} %fusion.23) | copy-start | bytes 3145732
  226.6 31.6 %collective-permute-start.11 = (bf16[2,2,128,256]{3,0,2,1:T(2,128)(2,1)}, bf16[2,2,128,256]{3,0,2,1:T(2,128)(2,1)}, u32[]{:S(2)}, u32[]{:S(2)}) collective-permute-start(bf16[2,2,128,256]{3,0,2,1:T(2,128)(2,1)} %get-tuple-element.72), channel_id=1, source_target_pairs={{0,20},{4,24},{8,28},{12,0},{16,4},{20,8},{24,12},{28,16},{1,21},{... | collective-permute-start | bytes 786440 | tf_op jit(solution)/shard_map/ppermute | solution.py:116
  229.3 30.7 %collective-permute-start.12 = (bf16[2,2,128,256]{3,0,2,1:T(2,128)(2,1)}, bf16[2,2,128,256]{3,0,2,1:T(2,128)(2,1)}, u32[]{:S(2)}, u32[]{:S(2)}) collective-permute-start(bf16[2,2,128,256]{3,0,2,1:T(2,128)(2,1)} %get-tuple-element.71), channel_id=1, source_target_pairs={{0,24},{4,28},{8,0},{12,4},{16,8},{20,12},{24,16},{28,20},{1,25},{... | collective-permute-start | bytes 786440 | tf_op jit(solution)/shard_map/ppermute | solution.py:116
  231.2 30.7 %collective-permute-start.13 = (bf16[2,2,128,256]{3,0,2,1:T(2,128)(2,1)}, bf16[2,2,128,256]{3,0,2,1:T(2,128)(2,1)}, u32[]{:S(2)}, u32[]{:S(2)}) collective-permute-start(bf16[2,2,128,256]{3,0,2,1:T(2,128)(2,1)} %get-tuple-element.70), channel_id=1, source_target_pairs={{0,28},{4,0},{8,4},{12,8},{16,12},{20,16},{24,20},{28,24},{1,29},{... | collective-permute-start | bytes 786440 | tf_op jit(solution)/shard_map/ppermute | solution.py:116
  250.1 53.2 %all-to-all-start.4 = ((bf16[512,16,128]{2,1,0:T(8,128)(2,1)}), bf16[512,16,128]{2,1,0:T(8,128)(2,1)}, u32[]{:S(2)}, u32[]{:S(2)}) async-start(bf16[512,16,128]{2,1,0:T(8,128)(2,1)} %bitcast.138), calls=%async_computation.4 | async-start | bytes 4194304 | tf_op jit(solution)/shard_map/all_to_all | solution.py:305
  255.4 15.6 %collective-permute-start.5 = (bf16[2,2,128,256]{3,2,1,0:T(8,128)(2,1)}, bf16[2,2,128,256]{3,2,1,0:T(8,128)(2,1)S(1)}, u32[]{:S(2)}, u32[]{:S(2)}) collective-permute-start(bf16[2,2,128,256]{3,2,1,0:T(8,128)(2,1)} %fusion.22), channel_id=1, source_target_pairs={{0,8},{4,12},{8,0},{12,4},{16,24},{20,28},{24,16},{28,20},{1,9},{5... | collective-permute-start | bytes 786440 | tf_op jit(solution)/shard_map/ppermute | solution.py:152
  271.1 8.4 %collective-permute-start.6 = (bf16[2,2,128,256]{3,2,1,0:T(8,128)(2,1)S(1)}, bf16[2,2,128,256]{3,2,1,0:T(8,128)(2,1)S(1)}, u32[]{:S(2)}, u32[]{:S(2)}) collective-permute-start(bf16[2,2,128,256]{3,2,1,0:T(8,128)(2,1)S(1)} %fusion.26), channel_id=1, source_target_pairs={{0,16},{4,20},{8,24},{12,28},{16,0},{20,4},{24,8},{28,12},{1,17},{... | collective-permute-start | bytes 786440 | tf_op jit(solution)/shard_map/ppermute | solution.py:152
  274.7 4.9 %copy-start.7 = (f32[2,4]{1,0:T(2,128)S(1)}, f32[2,4]{1,0:T(2,128)}, u32[]{:S(2)}) copy-start(f32[2,4]{1,0:T(2,128)} %and_convert_fusion) | copy-start | bytes 100
  276.0 3.9 %copy-start.4 = (f32[4,2,128,256]{3,2,1,0:T(8,128)S(1)}, f32[4,2,128,256]{3,2,1,0:T(8,128)}, u32[]{:S(2)}) copy-start(f32[4,2,128,256]{3,2,1,0:T(8,128)} %copy-done.3) | copy-start | bytes 3145732
Sparse Core Ops, SparseCore 0:
  34.5 35.9 all-gather.1

commit v7 on v6

--- a/solution.py
+++ b/solution.py
@@ -156,12 +156,12 @@
 
 
 def per_device(queries, keys, values, output_gradient, global_blocks, random_blocks):
-    query_loc, key_loc, value_loc, grad_loc = (
-        lax.all_to_all(queries, "head", split_axis=1, concat_axis=0, tiled=True),
-        lax.all_to_all(keys, "head", split_axis=1, concat_axis=0, tiled=True),
-        lax.all_to_all(values, "head", split_axis=1, concat_axis=0, tiled=True),
-        output_gradient,
-    )
+    kv_loc = lax.all_to_all(
+        jnp.stack([keys, values], axis=2), "head", split_axis=1, concat_axis=0, tiled=True
+    )
+    key_loc, value_loc = kv_loc[:, :, 0], kv_loc[:, :, 1]
+    query_loc = lax.all_to_all(queries, "head", split_axis=1, concat_axis=0, tiled=True)
+    grad_loc = output_gradient
     shard_len, heads_q, head_width = query_loc.shape
     heads_kv = key_loc.shape[1]
     heads_per_group = heads_q // heads_kv
@@ -304,9 +304,8 @@
     value_grad_all = kv_grad[1].reshape(shard_len, heads_kv, head_width)
     out_back = lax.all_to_all(out_all, "head", split_axis=0, concat_axis=1, tiled=True)
     query_back = lax.all_to_all(query_grad_all, "head", split_axis=0, concat_axis=1, tiled=True)
-    (out_back, query_back), kv_grad = lax.optimization_barrier(((out_back, query_back), kv_grad))
     kv_grad = kv_grad.reshape(2, shard_len, heads_kv, head_width)
-    kv_back = lax.all_to_all(kv_grad, "head", split_axis=1, concat_axis=2, tiled=True)
+    kv_back = exchange(kv_grad, "head", 1, 2)
     return (out_back, query_back, kv_back[0], kv_back[1])
 
 

time: 334 us -> 350 us (1.048)
  local copies, waits for them, and re-layouts: 75.2 us -> 83.1 us
  other arithmetic: 12.9 us -> 20.7 us
    ppermute x7 -> x10, waiting for transfers between devices: 1.71 us -> 40.4 us  [exchange(): part = lax.ppermute(part, axis, pairs)]
    all_to_all x1, waiting for transfers between devices: 21 us -> 0.01 us  [per_device(): lax.all_to_all(out_all, 'head', split_axis=0, concat_axis=1, tiled=True)]
    all_to_all x2 -> x0, waiting for transfers between devices: 13.7 us -> none  [the longest x1 7.22 us: per_device(): lax.all_to_all(keys, 'head', split_axis=1, concat_axis=0, tiled=True)]
    unnamed x39 -> x43, local copies, waits for them, and re-layouts: 25.5 us -> 15.9 us
    all_to_all x2 -> x0, starting transfers between devices: 8.28 us -> none  [the longest x1 4.87 us: per_device(): lax.all_to_all(keys, 'head', split_axis=1, concat_axis=0, tiled=True)]
    optimization_barrier x1 -> x2, local copies, waits for them, and re-layouts: 4.35 us -> 10.8 us  [per_device(): lax.optimization_barrier((query_loc, everything, grad_loc))]
    ppermute x7 -> x10, starting transfers between devices: 7.87 us -> 13.8 us  [exchange(): part = lax.ppermute(part, axis, pairs)]
    all_to_all x1, waiting for transfers between devices: 15.3 us -> 10.3 us  [per_device(): lax.all_to_all(query_grad_all, 'head', split_axis=0, concat_axis=1, tiled...]
  transfers between devices with their start and end apart: 21 -> 22, of which waited for: 8 -> 8; matrix products, arithmetic and copies ran while one was open for 20% -> 24% of each run, Pallas kernels for 8% -> 7%
where the time goes in v7:
time: 350 us; the launch traced here: 347 us
  waiting for transfers between devices  98.6 us (28%)
  local copies, waits for them, and re-layouts  83.1 us (24%)
  Pallas kernels  62.7 us (18%)
  starting transfers between devices  45.6 us (13%)
  other arithmetic  20.7 us (6%)
  blocking collectives  19.2 us (5%)
  between operations  14.6 us (4%)
    all_to_all x1, waiting for transfers between devices, per_device(): lax.all_to_all(queries, 'head', split_axis=1, concat_axis=0, tiled=True)  44.7 us
    ppermute x10, waiting for transfers between devices, exchange(): part = lax.ppermute(part, axis, pairs)  40.4 us
    pallas_call x1, Pallas kernels, attention_call(): pl.pallas_call(functools.partial(backward_kernel, scale=scale), cost_esti...  37.4 us
    pallas_call x1, Pallas kernels, attention_call(): pl.pallas_call(functools.partial(forward_kernel, scale=scale), cost_estim...  25.3 us
    all_to_all x1, blocking collectives, per_device(): lax.all_to_all(jnp.stack([keys, values], axis=2), 'head', split_axis=1, c...  19.2 us
    unnamed x43, local copies, waits for them, and re-layouts  15.9 us
    ppermute x10, starting transfers between devices, exchange(): part = lax.ppermute(part, axis, pairs)  13.8 us
    optimization_barrier x2, local copies, waits for them, and re-layouts, per_device(): lax.optimization_barrier((query_loc, everything, grad_loc))  10.8 us
  transfers between devices with their start and end apart: 22, of which 8 were waited for; matrix products, arithmetic and copies ran while one was open for 24% of the time, Pallas kernels for 7%

profile of v7, /device:TPU:4, one launch (start us, length us, event | category | flops | bytes accessed | tf_op | source)
XLA Modules:
  0.0 347.5 jit_solution(6684644324773973269)
XLA Ops:
  7.2 1.1 copy_bitcast_fusion.6
  8.4 19.2 %all_to_all.87 = bf16[128,8,2,128]{3,0,2,1:T(8,128)(2,1)S(1)} all-to-all(bf16[128,8,2,128]{3,0,2,1:T(8,128)(2,1)S(1)} %pad_maximum_fusion.6), channel_id=1, replica_groups=mesh['seq'=8,'head'=4] {'head'}, dimensions={1} | all-to-all | bytes 1048576 | tf_op jit(solution)/shard_map/all_to_all | solution.py:159
  29.4 2.7 copy.191
  32.1 3.8 %all-to-all-start = ((bf16[128,64,128]{2,0,1:T(8,128)(2,1)}), bf16[128,64,128]{2,0,1:T(8,128)(2,1)S(1)}, u32[]{:S(2)}, u32[]{:S(2)}) async-start(bf16[128,64,128]{2,0,1:T(8,128)(2,1)} %copy.191), calls=%async_computation | async-start | bytes 4194304 | tf_op jit(solution)/shard_map/all_to_all | solution.py:163
  38.5 44.7 %all-to-all-done = bf16[128,64,128]{2,0,1:T(8,128)(2,1)S(1)} async-done(((bf16[128,64,128]{2,0,1:T(8,128)(2,1)}), bf16[128,64,128]{2,0,1:T(8,128)(2,1)S(1)}, u32[]{:S(2)}, u32[]{:S(2)}) %all-to-all-start) | async-done | bytes 2097184 | tf_op jit(solution)/shard_map/all_to_all | solution.py:163
  83.2 2.7 copy.192
  85.8 4.2 %copy.210 = bf16[128,64,128]{2,0,1:T(8,128)(2,1)} copy(bf16[128,64,128]{2,1,0:T(8,128)(2,1)} %param.13) | data formatting | bytes 4194304 | tf_op jit(solution)/shard_map/optimization_barrier | solution.py:212
  90.1 3.6 %all-to-all-start.2 = ((bf16[128,64,128]{2,0,1:T(8,128)(2,1)}), bf16[128,64,128]{2,0,1:T(8,128)(2,1)S(1)}, u32[]{:S(2)}, u32[]{:S(2)}) async-start(bf16[128,64,128]{2,0,1:T(8,128)(2,1)} %copy.210), calls=%async_computation.2 | async-start | bytes 4194304 | tf_op jit(solution)/shard_map/all_to_all | solution.py:213
  95.5 1.9 collective-permute-start
  97.4 4.5 %collective-permute-start.1 = (bf16[2,128,256]{1,2,0:T(8,128)(2,1)S(1)}, bf16[2,128,256]{1,2,0:T(8,128)(2,1)}, u32[]{:S(2)}, u32[]{:S(2)}) collective-permute-start(bf16[2,128,256]{1,2,0:T(8,128)(2,1)S(1)} %get-tuple-element.92), channel_id=1, source_target_pairs={{4,0},{8,4},{12,8},{16,12},{20,16},{24,20},{28,24},{5,1},{9,5},{13... | collective-permute-start | bytes 393224 | tf_op jit(solution)/shard_map/ppermute | solution.py:135
  103.3 1.2 collective-permute-done.1
  104.5 2.0 pad_maximum_fusion.10
  106.4 1.2 copy.207
  108.4 1.2 copy.205
  110.8 6.6 %copy.200 = bf16[2,4096,256]{2,1,0:T(8,128)(2,1)} copy(bf16[2,4096,256]{1,2,0:T(8,128)(2,1)} %all-gather.2.cloned.1.call-done) | data formatting | bytes 8388608 | tf_op jit(solution)/shard_map/optimization_barrier | solution.py:212
  117.3 4.0 %gather_fusion.1 = bf16[12,2,128,256]{3,2,1,0:T(8,128)(2,1)} fusion(bf16[2,32,128,256]{3,2,1,0:T(8,128)(2,1)} %bitcast.149, s32[1024]{0:T(1024)S(1)} %get-tuple-element.105), kind=kCustom, calls=%fused_computation.1 | custom fusion | bytes 3145776 | tf_op jit(solution)/shard_map/jit(_take)/gather | solution.py:215
  121.4 1.6 broadcast_select_fusion.1
  123.0 1.3 copy.272
  124.3 2.7 gather_fusion
  127.0 4.2 %reshape.455.q_ref = bf16[4,128,2048]{2,1,0:T(8,128)(2,1)} reshape(bf16[512,16,128]{2,1,0:T(8,128)(2,1)} %bitcast.153) | data formatting | bytes 4194304 | tf_op jit(solution)/shard_map/reshape | solution.py:249
  131.3 1.5 slice_bitcast_fusion.6
  133.3 2.3 pad_maximum_fusion.k_ref.v_ref
  136.2 25.3 %shard_map.93.o_ref = bf16[4,128,2048]{2,1,0:T(8,128)(2,1)} custom-call(bf16[4,128,2048]{2,1,0:T(8,128)(2,1)} %reshape.455.q_ref, bf16[4,8,2,128,256]{4,3,2,1,0:T(8,128)(2,1)} %pad_maximum_fusion.k_ref.v_ref, bf16[4,8,2,128,256]{4,3,2,1,0:T(8,128)(2,1)} %pad_maximum_fusion.k_ref.v_ref, f32[4,1,1024]{2,1,0:T(1,128)} %bitcast.187), custom_call_target="tpu_custom_call" | custom-call | flops 4294967296 | bytes 23068672 | tf_op jit(solution)/shard_map/pallas_call | solution.py:79
  161.6 2.7 copy.271
  164.3 4.2 %reshape.465.do_ref = bf16[4,128,2048]{2,1,0:T(8,128)(2,1)} reshape(bf16[4,128,16,128]{3,2,1,0:T(8,128)(2,1)} %bitcast.157) | data formatting | bytes 4194304 | tf_op jit(solution)/shard_map/reshape | solution.py:251
  168.4 37.4 %shard_map.94 = (bf16[4,128,2048]{2,1,0:T(8,128)(2,1)}, f32[4,8,2,128,256]{4,3,2,1,0:T(8,128)}) custom-call(bf16[4,128,2048]{2,1,0:T(8,128)(2,1)} %reshape.455.q_ref, bf16[4,8,2,128,256]{4,3,2,1,0:T(8,128)(2,1)} %pad_maximum_fusion.k_ref.v_ref, bf16[4,8,2,128,256]{4,3,2,1,0:T(8,128)(2,1)} %pad_maximum_fusion.k_ref.v_ref, ...), custom_call_target="tpu_custom_call" | custom-call | flops 10737418240 | bytes 23068672 | tf_op jit(solution)/shard_map/pallas_call | solution.py:90
  205.9 1.8 slice_reduce_fusion
  207.7 2.7 slice_bitcast_fusion.1
  210.4 1.4 slice_bitcast_fusion.2
  212.5 1.1 collective-permute-start.4
  213.7 2.0 copy.244
  215.7 5.1 %all-to-all-start.4 = ((bf16[512,16,128]{2,1,0:T(8,128)(2,1)}), bf16[512,16,128]{2,1,0:T(8,128)(2,1)}, u32[]{:S(2)}, u32[]{:S(2)}) async-start(bf16[512,16,128]{2,1,0:T(8,128)(2,1)} %bitcast.155), calls=%async_computation.4 | async-start | bytes 4194304 | tf_op jit(solution)/shard_map/all_to_all | solution.py:306
  220.8 1.5 fusion.54
  222.3 1.9 collective-permute-start.2
  224.2 4.8 %collective-permute-start.3 = (bf16[2,128,256]{2,1,0:T(8,128)(2,1)S(1)}, bf16[2,128,256]{2,1,0:T(8,128)(2,1)S(1)}, u32[]{:S(2)}, u32[]{:S(2)}) collective-permute-start(bf16[2,128,256]{2,1,0:T(8,128)(2,1)S(1)} %get-tuple-element.80), channel_id=1, source_target_pairs={{4,0},{8,4},{12,8},{16,12},{20,16},{24,20},{28,24},{5,1},{9,5},{13... | collective-permute-start | bytes 393224 | tf_op jit(solution)/shard_map/ppermute | solution.py:135
  229.0 2.1 fusion.7
  231.8 1.0 fusion.4
  232.8 2.7 constant_dynamic-slice_fusion.4
  235.8 2.0 copy.243
  237.7 1.0 bitcast_dynamic-update-slice_fusion.7
  238.7 2.6 collective-permute-start.9
  242.9 1.8 collective-permute-done.7
  245.4 0.9 bitcast_dynamic-update-slice_fusion.6
  246.3 3.9 %collective-permute-start.13 = (bf16[2,2,128,256]{3,0,2,1:T(2,128)(2,1)}, bf16[2,2,128,256]{3,0,2,1:T(2,128)(2,1)S(1)}, u32[]{:S(2)}, u32[]{:S(2)}) collective-permute-start(bf16[2,2,128,256]{3,0,2,1:T(2,128)(2,1)} %get-tuple-element.68), channel_id=1, source_target_pairs={{0,28},{4,0},{8,4},{12,8},{16,12},{20,16},{24,20},{28,24},{1,29},{... | collective-permute-start | bytes 786440 | tf_op jit(solution)/shard_map/ppermute | solution.py:116
  250.2 0.9 bitcast_dynamic-update-slice_fusion.5
  251.1 5.2 %collective-permute-done.9 = bf16[2,2,128,256]{3,0,2,1:T(2,128)(2,1)S(1)} collective-permute-done((bf16[2,2,128,256]{3,0,2,1:T(2,128)(2,1)S(1)}, bf16[2,2,128,256]{3,0,2,1:T(2,128)(2,1)S(1)}, u32[]{:S(2)}, u32[]{:S(2)}) %collective-permute-start.9) | collective-permute-done | bytes 262176 | tf_op jit(solution)/shard_map/ppermute | solution.py:116
  256.3 0.9 bitcast_dynamic-update-slice_fusion.4
  257.2 0.9 bitcast_dynamic-update-slice_fusion.3
  258.1 0.9 bitcast_dynamic-update-slice_fusion.2
  259.0 10.3 %all-to-all-done.4 = bf16[512,16,128]{2,1,0:T(8,128)(2,1)} async-done(((bf16[512,16,128]{2,1,0:T(8,128)(2,1)}), bf16[512,16,128]{2,1,0:T(8,128)(2,1)}, u32[]{:S(2)}, u32[]{:S(2)}) %all-to-all-start.4) | async-done | bytes 2097184 | tf_op jit(solution)/shard_map/all_to_all | solution.py:306
  269.2 4.4 %all-to-all-start.3 = ((bf16[512,16,128]{2,1,0:T(8,128)(2,1)}), bf16[512,16,128]{2,1,0:T(8,128)(2,1)}, u32[]{:S(2)}, u32[]{:S(2)}) async-start(bf16[512,16,128]{2,1,0:T(8,128)(2,1)} %bitcast.154), calls=%async_computation.3 | async-start | bytes 4194304 | tf_op jit(solution)/shard_map/all_to_all | solution.py:305
  273.7 0.9 bitcast_dynamic-update-slice_fusion.1
  274.6 0.9 bitcast_dynamic-update-slice_fusion
  275.5 7.3 %gather_fusion.2 = bf16[8,2,2,128,256]{4,1,3,2,0:T(2,128)(2,1)} fusion(bf16[8,2,2,128,256]{4,1,3,2,0:T(2,128)(2,1)} %bitcast_dynamic-update-slice_fusion, s32[1024]{0:T(1024)S(1)} %pad_clamp_fusion.1), kind=kCustom, calls=%fused_computation.2 | custom fusion | bytes 4194336 | tf_op jit(solution)/shard_map/jit(_take)/gather | solution.py:119
  283.5 3.5 broadcast_select_fusion
  287.0 1.3 fusion.8
  288.3 2.0 collective-permute-done.6
  291.6 1.7 collective-permute-start.14
  293.4 2.4 collective-permute-start.15
  295.8 1.5 collective-permute-start.16
  297.4 18.3 %collective-permute-done.14 = bf16[2,128,2,128]{3,1,2,0:T(8,128)(2,1)S(1)} collective-permute-done((bf16[2,128,2,128]{3,1,2,0:T(8,128)(2,1)S(1)}, bf16[2,128,2,128]{3,1,2,0:T(8,128)(2,1)S(1)}, u32[]{:S(2)}, u32[]{:S(2)}) %collective-permute-start.14) | collective-permute-done | bytes 131104 | tf_op jit(solution)/shard_map/ppermute | solution.py:116
  315.8 15.1 %collective-permute-done.15 = bf16[2,128,2,128]{3,1,2,0:T(8,128)(2,1)S(1)} collective-permute-done((bf16[2,128,2,128]{3,1,2,0:T(8,128)(2,1)S(1)}, bf16[2,128,2,128]{3,1,2,0:T(8,128)(2,1)S(1)}, u32[]{:S(2)}, u32[]{:S(2)}) %collective-permute-start.15) | collective-permute-done | bytes 131104 | tf_op jit(solution)/shard_map/ppermute | solution.py:116
  333.5 3.6 %copy.213 = bf16[4,128,16,128]{3,2,0,1:T(8,128)(2,1)} copy(bf16[4,128,16,128]{3,2,1,0:T(8,128)(2,1)} %bitcast.38) | data formatting | bytes 4194304 | tf_op jit(solution)/shard_map/all_to_all | solution.py:306
  337.0 3.6 %copy.212 = bf16[4,128,16,128]{3,2,0,1:T(8,128)(2,1)} copy(bf16[4,128,16,128]{3,2,1,0:T(8,128)(2,1)} %bitcast.35) | data formatting | bytes 4194304 | tf_op jit(solution)/shard_map/all_to_all | solution.py:305
  (125 shorter events, 19.3 us)
Async XLA Ops:
  7.2 78.7 %all-gather.2.cloned.1.call-start = ((), (), s32[]{:S(2)}) async-start(), calls=%async_computation.5 | async-start | bytes 4718592 | tf_op jit(solution)/shard_map/all_gather | solution.py:211
  27.6 1.8 copy-start
  32.1 3.8 %copy-start.9 = (s32[32,3]{0,1:T(4,128)S(1)}, s32[32,3]{0,1:T(4,128)}, u32[]{:S(2)}) copy-start(s32[32,3]{0,1:T(4,128)} %param.15) | copy-start | bytes 1156
  32.1 5.4 %copy-start.10 = (s32[2]{0:T(128)S(1)}, s32[2]{0:T(128)}, u32[]{:S(2)}) copy-start(s32[2]{0:T(128)} %param.14) | copy-start | bytes 28
  32.1 51.1 %all-to-all-start = ((bf16[128,64,128]{2,0,1:T(8,128)(2,1)}), bf16[128,64,128]{2,0,1:T(8,128)(2,1)S(1)}, u32[]{:S(2)}, u32[]{:S(2)}) async-start(bf16[128,64,128]{2,0,1:T(8,128)(2,1)} %copy.191), calls=%async_computation | async-start | bytes 4194304 | tf_op jit(solution)/shard_map/all_to_all | solution.py:163
  90.1 71.5 %all-to-all-start.2 = ((bf16[128,64,128]{2,0,1:T(8,128)(2,1)}), bf16[128,64,128]{2,0,1:T(8,128)(2,1)S(1)}, u32[]{:S(2)}, u32[]{:S(2)}) async-start(bf16[128,64,128]{2,0,1:T(8,128)(2,1)} %copy.210), calls=%async_computation.2 | async-start | bytes 4194304 | tf_op jit(solution)/shard_map/all_to_all | solution.py:213
  95.5 7.8 %collective-permute-start = (bf16[2,128,256]{1,2,0:T(8,128)(2,1)S(1)}, bf16[2,128,256]{1,2,0:T(8,128)(2,1)S(1)}, u32[]{:S(2)}, u32[]{:S(2)}) collective-permute-start(bf16[2,128,256]{1,2,0:T(8,128)(2,1)S(1)} %get-tuple-element.91), channel_id=1, source_target_pairs={{0,4},{4,8},{8,12},{12,16},{16,20},{20,24},{24,28},{1,5},{5,9},{9,... | collective-permute-start | bytes 393224 | tf_op jit(solution)/shard_map/ppermute | solution.py:134
  97.4 7.0 %collective-permute-start.1 = (bf16[2,128,256]{1,2,0:T(8,128)(2,1)S(1)}, bf16[2,128,256]{1,2,0:T(8,128)(2,1)}, u32[]{:S(2)}, u32[]{:S(2)}) collective-permute-start(bf16[2,128,256]{1,2,0:T(8,128)(2,1)S(1)} %get-tuple-element.92), channel_id=1, source_target_pairs={{4,0},{8,4},{12,8},{16,12},{20,16},{24,20},{28,24},{5,1},{9,5},{13... | collective-permute-start | bytes 393224 | tf_op jit(solution)/shard_map/ppermute | solution.py:135
  117.3 4.0 %copy-start.13 = (pred[12]{0:T(512)(128)(4,1)S(1)}, pred[12]{0:T(512)(128)(4,1)}, u32[]{:S(2)}) copy-start(pred[12]{0:T(512)(128)(4,1)} %compare_and_fusion.4) | copy-start | bytes 40
  127.0 4.2 %copy-start.8 = (pred[2]{0:T(512)(128)(4,1)S(1)}, pred[2]{0:T(512)(128)(4,1)}, u32[]{:S(2)}) copy-start(pred[2]{0:T(512)(128)(4,1)} %get-tuple-element.102) | copy-start | bytes 10
  131.2 1.6 copy-start.3
  131.2 1.6 copy-start.4
  210.4 3.3 copy-start.2
  212.5 29.4 %collective-permute-start.4 = (bf16[2,2,128,256]{3,2,1,0:T(8,128)(2,1)}, bf16[2,2,128,256]{3,2,1,0:T(8,128)(2,1)S(1)}, u32[]{:S(2)}, u32[]{:S(2)}) collective-permute-start(bf16[2,2,128,256]{3,2,1,0:T(8,128)(2,1)} %convert_element_type.66), channel_id=1, source_target_pairs={{0,4},{4,0},{8,12},{12,8},{16,20},{20,16},{24,28},{28,24},{1,5},{5... | collective-permute-start | bytes 786440 | tf_op jit(solution)/shard_map/ppermute | solution.py:152
  215.7 53.5 %all-to-all-start.4 = ((bf16[512,16,128]{2,1,0:T(8,128)(2,1)}), bf16[512,16,128]{2,1,0:T(8,128)(2,1)}, u32[]{:S(2)}, u32[]{:S(2)}) async-start(bf16[512,16,128]{2,1,0:T(8,128)(2,1)} %bitcast.155), calls=%async_computation.4 | async-start | bytes 4194304 | tf_op jit(solution)/shard_map/all_to_all | solution.py:306
  222.3 16.4 %collective-permute-start.2 = (bf16[2,128,256]{2,1,0:T(8,128)(2,1)S(1)}, bf16[2,128,256]{2,1,0:T(8,128)(2,1)S(1)}, u32[]{:S(2)}, u32[]{:S(2)}) collective-permute-start(bf16[2,128,256]{2,1,0:T(8,128)(2,1)S(1)} %get-tuple-element.79), channel_id=1, source_target_pairs={{0,4},{4,8},{8,12},{12,16},{16,20},{20,24},{24,28},{1,5},{5,9},{9,... | collective-permute-start | bytes 393224 | tf_op jit(solution)/shard_map/ppermute | solution.py:134
  224.2 17.1 %collective-permute-start.3 = (bf16[2,128,256]{2,1,0:T(8,128)(2,1)S(1)}, bf16[2,128,256]{2,1,0:T(8,128)(2,1)S(1)}, u32[]{:S(2)}, u32[]{:S(2)}) collective-permute-start(bf16[2,128,256]{2,1,0:T(8,128)(2,1)S(1)} %get-tuple-element.80), channel_id=1, source_target_pairs={{4,0},{8,4},{12,8},{16,12},{20,16},{24,20},{28,24},{5,1},{9,5},{13... | collective-permute-start | bytes 393224 | tf_op jit(solution)/shard_map/ppermute | solution.py:135
  231.1 0.7 copy-start.7
  232.8 2.9 copy-start.1
  235.6 9.0 %collective-permute-start.7 = (bf16[2,2,128,256]{3,0,2,1:T(2,128)(2,1)S(1)}, bf16[2,2,128,256]{3,0,2,1:T(2,128)(2,1)S(1)}, u32[]{:S(2)}, u32[]{:S(2)}) collective-permute-start(bf16[2,2,128,256]{3,0,2,1:T(2,128)(2,1)S(1)} %get-tuple-element.74), channel_id=1, source_target_pairs={{0,4},{4,8},{8,12},{12,16},{16,20},{20,24},{24,28},{28,0},{1,5},{5... | collective-permute-start | bytes 786440 | tf_op jit(solution)/shard_map/ppermute | solution.py:116
  235.7 10.6 %collective-permute-start.8 = (bf16[2,2,128,256]{3,0,2,1:T(2,128)(2,1)S(1)}, bf16[2,2,128,256]{3,0,2,1:T(2,128)(2,1)S(1)}, u32[]{:S(2)}, u32[]{:S(2)}) collective-permute-start(bf16[2,2,128,256]{3,0,2,1:T(2,128)(2,1)S(1)} %get-tuple-element.73), channel_id=1, source_target_pairs={{0,8},{4,12},{8,16},{12,20},{16,24},{20,28},{24,0},{28,4},{1,9},{5... | collective-permute-start | bytes 786440 | tf_op jit(solution)/shard_map/ppermute | solution.py:116
  238.7 17.6 %collective-permute-start.9 = (bf16[2,2,128,256]{3,0,2,1:T(2,128)(2,1)S(1)}, bf16[2,2,128,256]{3,0,2,1:T(2,128)(2,1)S(1)}, u32[]{:S(2)}, u32[]{:S(2)}) collective-permute-start(bf16[2,2,128,256]{3,0,2,1:T(2,128)(2,1)S(1)} %get-tuple-element.72), channel_id=1, source_target_pairs={{0,12},{4,16},{8,20},{12,24},{16,28},{20,0},{24,4},{28,8},{1,13},{... | collective-permute-start | bytes 786440 | tf_op jit(solution)/shard_map/ppermute | solution.py:116
  241.3 15.9 %collective-permute-start.10 = (bf16[2,2,128,256]{3,0,2,1:T(2,128)(2,1)S(1)}, bf16[2,2,128,256]{3,0,2,1:T(2,128)(2,1)S(1)}, u32[]{:S(2)}, u32[]{:S(2)}) collective-permute-start(bf16[2,2,128,256]{3,0,2,1:T(2,128)(2,1)S(1)} %get-tuple-element.71), channel_id=1, source_target_pairs={{0,16},{4,20},{8,24},{12,28},{16,0},{20,4},{24,8},{28,12},{1,17},{... | collective-permute-start | bytes 786440 | tf_op jit(solution)/shard_map/ppermute | solution.py:116
  241.9 16.2 %collective-permute-start.11 = (bf16[2,2,128,256]{3,0,2,1:T(2,128)(2,1)S(1)}, bf16[2,2,128,256]{3,0,2,1:T(2,128)(2,1)S(1)}, u32[]{:S(2)}, u32[]{:S(2)}) collective-permute-start(bf16[2,2,128,256]{3,0,2,1:T(2,128)(2,1)S(1)} %get-tuple-element.70), channel_id=1, source_target_pairs={{0,20},{4,24},{8,28},{12,0},{16,4},{20,8},{24,12},{28,16},{1,21},{... | collective-permute-start | bytes 786440 | tf_op jit(solution)/shard_map/ppermute | solution.py:116
  244.6 29.1 %collective-permute-start.12 = (bf16[2,2,128,256]{3,0,2,1:T(2,128)(2,1)}, bf16[2,2,128,256]{3,0,2,1:T(2,128)(2,1)S(1)}, u32[]{:S(2)}, u32[]{:S(2)}) collective-permute-start(bf16[2,2,128,256]{3,0,2,1:T(2,128)(2,1)} %get-tuple-element.69), channel_id=1, source_target_pairs={{0,24},{4,28},{8,0},{12,4},{16,8},{20,12},{24,16},{28,20},{1,25},{... | collective-permute-start | bytes 786440 | tf_op jit(solution)/shard_map/ppermute | solution.py:116
  246.3 28.3 %collective-permute-start.13 = (bf16[2,2,128,256]{3,0,2,1:T(2,128)(2,1)}, bf16[2,2,128,256]{3,0,2,1:T(2,128)(2,1)S(1)}, u32[]{:S(2)}, u32[]{:S(2)}) collective-permute-start(bf16[2,2,128,256]{3,0,2,1:T(2,128)(2,1)} %get-tuple-element.68), channel_id=1, source_target_pairs={{0,28},{4,0},{8,4},{12,8},{16,12},{20,16},{24,20},{28,24},{1,29},{... | collective-permute-start | bytes 786440 | tf_op jit(solution)/shard_map/ppermute | solution.py:116
  256.3 26.5 %collective-permute-start.5 = (bf16[2,2,128,256]{3,2,1,0:T(8,128)(2,1)}, bf16[2,2,128,256]{3,2,1,0:T(8,128)(2,1)S(1)}, u32[]{:S(2)}, u32[]{:S(2)}) collective-permute-start(bf16[2,2,128,256]{3,2,1,0:T(8,128)(2,1)} %fusion.24), channel_id=1, source_target_pairs={{0,8},{4,12},{8,0},{12,4},{16,24},{20,28},{24,16},{28,20},{1,9},{5... | collective-permute-start | bytes 786440 | tf_op jit(solution)/shard_map/ppermute | solution.py:152
  269.2 67.8 %all-to-all-start.3 = ((bf16[512,16,128]{2,1,0:T(8,128)(2,1)}), bf16[512,16,128]{2,1,0:T(8,128)(2,1)}, u32[]{:S(2)}, u32[]{:S(2)}) async-start(bf16[512,16,128]{2,1,0:T(8,128)(2,1)} %bitcast.154), calls=%async_computation.3 | async-start | bytes 4194304 | tf_op jit(solution)/shard_map/all_to_all | solution.py:305
  275.5 8.0 %copy-start.11 = (pred[8]{0:T(512)(128)(4,1)S(1)}, pred[8]{0:T(512)(128)(4,1)}, u32[]{:S(2)}) copy-start(pred[8]{0:T(512)(128)(4,1)} %compare_and_fusion.2) | copy-start | bytes 28
  282.9 4.0 %copy-start.5 = (bf16[8,2,4,1,1]{2,1,0,4,3:T(2,128)(2,1)S(1)}, bf16[8,2,4,1,1]{2,1,0,4,3:T(2,128)(2,1)}, u32[]{:S(2)}) copy-start(bf16[8,2,4,1,1]{2,1,0,4,3:T(2,128)(2,1)} %fusion.11) | copy-start | bytes 388
  282.9 7.4 %collective-permute-start.6 = (bf16[2,2,128,256]{3,2,1,0:T(8,128)(2,1)S(1)}, bf16[2,2,128,256]{3,2,1,0:T(8,128)(2,1)S(1)}, u32[]{:S(2)}, u32[]{:S(2)}) collective-permute-start(bf16[2,2,128,256]{3,2,1,0:T(8,128)(2,1)S(1)} %fusion.28), channel_id=1, source_target_pairs={{0,16},{4,20},{8,24},{12,28},{16,0},{20,4},{24,8},{28,12},{1,17},{... | collective-permute-start | bytes 786440 | tf_op jit(solution)/shard_map/ppermute | solution.py:152
  287.0 3.5 copy-start.6
  291.0 6.3 %copy-start.12 = (s32[4]{0:T(128)S(1)}, s32[4]{0:T(128)}, u32[]{:S(2)}) copy-start(s32[4]{0:T(128)} %fusion.49) | copy-start | bytes 52
  291.6 24.1 %collective-permute-start.14 = (bf16[2,128,2,128]{3,1,2,0:T(8,128)(2,1)S(1)}, bf16[2,128,2,128]{3,1,2,0:T(8,128)(2,1)S(1)}, u32[]{:S(2)}, u32[]{:S(2)}) collective-permute-start(bf16[2,128,2,128]{3,1,2,0:T(8,128)(2,1)S(1)} %copy.240), channel_id=1, source_target_pairs={{0,1},{1,2},{2,3},{3,0},{4,5},{5,6},{6,7},{7,4},{8,9},{9,10},{10,1... | collective-permute-start | bytes 393224 | tf_op jit(solution)/shard_map/ppermute | solution.py:116
  293.4 37.4 %collective-permute-start.15 = (bf16[2,128,2,128]{3,1,2,0:T(8,128)(2,1)S(1)}, bf16[2,128,2,128]{3,1,2,0:T(8,128)(2,1)S(1)}, u32[]{:S(2)}, u32[]{:S(2)}) collective-permute-start(bf16[2,128,2,128]{3,1,2,0:T(8,128)(2,1)S(1)} %copy.241), channel_id=1, source_target_pairs={{0,2},{1,3},{2,0},{3,1},{4,6},{5,7},{6,4},{7,5},{8,10},{9,11},{10,... | collective-permute-start | bytes 393224 | tf_op jit(solution)/shard_map/ppermute | solution.py:116
  295.8 35.0 %collective-permute-start.16 = (bf16[2,128,2,128]{3,1,2,0:T(8,128)(2,1)S(1)}, bf16[2,128,2,128]{3,1,2,0:T(8,128)(2,1)S(1)}, u32[]{:S(2)}, u32[]{:S(2)}) collective-permute-start(bf16[2,128,2,128]{3,1,2,0:T(8,128)(2,1)S(1)} %copy.242), channel_id=1, source_target_pairs={{0,3},{1,0},{2,1},{3,2},{4,7},{5,4},{6,5},{7,6},{8,11},{9,8},{10,9... | collective-permute-start | bytes 393224 | tf_op jit(solution)/shard_map/ppermute | solution.py:116
Sparse Core Ops, SparseCore 0:
  28.9 35.6 all-gather.1

commit v8 on v6

--- a/solution.py
+++ b/solution.py
@@ -303,8 +303,8 @@
     key_grad_all = kv_grad[0].reshape(shard_len, heads_kv, head_width)
     value_grad_all = kv_grad[1].reshape(shard_len, heads_kv, head_width)
     out_back = lax.all_to_all(out_all, "head", split_axis=0, concat_axis=1, tiled=True)
-    query_back = lax.all_to_all(query_grad_all, "head", split_axis=0, concat_axis=1, tiled=True)
-    (out_back, query_back), kv_grad = lax.optimization_barrier(((out_back, query_back), kv_grad))
+    query_back = exchange(query_grad_all, "head", 0, 1)
+    out_back, kv_grad = lax.optimization_barrier((out_back, kv_grad))
     kv_grad = kv_grad.reshape(2, shard_len, heads_kv, head_width)
     kv_back = lax.all_to_all(kv_grad, "head", split_axis=1, concat_axis=2, tiled=True)
     return (out_back, query_back, kv_back[0], kv_back[1])

time: 334 us -> 336 us (level)
  blocking collectives: 16.6 us -> 0 us
  waiting for transfers between devices: 99.6 us -> 114 us
  other arithmetic: 12.9 us -> 18.7 us
    ppermute x7 -> x10, waiting for transfers between devices: 1.71 us -> 25.2 us  [exchange(): part = lax.ppermute(part, axis, pairs)]
    all_to_all x1 -> x0, blocking collectives: 16.6 us -> none  [per_device(): lax.all_to_all(kv_grad, 'head', split_axis=1, concat_axis=2, tiled=True)]
    all_to_all x1, waiting for transfers between devices: 15.3 us -> 7.33 us  [per_device(): lax.all_to_all(kv_grad, 'head', split_axis=1, concat_axis=2, tiled=True)]
    unnamed x39, local copies, waits for them, and re-layouts: 25.5 us -> 19.4 us
    gather x1 -> x2, local copies, waits for them, and re-layouts: 7.33 us -> 9.47 us  [exchange(): stacked = jnp.take(jnp.stack(received), order, axis=0)]
    ppermute x7 -> x10, starting transfers between devices: 7.87 us -> 6.32 us  [exchange(): part = lax.ppermute(part, axis, pairs)]
  transfers between devices with their start and end apart: 21 -> 24, of which waited for: 8 -> 14; matrix products, arithmetic and copies ran while one was open for 20% -> 22% of each run, Pallas kernels for 8% -> 8%
where the time goes in v8:
time: 336 us; the launch traced here: 335 us
  waiting for transfers between devices  114 us (34%)
  local copies, waits for them, and re-layouts  76.7 us (23%)
  Pallas kernels  62.8 us (19%)
  starting transfers between devices  45.6 us (14%)
  other arithmetic  18.7 us (6%)
  between operations  14.6 us (4%)
    all_to_all x1, waiting for transfers between devices, per_device(): lax.all_to_all(queries, 'head', split_axis=1, concat_axis=0, tiled=True)  42.7 us
    pallas_call x1, Pallas kernels, attention_call(): pl.pallas_call(functools.partial(backward_kernel, scale=scale), cost_esti...  37.4 us
    pallas_call x1, Pallas kernels, attention_call(): pl.pallas_call(functools.partial(forward_kernel, scale=scale), cost_estim...  25.3 us
    ppermute x10, waiting for transfers between devices, exchange(): part = lax.ppermute(part, axis, pairs)  25.2 us
    all_to_all x1, waiting for transfers between devices, per_device(): lax.all_to_all(out_all, 'head', split_axis=0, concat_axis=1, tiled=True)  20.9 us
    unnamed x39, local copies, waits for them, and re-layouts  19.4 us
    gather x2, local copies, waits for them, and re-layouts, exchange(): stacked = jnp.take(jnp.stack(received), order, axis=0)  9.47 us
    ppermute x2, starting transfers between devices, padded(): after = lax.ppermute(leading, axis, down)  8.98 us
  transfers between devices with their start and end apart: 24, of which 14 were waited for; matrix products, arithmetic and copies ran while one was open for 22% of the time, Pallas kernels for 8%

profile of v8, /device:TPU:4, one launch (start us, length us, event | category | flops | bytes accessed | tf_op | source)
XLA Modules:
  0.0 334.7 jit_solution(9884581555639386296)
XLA Ops:
  7.2 1.7 copy.163
  8.9 4.9 %all-to-all-start.1 = ((bf16[128,8,128]{2,0,1:T(8,128)(2,1)}), bf16[128,8,128]{2,0,1:T(8,128)(2,1)S(1)}, u32[]{:S(2)}, u32[]{:S(2)}) async-start(bf16[128,8,128]{2,0,1:T(8,128)(2,1)} %copy.163), calls=%async_computation.1 | async-start | bytes 524288 | tf_op jit(solution)/shard_map/all_to_all | solution.py:161
  13.7 1.7 copy.165
  15.4 7.2 %all-to-all-done.1 = bf16[128,8,128]{2,0,1:T(8,128)(2,1)S(1)} async-done(((bf16[128,8,128]{2,0,1:T(8,128)(2,1)}), bf16[128,8,128]{2,0,1:T(8,128)(2,1)S(1)}, u32[]{:S(2)}, u32[]{:S(2)}) %all-to-all-start.1) | async-done | bytes 262176 | tf_op jit(solution)/shard_map/all_to_all | solution.py:161
  22.6 3.4 %all-to-all-start.2 = ((bf16[128,8,128]{2,0,1:T(8,128)(2,1)}), bf16[128,8,128]{2,0,1:T(8,128)(2,1)S(1)}, u32[]{:S(2)}, u32[]{:S(2)}) async-start(bf16[128,8,128]{2,0,1:T(8,128)(2,1)} %copy.165), calls=%async_computation.2 | async-start | bytes 524288 | tf_op jit(solution)/shard_map/all_to_all | solution.py:162
  26.6 6.5 %all-to-all-done.2 = bf16[128,8,128]{2,0,1:T(8,128)(2,1)S(1)} async-done(((bf16[128,8,128]{2,0,1:T(8,128)(2,1)}), bf16[128,8,128]{2,0,1:T(8,128)(2,1)S(1)}, u32[]{:S(2)}, u32[]{:S(2)}) %all-to-all-start.2) | async-done | bytes 262176 | tf_op jit(solution)/shard_map/all_to_all | solution.py:162
  34.3 4.3 %copy.161 = bf16[128,64,128]{2,0,1:T(8,128)(2,1)} copy(bf16[128,64,128]{2,1,0:T(8,128)(2,1)} %param.10) | data formatting | bytes 4194304 | tf_op args[0]
  38.6 3.8 %all-to-all-start = ((bf16[128,64,128]{2,0,1:T(8,128)(2,1)}), bf16[128,64,128]{2,0,1:T(8,128)(2,1)S(1)}, u32[]{:S(2)}, u32[]{:S(2)}) async-start(bf16[128,64,128]{2,0,1:T(8,128)(2,1)} %copy.161), calls=%async_computation | async-start | bytes 4194304 | tf_op jit(solution)/shard_map/all_to_all | solution.py:160
  45.1 42.7 %all-to-all-done = bf16[128,64,128]{2,0,1:T(8,128)(2,1)S(1)} async-done(((bf16[128,64,128]{2,0,1:T(8,128)(2,1)}), bf16[128,64,128]{2,0,1:T(8,128)(2,1)S(1)}, u32[]{:S(2)}, u32[]{:S(2)}) %all-to-all-start) | async-done | bytes 2097184 | tf_op jit(solution)/shard_map/all_to_all | solution.py:160
  87.8 2.7 copy.162
  90.5 4.3 %copy.174 = bf16[128,64,128]{2,0,1:T(8,128)(2,1)} copy(bf16[128,64,128]{2,1,0:T(8,128)(2,1)} %param.13) | data formatting | bytes 4194304 | tf_op jit(solution)/shard_map/optimization_barrier | solution.py:212
  94.8 3.7 %all-to-all-start.3 = ((bf16[128,64,128]{2,0,1:T(8,128)(2,1)}), bf16[128,64,128]{2,0,1:T(8,128)(2,1)S(1)}, u32[]{:S(2)}, u32[]{:S(2)}) async-start(bf16[128,64,128]{2,0,1:T(8,128)(2,1)} %copy.174), calls=%async_computation.3 | async-start | bytes 4194304 | tf_op jit(solution)/shard_map/all_to_all | solution.py:213
  99.1 1.9 collective-permute-start
  101.1 4.7 %collective-permute-start.1 = (bf16[2,128,256]{2,1,0:T(8,128)(2,1)S(1)}, bf16[2,128,256]{2,1,0:T(8,128)(2,1)S(1)}, u32[]{:S(2)}, u32[]{:S(2)}) collective-permute-start(bf16[2,128,256]{2,1,0:T(8,128)(2,1)S(1)} %get-tuple-element.92), channel_id=1, source_target_pairs={{4,0},{8,4},{12,8},{16,12},{20,16},{24,20},{28,24},{5,1},{9,5},{13... | collective-permute-start | bytes 393224 | tf_op jit(solution)/shard_map/ppermute | solution.py:135
  106.5 1.6 collective-permute-done.1
  109.1 4.0 %gather_fusion.1 = bf16[12,2,128,256]{3,2,1,0:T(8,128)(2,1)} fusion(bf16[2,32,128,256]{3,2,1,0:T(8,128)(2,1)} %bitcast.166, s32[1024]{0:T(1024)S(1)} %get-tuple-element.101), kind=kCustom, calls=%fused_computation.1 | custom fusion | bytes 3145776 | tf_op jit(solution)/shard_map/jit(_take)/gather | solution.py:215
  113.2 1.6 broadcast_select_fusion.1
  114.8 1.3 copy.232
  116.1 2.7 gather_fusion
  118.8 4.2 %reshape.460.q_ref = bf16[4,128,2048]{2,1,0:T(8,128)(2,1)} reshape(bf16[512,16,128]{2,1,0:T(8,128)(2,1)} %bitcast.143) | data formatting | bytes 4194304 | tf_op jit(solution)/shard_map/reshape | solution.py:249
  123.1 1.5 slice_bitcast_fusion.6
  125.0 2.3 pad_maximum_fusion.k_ref.v_ref
  128.0 25.3 %shard_map.93.o_ref = bf16[4,128,2048]{2,1,0:T(8,128)(2,1)} custom-call(bf16[4,128,2048]{2,1,0:T(8,128)(2,1)} %reshape.460.q_ref, bf16[4,8,2,128,256]{4,3,2,1,0:T(8,128)(2,1)} %pad_maximum_fusion.k_ref.v_ref, bf16[4,8,2,128,256]{4,3,2,1,0:T(8,128)(2,1)} %pad_maximum_fusion.k_ref.v_ref, f32[4,1,1024]{2,1,0:T(1,128)} %bitcast.169), custom_call_target="tpu_custom_call" | custom-call | flops 4294967296 | bytes 23068672 | tf_op jit(solution)/shard_map/pallas_call | solution.py:79
  153.3 2.7 copy.231
  156.0 4.2 %reshape.470.do_ref = bf16[4,128,2048]{2,1,0:T(8,128)(2,1)} reshape(bf16[4,128,16,128]{3,2,1,0:T(8,128)(2,1)} %bitcast.147) | data formatting | bytes 4194304 | tf_op jit(solution)/shard_map/reshape | solution.py:251
  160.2 37.4 %shard_map.94 = (bf16[4,128,2048]{2,1,0:T(8,128)(2,1)}, f32[4,8,2,128,256]{4,3,2,1,0:T(8,128)}) custom-call(bf16[4,128,2048]{2,1,0:T(8,128)(2,1)} %reshape.460.q_ref, bf16[4,8,2,128,256]{4,3,2,1,0:T(8,128)(2,1)} %pad_maximum_fusion.k_ref.v_ref, bf16[4,8,2,128,256]{4,3,2,1,0:T(8,128)(2,1)} %pad_maximum_fusion.k_ref.v_ref, ...), custom_call_target="tpu_custom_call" | custom-call | flops 10737418240 | bytes 23068672 | tf_op jit(solution)/shard_map/pallas_call | solution.py:90
  197.6 1.8 slice_reduce_fusion
  199.4 1.7 slice_bitcast_fusion.1
  201.2 1.3 slice_bitcast_fusion.2
  202.5 2.2 fusion.7
  205.7 1.3 dynamic-slice_bitcast_fusion
  207.0 2.0 collective-permute-start.14
  208.9 2.4 collective-permute-start.15
  211.3 1.5 collective-permute-start.16
  212.8 1.4 fusion.50
  214.2 2.3 collective-permute-start.2
  216.6 4.3 %collective-permute-start.3 = (bf16[2,128,256]{2,1,0:T(8,128)(2,1)S(1)}, bf16[2,128,256]{2,1,0:T(8,128)(2,1)S(1)}, u32[]{:S(2)}, u32[]{:S(2)}) collective-permute-start(bf16[2,128,256]{2,1,0:T(8,128)(2,1)S(1)} %get-tuple-element.84), channel_id=1, source_target_pairs={{4,0},{8,4},{12,8},{16,12},{20,16},{24,20},{28,24},{5,1},{9,5},{13... | collective-permute-start | bytes 393224 | tf_op jit(solution)/shard_map/ppermute | solution.py:135
  220.9 2.0 copy.204
  222.9 4.6 %all-to-all-start.4 = ((bf16[512,16,128]{2,1,0:T(8,128)(2,1)}), bf16[512,16,128]{2,1,0:T(8,128)(2,1)}, u32[]{:S(2)}, u32[]{:S(2)}) async-start(bf16[512,16,128]{2,1,0:T(8,128)(2,1)} %bitcast.144), calls=%async_computation.4 | async-start | bytes 4194304 | tf_op jit(solution)/shard_map/all_to_all | solution.py:305
  227.5 1.0 fusion.4
  228.6 2.3 constant_dynamic-slice_fusion.3
  231.0 1.0 bitcast_dynamic-update-slice_fusion.7
  232.6 0.9 collective-permute-done.4
  233.6 5.9 %collective-permute-done.7 = bf16[2,2,128,256]{3,0,2,1:T(2,128)(2,1)S(1)} collective-permute-done((bf16[2,2,128,256]{3,0,2,1:T(2,128)(2,1)S(1)}, bf16[2,2,128,256]{3,0,2,1:T(2,128)(2,1)S(1)}, u32[]{:S(2)}, u32[]{:S(2)}) %collective-permute-start.7) | collective-permute-done | bytes 262176 | tf_op jit(solution)/shard_map/ppermute | solution.py:116
  239.5 0.9 bitcast_dynamic-update-slice_fusion.6
  240.4 3.3 collective-permute-done.8
  244.6 8.1 %collective-permute-done.9 = bf16[2,2,128,256]{3,0,2,1:T(2,128)(2,1)S(1)} collective-permute-done((bf16[2,2,128,256]{3,0,2,1:T(2,128)(2,1)S(1)}, bf16[2,2,128,256]{3,0,2,1:T(2,128)(2,1)S(1)}, u32[]{:S(2)}, u32[]{:S(2)}) %collective-permute-start.9) | collective-permute-done | bytes 262176 | tf_op jit(solution)/shard_map/ppermute | solution.py:116
  253.6 0.9 bitcast_dynamic-update-slice_fusion.3
  254.5 5.4 %collective-permute-done.11 = bf16[2,2,128,256]{3,0,2,1:T(2,128)(2,1)S(1)} collective-permute-done((bf16[2,2,128,256]{3,0,2,1:T(2,128)(2,1)S(1)}, bf16[2,2,128,256]{3,0,2,1:T(2,128)(2,1)S(1)}, u32[]{:S(2)}, u32[]{:S(2)}) %collective-permute-start.11) | collective-permute-done | bytes 262176 | tf_op jit(solution)/shard_map/ppermute | solution.py:116
  262.8 1.7 collective-permute-done.13
  265.4 7.3 %gather_fusion.2 = bf16[8,2,2,128,256]{4,1,3,2,0:T(2,128)(2,1)} fusion(bf16[8,2,2,128,256]{4,1,3,2,0:T(2,128)(2,1)} %bitcast_dynamic-update-slice_fusion, s32[1024]{0:T(1024)S(1)} %pad_clamp_fusion.1), kind=kCustom, calls=%fused_computation.2 | custom fusion | bytes 4194336 | tf_op jit(solution)/shard_map/jit(_take)/gather | solution.py:119
  272.9 1.6 collective-permute-start.6
  274.5 3.5 %broadcast_select_fusion = bf16[8,2,2,128,256]{4,1,3,2,0:T(2,128)(2,1)S(1)} fusion(bf16[8,2,2,128,256]{4,1,3,2,0:T(2,128)(2,1)} %gather_fusion.2, pred[8]{0:T(512)(128)(4,1)S(1)} %copy-done.11), kind=kLoop, calls=%fused_computation.5 | loop fusion | flops 1048576 | bytes 4194312 | tf_op jit(solution)/shard_map/jit(_take)/select_n | solution.py:119
  278.0 1.3 fusion.8
  279.3 1.6 collective-permute-done.6
  281.7 20.9 %all-to-all-done.4 = bf16[512,16,128]{2,1,0:T(8,128)(2,1)} async-done(((bf16[512,16,128]{2,1,0:T(8,128)(2,1)}), bf16[512,16,128]{2,1,0:T(8,128)(2,1)}, u32[]{:S(2)}, u32[]{:S(2)}) %all-to-all-start.4) | async-done | bytes 2097184 | tf_op jit(solution)/shard_map/all_to_all | solution.py:305
  302.6 3.6 %copy.176 = bf16[4,128,16,128]{3,2,0,1:T(8,128)(2,1)} copy(bf16[4,128,16,128]{3,2,1,0:T(8,128)(2,1)} %bitcast.32) | data formatting | bytes 4194304 | tf_op jit(solution)/shard_map/all_to_all | solution.py:305
  306.3 1.2 copy.193
  307.5 3.5 %all-to-all-start.5 = ((bf16[2,512,2,128]{3,2,0,1:T(2,128)(2,1)}), bf16[2,512,2,128]{3,2,0,1:T(2,128)(2,1)S(1)}, u32[]{:S(2)}, u32[]{:S(2)}) async-start(bf16[2,512,2,128]{3,2,0,1:T(2,128)(2,1)} %copy.193), calls=%async_computation.5 | async-start | bytes 1048576 | tf_op jit(solution)/shard_map/all_to_all | solution.py:309
  311.0 1.6 pad_maximum_fusion.1
  312.6 2.1 gather_fusion.3
  314.8 1.9 select_bitcast_fusion
  316.6 2.0 copy.192
  318.6 7.3 %all-to-all-done.5 = bf16[2,512,2,128]{3,2,0,1:T(2,128)(2,1)S(1)} async-done(((bf16[2,512,2,128]{3,2,0,1:T(2,128)(2,1)}), bf16[2,512,2,128]{3,2,0,1:T(2,128)(2,1)S(1)}, u32[]{:S(2)}, u32[]{:S(2)}) %all-to-all-start.5) | async-done | bytes 524320 | tf_op jit(solution)/shard_map/all_to_all | solution.py:309
  (118 shorter events, 18.3 us)
Async XLA Ops:
  8.9 13.8 %all-to-all-start.1 = ((bf16[128,8,128]{2,0,1:T(8,128)(2,1)}), bf16[128,8,128]{2,0,1:T(8,128)(2,1)S(1)}, u32[]{:S(2)}, u32[]{:S(2)}) async-start(bf16[128,8,128]{2,0,1:T(8,128)(2,1)} %copy.163), calls=%async_computation.1 | async-start | bytes 524288 | tf_op jit(solution)/shard_map/all_to_all | solution.py:161
  22.6 10.4 %all-to-all-start.2 = ((bf16[128,8,128]{2,0,1:T(8,128)(2,1)}), bf16[128,8,128]{2,0,1:T(8,128)(2,1)S(1)}, u32[]{:S(2)}, u32[]{:S(2)}) async-start(bf16[128,8,128]{2,0,1:T(8,128)(2,1)} %copy.165), calls=%async_computation.2 | async-start | bytes 524288 | tf_op jit(solution)/shard_map/all_to_all | solution.py:162
  26.1 64.4 %all-gather.2.cloned.1.call-start = ((), (), s32[]{:S(2)}) async-start(), calls=%async_computation.6 | async-start | bytes 4718592 | tf_op jit(solution)/shard_map/all_gather | solution.py:211
  33.5 0.8 copy-start
  38.6 3.8 %copy-start.9 = (s32[32,3]{0,1:T(4,128)S(1)}, s32[32,3]{0,1:T(4,128)}, u32[]{:S(2)}) copy-start(s32[32,3]{0,1:T(4,128)} %param.15) | copy-start | bytes 1156
  38.6 4.6 %copy-start.10 = (s32[2]{0:T(128)S(1)}, s32[2]{0:T(128)}, u32[]{:S(2)}) copy-start(s32[2]{0:T(128)} %param.14) | copy-start | bytes 28
  38.6 49.2 %all-to-all-start = ((bf16[128,64,128]{2,0,1:T(8,128)(2,1)}), bf16[128,64,128]{2,0,1:T(8,128)(2,1)S(1)}, u32[]{:S(2)}, u32[]{:S(2)}) async-start(bf16[128,64,128]{2,0,1:T(8,128)(2,1)} %copy.161), calls=%async_computation | async-start | bytes 4194304 | tf_op jit(solution)/shard_map/all_to_all | solution.py:160
  94.8 4.3 %copy-start.1 = (bf16[2,512,256]{2,1,0:T(8,128)(2,1)S(1)}, bf16[2,512,256]{2,1,0:T(8,128)(2,1)}, u32[]{:S(2)}) copy-start(bf16[2,512,256]{2,1,0:T(8,128)(2,1)} %copy-done) | copy-start | bytes 1572868
  94.8 58.6 %all-to-all-start.3 = ((bf16[128,64,128]{2,0,1:T(8,128)(2,1)}), bf16[128,64,128]{2,0,1:T(8,128)(2,1)S(1)}, u32[]{:S(2)}, u32[]{:S(2)}) async-start(bf16[128,64,128]{2,0,1:T(8,128)(2,1)} %copy.174), calls=%async_computation.3 | async-start | bytes 4194304 | tf_op jit(solution)/shard_map/all_to_all | solution.py:213
  99.1 7.4 %collective-permute-start = (bf16[2,128,256]{2,1,0:T(8,128)(2,1)S(1)}, bf16[2,128,256]{2,1,0:T(8,128)(2,1)S(1)}, u32[]{:S(2)}, u32[]{:S(2)}) collective-permute-start(bf16[2,128,256]{2,1,0:T(8,128)(2,1)S(1)} %get-tuple-element.91), channel_id=1, source_target_pairs={{0,4},{4,8},{8,12},{12,16},{16,20},{20,24},{24,28},{1,5},{5,9},{9,... | collective-permute-start | bytes 393224 | tf_op jit(solution)/shard_map/ppermute | solution.py:134
  101.1 7.0 %collective-permute-start.1 = (bf16[2,128,256]{2,1,0:T(8,128)(2,1)S(1)}, bf16[2,128,256]{2,1,0:T(8,128)(2,1)S(1)}, u32[]{:S(2)}, u32[]{:S(2)}) collective-permute-start(bf16[2,128,256]{2,1,0:T(8,128)(2,1)S(1)} %get-tuple-element.92), channel_id=1, source_target_pairs={{4,0},{8,4},{12,8},{16,12},{20,16},{24,20},{28,24},{5,1},{9,5},{13... | collective-permute-start | bytes 393224 | tf_op jit(solution)/shard_map/ppermute | solution.py:135
  118.8 4.2 %copy-start.8 = (pred[2]{0:T(512)(128)(4,1)S(1)}, pred[2]{0:T(512)(128)(4,1)}, u32[]{:S(2)}) copy-start(pred[2]{0:T(512)(128)(4,1)} %get-tuple-element.100) | copy-start | bytes 10
  123.0 1.6 copy-start.5
  202.5 2.5 copy-start.4
  207.0 104.0 %collective-permute-start.14 = (bf16[128,16,128]{2,1,0:T(8,128)(2,1)}, bf16[128,16,128]{2,1,0:T(8,128)(2,1)}, u32[]{:S(2)}, u32[]{:S(2)}) collective-permute-start(bf16[128,16,128]{2,1,0:T(8,128)(2,1)} %get-tuple-element.71), channel_id=1, source_target_pairs={{0,1},{1,2},{2,3},{3,0},{4,5},{5,6},{6,7},{7,4},{8,9},{9,10},{10,1... | collective-permute-start | bytes 1572872 | tf_op jit(solution)/shard_map/ppermute | solution.py:116
  208.9 102.1 %collective-permute-start.15 = (bf16[128,16,128]{2,1,0:T(8,128)(2,1)}, bf16[128,16,128]{2,1,0:T(8,128)(2,1)}, u32[]{:S(2)}, u32[]{:S(2)}) collective-permute-start(bf16[128,16,128]{2,1,0:T(8,128)(2,1)} %get-tuple-element.70), channel_id=1, source_target_pairs={{0,2},{1,3},{2,0},{3,1},{4,6},{5,7},{6,4},{7,5},{8,10},{9,11},{10,... | collective-permute-start | bytes 1572872 | tf_op jit(solution)/shard_map/ppermute | solution.py:116
  211.3 99.7 %collective-permute-start.16 = (bf16[128,16,128]{2,1,0:T(8,128)(2,1)}, bf16[128,16,128]{2,1,0:T(8,128)(2,1)}, u32[]{:S(2)}, u32[]{:S(2)}) collective-permute-start(bf16[128,16,128]{2,1,0:T(8,128)(2,1)} %get-tuple-element.69), channel_id=1, source_target_pairs={{0,3},{1,0},{2,1},{3,2},{4,7},{5,4},{6,5},{7,6},{8,11},{9,8},{10,9... | collective-permute-start | bytes 1572872 | tf_op jit(solution)/shard_map/ppermute | solution.py:116
  214.2 6.7 %copy-start.3 = (bf16[4,128,2048]{2,1,0:T(8,128)(2,1)S(1)}, bf16[4,128,2048]{2,1,0:T(8,128)(2,1)}, u32[]{:S(2)}) copy-start(bf16[4,128,2048]{2,1,0:T(8,128)(2,1)} %shard_map.93.o_ref) | copy-start | bytes 6291460
  214.2 17.8 %collective-permute-start.2 = (bf16[2,128,256]{2,1,0:T(8,128)(2,1)S(1)}, bf16[2,128,256]{2,1,0:T(8,128)(2,1)S(1)}, u32[]{:S(2)}, u32[]{:S(2)}) collective-permute-start(bf16[2,128,256]{2,1,0:T(8,128)(2,1)S(1)} %get-tuple-element.83), channel_id=1, source_target_pairs={{0,4},{4,8},{8,12},{12,16},{16,20},{20,24},{24,28},{1,5},{5,9},{9,... | collective-permute-start | bytes 393224 | tf_op jit(solution)/shard_map/ppermute | solution.py:134
  216.6 15.4 %collective-permute-start.3 = (bf16[2,128,256]{2,1,0:T(8,128)(2,1)S(1)}, bf16[2,128,256]{2,1,0:T(8,128)(2,1)S(1)}, u32[]{:S(2)}, u32[]{:S(2)}) collective-permute-start(bf16[2,128,256]{2,1,0:T(8,128)(2,1)S(1)} %get-tuple-element.84), channel_id=1, source_target_pairs={{4,0},{8,4},{12,8},{16,12},{20,16},{24,20},{28,24},{5,1},{9,5},{13... | collective-permute-start | bytes 393224 | tf_op jit(solution)/shard_map/ppermute | solution.py:135
  222.9 4.6 %copy-start.7 = (s32[12]{0:T(128)S(1)}, s32[12]{0:T(128)}, u32[]{:S(2)}) copy-start(s32[12]{0:T(128)} %fusion.48) | copy-start | bytes 148
  222.9 79.7 %all-to-all-start.4 = ((bf16[512,16,128]{2,1,0:T(8,128)(2,1)}), bf16[512,16,128]{2,1,0:T(8,128)(2,1)}, u32[]{:S(2)}, u32[]{:S(2)}) async-start(bf16[512,16,128]{2,1,0:T(8,128)(2,1)} %bitcast.144), calls=%async_computation.4 | async-start | bytes 4194304 | tf_op jit(solution)/shard_map/all_to_all | solution.py:305
  228.5 2.4 copy-start.2
  232.0 1.5 collective-permute-start.4
  232.0 7.5 %collective-permute-start.7 = (bf16[2,2,128,256]{3,0,2,1:T(2,128)(2,1)S(1)}, bf16[2,2,128,256]{3,0,2,1:T(2,128)(2,1)S(1)}, u32[]{:S(2)}, u32[]{:S(2)}) collective-permute-start(bf16[2,2,128,256]{3,0,2,1:T(2,128)(2,1)S(1)} %get-tuple-element.78), channel_id=1, source_target_pairs={{0,4},{4,8},{8,12},{12,16},{16,20},{20,24},{24,28},{28,0},{1,5},{5... | collective-permute-start | bytes 786440 | tf_op jit(solution)/shard_map/ppermute | solution.py:116
  233.5 10.2 %collective-permute-start.8 = (bf16[2,2,128,256]{3,0,2,1:T(2,128)(2,1)S(1)}, bf16[2,2,128,256]{3,0,2,1:T(2,128)(2,1)S(1)}, u32[]{:S(2)}, u32[]{:S(2)}) collective-permute-start(bf16[2,2,128,256]{3,0,2,1:T(2,128)(2,1)S(1)} %get-tuple-element.77), channel_id=1, source_target_pairs={{0,8},{4,12},{8,16},{12,20},{16,24},{20,28},{24,0},{28,4},{1,9},{5... | collective-permute-start | bytes 786440 | tf_op jit(solution)/shard_map/ppermute | solution.py:116
  239.5 13.2 %collective-permute-start.9 = (bf16[2,2,128,256]{3,0,2,1:T(2,128)(2,1)S(1)}, bf16[2,2,128,256]{3,0,2,1:T(2,128)(2,1)S(1)}, u32[]{:S(2)}, u32[]{:S(2)}) collective-permute-start(bf16[2,2,128,256]{3,0,2,1:T(2,128)(2,1)S(1)} %get-tuple-element.76), channel_id=1, source_target_pairs={{0,12},{4,16},{8,20},{12,24},{16,28},{20,0},{24,4},{28,8},{1,13},{... | collective-permute-start | bytes 786440 | tf_op jit(solution)/shard_map/ppermute | solution.py:116
  243.7 9.9 %collective-permute-start.10 = (bf16[2,2,128,256]{3,0,2,1:T(2,128)(2,1)S(1)}, bf16[2,2,128,256]{3,0,2,1:T(2,128)(2,1)S(1)}, u32[]{:S(2)}, u32[]{:S(2)}) collective-permute-start(bf16[2,2,128,256]{3,0,2,1:T(2,128)(2,1)S(1)} %get-tuple-element.75), channel_id=1, source_target_pairs={{0,16},{4,20},{8,24},{12,28},{16,0},{20,4},{24,8},{28,12},{1,17},{... | collective-permute-start | bytes 786440 | tf_op jit(solution)/shard_map/ppermute | solution.py:116
  252.7 7.1 %collective-permute-start.11 = (bf16[2,2,128,256]{3,0,2,1:T(2,128)(2,1)S(1)}, bf16[2,2,128,256]{3,0,2,1:T(2,128)(2,1)S(1)}, u32[]{:S(2)}, u32[]{:S(2)}) collective-permute-start(bf16[2,2,128,256]{3,0,2,1:T(2,128)(2,1)S(1)} %get-tuple-element.74), channel_id=1, source_target_pairs={{0,20},{4,24},{8,28},{12,0},{16,4},{20,8},{24,12},{28,16},{1,21},{... | collective-permute-start | bytes 786440 | tf_op jit(solution)/shard_map/ppermute | solution.py:116
  253.6 7.9 %collective-permute-start.12 = (bf16[2,2,128,256]{3,0,2,1:T(2,128)(2,1)S(1)}, bf16[2,2,128,256]{3,0,2,1:T(2,128)(2,1)S(1)}, u32[]{:S(2)}, u32[]{:S(2)}) collective-permute-start(bf16[2,2,128,256]{3,0,2,1:T(2,128)(2,1)S(1)} %get-tuple-element.73), channel_id=1, source_target_pairs={{0,24},{4,28},{8,0},{12,4},{16,8},{20,12},{24,16},{28,20},{1,25},{... | collective-permute-start | bytes 786440 | tf_op jit(solution)/shard_map/ppermute | solution.py:116
  259.8 4.7 %collective-permute-start.13 = (bf16[2,2,128,256]{3,0,2,1:T(2,128)(2,1)S(1)}, bf16[2,2,128,256]{3,0,2,1:T(2,128)(2,1)S(1)}, u32[]{:S(2)}, u32[]{:S(2)}) collective-permute-start(bf16[2,2,128,256]{3,0,2,1:T(2,128)(2,1)S(1)} %get-tuple-element.72), channel_id=1, source_target_pairs={{0,28},{4,0},{8,4},{12,8},{16,12},{20,16},{24,20},{28,24},{1,29},{... | collective-permute-start | bytes 786440 | tf_op jit(solution)/shard_map/ppermute | solution.py:116
  261.5 11.3 %collective-permute-start.5 = (bf16[2,2,128,256]{3,2,1,0:T(8,128)(2,1)S(1)}, bf16[2,2,128,256]{3,2,1,0:T(8,128)(2,1)S(1)}, u32[]{:S(2)}, u32[]{:S(2)}) collective-permute-start(bf16[2,2,128,256]{3,2,1,0:T(8,128)(2,1)S(1)} %fusion.22), channel_id=1, source_target_pairs={{0,8},{4,12},{8,0},{12,4},{16,24},{20,28},{24,16},{28,20},{1,9},{5... | collective-permute-start | bytes 786440 | tf_op jit(solution)/shard_map/ppermute | solution.py:152
  265.4 9.1 %copy-start.11 = (pred[8]{0:T(512)(128)(4,1)S(1)}, pred[8]{0:T(512)(128)(4,1)}, u32[]{:S(2)}) copy-start(pred[8]{0:T(512)(128)(4,1)} %compare_and_fusion.3) | copy-start | bytes 28
  272.9 8.0 %collective-permute-start.6 = (bf16[2,2,128,256]{3,2,1,0:T(8,128)(2,1)S(1)}, bf16[2,2,128,256]{3,2,1,0:T(8,128)(2,1)S(1)}, u32[]{:S(2)}, u32[]{:S(2)}) collective-permute-start(bf16[2,2,128,256]{3,2,1,0:T(8,128)(2,1)S(1)} %fusion.26), channel_id=1, source_target_pairs={{0,16},{4,20},{8,24},{12,28},{16,0},{20,4},{24,8},{28,12},{1,17},{... | collective-permute-start | bytes 786440 | tf_op jit(solution)/shard_map/ppermute | solution.py:152
  278.0 3.0 copy-start.6
  307.5 18.5 %all-to-all-start.5 = ((bf16[2,512,2,128]{3,2,0,1:T(2,128)(2,1)}), bf16[2,512,2,128]{3,2,0,1:T(2,128)(2,1)S(1)}, u32[]{:S(2)}, u32[]{:S(2)}) async-start(bf16[2,512,2,128]{3,2,0,1:T(2,128)(2,1)} %copy.193), calls=%async_computation.5 | async-start | bytes 1048576 | tf_op jit(solution)/shard_map/all_to_all | solution.py:309
Sparse Core Ops, SparseCore 0:
  34.5 35.9 all-gather.1

commit v9 on v7

--- a/solution.py
+++ b/solution.py
@@ -304,8 +304,9 @@
     value_grad_all = kv_grad[1].reshape(shard_len, heads_kv, head_width)
     out_back = lax.all_to_all(out_all, "head", split_axis=0, concat_axis=1, tiled=True)
     query_back = lax.all_to_all(query_grad_all, "head", split_axis=0, concat_axis=1, tiled=True)
+    (out_back, query_back), kv_grad = lax.optimization_barrier(((out_back, query_back), kv_grad))
     kv_grad = kv_grad.reshape(2, shard_len, heads_kv, head_width)
-    kv_back = exchange(kv_grad, "head", 1, 2)
+    kv_back = lax.all_to_all(kv_grad, "head", split_axis=1, concat_axis=2, tiled=True)
     return (out_back, query_back, kv_back[0], kv_back[1])
 
 

time: 350 us -> 346 us (0.989)
  blocking collectives: 19.2 us -> 35.6 us
  waiting for transfers between devices: 98.6 us -> 90.2 us
  starting transfers between devices: 45.6 us -> 39.5 us
  other arithmetic: 20.7 us -> 14.6 us
    ppermute x10 -> x7, waiting for transfers between devices: 40.4 us -> 1.73 us  [exchange(): part = lax.ppermute(part, axis, pairs)]
    all_to_all x1, waiting for transfers between devices: 0.01 us -> 20.8 us  [per_device(): lax.all_to_all(out_all, 'head', split_axis=0, concat_axis=1, tiled=True)]
    all_to_all x0 -> x1, blocking collectives: none -> 16.5 us  [per_device(): lax.all_to_all(kv_grad, 'head', split_axis=1, concat_axis=2, tiled=True)]
    ppermute x10 -> x7, starting transfers between devices: 13.8 us -> 8 us  [exchange(): part = lax.ppermute(part, axis, pairs)]
    all_to_all x1, waiting for transfers between devices: 10.3 us -> 16 us  [per_device(): lax.all_to_all(query_grad_all, 'head', split_axis=0, concat_axis=1, tiled...]
    unnamed x43 -> x28, local copies, waits for them, and re-layouts: 15.9 us -> 19.7 us
    gather x2 -> x1, local copies, waits for them, and re-layouts: 7.98 us -> 7.33 us  [exchange(): stacked = jnp.take(jnp.stack(received), order, axis=0)]
  transfers between devices with their start and end apart: 22 -> 19, of which waited for: 8 -> 7; matrix products, arithmetic and copies ran while one was open for 24% -> 23% of each run, Pallas kernels for 7% -> 7%
where the time goes in v9:
time: 346 us; the launch traced here: 344 us
  waiting for transfers between devices  90.2 us (26%)
  local copies, waits for them, and re-layouts  84.5 us (24%)
  Pallas kernels  62.8 us (18%)
  starting transfers between devices  39.5 us (11%)
  blocking collectives  35.6 us (10%)
  between operations  14.7 us (4%)
  other arithmetic  14.6 us (4%)
    all_to_all x1, waiting for transfers between devices, per_device(): lax.all_to_all(queries, 'head', split_axis=1, concat_axis=0, tiled=True)  46.2 us
    pallas_call x1, Pallas kernels, attention_call(): pl.pallas_call(functools.partial(backward_kernel, scale=scale), cost_esti...  37.4 us
    pallas_call x1, Pallas kernels, attention_call(): pl.pallas_call(functools.partial(forward_kernel, scale=scale), cost_estim...  25.3 us
    all_to_all x1, waiting for transfers between devices, per_device(): lax.all_to_all(out_all, 'head', split_axis=0, concat_axis=1, tiled=True)  20.8 us
    unnamed x28, local copies, waits for them, and re-layouts  19.7 us
    all_to_all x1, blocking collectives, per_device(): lax.all_to_all(jnp.stack([keys, values], axis=2), 'head', split_axis=1, c...  19.2 us
    all_to_all x1, blocking collectives, per_device(): lax.all_to_all(kv_grad, 'head', split_axis=1, concat_axis=2, tiled=True)  16.5 us
    all_to_all x1, waiting for transfers between devices, per_device(): lax.all_to_all(query_grad_all, 'head', split_axis=0, concat_axis=1, tiled...  16 us
  transfers between devices with their start and end apart: 19, of which 7 were waited for; matrix products, arithmetic and copies ran while one was open for 23% of the time, Pallas kernels for 7%

profile of v9, /device:TPU:4, one launch (start us, length us, event | category | flops | bytes accessed | tf_op | source)
XLA Modules:
  0.0 344.4 jit_solution(15295394294912781481)
XLA Ops:
  7.2 1.1 copy_bitcast_fusion.6
  8.4 19.2 %all_to_all.102 = bf16[128,8,2,128]{3,0,2,1:T(8,128)(2,1)S(1)} all-to-all(bf16[128,8,2,128]{3,0,2,1:T(8,128)(2,1)S(1)} %pad_maximum_fusion.6), channel_id=1, replica_groups=mesh['seq'=8,'head'=4] {'head'}, dimensions={1} | all-to-all | bytes 1048576 | tf_op jit(solution)/shard_map/all_to_all | solution.py:159
  28.0 0.8 pad_maximum_fusion.5
  29.4 2.7 copy.185
  32.1 3.8 %all-to-all-start = ((bf16[128,64,128]{2,0,1:T(8,128)(2,1)}), bf16[128,64,128]{2,0,1:T(8,128)(2,1)S(1)}, u32[]{:S(2)}, u32[]{:S(2)}) async-start(bf16[128,64,128]{2,0,1:T(8,128)(2,1)} %copy.185), calls=%async_computation | async-start | bytes 4194304 | tf_op jit(solution)/shard_map/all_to_all | solution.py:163
  36.9 46.2 %all-to-all-done = bf16[128,64,128]{2,0,1:T(8,128)(2,1)S(1)} async-done(((bf16[128,64,128]{2,0,1:T(8,128)(2,1)}), bf16[128,64,128]{2,0,1:T(8,128)(2,1)S(1)}, u32[]{:S(2)}, u32[]{:S(2)}) %all-to-all-start) | async-done | bytes 2097184 | tf_op jit(solution)/shard_map/all_to_all | solution.py:163
  83.2 2.7 copy.186
  85.8 4.2 %copy.204 = bf16[128,64,128]{2,0,1:T(8,128)(2,1)} copy(bf16[128,64,128]{2,1,0:T(8,128)(2,1)} %param.13) | data formatting | bytes 4194304 | tf_op jit(solution)/shard_map/optimization_barrier | solution.py:212
  90.1 3.6 %all-to-all-start.2 = ((bf16[128,64,128]{2,0,1:T(8,128)(2,1)}), bf16[128,64,128]{2,0,1:T(8,128)(2,1)S(1)}, u32[]{:S(2)}, u32[]{:S(2)}) async-start(bf16[128,64,128]{2,0,1:T(8,128)(2,1)} %copy.204), calls=%async_computation.2 | async-start | bytes 4194304 | tf_op jit(solution)/shard_map/all_to_all | solution.py:213
  94.4 1.9 collective-permute-start
  96.4 4.7 %collective-permute-start.1 = (bf16[2,128,256]{1,2,0:T(8,128)(2,1)S(1)}, bf16[2,128,256]{1,2,0:T(8,128)(2,1)S(1)}, u32[]{:S(2)}, u32[]{:S(2)}) collective-permute-start(bf16[2,128,256]{1,2,0:T(8,128)(2,1)S(1)} %get-tuple-element.90), channel_id=1, source_target_pairs={{4,0},{8,4},{12,8},{16,12},{20,16},{24,20},{28,24},{5,1},{9,5},{13... | collective-permute-start | bytes 393224 | tf_op jit(solution)/shard_map/ppermute | solution.py:135
  101.6 1.8 collective-permute-done.1
  103.4 1.1 pad_maximum_fusion.9
  104.5 1.2 copy.201
  106.4 1.2 copy.199
  108.9 6.4 %copy.194 = bf16[2,4096,256]{2,1,0:T(8,128)(2,1)} copy(bf16[2,4096,256]{1,2,0:T(8,128)(2,1)} %all-gather.2.cloned.1.call-done) | data formatting | bytes 8388608 | tf_op jit(solution)/shard_map/optimization_barrier | solution.py:212
  115.2 4.0 %gather_fusion.1 = bf16[12,2,128,256]{3,2,1,0:T(8,128)(2,1)} fusion(bf16[2,32,128,256]{3,2,1,0:T(8,128)(2,1)} %bitcast.141, s32[1024]{0:T(1024)S(1)} %get-tuple-element.103), kind=kCustom, calls=%fused_computation.1 | custom fusion | bytes 3145776 | tf_op jit(solution)/shard_map/jit(_take)/gather | solution.py:215
  119.3 1.6 broadcast_select_fusion.1
  120.9 1.3 copy.262
  122.2 2.7 gather_fusion
  124.9 4.2 %reshape.401.q_ref = bf16[4,128,2048]{2,1,0:T(8,128)(2,1)} reshape(bf16[512,16,128]{2,1,0:T(8,128)(2,1)} %bitcast.148) | data formatting | bytes 4194304 | tf_op jit(solution)/shard_map/reshape | solution.py:249
  129.2 1.5 slice_bitcast_fusion.6
  131.1 2.3 pad_maximum_fusion.k_ref.v_ref
  134.1 25.3 %shard_map.93.o_ref = bf16[4,128,2048]{2,1,0:T(8,128)(2,1)} custom-call(bf16[4,128,2048]{2,1,0:T(8,128)(2,1)} %reshape.401.q_ref, bf16[4,8,2,128,256]{4,3,2,1,0:T(8,128)(2,1)} %pad_maximum_fusion.k_ref.v_ref, bf16[4,8,2,128,256]{4,3,2,1,0:T(8,128)(2,1)} %pad_maximum_fusion.k_ref.v_ref, f32[4,1,1024]{2,1,0:T(1,128)} %bitcast.178), custom_call_target="tpu_custom_call" | custom-call | flops 4294967296 | bytes 23068672 | tf_op jit(solution)/shard_map/pallas_call | solution.py:79
  159.4 2.7 copy.261
  162.1 4.2 %reshape.411.do_ref = bf16[4,128,2048]{2,1,0:T(8,128)(2,1)} reshape(bf16[4,128,16,128]{3,2,1,0:T(8,128)(2,1)} %bitcast.150) | data formatting | bytes 4194304 | tf_op jit(solution)/shard_map/reshape | solution.py:251
  166.3 37.4 %shard_map.94 = (bf16[4,128,2048]{2,1,0:T(8,128)(2,1)}, f32[4,8,2,128,256]{4,3,2,1,0:T(8,128)}) custom-call(bf16[4,128,2048]{2,1,0:T(8,128)(2,1)} %reshape.401.q_ref, bf16[4,8,2,128,256]{4,3,2,1,0:T(8,128)(2,1)} %pad_maximum_fusion.k_ref.v_ref, bf16[4,8,2,128,256]{4,3,2,1,0:T(8,128)(2,1)} %pad_maximum_fusion.k_ref.v_ref, ...), custom_call_target="tpu_custom_call" | custom-call | flops 10737418240 | bytes 23068672 | tf_op jit(solution)/shard_map/pallas_call | solution.py:90
  203.8 3.6 %copy.235 = bf16[64,8,16,128]{3,2,1,0:T(8,128)(2,1)} copy(bf16[64,8,16,128]{3,1,2,0:T(8,128)(2,1)} %bitcast.162) | data formatting | bytes 4194304
  207.4 5.1 %all-to-all-start.4 = ((bf16[512,16,128]{2,1,0:T(8,128)(2,1)}), bf16[512,16,128]{2,1,0:T(8,128)(2,1)S(1)}, u32[]{:S(2)}, u32[]{:S(2)}) async-start(bf16[512,16,128]{2,1,0:T(8,128)(2,1)} %bitcast.145), calls=%async_computation.4 | async-start | bytes 4194304 | tf_op jit(solution)/shard_map/all_to_all | solution.py:306
  212.5 1.8 slice_reduce_fusion
  214.4 0.9 collective-permute-start.4
  215.3 1.3 slice_bitcast_fusion.2
  216.6 1.7 slice_bitcast_fusion.1
  218.7 1.9 collective-permute-start.2
  220.7 4.5 %collective-permute-start.3 = (bf16[2,128,256]{2,1,0:T(8,128)(2,1)S(1)}, bf16[2,128,256]{2,1,0:T(8,128)(2,1)S(1)}, u32[]{:S(2)}, u32[]{:S(2)}) collective-permute-start(bf16[2,128,256]{2,1,0:T(8,128)(2,1)S(1)} %get-tuple-element.82), channel_id=1, source_target_pairs={{4,0},{8,4},{12,8},{16,12},{20,16},{24,20},{28,24},{5,1},{9,5},{13... | collective-permute-start | bytes 393224 | tf_op jit(solution)/shard_map/ppermute | solution.py:135
  225.2 2.1 fusion.7
  227.4 1.0 fusion.4
  228.5 2.8 constant_dynamic-slice_fusion
  231.5 2.0 copy.234
  233.4 1.0 bitcast_dynamic-update-slice_fusion.7
  234.4 2.5 collective-permute-start.9
  237.7 0.9 fusion.24
  238.6 1.7 collective-permute-done.7
  240.3 0.9 collective-permute-start.12
  241.3 0.9 bitcast_dynamic-update-slice_fusion.6
  242.2 3.8 %collective-permute-start.13 = (bf16[2,2,128,256]{3,0,2,1:T(2,128)(2,1)}, bf16[2,2,128,256]{3,0,2,1:T(2,128)(2,1)}, u32[]{:S(2)}, u32[]{:S(2)}) collective-permute-start(bf16[2,2,128,256]{3,0,2,1:T(2,128)(2,1)} %get-tuple-element.70), channel_id=1, source_target_pairs={{0,28},{4,0},{8,4},{12,8},{16,12},{20,16},{24,20},{28,24},{1,29},{... | collective-permute-start | bytes 786440 | tf_op jit(solution)/shard_map/ppermute | solution.py:116
  245.9 16.0 %all-to-all-done.4 = bf16[512,16,128]{2,1,0:T(8,128)(2,1)S(1)} async-done(((bf16[512,16,128]{2,1,0:T(8,128)(2,1)}), bf16[512,16,128]{2,1,0:T(8,128)(2,1)S(1)}, u32[]{:S(2)}, u32[]{:S(2)}) %all-to-all-start.4) | async-done | bytes 2097184 | tf_op jit(solution)/shard_map/all_to_all | solution.py:306
  261.9 4.7 %all-to-all-start.3 = ((bf16[512,16,128]{2,1,0:T(8,128)(2,1)}), bf16[512,16,128]{2,1,0:T(8,128)(2,1)}, u32[]{:S(2)}, u32[]{:S(2)}) async-start(bf16[512,16,128]{2,1,0:T(8,128)(2,1)} %bitcast.146), calls=%async_computation.3 | async-start | bytes 4194304 | tf_op jit(solution)/shard_map/all_to_all | solution.py:305
  266.6 0.9 bitcast_dynamic-update-slice_fusion.5
  267.5 0.9 bitcast_dynamic-update-slice_fusion.4
  268.4 1.8 bitcast_dynamic-update-slice_fusion.3
  270.2 1.8 bitcast_dynamic-update-slice_fusion.2
  272.1 1.8 bitcast_dynamic-update-slice_fusion.1
  273.9 1.8 bitcast_dynamic-update-slice_fusion
  275.7 7.3 %gather_fusion.2 = bf16[8,2,2,128,256]{4,1,3,2,0:T(2,128)(2,1)} fusion(bf16[8,2,2,128,256]{4,1,3,2,0:T(2,128)(2,1)} %bitcast_dynamic-update-slice_fusion, s32[1024]{0:T(1024)S(1)} %pad_clamp_fusion), kind=kCustom, calls=%fused_computation.2 | custom fusion | bytes 4194336 | tf_op jit(solution)/shard_map/jit(_take)/gather | solution.py:119
  283.4 3.5 %broadcast_select_fusion = bf16[8,2,2,128,256]{4,1,3,2,0:T(2,128)(2,1)S(1)} fusion(bf16[8,2,2,128,256]{4,1,3,2,0:T(2,128)(2,1)} %gather_fusion.2, pred[8]{0:T(512)(128)(4,1)S(1)} %compare_and_fusion.2), kind=kLoop, calls=%fused_computation.4 | loop fusion | flops 1048576 | bytes 4194312 | tf_op jit(solution)/shard_map/jit(_take)/select_n | solution.py:119
  286.9 1.3 fusion.8
  288.2 3.2 collective-permute-done.6
  292.2 2.0 copy.207
  294.2 20.8 %all-to-all-done.3 = bf16[512,16,128]{2,1,0:T(8,128)(2,1)} async-done(((bf16[512,16,128]{2,1,0:T(8,128)(2,1)}), bf16[512,16,128]{2,1,0:T(8,128)(2,1)}, u32[]{:S(2)}, u32[]{:S(2)}) %all-to-all-start.3) | async-done | bytes 2097184 | tf_op jit(solution)/shard_map/all_to_all | solution.py:305
  315.0 3.6 %copy.206 = bf16[4,128,16,128]{3,2,0,1:T(8,128)(2,1)} copy(bf16[4,128,16,128]{3,2,1,0:T(8,128)(2,1)} %bitcast.35) | data formatting | bytes 4194304 | tf_op jit(solution)/shard_map/all_to_all | solution.py:305
  319.1 16.5 %all_to_all.103 = bf16[2,512,2,128]{3,2,0,1:T(2,128)(2,1)S(1)} all-to-all(bf16[2,512,2,128]{3,2,0,1:T(2,128)(2,1)S(1)} %copy.223), channel_id=1, replica_groups=mesh['seq'=8,'head'=4] {'head'}, dimensions={1} | all-to-all | bytes 1048576 | tf_op jit(solution)/shard_map/all_to_all | solution.py:309
  335.8 0.9 copy.227
  336.6 0.9 copy.228
  (101 shorter events, 9.7 us)
Async XLA Ops:
  7.2 78.7 %all-gather.2.cloned.1.call-start = ((), (), s32[]{:S(2)}) async-start(), calls=%async_computation.6 | async-start | bytes 4718592 | tf_op jit(solution)/shard_map/all_gather | solution.py:211
  27.6 1.8 copy-start.2
  32.1 3.8 %copy-start.6 = (s32[32,3]{0,1:T(4,128)S(1)}, s32[32,3]{0,1:T(4,128)}, u32[]{:S(2)}) copy-start(s32[32,3]{0,1:T(4,128)} %param.15) | copy-start | bytes 1156
  32.1 4.4 %copy-start.7 = (s32[2]{0:T(128)S(1)}, s32[2]{0:T(128)}, u32[]{:S(2)}) copy-start(s32[2]{0:T(128)} %param.14) | copy-start | bytes 28
  32.1 51.1 %all-to-all-start = ((bf16[128,64,128]{2,0,1:T(8,128)(2,1)}), bf16[128,64,128]{2,0,1:T(8,128)(2,1)S(1)}, u32[]{:S(2)}, u32[]{:S(2)}) async-start(bf16[128,64,128]{2,0,1:T(8,128)(2,1)} %copy.185), calls=%async_computation | async-start | bytes 4194304 | tf_op jit(solution)/shard_map/all_to_all | solution.py:163
  90.1 69.3 %all-to-all-start.2 = ((bf16[128,64,128]{2,0,1:T(8,128)(2,1)}), bf16[128,64,128]{2,0,1:T(8,128)(2,1)S(1)}, u32[]{:S(2)}, u32[]{:S(2)}) async-start(bf16[128,64,128]{2,0,1:T(8,128)(2,1)} %copy.204), calls=%async_computation.2 | async-start | bytes 4194304 | tf_op jit(solution)/shard_map/all_to_all | solution.py:213
  94.4 7.2 %collective-permute-start = (bf16[2,128,256]{1,2,0:T(8,128)(2,1)S(1)}, bf16[2,128,256]{1,2,0:T(8,128)(2,1)S(1)}, u32[]{:S(2)}, u32[]{:S(2)}) collective-permute-start(bf16[2,128,256]{1,2,0:T(8,128)(2,1)S(1)} %get-tuple-element.89), channel_id=1, source_target_pairs={{0,4},{4,8},{8,12},{12,16},{16,20},{20,24},{24,28},{1,5},{5,9},{9,... | collective-permute-start | bytes 393224 | tf_op jit(solution)/shard_map/ppermute | solution.py:134
  96.4 7.0 %collective-permute-start.1 = (bf16[2,128,256]{1,2,0:T(8,128)(2,1)S(1)}, bf16[2,128,256]{1,2,0:T(8,128)(2,1)S(1)}, u32[]{:S(2)}, u32[]{:S(2)}) collective-permute-start(bf16[2,128,256]{1,2,0:T(8,128)(2,1)S(1)} %get-tuple-element.90), channel_id=1, source_target_pairs={{4,0},{8,4},{12,8},{16,12},{20,16},{24,20},{28,24},{5,1},{9,5},{13... | collective-permute-start | bytes 393224 | tf_op jit(solution)/shard_map/ppermute | solution.py:135
  129.1 1.6 copy-start.4
  129.1 1.6 copy-start.5
  207.4 54.5 %all-to-all-start.4 = ((bf16[512,16,128]{2,1,0:T(8,128)(2,1)}), bf16[512,16,128]{2,1,0:T(8,128)(2,1)S(1)}, u32[]{:S(2)}, u32[]{:S(2)}) async-start(bf16[512,16,128]{2,1,0:T(8,128)(2,1)} %bitcast.145), calls=%async_computation.4 | async-start | bytes 4194304 | tf_op jit(solution)/shard_map/all_to_all | solution.py:306
  214.4 23.3 %collective-permute-start.4 = (bf16[2,2,128,256]{3,2,1,0:T(8,128)(2,1)S(1)}, bf16[2,2,128,256]{3,2,1,0:T(8,128)(2,1)S(1)}, u32[]{:S(2)}, u32[]{:S(2)}) collective-permute-start(bf16[2,2,128,256]{3,2,1,0:T(8,128)(2,1)S(1)} %convert_element_type.65), channel_id=1, source_target_pairs={{0,4},{4,0},{8,12},{12,8},{16,20},{20,16},{24,28},{28,24},{1,5},{5... | collective-permute-start | bytes 786440 | tf_op jit(solution)/shard_map/ppermute | solution.py:152
  218.7 15.7 %collective-permute-start.2 = (bf16[2,128,256]{2,1,0:T(8,128)(2,1)S(1)}, bf16[2,128,256]{2,1,0:T(8,128)(2,1)S(1)}, u32[]{:S(2)}, u32[]{:S(2)}) collective-permute-start(bf16[2,128,256]{2,1,0:T(8,128)(2,1)S(1)} %get-tuple-element.81), channel_id=1, source_target_pairs={{0,4},{4,8},{8,12},{12,16},{16,20},{20,24},{24,28},{1,5},{5,9},{9,... | collective-permute-start | bytes 393224 | tf_op jit(solution)/shard_map/ppermute | solution.py:134
  220.7 16.3 %collective-permute-start.3 = (bf16[2,128,256]{2,1,0:T(8,128)(2,1)S(1)}, bf16[2,128,256]{2,1,0:T(8,128)(2,1)S(1)}, u32[]{:S(2)}, u32[]{:S(2)}) collective-permute-start(bf16[2,128,256]{2,1,0:T(8,128)(2,1)S(1)} %get-tuple-element.82), channel_id=1, source_target_pairs={{4,0},{8,4},{12,8},{16,12},{20,16},{24,20},{28,24},{5,1},{9,5},{13... | collective-permute-start | bytes 393224 | tf_op jit(solution)/shard_map/ppermute | solution.py:135
  228.5 3.0 copy-start.3
  231.3 9.0 %collective-permute-start.7 = (bf16[2,2,128,256]{3,0,2,1:T(2,128)(2,1)S(1)}, bf16[2,2,128,256]{3,0,2,1:T(2,128)(2,1)S(1)}, u32[]{:S(2)}, u32[]{:S(2)}) collective-permute-start(bf16[2,2,128,256]{3,0,2,1:T(2,128)(2,1)S(1)} %get-tuple-element.76), channel_id=1, source_target_pairs={{0,4},{4,8},{8,12},{12,16},{16,20},{20,24},{24,28},{28,0},{1,5},{5... | collective-permute-start | bytes 786440 | tf_op jit(solution)/shard_map/ppermute | solution.py:116
  231.4 10.8 %collective-permute-start.8 = (bf16[2,2,128,256]{3,0,2,1:T(2,128)(2,1)S(1)}, bf16[2,2,128,256]{3,0,2,1:T(2,128)(2,1)S(1)}, u32[]{:S(2)}, u32[]{:S(2)}) collective-permute-start(bf16[2,2,128,256]{3,0,2,1:T(2,128)(2,1)S(1)} %get-tuple-element.75), channel_id=1, source_target_pairs={{0,8},{4,12},{8,16},{12,20},{16,24},{20,28},{24,0},{28,4},{1,9},{5... | collective-permute-start | bytes 786440 | tf_op jit(solution)/shard_map/ppermute | solution.py:116
  234.4 33.1 %collective-permute-start.9 = (bf16[2,2,128,256]{3,0,2,1:T(2,128)(2,1)}, bf16[2,2,128,256]{3,0,2,1:T(2,128)(2,1)S(1)}, u32[]{:S(2)}, u32[]{:S(2)}) collective-permute-start(bf16[2,2,128,256]{3,0,2,1:T(2,128)(2,1)} %get-tuple-element.74), channel_id=1, source_target_pairs={{0,12},{4,16},{8,20},{12,24},{16,28},{20,0},{24,4},{28,8},{1,13},{... | collective-permute-start | bytes 786440 | tf_op jit(solution)/shard_map/ppermute | solution.py:116
  236.9 31.5 %collective-permute-start.10 = (bf16[2,2,128,256]{3,0,2,1:T(2,128)(2,1)}, bf16[2,2,128,256]{3,0,2,1:T(2,128)(2,1)}, u32[]{:S(2)}, u32[]{:S(2)}) collective-permute-start(bf16[2,2,128,256]{3,0,2,1:T(2,128)(2,1)} %get-tuple-element.73), channel_id=1, source_target_pairs={{0,16},{4,20},{8,24},{12,28},{16,0},{20,4},{24,8},{28,12},{1,17},{... | collective-permute-start | bytes 786440 | tf_op jit(solution)/shard_map/ppermute | solution.py:116
  237.6 4.5 %copy-start = (f32[4,2,128,256]{3,2,1,0:T(8,128)}, f32[4,2,128,256]{3,2,1,0:T(8,128)S(1)}, u32[]{:S(2)}) copy-start(f32[4,2,128,256]{3,2,1,0:T(8,128)S(1)} %fusion.25) | copy-start | bytes 3145732
  237.7 32.6 %collective-permute-start.11 = (bf16[2,2,128,256]{3,0,2,1:T(2,128)(2,1)}, bf16[2,2,128,256]{3,0,2,1:T(2,128)(2,1)}, u32[]{:S(2)}, u32[]{:S(2)}) collective-permute-start(bf16[2,2,128,256]{3,0,2,1:T(2,128)(2,1)} %get-tuple-element.72), channel_id=1, source_target_pairs={{0,20},{4,24},{8,28},{12,0},{16,4},{20,8},{24,12},{28,16},{1,21},{... | collective-permute-start | bytes 786440 | tf_op jit(solution)/shard_map/ppermute | solution.py:116
  240.3 31.7 %collective-permute-start.12 = (bf16[2,2,128,256]{3,0,2,1:T(2,128)(2,1)}, bf16[2,2,128,256]{3,0,2,1:T(2,128)(2,1)}, u32[]{:S(2)}, u32[]{:S(2)}) collective-permute-start(bf16[2,2,128,256]{3,0,2,1:T(2,128)(2,1)} %get-tuple-element.71), channel_id=1, source_target_pairs={{0,24},{4,28},{8,0},{12,4},{16,8},{20,12},{24,16},{28,20},{1,25},{... | collective-permute-start | bytes 786440 | tf_op jit(solution)/shard_map/ppermute | solution.py:116
  242.2 31.7 %collective-permute-start.13 = (bf16[2,2,128,256]{3,0,2,1:T(2,128)(2,1)}, bf16[2,2,128,256]{3,0,2,1:T(2,128)(2,1)}, u32[]{:S(2)}, u32[]{:S(2)}) collective-permute-start(bf16[2,2,128,256]{3,0,2,1:T(2,128)(2,1)} %get-tuple-element.70), channel_id=1, source_target_pairs={{0,28},{4,0},{8,4},{12,8},{16,12},{20,16},{24,20},{28,24},{1,29},{... | collective-permute-start | bytes 786440 | tf_op jit(solution)/shard_map/ppermute | solution.py:116
  261.9 53.1 %all-to-all-start.3 = ((bf16[512,16,128]{2,1,0:T(8,128)(2,1)}), bf16[512,16,128]{2,1,0:T(8,128)(2,1)}, u32[]{:S(2)}, u32[]{:S(2)}) async-start(bf16[512,16,128]{2,1,0:T(8,128)(2,1)} %bitcast.146), calls=%async_computation.3 | async-start | bytes 4194304 | tf_op jit(solution)/shard_map/all_to_all | solution.py:305
  267.5 15.6 %collective-permute-start.5 = (bf16[2,2,128,256]{3,2,1,0:T(8,128)(2,1)}, bf16[2,2,128,256]{3,2,1,0:T(8,128)(2,1)S(1)}, u32[]{:S(2)}, u32[]{:S(2)}) collective-permute-start(bf16[2,2,128,256]{3,2,1,0:T(8,128)(2,1)} %fusion.24), channel_id=1, source_target_pairs={{0,8},{4,12},{8,0},{12,4},{16,24},{20,28},{24,16},{28,20},{1,9},{5... | collective-permute-start | bytes 786440 | tf_op jit(solution)/shard_map/ppermute | solution.py:152
  283.2 8.3 %collective-permute-start.6 = (bf16[2,2,128,256]{3,2,1,0:T(8,128)(2,1)S(1)}, bf16[2,2,128,256]{3,2,1,0:T(8,128)(2,1)S(1)}, u32[]{:S(2)}, u32[]{:S(2)}) collective-permute-start(bf16[2,2,128,256]{3,2,1,0:T(8,128)(2,1)S(1)} %fusion.28), channel_id=1, source_target_pairs={{0,16},{4,20},{8,24},{12,28},{16,0},{20,4},{24,8},{28,12},{1,17},{... | collective-permute-start | bytes 786440 | tf_op jit(solution)/shard_map/ppermute | solution.py:152
  288.2 3.6 %copy-start.1 = (f32[4,2,128,256]{3,2,1,0:T(8,128)S(1)}, f32[4,2,128,256]{3,2,1,0:T(8,128)}, u32[]{:S(2)}) copy-start(f32[4,2,128,256]{3,2,1,0:T(8,128)} %copy-done) | copy-start | bytes 3145732
Sparse Core Ops, SparseCore 0:
  28.9 35.6 all-gather.1

commit v10 on v6

--- a/solution.py
+++ b/solution.py
@@ -29,22 +29,20 @@
 
 
 def forward_kernel(q_ref, k_ref, v_ref, bias_ref, out_ref, *, scale):
-    group = q_ref.shape[1] // q_ref.shape[0]
     width = k_ref.shape[-1]
-    q = rows_of(q_ref, group, width)
+    q = q_ref[...].reshape(-1, width)
     k = k_ref[...].reshape(-1, width)
     v = v_ref[...].reshape(-1, width)
     p_low = softmax_rows(q, k, bias_ref[...], scale).astype(jnp.bfloat16)
     o_low = jnp.dot(p_low, v, preferred_element_type=jnp.float32).astype(jnp.bfloat16)
-    store_rows(out_ref, o_low, group, width)
+    out_ref[...] = o_low.reshape(out_ref.shape)
 
 
 def backward_kernel(q_ref, k_ref, v_ref, do_ref, o_ref, bias_ref, dq_ref, grad_ref, *, scale):
-    group = q_ref.shape[1] // q_ref.shape[0]
     width = k_ref.shape[-1]
-    q = rows_of(q_ref, group, width)
-    do = rows_of(do_ref, group, width)
-    o_low = rows_of(o_ref, group, width)
+    q = q_ref[...].reshape(-1, width)
+    do = do_ref[...].reshape(-1, width)
+    o_low = o_ref[...].reshape(-1, width)
     k = k_ref[...].reshape(-1, width)
     v = v_ref[...].reshape(-1, width)
     rows_by_cols = (((1,), (1,)), ((), ()))
@@ -55,7 +53,7 @@
     dp = lax.dot_general(do, v, rows_by_cols, preferred_element_type=jnp.float32)
     ds_low = (p * (dp - delta)).astype(jnp.bfloat16)
     dq = jnp.dot(ds_low, k, preferred_element_type=jnp.float32) * scale
-    store_rows(dq_ref, dq.astype(jnp.bfloat16), group, width)
+    dq_ref[...] = dq.astype(jnp.bfloat16).reshape(dq_ref.shape)
     dk = lax.dot_general(ds_low, q, over_rows, preferred_element_type=jnp.float32) * scale
     dv = lax.dot_general(p_low, do, over_rows, preferred_element_type=jnp.float32)
     grad_ref[:, 0] = dk.reshape(grad_ref.shape[0], -1, width)
@@ -63,10 +61,10 @@
 
 
 def attention_call(q, tiles, do, bias, heads_kv, scale):
-    blocks, tokens, q_width = q.shape
-    tile_count, head_width = tiles.shape[1], tiles.shape[-1] // heads_kv
-    rows_width = q_width // heads_kv
-    q_spec = pl.BlockSpec((None, tokens, rows_width), lambda j, h: (j, 0, h))
+    heads_kv, group, blocks, tokens, head_width = q.shape
+    tile_count = tiles.shape[1]
+    rows_width = group * head_width
+    q_spec = pl.BlockSpec((None, group, None, tokens, head_width), lambda j, h: (h, 0, j, 0, 0))
     k_spec = pl.BlockSpec((None, tile_count, None, tokens, head_width), lambda j, h: (j, 0, 0, 0, h))
     v_spec = pl.BlockSpec((None, tile_count, None, tokens, head_width), lambda j, h: (j, 0, 1, 0, h))
     b_spec = pl.BlockSpec((None, 1, bias.shape[-1]), lambda j, h: (j, 0, 0))
@@ -157,12 +155,12 @@
 
 def per_device(queries, keys, values, output_gradient, global_blocks, random_blocks):
     query_loc, key_loc, value_loc, grad_loc = (
-        lax.all_to_all(queries, "head", split_axis=1, concat_axis=0, tiled=True),
+        lax.all_to_all(queries.transpose(1, 0, 2), "head", split_axis=0, concat_axis=1, tiled=True),
         lax.all_to_all(keys, "head", split_axis=1, concat_axis=0, tiled=True),
         lax.all_to_all(values, "head", split_axis=1, concat_axis=0, tiled=True),
         output_gradient,
     )
-    shard_len, heads_q, head_width = query_loc.shape
+    heads_q, shard_len, head_width = query_loc.shape
     heads_kv = key_loc.shape[1]
     heads_per_group = heads_q // heads_kv
     kv_width = heads_kv * head_width
@@ -210,7 +208,7 @@
     ).astype(jnp.bfloat16)
     everything = lax.all_gather(kv_pair, "seq", axis=1, tiled=True)
     query_loc, everything, grad_loc = lax.optimization_barrier((query_loc, everything, grad_loc))
-    grad_loc = lax.all_to_all(grad_loc, "head", split_axis=1, concat_axis=0, tiled=True)
+    grad_loc = lax.all_to_all(grad_loc.transpose(1, 0, 2), "head", split_axis=0, concat_axis=1, tiled=True)
     tiled_all = everything.reshape(2, block_total_count, BLOCK_TOKENS, kv_width)
     random_tiles = jnp.take(tiled_all, my_entries, axis=1).transpose(1, 0, 2, 3)
     global_tiles = jnp.take(tiled_all, global_blocks, axis=1).transpose(1, 0, 2, 3)
@@ -246,15 +244,13 @@
     bias = jnp.where(live, 0.0, -jnp.inf).astype(jnp.float32)
     bias = jnp.repeat(bias, BLOCK_TOKENS, axis=1).reshape(blocks, 1, tile_count * BLOCK_TOKENS)
     out_q, grad_q, tile_grads = attention_call(
-        query_loc.reshape(blocks, BLOCK_TOKENS, heads_q * head_width),
+        query_loc.reshape(heads_kv, heads_per_group, blocks, BLOCK_TOKENS, head_width),
         all_tiles,
-        grad_loc.reshape(blocks, BLOCK_TOKENS, heads_q * head_width),
+        grad_loc.reshape(heads_kv, heads_per_group, blocks, BLOCK_TOKENS, head_width),
         bias,
         heads_kv,
         score_scale,
     )
-    output_block_rows = out_q.reshape(blocks, BLOCK_TOKENS, heads_q, head_width)
-    query_gradient_rows = grad_q.reshape(blocks, BLOCK_TOKENS, heads_q, head_width)
     pad_spec_low = ((0, 2), (0, 0), (0, 0), (0, 0))
     pad_spec_mid = ((1, 1), (0, 0), (0, 0), (0, 0))
     pad_spec_high = ((2, 0), (0, 0), (0, 0), (0, 0))
@@ -298,16 +294,16 @@
         preferred_element_type=jnp.float32,
     )
     kv_grad = interior.transpose(1, 0, 2, 3).reshape(2, shard_len, kv_width).astype(jnp.bfloat16)
-    out_all = output_block_rows.reshape(shard_len, heads_q, head_width)
-    query_grad_all = query_gradient_rows.reshape(shard_len, heads_q, head_width)
+    out_all = out_q.reshape(heads_q, shard_len, head_width)
+    query_grad_all = grad_q.reshape(heads_q, shard_len, head_width)
     key_grad_all = kv_grad[0].reshape(shard_len, heads_kv, head_width)
     value_grad_all = kv_grad[1].reshape(shard_len, heads_kv, head_width)
-    out_back = lax.all_to_all(out_all, "head", split_axis=0, concat_axis=1, tiled=True)
-    query_back = lax.all_to_all(query_grad_all, "head", split_axis=0, concat_axis=1, tiled=True)
+    out_back = lax.all_to_all(out_all, "head", split_axis=1, concat_axis=0, tiled=True)
+    query_back = lax.all_to_all(query_grad_all, "head", split_axis=1, concat_axis=0, tiled=True)
     (out_back, query_back), kv_grad = lax.optimization_barrier(((out_back, query_back), kv_grad))
     kv_grad = kv_grad.reshape(2, shard_len, heads_kv, head_width)
     kv_back = lax.all_to_all(kv_grad, "head", split_axis=1, concat_axis=2, tiled=True)
-    return (out_back, query_back, kv_back[0], kv_back[1])
+    return (out_back.transpose(1, 0, 2), query_back.transpose(1, 0, 2), kv_back[0], kv_back[1])
 
 
 def solution(mesh):

time: 334 us -> 329 us (0.985)
  local copies, waits for them, and re-layouts: 75.2 us -> 68.7 us
    unnamed x39 -> x29, local copies, waits for them, and re-layouts: 25.5 us -> 20.1 us
  transfers between devices with their start and end apart: 21 -> 21, of which waited for: 8 -> 10; matrix products, arithmetic and copies ran while one was open for 20% -> 19% of each run, Pallas kernels for 8% -> 8%
where the time goes in v10:
time: 329 us; the launch traced here: 326 us
  waiting for transfers between devices  99.8 us (30%)
  local copies, waits for them, and re-layouts  68.7 us (21%)
  Pallas kernels  63 us (19%)
  starting transfers between devices  49.2 us (15%)
  blocking collectives  16.4 us (5%)
  between operations  14.7 us (4%)
  other arithmetic  11.3 us (3%)
    all_to_all x1, waiting for transfers between devices, per_device(): lax.all_to_all(queries.transpose(1, 0, 2), 'head', split_axis=0, concat_a...  43.7 us
    pallas_call x1, Pallas kernels, attention_call(): pl.pallas_call(functools.partial(backward_kernel, scale=scale), cost_esti...  37.6 us
    pallas_call x1, Pallas kernels, attention_call(): pl.pallas_call(functools.partial(forward_kernel, scale=scale), cost_estim...  25.4 us
    unnamed x29, local copies, waits for them, and re-layouts  20.1 us
    all_to_all x1, waiting for transfers between devices, per_device(): lax.all_to_all(out_all, 'head', split_axis=1, concat_axis=0, tiled=True)  19.9 us
    all_to_all x1, blocking collectives, per_device(): lax.all_to_all(kv_grad, 'head', split_axis=1, concat_axis=2, tiled=True)  16.4 us
    all_to_all x1, waiting for transfers between devices, per_device(): lax.all_to_all(query_grad_all, 'head', split_axis=1, concat_axis=0, tiled...  15.9 us
    ppermute x2, starting transfers between devices, padded(): after = lax.ppermute(leading, axis, down)  9.29 us
  transfers between devices with their start and end apart: 21, of which 10 were waited for; matrix products, arithmetic and copies ran while one was open for 19% of the time, Pallas kernels for 8%

profile of v10, /device:TPU:4, one launch (start us, length us, event | category | flops | bytes accessed | tf_op | source)
XLA Modules:
  0.0 325.6 jit_solution(1527587646781431474)
XLA Ops:
  7.2 1.7 copy.167
  8.9 4.9 %all-to-all-start.1 = ((bf16[128,8,128]{2,0,1:T(8,128)(2,1)}), bf16[128,8,128]{2,0,1:T(8,128)(2,1)S(1)}, u32[]{:S(2)}, u32[]{:S(2)}) async-start(bf16[128,8,128]{2,0,1:T(8,128)(2,1)} %copy.167), calls=%async_computation.1 | async-start | bytes 524288 | tf_op jit(solution)/shard_map/all_to_all | solution.py:159
  13.7 1.7 copy.169
  15.4 7.2 %all-to-all-done.1 = bf16[128,8,128]{2,0,1:T(8,128)(2,1)S(1)} async-done(((bf16[128,8,128]{2,0,1:T(8,128)(2,1)}), bf16[128,8,128]{2,0,1:T(8,128)(2,1)S(1)}, u32[]{:S(2)}, u32[]{:S(2)}) %all-to-all-start.1) | async-done | bytes 262176 | tf_op jit(solution)/shard_map/all_to_all | solution.py:159
  22.6 3.4 %all-to-all-start.2 = ((bf16[128,8,128]{2,0,1:T(8,128)(2,1)}), bf16[128,8,128]{2,0,1:T(8,128)(2,1)S(1)}, u32[]{:S(2)}, u32[]{:S(2)}) async-start(bf16[128,8,128]{2,0,1:T(8,128)(2,1)} %copy.169), calls=%async_computation.2 | async-start | bytes 524288 | tf_op jit(solution)/shard_map/all_to_all | solution.py:160
  26.6 6.5 %all-to-all-done.2 = bf16[128,8,128]{2,0,1:T(8,128)(2,1)S(1)} async-done(((bf16[128,8,128]{2,0,1:T(8,128)(2,1)}), bf16[128,8,128]{2,0,1:T(8,128)(2,1)S(1)}, u32[]{:S(2)}, u32[]{:S(2)}) %all-to-all-start.2) | async-done | bytes 262176 | tf_op jit(solution)/shard_map/all_to_all | solution.py:160
  33.5 0.8 copy-done
  34.3 4.3 %copy.237 = bf16[128,64,128]{2,0,1:T(8,128)(2,1)} copy(bf16[128,64,128]{2,1,0:T(8,128)(2,1)} %param.10) | data formatting | bytes 4194304 | tf_op args[0]
  38.6 3.8 %all-to-all-start = ((bf16[64,128,128]{2,1,0:T(8,128)(2,1)}), bf16[64,128,128]{2,1,0:T(8,128)(2,1)S(1)}, u32[]{:S(2)}, u32[]{:S(2)}) async-start(bf16[64,128,128]{2,1,0:T(8,128)(2,1)} %bitcast.142), calls=%async_computation | async-start | bytes 4194304 | tf_op jit(solution)/shard_map/all_to_all | solution.py:158
  44.1 43.7 %all-to-all-done = bf16[64,128,128]{2,1,0:T(8,128)(2,1)S(1)} async-done(((bf16[64,128,128]{2,1,0:T(8,128)(2,1)}), bf16[64,128,128]{2,1,0:T(8,128)(2,1)S(1)}, u32[]{:S(2)}, u32[]{:S(2)}) %all-to-all-start) | async-done | bytes 2097184 | tf_op jit(solution)/shard_map/all_to_all | solution.py:158
  87.8 1.6 copy.166
  89.4 4.3 %copy.236 = bf16[128,64,128]{2,0,1:T(8,128)(2,1)} copy(bf16[128,64,128]{2,1,0:T(8,128)(2,1)} %param.13) | data formatting | bytes 4194304 | tf_op jit(solution)/shard_map/optimization_barrier | solution.py:210
  93.7 4.6 %all-to-all-start.3 = ((bf16[64,128,128]{2,1,0:T(8,128)(2,1)}), bf16[64,128,128]{2,1,0:T(8,128)(2,1)}, u32[]{:S(2)}, u32[]{:S(2)}) async-start(bf16[64,128,128]{2,1,0:T(8,128)(2,1)} %bitcast.140), calls=%async_computation.3 | async-start | bytes 4194304 | tf_op jit(solution)/shard_map/all_to_all | solution.py:211
  98.4 1.9 collective-permute-start
  100.4 4.7 %collective-permute-start.1 = (bf16[2,128,256]{2,1,0:T(8,128)(2,1)S(1)}, bf16[2,128,256]{2,1,0:T(8,128)(2,1)S(1)}, u32[]{:S(2)}, u32[]{:S(2)}) collective-permute-start(bf16[2,128,256]{2,1,0:T(8,128)(2,1)S(1)} %get-tuple-element.90), channel_id=1, source_target_pairs={{4,0},{8,4},{12,8},{16,12},{20,16},{24,20},{28,24},{5,1},{9,5},{13... | collective-permute-start | bytes 393224 | tf_op jit(solution)/shard_map/ppermute | solution.py:133
  105.6 1.8 collective-permute-done.1
  107.6 0.8 copy_bitcast_fusion.5
  108.4 2.8 gather_fusion.1
  111.6 2.8 gather_fusion
  114.6 0.8 copy-done.5
  115.7 2.3 pad_maximum_fusion.k_ref.v_ref
  118.0 0.7 broadcast_in_dim.79
  118.7 25.4 %shard_map.93.o_ref = bf16[2,8,4,128,128]{4,3,2,1,0:T(8,128)(2,1)} custom-call(bf16[2,8,4,128,128]{4,3,2,1,0:T(8,128)(2,1)} %bitcast.146, bf16[4,8,2,128,256]{4,3,2,1,0:T(8,128)(2,1)} %pad_maximum_fusion.k_ref.v_ref, bf16[4,8,2,128,256]{4,3,2,1,0:T(8,128)(2,1)} %pad_maximum_fusion.k_ref.v_ref, f32[4,1,1024]{2,1,0:T(1,128)} %bitcast.167), custom_call_target="tpu_custom_call" | custom-call | flops 4294967296 | bytes 23068672 | tf_op jit(solution)/shard_map/pallas_call | solution.py:77
  144.0 2.1 all-to-all-done.3
  146.1 3.1 copy.179
  149.3 37.6 %shard_map.94 = (bf16[2,8,4,128,128]{4,3,2,1,0:T(8,128)(2,1)}, f32[4,8,2,128,256]{4,3,2,1,0:T(8,128)}) custom-call(bf16[2,8,4,128,128]{4,3,2,1,0:T(8,128)(2,1)} %bitcast.147, bf16[4,8,2,128,256]{4,3,2,1,0:T(8,128)(2,1)} %pad_maximum_fusion.k_ref.v_ref, bf16[4,8,2,128,256]{4,3,2,1,0:T(8,128)(2,1)} %pad_maximum_fusion.k_ref.v_ref, ...), custom_call_target="tpu_custom_call" | custom-call | flops 10737418240 | bytes 23068672 | tf_op jit(solution)/shard_map/pallas_call | solution.py:88
  186.8 4.3 %copy.182 = bf16[16,512,128]{2,0,1:T(8,128)(2,1)} copy(bf16[16,512,128]{2,1,0:T(8,128)(2,1)} %bitcast.151) | data formatting | bytes 4194304 | tf_op jit(solution)/shard_map/reshape | solution.py:298
  191.1 3.6 %all-to-all-start.5 = ((bf16[16,512,128]{2,0,1:T(8,128)(2,1)}), bf16[16,512,128]{2,0,1:T(8,128)(2,1)S(1)}, u32[]{:S(2)}, u32[]{:S(2)}) async-start(bf16[16,512,128]{2,0,1:T(8,128)(2,1)} %copy.182), calls=%async_computation.5 | async-start | bytes 4194304 | tf_op jit(solution)/shard_map/all_to_all | solution.py:302
  194.9 1.8 slice_reduce_fusion
  197.1 1.3 slice_bitcast_fusion.2
  198.4 1.7 slice_bitcast_fusion.1
  200.5 2.1 collective-permute-start.2
  202.6 4.6 %collective-permute-start.3 = (bf16[2,128,256]{2,1,0:T(8,128)(2,1)S(1)}, bf16[2,128,256]{2,1,0:T(8,128)(2,1)S(1)}, u32[]{:S(2)}, u32[]{:S(2)}) collective-permute-start(bf16[2,128,256]{2,1,0:T(8,128)(2,1)S(1)} %get-tuple-element.82), channel_id=1, source_target_pairs={{4,0},{8,4},{12,8},{16,12},{20,16},{24,20},{28,24},{5,1},{9,5},{13... | collective-permute-start | bytes 393224 | tf_op jit(solution)/shard_map/ppermute | solution.py:133
  207.2 2.1 fusion.7
  209.4 1.0 fusion.4
  210.5 2.8 constant_dynamic-slice_fusion
  213.7 2.7 copy.180
  216.4 1.0 bitcast_dynamic-update-slice_fusion.7
  217.4 2.1 collective-permute-start.9
  219.5 0.7 collective-permute-start.10
  220.4 0.9 fusion.22
  221.4 0.9 collective-permute-done.7
  222.3 1.7 collective-permute-start.12
  224.0 0.9 bitcast_dynamic-update-slice_fusion.6
  224.9 2.9 collective-permute-start.13
  227.8 15.9 %all-to-all-done.5 = bf16[16,512,128]{2,0,1:T(8,128)(2,1)S(1)} async-done(((bf16[16,512,128]{2,0,1:T(8,128)(2,1)}), bf16[16,512,128]{2,0,1:T(8,128)(2,1)S(1)}, u32[]{:S(2)}, u32[]{:S(2)}) %all-to-all-start.5) | async-done | bytes 2097184 | tf_op jit(solution)/shard_map/all_to_all | solution.py:302
  243.7 4.7 %all-to-all-start.4 = ((bf16[16,512,128]{2,0,1:T(8,128)(2,1)}), bf16[16,512,128]{2,0,1:T(8,128)(2,1)}, u32[]{:S(2)}, u32[]{:S(2)}) async-start(bf16[16,512,128]{2,0,1:T(8,128)(2,1)} %copy.180), calls=%async_computation.4 | async-start | bytes 4194304 | tf_op jit(solution)/shard_map/all_to_all | solution.py:301
  248.4 0.9 bitcast_dynamic-update-slice_fusion.5
  249.5 0.9 bitcast_dynamic-update-slice_fusion.4
  250.4 1.8 bitcast_dynamic-update-slice_fusion.3
  252.2 1.8 bitcast_dynamic-update-slice_fusion.2
  254.0 1.8 bitcast_dynamic-update-slice_fusion.1
  255.9 1.8 bitcast_dynamic-update-slice_fusion
  257.7 7.3 %gather_fusion.2 = bf16[8,2,2,128,256]{4,1,3,2,0:T(2,128)(2,1)} fusion(bf16[8,2,2,128,256]{4,1,3,2,0:T(2,128)(2,1)} %bitcast_dynamic-update-slice_fusion, s32[1024]{0:T(1024)S(1)} %pad_clamp_fusion), kind=kCustom, calls=%fused_computation.2 | custom fusion | bytes 4194336 | tf_op jit(solution)/shard_map/jit(_take)/gather | solution.py:117
  265.1 2.3 collective-permute-start.6
  267.4 3.5 %broadcast_select_fusion = bf16[8,2,2,128,256]{4,1,3,2,0:T(2,128)(2,1)S(1)} fusion(bf16[8,2,2,128,256]{4,1,3,2,0:T(2,128)(2,1)} %gather_fusion.2, pred[8]{0:T(512)(128)(4,1)S(1)} %compare_and_fusion.2), kind=kLoop, calls=%fused_computation.4 | loop fusion | flops 1048576 | bytes 4194312 | tf_op jit(solution)/shard_map/jit(_take)/select_n | solution.py:117
  270.9 1.3 fusion.8
  272.2 1.4 collective-permute-done.6
  274.4 2.0 copy.183
  276.4 19.9 %all-to-all-done.4 = bf16[16,512,128]{2,0,1:T(8,128)(2,1)} async-done(((bf16[16,512,128]{2,0,1:T(8,128)(2,1)}), bf16[16,512,128]{2,0,1:T(8,128)(2,1)}, u32[]{:S(2)}, u32[]{:S(2)}) %all-to-all-start.4) | async-done | bytes 2097184 | tf_op jit(solution)/shard_map/all_to_all | solution.py:301
  296.3 3.6 %copy.181 = bf16[4,16,128,128]{3,1,0,2:T(8,128)(2,1)} copy(bf16[4,16,128,128]{3,1,2,0:T(8,128)(2,1)} %bitcast.38) | data formatting | bytes 4194304 | tf_op jit(solution)/shard_map/all_to_all | solution.py:301
  300.4 16.4 %all_to_all.114 = bf16[2,512,2,128]{3,2,0,1:T(2,128)(2,1)S(1)} all-to-all(bf16[2,512,2,128]{3,2,0,1:T(2,128)(2,1)S(1)} %copy.199), channel_id=1, replica_groups=mesh['seq'=8,'head'=4] {'head'}, dimensions={1} | all-to-all | bytes 1048576 | tf_op jit(solution)/shard_map/all_to_all | solution.py:305
  317.0 0.9 copy.203
  317.9 0.9 copy.204
  (96 shorter events, 7.6 us)
Async XLA Ops:
  8.9 13.8 %all-to-all-start.1 = ((bf16[128,8,128]{2,0,1:T(8,128)(2,1)}), bf16[128,8,128]{2,0,1:T(8,128)(2,1)S(1)}, u32[]{:S(2)}, u32[]{:S(2)}) async-start(bf16[128,8,128]{2,0,1:T(8,128)(2,1)} %copy.167), calls=%async_computation.1 | async-start | bytes 524288 | tf_op jit(solution)/shard_map/all_to_all | solution.py:159
  22.6 10.4 %all-to-all-start.2 = ((bf16[128,8,128]{2,0,1:T(8,128)(2,1)}), bf16[128,8,128]{2,0,1:T(8,128)(2,1)S(1)}, u32[]{:S(2)}, u32[]{:S(2)}) async-start(bf16[128,8,128]{2,0,1:T(8,128)(2,1)} %copy.169), calls=%async_computation.2 | async-start | bytes 524288 | tf_op jit(solution)/shard_map/all_to_all | solution.py:160
  26.1 63.3 %all-gather.2.cloned.1.call-start = ((), (), s32[]{:S(2)}) async-start(), calls=%async_computation.7 | async-start | bytes 4718592 | tf_op jit(solution)/shard_map/all_gather | solution.py:209
  33.5 0.8 copy-start
  38.6 3.8 %copy-start.6 = (s32[32,3]{0,1:T(4,128)S(1)}, s32[32,3]{0,1:T(4,128)}, u32[]{:S(2)}) copy-start(s32[32,3]{0,1:T(4,128)} %param.15) | copy-start | bytes 1156
  38.6 4.6 %copy-start.7 = (s32[2]{0:T(128)S(1)}, s32[2]{0:T(128)}, u32[]{:S(2)}) copy-start(s32[2]{0:T(128)} %param.14) | copy-start | bytes 28
  38.6 49.2 %all-to-all-start = ((bf16[64,128,128]{2,1,0:T(8,128)(2,1)}), bf16[64,128,128]{2,1,0:T(8,128)(2,1)S(1)}, u32[]{:S(2)}, u32[]{:S(2)}) async-start(bf16[64,128,128]{2,1,0:T(8,128)(2,1)} %bitcast.142), calls=%async_computation | async-start | bytes 4194304 | tf_op jit(solution)/shard_map/all_to_all | solution.py:158
  93.7 4.7 %copy-start.1 = (bf16[2,512,256]{2,1,0:T(8,128)(2,1)S(1)}, bf16[2,512,256]{2,1,0:T(8,128)(2,1)}, u32[]{:S(2)}) copy-start(bf16[2,512,256]{2,1,0:T(8,128)(2,1)} %copy-done) | copy-start | bytes 1572868
  93.7 52.4 %all-to-all-start.3 = ((bf16[64,128,128]{2,1,0:T(8,128)(2,1)}), bf16[64,128,128]{2,1,0:T(8,128)(2,1)}, u32[]{:S(2)}, u32[]{:S(2)}) async-start(bf16[64,128,128]{2,1,0:T(8,128)(2,1)} %bitcast.140), calls=%async_computation.3 | async-start | bytes 4194304 | tf_op jit(solution)/shard_map/all_to_all | solution.py:211
  98.4 7.2 %collective-permute-start = (bf16[2,128,256]{2,1,0:T(8,128)(2,1)S(1)}, bf16[2,128,256]{2,1,0:T(8,128)(2,1)S(1)}, u32[]{:S(2)}, u32[]{:S(2)}) collective-permute-start(bf16[2,128,256]{2,1,0:T(8,128)(2,1)S(1)} %get-tuple-element.89), channel_id=1, source_target_pairs={{0,4},{4,8},{8,12},{12,16},{16,20},{20,24},{24,28},{1,5},{5,9},{9,... | collective-permute-start | bytes 393224 | tf_op jit(solution)/shard_map/ppermute | solution.py:132
  100.4 7.0 %collective-permute-start.1 = (bf16[2,128,256]{2,1,0:T(8,128)(2,1)S(1)}, bf16[2,128,256]{2,1,0:T(8,128)(2,1)S(1)}, u32[]{:S(2)}, u32[]{:S(2)}) collective-permute-start(bf16[2,128,256]{2,1,0:T(8,128)(2,1)S(1)} %get-tuple-element.90), channel_id=1, source_target_pairs={{4,0},{8,4},{12,8},{16,12},{20,16},{24,20},{28,24},{5,1},{9,5},{13... | collective-permute-start | bytes 393224 | tf_op jit(solution)/shard_map/ppermute | solution.py:133
  114.3 1.0 copy-start.5
  191.1 52.6 %all-to-all-start.5 = ((bf16[16,512,128]{2,0,1:T(8,128)(2,1)}), bf16[16,512,128]{2,0,1:T(8,128)(2,1)S(1)}, u32[]{:S(2)}, u32[]{:S(2)}) async-start(bf16[16,512,128]{2,0,1:T(8,128)(2,1)} %copy.182), calls=%async_computation.5 | async-start | bytes 4194304 | tf_op jit(solution)/shard_map/all_to_all | solution.py:302
  196.7 23.7 %collective-permute-start.4 = (bf16[2,2,128,256]{3,2,1,0:T(8,128)(2,1)S(1)}, bf16[2,2,128,256]{3,2,1,0:T(8,128)(2,1)S(1)}, u32[]{:S(2)}, u32[]{:S(2)}) collective-permute-start(bf16[2,2,128,256]{3,2,1,0:T(8,128)(2,1)S(1)} %convert_element_type.65), channel_id=1, source_target_pairs={{0,4},{4,0},{8,12},{12,8},{16,20},{20,16},{24,28},{28,24},{1,5},{5... | collective-permute-start | bytes 786440 | tf_op jit(solution)/shard_map/ppermute | solution.py:150
  200.5 16.9 %collective-permute-start.2 = (bf16[2,128,256]{2,1,0:T(8,128)(2,1)S(1)}, bf16[2,128,256]{2,1,0:T(8,128)(2,1)S(1)}, u32[]{:S(2)}, u32[]{:S(2)}) collective-permute-start(bf16[2,128,256]{2,1,0:T(8,128)(2,1)S(1)} %get-tuple-element.81), channel_id=1, source_target_pairs={{0,4},{4,8},{8,12},{12,16},{16,20},{20,24},{24,28},{1,5},{5,9},{9,... | collective-permute-start | bytes 393224 | tf_op jit(solution)/shard_map/ppermute | solution.py:132
  202.6 16.9 %collective-permute-start.3 = (bf16[2,128,256]{2,1,0:T(8,128)(2,1)S(1)}, bf16[2,128,256]{2,1,0:T(8,128)(2,1)S(1)}, u32[]{:S(2)}, u32[]{:S(2)}) collective-permute-start(bf16[2,128,256]{2,1,0:T(8,128)(2,1)S(1)} %get-tuple-element.82), channel_id=1, source_target_pairs={{4,0},{8,4},{12,8},{16,12},{20,16},{24,20},{28,24},{5,1},{9,5},{13... | collective-permute-start | bytes 393224 | tf_op jit(solution)/shard_map/ppermute | solution.py:133
  210.5 3.3 %copy-start.4 = (bf16[2,8,4,128,128]{4,3,2,1,0:T(8,128)(2,1)S(1)}, bf16[2,8,4,128,128]{4,3,2,1,0:T(8,128)(2,1)}, u32[]{:S(2)}) copy-start(bf16[2,8,4,128,128]{4,3,2,1,0:T(8,128)(2,1)} %shard_map.93.o_ref) | copy-start | bytes 6291460
  213.3 9.0 %collective-permute-start.7 = (bf16[2,2,128,256]{3,0,2,1:T(2,128)(2,1)S(1)}, bf16[2,2,128,256]{3,0,2,1:T(2,128)(2,1)S(1)}, u32[]{:S(2)}, u32[]{:S(2)}) collective-permute-start(bf16[2,2,128,256]{3,0,2,1:T(2,128)(2,1)S(1)} %get-tuple-element.76), channel_id=1, source_target_pairs={{0,4},{4,8},{8,12},{12,16},{16,20},{20,24},{24,28},{28,0},{1,5},{5... | collective-permute-start | bytes 786440 | tf_op jit(solution)/shard_map/ppermute | solution.py:114
  213.4 11.5 %collective-permute-start.8 = (bf16[2,2,128,256]{3,0,2,1:T(2,128)(2,1)S(1)}, bf16[2,2,128,256]{3,0,2,1:T(2,128)(2,1)S(1)}, u32[]{:S(2)}, u32[]{:S(2)}) collective-permute-start(bf16[2,2,128,256]{3,0,2,1:T(2,128)(2,1)S(1)} %get-tuple-element.75), channel_id=1, source_target_pairs={{0,8},{4,12},{8,16},{12,20},{16,24},{20,28},{24,0},{28,4},{1,9},{5... | collective-permute-start | bytes 786440 | tf_op jit(solution)/shard_map/ppermute | solution.py:114
  217.4 31.9 %collective-permute-start.9 = (bf16[2,2,128,256]{3,0,2,1:T(2,128)(2,1)}, bf16[2,2,128,256]{3,0,2,1:T(2,128)(2,1)S(1)}, u32[]{:S(2)}, u32[]{:S(2)}) collective-permute-start(bf16[2,2,128,256]{3,0,2,1:T(2,128)(2,1)} %get-tuple-element.74), channel_id=1, source_target_pairs={{0,12},{4,16},{8,20},{12,24},{16,28},{20,0},{24,4},{28,8},{1,13},{... | collective-permute-start | bytes 786440 | tf_op jit(solution)/shard_map/ppermute | solution.py:114
  219.5 30.9 %collective-permute-start.10 = (bf16[2,2,128,256]{3,0,2,1:T(2,128)(2,1)}, bf16[2,2,128,256]{3,0,2,1:T(2,128)(2,1)}, u32[]{:S(2)}, u32[]{:S(2)}) collective-permute-start(bf16[2,2,128,256]{3,0,2,1:T(2,128)(2,1)} %get-tuple-element.73), channel_id=1, source_target_pairs={{0,16},{4,20},{8,24},{12,28},{16,0},{20,4},{24,8},{28,12},{1,17},{... | collective-permute-start | bytes 786440 | tf_op jit(solution)/shard_map/ppermute | solution.py:114
  220.4 4.5 %copy-start.2 = (f32[4,2,128,256]{3,2,1,0:T(8,128)}, f32[4,2,128,256]{3,2,1,0:T(8,128)S(1)}, u32[]{:S(2)}) copy-start(f32[4,2,128,256]{3,2,1,0:T(8,128)S(1)} %fusion.23) | copy-start | bytes 3145732
  220.4 31.8 %collective-permute-start.11 = (bf16[2,2,128,256]{3,0,2,1:T(2,128)(2,1)}, bf16[2,2,128,256]{3,0,2,1:T(2,128)(2,1)}, u32[]{:S(2)}, u32[]{:S(2)}) collective-permute-start(bf16[2,2,128,256]{3,0,2,1:T(2,128)(2,1)} %get-tuple-element.72), channel_id=1, source_target_pairs={{0,20},{4,24},{8,28},{12,0},{16,4},{20,8},{24,12},{28,16},{1,21},{... | collective-permute-start | bytes 786440 | tf_op jit(solution)/shard_map/ppermute | solution.py:114
  222.3 31.7 %collective-permute-start.12 = (bf16[2,2,128,256]{3,0,2,1:T(2,128)(2,1)}, bf16[2,2,128,256]{3,0,2,1:T(2,128)(2,1)}, u32[]{:S(2)}, u32[]{:S(2)}) collective-permute-start(bf16[2,2,128,256]{3,0,2,1:T(2,128)(2,1)} %get-tuple-element.71), channel_id=1, source_target_pairs={{0,24},{4,28},{8,0},{12,4},{16,8},{20,12},{24,16},{28,20},{1,25},{... | collective-permute-start | bytes 786440 | tf_op jit(solution)/shard_map/ppermute | solution.py:114
  224.9 31.0 %collective-permute-start.13 = (bf16[2,2,128,256]{3,0,2,1:T(2,128)(2,1)}, bf16[2,2,128,256]{3,0,2,1:T(2,128)(2,1)}, u32[]{:S(2)}, u32[]{:S(2)}) collective-permute-start(bf16[2,2,128,256]{3,0,2,1:T(2,128)(2,1)} %get-tuple-element.70), channel_id=1, source_target_pairs={{0,28},{4,0},{8,4},{12,8},{16,12},{20,16},{24,20},{28,24},{1,29},{... | collective-permute-start | bytes 786440 | tf_op jit(solution)/shard_map/ppermute | solution.py:114
  243.7 52.6 %all-to-all-start.4 = ((bf16[16,512,128]{2,0,1:T(8,128)(2,1)}), bf16[16,512,128]{2,0,1:T(8,128)(2,1)}, u32[]{:S(2)}, u32[]{:S(2)}) async-start(bf16[16,512,128]{2,0,1:T(8,128)(2,1)} %copy.180), calls=%async_computation.4 | async-start | bytes 4194304 | tf_op jit(solution)/shard_map/all_to_all | solution.py:301
  249.3 15.8 %collective-permute-start.5 = (bf16[2,2,128,256]{3,2,1,0:T(8,128)(2,1)}, bf16[2,2,128,256]{3,2,1,0:T(8,128)(2,1)S(1)}, u32[]{:S(2)}, u32[]{:S(2)}) collective-permute-start(bf16[2,2,128,256]{3,2,1,0:T(8,128)(2,1)} %fusion.22), channel_id=1, source_target_pairs={{0,8},{4,12},{8,0},{12,4},{16,24},{20,28},{24,16},{28,20},{1,9},{5... | collective-permute-start | bytes 786440 | tf_op jit(solution)/shard_map/ppermute | solution.py:150
  265.1 8.5 %collective-permute-start.6 = (bf16[2,2,128,256]{3,2,1,0:T(8,128)(2,1)S(1)}, bf16[2,2,128,256]{3,2,1,0:T(8,128)(2,1)S(1)}, u32[]{:S(2)}, u32[]{:S(2)}) collective-permute-start(bf16[2,2,128,256]{3,2,1,0:T(8,128)(2,1)S(1)} %fusion.26), channel_id=1, source_target_pairs={{0,16},{4,20},{8,24},{12,28},{16,0},{20,4},{24,8},{28,12},{1,17},{... | collective-permute-start | bytes 786440 | tf_op jit(solution)/shard_map/ppermute | solution.py:150
  272.2 1.8 copy-start.3
Sparse Core Ops, SparseCore 0:
  34.5 35.9 all-gather.1

commit v11 on v10

--- a/solution.py
+++ b/solution.py
@@ -65,6 +65,8 @@
     tile_count = tiles.shape[1]
     rows_width = group * head_width
     q_spec = pl.BlockSpec((None, group, None, tokens, head_width), lambda j, h: (h, 0, j, 0, 0))
+    o_spec = pl.BlockSpec((None, None, group, tokens, head_width), lambda j, h: (j, h, 0, 0, 0))
+    o_shape = jax.ShapeDtypeStruct((blocks, heads_kv, group, tokens, head_width), jnp.bfloat16)
     k_spec = pl.BlockSpec((None, tile_count, None, tokens, head_width), lambda j, h: (j, 0, 0, 0, h))
     v_spec = pl.BlockSpec((None, tile_count, None, tokens, head_width), lambda j, h: (j, 0, 1, 0, h))
     b_spec = pl.BlockSpec((None, 1, bias.shape[-1]), lambda j, h: (j, 0, 0))
@@ -81,8 +83,8 @@
         ),
         grid=(blocks, heads_kv),
         in_specs=[q_spec, k_spec, v_spec, b_spec],
-        out_specs=q_spec,
-        out_shape=jax.ShapeDtypeStruct(q.shape, jnp.bfloat16),
+        out_specs=o_spec,
+        out_shape=o_shape,
     )(q, tiles, tiles, bias)
     out, do = lax.optimization_barrier((out, do))
     grad_q, grads = pl.pallas_call(
@@ -91,10 +93,10 @@
             flops=5 * matmul, transcendentals=rows * keys_n * steps, bytes_accessed=moved
         ),
         grid=(blocks, heads_kv),
-        in_specs=[q_spec, k_spec, v_spec, q_spec, q_spec, b_spec],
-        out_specs=[q_spec, g_spec],
+        in_specs=[q_spec, k_spec, v_spec, q_spec, o_spec, b_spec],
+        out_specs=[o_spec, g_spec],
         out_shape=[
-            jax.ShapeDtypeStruct(q.shape, jnp.bfloat16),
+            o_shape,
             jax.ShapeDtypeStruct(tiles.shape, jnp.float32),
         ],
     )(q, tiles, tiles, do, out, bias)
@@ -207,8 +209,9 @@
         preferred_element_type=jnp.float32,
     ).astype(jnp.bfloat16)
     everything = lax.all_gather(kv_pair, "seq", axis=1, tiled=True)
+    grad_loc = grad_loc.transpose(1, 0, 2)
     query_loc, everything, grad_loc = lax.optimization_barrier((query_loc, everything, grad_loc))
-    grad_loc = lax.all_to_all(grad_loc.transpose(1, 0, 2), "head", split_axis=0, concat_axis=1, tiled=True)
+    grad_loc = lax.all_to_all(grad_loc, "head", split_axis=0, concat_axis=1, tiled=True)
     tiled_all = everything.reshape(2, block_total_count, BLOCK_TOKENS, kv_width)
     random_tiles = jnp.take(tiled_all, my_entries, axis=1).transpose(1, 0, 2, 3)
     global_tiles = jnp.take(tiled_all, global_blocks, axis=1).transpose(1, 0, 2, 3)
@@ -294,16 +297,18 @@
         preferred_element_type=jnp.float32,
     )
     kv_grad = interior.transpose(1, 0, 2, 3).reshape(2, shard_len, kv_width).astype(jnp.bfloat16)
-    out_all = out_q.reshape(heads_q, shard_len, head_width)
-    query_grad_all = grad_q.reshape(heads_q, shard_len, head_width)
+    out_all = out_q.reshape(blocks, heads_q, BLOCK_TOKENS, head_width)
+    query_grad_all = grad_q.reshape(blocks, heads_q, BLOCK_TOKENS, head_width)
     key_grad_all = kv_grad[0].reshape(shard_len, heads_kv, head_width)
     value_grad_all = kv_grad[1].reshape(shard_len, heads_kv, head_width)
-    out_back = lax.all_to_all(out_all, "head", split_axis=1, concat_axis=0, tiled=True)
-    query_back = lax.all_to_all(query_grad_all, "head", split_axis=1, concat_axis=0, tiled=True)
+    out_back = lax.all_to_all(out_all, "head", split_axis=0, concat_axis=1, tiled=True)
+    query_back = lax.all_to_all(query_grad_all, "head", split_axis=0, concat_axis=1, tiled=True)
     (out_back, query_back), kv_grad = lax.optimization_barrier(((out_back, query_back), kv_grad))
     kv_grad = kv_grad.reshape(2, shard_len, heads_kv, head_width)
     kv_back = lax.all_to_all(kv_grad, "head", split_axis=1, concat_axis=2, tiled=True)
-    return (out_back.transpose(1, 0, 2), query_back.transpose(1, 0, 2), kv_back[0], kv_back[1])
+    out_back = out_back.reshape(-1, BLOCK_TOKENS, head_width).transpose(1, 0, 2)
+    query_back = query_back.reshape(-1, BLOCK_TOKENS, head_width).transpose(1, 0, 2)
+    return (out_back, query_back, kv_back[0], kv_back[1])
 
 
 def solution(mesh):

time: 329 us -> 322 us (0.979)
  other arithmetic: 11.3 us -> 15 us
  local copies, waits for them, and re-layouts: 68.7 us -> 65.2 us
  waiting for transfers between devices: 99.8 us -> 96.4 us
    reshape x2 -> x0, local copies, waits for them, and re-layouts: 6.93 us -> none  [the longest x1 4.26 us: per_device(): query_grad_all = grad_q.reshape(heads_q, shard_len, head_width)]
    all_to_all x1, waiting for transfers between devices: 43.7 us -> 38.3 us  [per_device(): lax.all_to_all(queries.transpose(1, 0, 2), 'head', split_axis=0, concat_a...]
    optimization_barrier x1 -> x0, local copies, waits for them, and re-layouts: 4.35 us -> none  [per_device(): lax.optimization_barrier((query_loc, everything, grad_loc))]
    unnamed x29 -> x32, local copies, waits for them, and re-layouts: 20.1 us -> 24.3 us
  transfers between devices with their start and end apart: 21 -> 21, of which waited for: 10 -> 9; matrix products, arithmetic and copies ran while one was open for 19% -> 22% of each run, Pallas kernels for 8% -> 8%
where the time goes in v11:
time: 322 us; the launch traced here: 321 us
  waiting for transfers between devices  96.4 us (30%)
  local copies, waits for them, and re-layouts  65.2 us (20%)
  Pallas kernels  62.8 us (20%)
  starting transfers between devices  47.6 us (15%)
  blocking collectives  16.5 us (5%)
  other arithmetic  15 us (5%)
  between operations  14.7 us (5%)
    all_to_all x1, waiting for transfers between devices, per_device(): lax.all_to_all(queries.transpose(1, 0, 2), 'head', split_axis=0, concat_a...  38.3 us
    pallas_call x1, Pallas kernels, attention_call(): pl.pallas_call(functools.partial(backward_kernel, scale=scale), cost_esti...  37.4 us
    pallas_call x1, Pallas kernels, attention_call(): pl.pallas_call(functools.partial(forward_kernel, scale=scale), cost_estim...  25.3 us
    unnamed x32, local copies, waits for them, and re-layouts  24.3 us
    all_to_all x1, waiting for transfers between devices, per_device(): lax.all_to_all(out_all, 'head', split_axis=0, concat_axis=1, tiled=True)  20.3 us
    all_to_all x1, blocking collectives, per_device(): lax.all_to_all(kv_grad, 'head', split_axis=1, concat_axis=2, tiled=True)  16.5 us
    all_to_all x1, waiting for transfers between devices, per_device(): lax.all_to_all(query_grad_all, 'head', split_axis=0, concat_axis=1, tiled...  15.2 us
    ppermute x2, starting transfers between devices, padded(): after = lax.ppermute(leading, axis, down)  9.48 us
  transfers between devices with their start and end apart: 21, of which 9 were waited for; matrix products, arithmetic and copies ran while one was open for 22% of the time, Pallas kernels for 8%

profile of v11, /device:TPU:4, one launch (start us, length us, event | category | flops | bytes accessed | tf_op | source)
XLA Modules:
  0.0 320.6 jit_solution(16678083788123404080)
XLA Ops:
  7.2 1.7 copy.163
  8.9 4.9 %all-to-all-start.1 = ((bf16[128,8,128]{2,0,1:T(8,128)(2,1)}), bf16[128,8,128]{2,0,1:T(8,128)(2,1)S(1)}, u32[]{:S(2)}, u32[]{:S(2)}) async-start(bf16[128,8,128]{2,0,1:T(8,128)(2,1)} %copy.163), calls=%async_computation.1 | async-start | bytes 524288 | tf_op jit(solution)/shard_map/all_to_all | solution.py:161
  13.7 1.7 copy.165
  15.4 7.2 %all-to-all-done.1 = bf16[128,8,128]{2,0,1:T(8,128)(2,1)S(1)} async-done(((bf16[128,8,128]{2,0,1:T(8,128)(2,1)}), bf16[128,8,128]{2,0,1:T(8,128)(2,1)S(1)}, u32[]{:S(2)}, u32[]{:S(2)}) %all-to-all-start.1) | async-done | bytes 262176 | tf_op jit(solution)/shard_map/all_to_all | solution.py:161
  22.6 3.4 %all-to-all-start.2 = ((bf16[128,8,128]{2,0,1:T(8,128)(2,1)}), bf16[128,8,128]{2,0,1:T(8,128)(2,1)S(1)}, u32[]{:S(2)}, u32[]{:S(2)}) async-start(bf16[128,8,128]{2,0,1:T(8,128)(2,1)} %copy.165), calls=%async_computation.2 | async-start | bytes 524288 | tf_op jit(solution)/shard_map/all_to_all | solution.py:162
  26.6 6.5 %all-to-all-done.2 = bf16[128,8,128]{2,0,1:T(8,128)(2,1)S(1)} async-done(((bf16[128,8,128]{2,0,1:T(8,128)(2,1)}), bf16[128,8,128]{2,0,1:T(8,128)(2,1)S(1)}, u32[]{:S(2)}, u32[]{:S(2)}) %all-to-all-start.2) | async-done | bytes 262176 | tf_op jit(solution)/shard_map/all_to_all | solution.py:162
  33.5 0.8 copy-done
  34.3 4.3 %copy.231 = bf16[128,64,128]{2,0,1:T(8,128)(2,1)} copy(bf16[128,64,128]{2,1,0:T(8,128)(2,1)} %param.10) | data formatting | bytes 4194304 | tf_op args[0]
  38.6 3.8 %all-to-all-start = ((bf16[64,128,128]{2,1,0:T(8,128)(2,1)}), bf16[64,128,128]{2,1,0:T(8,128)(2,1)S(1)}, u32[]{:S(2)}, u32[]{:S(2)}) async-start(bf16[64,128,128]{2,1,0:T(8,128)(2,1)} %bitcast.139), calls=%async_computation | async-start | bytes 4194304 | tf_op jit(solution)/shard_map/all_to_all | solution.py:160
  42.6 4.4 %copy.230 = bf16[128,64,128]{2,0,1:T(8,128)(2,1)} copy(bf16[128,64,128]{2,1,0:T(8,128)(2,1)} %param.13) | data formatting | bytes 4194304 | tf_op args[3]
  48.8 0.6 and_convert_fusion
  49.4 38.3 %all-to-all-done = bf16[64,128,128]{2,1,0:T(8,128)(2,1)S(1)} async-done(((bf16[64,128,128]{2,1,0:T(8,128)(2,1)}), bf16[64,128,128]{2,1,0:T(8,128)(2,1)S(1)}, u32[]{:S(2)}, u32[]{:S(2)}) %all-to-all-start) | async-done | bytes 2097184 | tf_op jit(solution)/shard_map/all_to_all | solution.py:160
  87.8 1.6 copy.162
  89.4 3.7 %all-to-all-start.3 = ((bf16[64,128,128]{2,1,0:T(8,128)(2,1)}), bf16[64,128,128]{2,1,0:T(8,128)(2,1)S(1)}, u32[]{:S(2)}, u32[]{:S(2)}) async-start(bf16[64,128,128]{2,1,0:T(8,128)(2,1)} %bitcast.131), calls=%async_computation.3 | async-start | bytes 4194304 | tf_op jit(solution)/shard_map/all_to_all | solution.py:214
  93.2 1.9 collective-permute-start
  95.2 4.7 %collective-permute-start.1 = (bf16[2,128,256]{2,1,0:T(8,128)(2,1)S(1)}, bf16[2,128,256]{2,1,0:T(8,128)(2,1)S(1)}, u32[]{:S(2)}, u32[]{:S(2)}) collective-permute-start(bf16[2,128,256]{2,1,0:T(8,128)(2,1)S(1)} %get-tuple-element.90), channel_id=1, source_target_pairs={{4,0},{8,4},{12,8},{16,12},{20,16},{24,20},{28,24},{5,1},{9,5},{13... | collective-permute-start | bytes 393224 | tf_op jit(solution)/shard_map/ppermute | solution.py:135
  100.6 1.7 collective-permute-done.1
  102.4 0.8 copy_bitcast_fusion.5
  103.2 4.0 %gather_fusion.1 = bf16[12,2,128,256]{3,2,1,0:T(8,128)(2,1)} fusion(bf16[2,32,128,256]{3,2,1,0:T(8,128)(2,1)} %bitcast.161, s32[1024]{0:T(1024)S(1)} %get-tuple-element.99), kind=kCustom, calls=%fused_computation.1 | custom fusion | bytes 3145776 | tf_op jit(solution)/shard_map/jit(_take)/gather | solution.py:216
  107.3 1.6 broadcast_select_fusion.1
  108.9 1.2 copy.232
  110.1 2.7 gather_fusion
  112.9 0.8 broadcast_select_fusion.2
  113.7 1.5 slice_bitcast_fusion.6
  115.6 2.3 pad_maximum_fusion.k_ref.v_ref
  117.9 0.7 broadcast_in_dim.79
  118.5 25.3 %shard_map.93.o_ref = bf16[4,2,8,128,128]{4,3,2,1,0:T(8,128)(2,1)} custom-call(bf16[2,8,4,128,128]{4,3,2,1,0:T(8,128)(2,1)} %bitcast.144, bf16[4,8,2,128,256]{4,3,2,1,0:T(8,128)(2,1)} %pad_maximum_fusion.k_ref.v_ref, bf16[4,8,2,128,256]{4,3,2,1,0:T(8,128)(2,1)} %pad_maximum_fusion.k_ref.v_ref, f32[4,1,1024]{2,1,0:T(1,128)} %bitcast.164), custom_call_target="tpu_custom_call" | custom-call | flops 4294967296 | bytes 23068672 | tf_op jit(solution)/shard_map/pallas_call | solution.py:79
  143.9 1.6 copy.175
  145.4 37.4 %shard_map.94 = (bf16[4,2,8,128,128]{4,3,2,1,0:T(8,128)(2,1)}, f32[4,8,2,128,256]{4,3,2,1,0:T(8,128)}) custom-call(bf16[2,8,4,128,128]{4,3,2,1,0:T(8,128)(2,1)} %bitcast.145, bf16[4,8,2,128,256]{4,3,2,1,0:T(8,128)(2,1)} %pad_maximum_fusion.k_ref.v_ref, bf16[4,8,2,128,256]{4,3,2,1,0:T(8,128)(2,1)} %pad_maximum_fusion.k_ref.v_ref, ...), custom_call_target="tpu_custom_call" | custom-call | flops 10737418240 | bytes 23068672 | tf_op jit(solution)/shard_map/pallas_call | solution.py:90
  182.9 5.1 %all-to-all-start.5 = ((bf16[4,16,128,128]{3,2,1,0:T(8,128)(2,1)}), bf16[4,16,128,128]{3,2,1,0:T(8,128)(2,1)S(1)}, u32[]{:S(2)}, u32[]{:S(2)}) async-start(bf16[4,16,128,128]{3,2,1,0:T(8,128)(2,1)} %bitcast.143), calls=%async_computation.5 | async-start | bytes 4194304 | tf_op jit(solution)/shard_map/all_to_all | solution.py:305
  188.0 1.8 slice_reduce_fusion
  189.9 0.9 collective-permute-start.4
  190.8 1.3 slice_bitcast_fusion.2
  192.1 1.7 slice_bitcast_fusion.1
  194.2 1.9 collective-permute-start.2
  196.2 4.8 %collective-permute-start.3 = (bf16[2,128,256]{2,1,0:T(8,128)(2,1)S(1)}, bf16[2,128,256]{2,1,0:T(8,128)(2,1)S(1)}, u32[]{:S(2)}, u32[]{:S(2)}) collective-permute-start(bf16[2,128,256]{2,1,0:T(8,128)(2,1)S(1)} %get-tuple-element.82), channel_id=1, source_target_pairs={{4,0},{8,4},{12,8},{16,12},{20,16},{24,20},{28,24},{5,1},{9,5},{13... | collective-permute-start | bytes 393224 | tf_op jit(solution)/shard_map/ppermute | solution.py:135
  200.9 2.1 fusion.7
  203.7 1.0 fusion.4
  204.7 2.8 constant_dynamic-slice_fusion
  207.7 1.0 bitcast_dynamic-update-slice_fusion.7
  208.7 2.5 collective-permute-start.9
  211.3 0.6 collective-permute-start.10
  212.0 1.0 fusion.22
  213.0 3.6 %collective-permute-done.7 = bf16[2,2,128,256]{3,0,2,1:T(2,128)(2,1)S(1)} collective-permute-done((bf16[2,2,128,256]{3,0,2,1:T(2,128)(2,1)S(1)}, bf16[2,2,128,256]{3,0,2,1:T(2,128)(2,1)S(1)}, u32[]{:S(2)}, u32[]{:S(2)}) %collective-permute-start.7) | collective-permute-done | bytes 262176 | tf_op jit(solution)/shard_map/ppermute | solution.py:116
  216.8 0.9 bitcast_dynamic-update-slice_fusion.6
  217.9 4.3 %collective-permute-start.13 = (bf16[2,2,128,256]{3,0,2,1:T(2,128)(2,1)}, bf16[2,2,128,256]{3,0,2,1:T(2,128)(2,1)}, u32[]{:S(2)}, u32[]{:S(2)}) collective-permute-start(bf16[2,2,128,256]{3,0,2,1:T(2,128)(2,1)} %get-tuple-element.70), channel_id=1, source_target_pairs={{0,28},{4,0},{8,4},{12,8},{16,12},{20,16},{24,20},{28,24},{1,29},{... | collective-permute-start | bytes 786440 | tf_op jit(solution)/shard_map/ppermute | solution.py:116
  222.2 15.2 %all-to-all-done.5 = bf16[4,16,128,128]{3,2,1,0:T(8,128)(2,1)S(1)} async-done(((bf16[4,16,128,128]{3,2,1,0:T(8,128)(2,1)}), bf16[4,16,128,128]{3,2,1,0:T(8,128)(2,1)S(1)}, u32[]{:S(2)}, u32[]{:S(2)}) %all-to-all-start.5) | async-done | bytes 2097184 | tf_op jit(solution)/shard_map/all_to_all | solution.py:305
  237.4 4.5 %all-to-all-start.4 = ((bf16[4,16,128,128]{3,2,1,0:T(8,128)(2,1)}), bf16[4,16,128,128]{3,2,1,0:T(8,128)(2,1)}, u32[]{:S(2)}, u32[]{:S(2)}) async-start(bf16[4,16,128,128]{3,2,1,0:T(8,128)(2,1)} %bitcast.142), calls=%async_computation.4 | async-start | bytes 4194304 | tf_op jit(solution)/shard_map/all_to_all | solution.py:304
  241.9 0.9 bitcast_dynamic-update-slice_fusion.5
  242.8 0.9 bitcast_dynamic-update-slice_fusion.4
  243.6 1.8 bitcast_dynamic-update-slice_fusion.3
  245.5 1.8 bitcast_dynamic-update-slice_fusion.2
  247.3 1.8 bitcast_dynamic-update-slice_fusion.1
  249.2 1.8 bitcast_dynamic-update-slice_fusion
  251.0 7.4 %gather_fusion.2 = bf16[8,2,2,128,256]{4,1,3,2,0:T(2,128)(2,1)} fusion(bf16[8,2,2,128,256]{4,1,3,2,0:T(2,128)(2,1)} %bitcast_dynamic-update-slice_fusion, s32[1024]{0:T(1024)S(1)} %pad_clamp_fusion), kind=kCustom, calls=%fused_computation.2 | custom fusion | bytes 4194336 | tf_op jit(solution)/shard_map/jit(_take)/gather | solution.py:119
  258.7 3.5 %broadcast_select_fusion = bf16[8,2,2,128,256]{4,1,3,2,0:T(2,128)(2,1)S(1)} fusion(bf16[8,2,2,128,256]{4,1,3,2,0:T(2,128)(2,1)} %gather_fusion.2, pred[8]{0:T(512)(128)(4,1)S(1)} %compare_and_fusion.2), kind=kLoop, calls=%fused_computation.4 | loop fusion | flops 1048576 | bytes 4194312 | tf_op jit(solution)/shard_map/jit(_take)/select_n | solution.py:119
  262.2 1.3 fusion.8
  263.5 3.2 %collective-permute-done.6 = bf16[2,2,128,256]{3,2,1,0:T(8,128)(2,1)S(1)} collective-permute-done((bf16[2,2,128,256]{3,2,1,0:T(8,128)(2,1)S(1)}, bf16[2,2,128,256]{3,2,1,0:T(8,128)(2,1)S(1)}, u32[]{:S(2)}, u32[]{:S(2)}) %collective-permute-start.6) | collective-permute-done | bytes 262176 | tf_op jit(solution)/shard_map/ppermute | solution.py:152
  267.5 2.7 copy.177
  270.2 20.3 %all-to-all-done.4 = bf16[4,16,128,128]{3,2,1,0:T(8,128)(2,1)} async-done(((bf16[4,16,128,128]{3,2,1,0:T(8,128)(2,1)}), bf16[4,16,128,128]{3,2,1,0:T(8,128)(2,1)}, u32[]{:S(2)}, u32[]{:S(2)}) %all-to-all-start.4) | async-done | bytes 2097184 | tf_op jit(solution)/shard_map/all_to_all | solution.py:304
  290.6 4.3 %copy.176 = bf16[4,16,128,128]{3,1,0,2:T(8,128)(2,1)} copy(bf16[4,16,128,128]{3,2,1,0:T(8,128)(2,1)} %all-to-all-done.4) | data formatting | bytes 4194304 | tf_op jit(solution)/shard_map/all_to_all | solution.py:304
  295.3 16.5 %all_to_all.102 = bf16[2,512,2,128]{3,2,0,1:T(2,128)(2,1)S(1)} all-to-all(bf16[2,512,2,128]{3,2,0,1:T(2,128)(2,1)S(1)} %copy.193), channel_id=1, replica_groups=mesh['seq'=8,'head'=4] {'head'}, dimensions={1} | all-to-all | bytes 1048576 | tf_op jit(solution)/shard_map/all_to_all | solution.py:308
  311.9 0.9 copy.197
  312.8 0.9 copy.198
  (96 shorter events, 8.0 us)
Async XLA Ops:
  8.9 13.8 %all-to-all-start.1 = ((bf16[128,8,128]{2,0,1:T(8,128)(2,1)}), bf16[128,8,128]{2,0,1:T(8,128)(2,1)S(1)}, u32[]{:S(2)}, u32[]{:S(2)}) async-start(bf16[128,8,128]{2,0,1:T(8,128)(2,1)} %copy.163), calls=%async_computation.1 | async-start | bytes 524288 | tf_op jit(solution)/shard_map/all_to_all | solution.py:161
  22.6 10.4 %all-to-all-start.2 = ((bf16[128,8,128]{2,0,1:T(8,128)(2,1)}), bf16[128,8,128]{2,0,1:T(8,128)(2,1)S(1)}, u32[]{:S(2)}, u32[]{:S(2)}) async-start(bf16[128,8,128]{2,0,1:T(8,128)(2,1)} %copy.165), calls=%async_computation.2 | async-start | bytes 524288 | tf_op jit(solution)/shard_map/all_to_all | solution.py:162
  26.1 63.3 %all-gather.2.cloned.1.call-start = ((), (), s32[]{:S(2)}) async-start(), calls=%async_computation.7 | async-start | bytes 4718592 | tf_op jit(solution)/shard_map/all_gather | solution.py:211
  33.5 0.8 copy-start
  38.6 3.8 %copy-start.7 = (s32[32,3]{0,1:T(4,128)S(1)}, s32[32,3]{0,1:T(4,128)}, u32[]{:S(2)}) copy-start(s32[32,3]{0,1:T(4,128)} %param.15) | copy-start | bytes 1156
  38.6 49.2 %all-to-all-start = ((bf16[64,128,128]{2,1,0:T(8,128)(2,1)}), bf16[64,128,128]{2,1,0:T(8,128)(2,1)S(1)}, u32[]{:S(2)}, u32[]{:S(2)}) async-start(bf16[64,128,128]{2,1,0:T(8,128)(2,1)} %bitcast.139), calls=%async_computation | async-start | bytes 4194304 | tf_op jit(solution)/shard_map/all_to_all | solution.py:160
  42.6 4.9 %copy-start.8 = (s32[2]{0:T(128)S(1)}, s32[2]{0:T(128)}, u32[]{:S(2)}) copy-start(s32[2]{0:T(128)} %param.14) | copy-start | bytes 28
  89.4 3.8 %copy-start.1 = (bf16[2,512,256]{2,1,0:T(8,128)(2,1)S(1)}, bf16[2,512,256]{2,1,0:T(8,128)(2,1)}, u32[]{:S(2)}) copy-start(bf16[2,512,256]{2,1,0:T(8,128)(2,1)} %copy-done) | copy-start | bytes 1572868
  89.4 54.5 %all-to-all-start.3 = ((bf16[64,128,128]{2,1,0:T(8,128)(2,1)}), bf16[64,128,128]{2,1,0:T(8,128)(2,1)S(1)}, u32[]{:S(2)}, u32[]{:S(2)}) async-start(bf16[64,128,128]{2,1,0:T(8,128)(2,1)} %bitcast.131), calls=%async_computation.3 | async-start | bytes 4194304 | tf_op jit(solution)/shard_map/all_to_all | solution.py:214
  93.2 7.3 %collective-permute-start = (bf16[2,128,256]{2,1,0:T(8,128)(2,1)S(1)}, bf16[2,128,256]{2,1,0:T(8,128)(2,1)S(1)}, u32[]{:S(2)}, u32[]{:S(2)}) collective-permute-start(bf16[2,128,256]{2,1,0:T(8,128)(2,1)S(1)} %get-tuple-element.89), channel_id=1, source_target_pairs={{0,4},{4,8},{8,12},{12,16},{16,20},{20,24},{24,28},{1,5},{5,9},{9,... | collective-permute-start | bytes 393224 | tf_op jit(solution)/shard_map/ppermute | solution.py:134
  95.2 7.0 %collective-permute-start.1 = (bf16[2,128,256]{2,1,0:T(8,128)(2,1)S(1)}, bf16[2,128,256]{2,1,0:T(8,128)(2,1)S(1)}, u32[]{:S(2)}, u32[]{:S(2)}) collective-permute-start(bf16[2,128,256]{2,1,0:T(8,128)(2,1)S(1)} %get-tuple-element.90), channel_id=1, source_target_pairs={{4,0},{8,4},{12,8},{16,12},{20,16},{24,20},{28,24},{5,1},{9,5},{13... | collective-permute-start | bytes 393224 | tf_op jit(solution)/shard_map/ppermute | solution.py:135
  112.9 2.3 copy-start.4
  182.9 54.5 %all-to-all-start.5 = ((bf16[4,16,128,128]{3,2,1,0:T(8,128)(2,1)}), bf16[4,16,128,128]{3,2,1,0:T(8,128)(2,1)S(1)}, u32[]{:S(2)}, u32[]{:S(2)}) async-start(bf16[4,16,128,128]{3,2,1,0:T(8,128)(2,1)} %bitcast.143), calls=%async_computation.5 | async-start | bytes 4194304 | tf_op jit(solution)/shard_map/all_to_all | solution.py:305
  189.9 22.1 %collective-permute-start.4 = (bf16[2,2,128,256]{3,2,1,0:T(8,128)(2,1)S(1)}, bf16[2,2,128,256]{3,2,1,0:T(8,128)(2,1)S(1)}, u32[]{:S(2)}, u32[]{:S(2)}) collective-permute-start(bf16[2,2,128,256]{3,2,1,0:T(8,128)(2,1)S(1)} %convert_element_type.65), channel_id=1, source_target_pairs={{0,4},{4,0},{8,12},{12,8},{16,20},{20,16},{24,28},{28,24},{1,5},{5... | collective-permute-start | bytes 786440 | tf_op jit(solution)/shard_map/ppermute | solution.py:152
  194.2 14.5 %collective-permute-start.2 = (bf16[2,128,256]{2,1,0:T(8,128)(2,1)S(1)}, bf16[2,128,256]{2,1,0:T(8,128)(2,1)S(1)}, u32[]{:S(2)}, u32[]{:S(2)}) collective-permute-start(bf16[2,128,256]{2,1,0:T(8,128)(2,1)S(1)} %get-tuple-element.81), channel_id=1, source_target_pairs={{0,4},{4,8},{8,12},{12,16},{16,20},{20,24},{24,28},{1,5},{5,9},{9,... | collective-permute-start | bytes 393224 | tf_op jit(solution)/shard_map/ppermute | solution.py:134
  196.2 15.1 %collective-permute-start.3 = (bf16[2,128,256]{2,1,0:T(8,128)(2,1)S(1)}, bf16[2,128,256]{2,1,0:T(8,128)(2,1)S(1)}, u32[]{:S(2)}, u32[]{:S(2)}) collective-permute-start(bf16[2,128,256]{2,1,0:T(8,128)(2,1)S(1)} %get-tuple-element.82), channel_id=1, source_target_pairs={{4,0},{8,4},{12,8},{16,12},{20,16},{24,20},{28,24},{5,1},{9,5},{13... | collective-permute-start | bytes 393224 | tf_op jit(solution)/shard_map/ppermute | solution.py:135
  203.0 0.7 copy-start.6
  207.6 9.0 %collective-permute-start.7 = (bf16[2,2,128,256]{3,0,2,1:T(2,128)(2,1)S(1)}, bf16[2,2,128,256]{3,0,2,1:T(2,128)(2,1)S(1)}, u32[]{:S(2)}, u32[]{:S(2)}) collective-permute-start(bf16[2,2,128,256]{3,0,2,1:T(2,128)(2,1)S(1)} %get-tuple-element.76), channel_id=1, source_target_pairs={{0,4},{4,8},{8,12},{12,16},{16,20},{20,24},{24,28},{28,0},{1,5},{5... | collective-permute-start | bytes 786440 | tf_op jit(solution)/shard_map/ppermute | solution.py:116
  207.7 10.2 %collective-permute-start.8 = (bf16[2,2,128,256]{3,0,2,1:T(2,128)(2,1)S(1)}, bf16[2,2,128,256]{3,0,2,1:T(2,128)(2,1)S(1)}, u32[]{:S(2)}, u32[]{:S(2)}) collective-permute-start(bf16[2,2,128,256]{3,0,2,1:T(2,128)(2,1)S(1)} %get-tuple-element.75), channel_id=1, source_target_pairs={{0,8},{4,12},{8,16},{12,20},{16,24},{20,28},{24,0},{28,4},{1,9},{5... | collective-permute-start | bytes 786440 | tf_op jit(solution)/shard_map/ppermute | solution.py:116
  208.7 34.0 %collective-permute-start.9 = (bf16[2,2,128,256]{3,0,2,1:T(2,128)(2,1)}, bf16[2,2,128,256]{3,0,2,1:T(2,128)(2,1)S(1)}, u32[]{:S(2)}, u32[]{:S(2)}) collective-permute-start(bf16[2,2,128,256]{3,0,2,1:T(2,128)(2,1)} %get-tuple-element.74), channel_id=1, source_target_pairs={{0,12},{4,16},{8,20},{12,24},{16,28},{20,0},{24,4},{28,8},{1,13},{... | collective-permute-start | bytes 786440 | tf_op jit(solution)/shard_map/ppermute | solution.py:116
  211.3 32.4 %collective-permute-start.10 = (bf16[2,2,128,256]{3,0,2,1:T(2,128)(2,1)}, bf16[2,2,128,256]{3,0,2,1:T(2,128)(2,1)}, u32[]{:S(2)}, u32[]{:S(2)}) collective-permute-start(bf16[2,2,128,256]{3,0,2,1:T(2,128)(2,1)} %get-tuple-element.73), channel_id=1, source_target_pairs={{0,16},{4,20},{8,24},{12,28},{16,0},{20,4},{24,8},{28,12},{1,17},{... | collective-permute-start | bytes 786440 | tf_op jit(solution)/shard_map/ppermute | solution.py:116
  211.9 6.0 %copy-start.2 = (f32[4,2,128,256]{3,2,1,0:T(8,128)}, f32[4,2,128,256]{3,2,1,0:T(8,128)S(1)}, u32[]{:S(2)}) copy-start(f32[4,2,128,256]{3,2,1,0:T(8,128)S(1)} %fusion.23) | copy-start | bytes 3145732
  212.0 33.5 %collective-permute-start.11 = (bf16[2,2,128,256]{3,0,2,1:T(2,128)(2,1)}, bf16[2,2,128,256]{3,0,2,1:T(2,128)(2,1)}, u32[]{:S(2)}, u32[]{:S(2)}) collective-permute-start(bf16[2,2,128,256]{3,0,2,1:T(2,128)(2,1)} %get-tuple-element.72), channel_id=1, source_target_pairs={{0,20},{4,24},{8,28},{12,0},{16,4},{20,8},{24,12},{28,16},{1,21},{... | collective-permute-start | bytes 786440 | tf_op jit(solution)/shard_map/ppermute | solution.py:116
  216.6 30.7 %collective-permute-start.12 = (bf16[2,2,128,256]{3,0,2,1:T(2,128)(2,1)}, bf16[2,2,128,256]{3,0,2,1:T(2,128)(2,1)}, u32[]{:S(2)}, u32[]{:S(2)}) collective-permute-start(bf16[2,2,128,256]{3,0,2,1:T(2,128)(2,1)} %get-tuple-element.71), channel_id=1, source_target_pairs={{0,24},{4,28},{8,0},{12,4},{16,8},{20,12},{24,16},{28,20},{1,25},{... | collective-permute-start | bytes 786440 | tf_op jit(solution)/shard_map/ppermute | solution.py:116
  217.9 31.3 %collective-permute-start.13 = (bf16[2,2,128,256]{3,0,2,1:T(2,128)(2,1)}, bf16[2,2,128,256]{3,0,2,1:T(2,128)(2,1)}, u32[]{:S(2)}, u32[]{:S(2)}) collective-permute-start(bf16[2,2,128,256]{3,0,2,1:T(2,128)(2,1)} %get-tuple-element.70), channel_id=1, source_target_pairs={{0,28},{4,0},{8,4},{12,8},{16,12},{20,16},{24,20},{28,24},{1,29},{... | collective-permute-start | bytes 786440 | tf_op jit(solution)/shard_map/ppermute | solution.py:116
  237.4 53.1 %all-to-all-start.4 = ((bf16[4,16,128,128]{3,2,1,0:T(8,128)(2,1)}), bf16[4,16,128,128]{3,2,1,0:T(8,128)(2,1)}, u32[]{:S(2)}, u32[]{:S(2)}) async-start(bf16[4,16,128,128]{3,2,1,0:T(8,128)(2,1)} %bitcast.142), calls=%async_computation.4 | async-start | bytes 4194304 | tf_op jit(solution)/shard_map/all_to_all | solution.py:304
  242.8 15.6 %collective-permute-start.5 = (bf16[2,2,128,256]{3,2,1,0:T(8,128)(2,1)}, bf16[2,2,128,256]{3,2,1,0:T(8,128)(2,1)S(1)}, u32[]{:S(2)}, u32[]{:S(2)}) collective-permute-start(bf16[2,2,128,256]{3,2,1,0:T(8,128)(2,1)} %fusion.22), channel_id=1, source_target_pairs={{0,8},{4,12},{8,0},{12,4},{16,24},{20,28},{24,16},{28,20},{1,9},{5... | collective-permute-start | bytes 786440 | tf_op jit(solution)/shard_map/ppermute | solution.py:152
  258.5 8.3 %collective-permute-start.6 = (bf16[2,2,128,256]{3,2,1,0:T(8,128)(2,1)S(1)}, bf16[2,2,128,256]{3,2,1,0:T(8,128)(2,1)S(1)}, u32[]{:S(2)}, u32[]{:S(2)}) collective-permute-start(bf16[2,2,128,256]{3,2,1,0:T(8,128)(2,1)S(1)} %fusion.26), channel_id=1, source_target_pairs={{0,16},{4,20},{8,24},{12,28},{16,0},{20,4},{24,8},{28,12},{1,17},{... | collective-permute-start | bytes 786440 | tf_op jit(solution)/shard_map/ppermute | solution.py:152
  262.2 4.7 %copy-start.5 = (f32[2,4]{1,0:T(2,128)S(1)}, f32[2,4]{1,0:T(2,128)}, u32[]{:S(2)}) copy-start(f32[2,4]{1,0:T(2,128)} %and_convert_fusion) | copy-start | bytes 100
  263.5 3.6 %copy-start.3 = (f32[4,2,128,256]{3,2,1,0:T(8,128)S(1)}, f32[4,2,128,256]{3,2,1,0:T(8,128)}, u32[]{:S(2)}) copy-start(f32[4,2,128,256]{3,2,1,0:T(8,128)} %copy-done.2) | copy-start | bytes 3145732
Sparse Core Ops, SparseCore 0:
  34.5 35.9 all-gather.1

commit v12 on v11

--- a/solution.py
+++ b/solution.py
@@ -158,10 +158,14 @@
 def per_device(queries, keys, values, output_gradient, global_blocks, random_blocks):
     query_loc, key_loc, value_loc, grad_loc = (
         lax.all_to_all(queries.transpose(1, 0, 2), "head", split_axis=0, concat_axis=1, tiled=True),
-        lax.all_to_all(keys, "head", split_axis=1, concat_axis=0, tiled=True),
-        lax.all_to_all(values, "head", split_axis=1, concat_axis=0, tiled=True),
+        None,
+        None,
         output_gradient,
     )
+    kv_loc = lax.all_to_all(
+        jnp.stack([keys, values]), "head", split_axis=2, concat_axis=1, tiled=True
+    )
+    key_loc, value_loc = kv_loc[0], kv_loc[1]
     heads_q, shard_len, head_width = query_loc.shape
     heads_kv = key_loc.shape[1]
     heads_per_group = heads_q // heads_kv
@@ -173,9 +177,7 @@
     capacity = (3 * blocks + seq_count - 2) // (seq_count - 1)
     entry_count = 3 * blocks
     score_scale = 1.0 / math.sqrt(head_width)
-    kv_pair = jnp.stack(
-        [key_loc.reshape(shard_len, kv_width), value_loc.reshape(shard_len, kv_width)]
-    )
+    kv_pair = kv_loc.reshape(2, shard_len, kv_width)
     extended = padded(kv_pair, (("seq", 1),), BLOCK_TOKENS)
     kv_tiles = kv_pair.reshape(2, blocks, BLOCK_TOKENS, kv_width).transpose(1, 0, 2, 3)
     global_owner = global_blocks // blocks
@@ -303,9 +305,11 @@
     value_grad_all = kv_grad[1].reshape(shard_len, heads_kv, head_width)
     out_back = lax.all_to_all(out_all, "head", split_axis=0, concat_axis=1, tiled=True)
     query_back = lax.all_to_all(query_grad_all, "head", split_axis=0, concat_axis=1, tiled=True)
-    (out_back, query_back), kv_grad = lax.optimization_barrier(((out_back, query_back), kv_grad))
-    kv_grad = kv_grad.reshape(2, shard_len, heads_kv, head_width)
-    kv_back = lax.all_to_all(kv_grad, "head", split_axis=1, concat_axis=2, tiled=True)
+    kv_blocks = interior.astype(jnp.bfloat16).reshape(
+        blocks, 2, BLOCK_TOKENS, heads_kv, head_width
+    )
+    (out_back, query_back), kv_blocks = lax.optimization_barrier(((out_back, query_back), kv_blocks))
+    kv_back = lax.all_to_all(kv_blocks, "head", split_axis=0, concat_axis=3, tiled=True)[0]
     out_back = out_back.reshape(-1, BLOCK_TOKENS, head_width).transpose(1, 0, 2)
     query_back = query_back.reshape(-1, BLOCK_TOKENS, head_width).transpose(1, 0, 2)
     return (out_back, query_back, kv_back[0], kv_back[1])

time: 322 us -> 317 us (0.984)
  blocking collectives: 16.5 us -> 35.8 us
  waiting for transfers between devices: 96.4 us -> 85.1 us
  starting transfers between devices: 47.6 us -> 39.3 us
  local copies, waits for them, and re-layouts: 65.2 us -> 61.1 us
    all_to_all x1 -> x2, blocking collectives: 16.5 us -> 35.8 us  [the longest x1 19.3 us: per_device(): lax.all_to_all(jnp.stack([keys, values]), 'head', split_axis=2, concat_ax...]
    all_to_all x2 -> x0, waiting for transfers between devices: 13.7 us -> none  [the longest x1 7.22 us: per_device(): lax.all_to_all(keys, 'head', split_axis=1, concat_axis=0, tiled=True)]
    all_to_all x2 -> x0, starting transfers between devices: 8.28 us -> none  [the longest x1 4.87 us: per_device(): lax.all_to_all(keys, 'head', split_axis=1, concat_axis=0, tiled=True)]
    unnamed x32 -> x27, local copies, waits for them, and re-layouts: 24.3 us -> 16.8 us
  transfers between devices with their start and end apart: 21 -> 19, of which waited for: 9 -> 7; matrix products, arithmetic and copies ran while one was open for 22% -> 21% of each run, Pallas kernels for 8% -> 8%
where the time goes in v12:
time: 317 us; the launch traced here: 316 us
  waiting for transfers between devices  85.1 us (27%)
  Pallas kernels  62.8 us (20%)
  local copies, waits for them, and re-layouts  61.1 us (19%)
  starting transfers between devices  39.3 us (12%)
  blocking collectives  35.8 us (11%)
  other arithmetic  15.1 us (5%)
  between operations  14.6 us (5%)
    all_to_all x1, waiting for transfers between devices, per_device(): lax.all_to_all(queries.transpose(1, 0, 2), 'head', split_axis=0, concat_a...  40.7 us
    pallas_call x1, Pallas kernels, attention_call(): pl.pallas_call(functools.partial(backward_kernel, scale=scale), cost_esti...  37.5 us
    pallas_call x1, Pallas kernels, attention_call(): pl.pallas_call(functools.partial(forward_kernel, scale=scale), cost_estim...  25.3 us
    all_to_all x1, waiting for transfers between devices, per_device(): lax.all_to_all(out_all, 'head', split_axis=0, concat_axis=1, tiled=True)  20.3 us
    all_to_all x1, blocking collectives, per_device(): lax.all_to_all(jnp.stack([keys, values]), 'head', split_axis=2, concat_ax...  19.3 us
    unnamed x27, local copies, waits for them, and re-layouts  16.8 us
    all_to_all x1, blocking collectives, per_device(): lax.all_to_all(kv_blocks, 'head', split_axis=0, concat_axis=3, tiled=True)  16.5 us
    all_to_all x1, waiting for transfers between devices, per_device(): lax.all_to_all(query_grad_all, 'head', split_axis=0, concat_axis=1, tiled...  15.2 us
  transfers between devices with their start and end apart: 19, of which 7 were waited for; matrix products, arithmetic and copies ran while one was open for 21% of the time, Pallas kernels for 8%

profile of v12, /device:TPU:4, one launch (start us, length us, event | category | flops | bytes accessed | tf_op | source)
XLA Modules:
  0.0 316.2 jit_solution(7568410486379598170)
XLA Ops:
  7.2 1.1 copy_bitcast_fusion.8
  8.4 19.3 %all_to_all.87 = bf16[2,128,8,128]{3,1,0,2:T(8,128)(2,1)S(1)} all-to-all(bf16[2,128,8,128]{3,1,0,2:T(8,128)(2,1)S(1)} %pad_maximum_fusion.5), channel_id=1, replica_groups=mesh['seq'=8,'head'=4] {'head'}, dimensions={2} | all-to-all | bytes 1048576 | tf_op jit(solution)/shard_map/all_to_all | solution.py:165
  27.7 0.5 copy.182
  28.3 1.1 reshape.422
  29.4 2.7 copy.180
  32.1 3.7 %all-to-all-start = ((bf16[64,128,128]{2,1,0:T(8,128)(2,1)}), bf16[64,128,128]{2,1,0:T(8,128)(2,1)S(1)}, u32[]{:S(2)}, u32[]{:S(2)}) async-start(bf16[64,128,128]{2,1,0:T(8,128)(2,1)} %bitcast.142), calls=%async_computation | async-start | bytes 4194304 | tf_op jit(solution)/shard_map/all_to_all | solution.py:160
  36.0 4.4 %copy.179 = bf16[128,64,128]{2,0,1:T(8,128)(2,1)} copy(bf16[128,64,128]{2,1,0:T(8,128)(2,1)} %param.13) | data formatting | bytes 4194304 | tf_op args[3]
  41.3 0.5 fusion.45
  41.8 0.6 and_convert_fusion
  42.5 40.7 %all-to-all-done = bf16[64,128,128]{2,1,0:T(8,128)(2,1)S(1)} async-done(((bf16[64,128,128]{2,1,0:T(8,128)(2,1)}), bf16[64,128,128]{2,1,0:T(8,128)(2,1)S(1)}, u32[]{:S(2)}, u32[]{:S(2)}) %all-to-all-start) | async-done | bytes 2097184 | tf_op jit(solution)/shard_map/all_to_all | solution.py:160
  83.2 1.6 copy.118
  84.8 3.7 %all-to-all-start.2 = ((bf16[64,128,128]{2,1,0:T(8,128)(2,1)}), bf16[64,128,128]{2,1,0:T(8,128)(2,1)S(1)}, u32[]{:S(2)}, u32[]{:S(2)}) async-start(bf16[64,128,128]{2,1,0:T(8,128)(2,1)} %bitcast.131), calls=%async_computation.2 | async-start | bytes 4194304 | tf_op jit(solution)/shard_map/all_to_all | solution.py:216
  89.2 1.9 collective-permute-start
  91.1 4.7 %collective-permute-start.1 = (bf16[2,128,256]{2,1,0:T(8,128)(2,1)S(1)}, bf16[2,128,256]{2,1,0:T(8,128)(2,1)S(1)}, u32[]{:S(2)}, u32[]{:S(2)}) collective-permute-start(bf16[2,128,256]{2,1,0:T(8,128)(2,1)S(1)} %get-tuple-element.74), channel_id=1, source_target_pairs={{4,0},{8,4},{12,8},{16,12},{20,16},{24,20},{28,24},{5,1},{9,5},{13... | collective-permute-start | bytes 393224 | tf_op jit(solution)/shard_map/ppermute | solution.py:135
  95.8 0.5 fusion.44
  96.5 1.7 collective-permute-done.1
  98.4 0.8 copy.186
  99.2 4.0 %gather_fusion.1 = bf16[12,2,128,256]{3,2,1,0:T(8,128)(2,1)} fusion(bf16[2,32,128,256]{3,2,1,0:T(8,128)(2,1)} %bitcast.163, s32[1024]{0:T(1024)S(1)} %get-tuple-element.85), kind=kCustom, calls=%fused_computation.1 | custom fusion | bytes 3145776 | tf_op jit(solution)/shard_map/jit(_take)/gather | solution.py:218
  103.2 1.6 broadcast_select_fusion.1
  104.8 1.2 copy.181
  106.1 2.7 gather_fusion
  108.8 0.8 broadcast_select_fusion.2
  109.6 1.5 slice_bitcast_fusion.6
  111.6 2.3 pad_maximum_fusion.k_ref.v_ref
  113.8 0.7 broadcast_in_dim.79
  114.5 25.3 %shard_map.93.o_ref = bf16[4,2,8,128,128]{4,3,2,1,0:T(8,128)(2,1)} custom-call(bf16[2,8,4,128,128]{4,3,2,1,0:T(8,128)(2,1)} %bitcast.147, bf16[4,8,2,128,256]{4,3,2,1,0:T(8,128)(2,1)} %pad_maximum_fusion.k_ref.v_ref, bf16[4,8,2,128,256]{4,3,2,1,0:T(8,128)(2,1)} %pad_maximum_fusion.k_ref.v_ref, f32[4,1,1024]{2,1,0:T(1,128)} %bitcast.168), custom_call_target="tpu_custom_call" | custom-call | flops 4294967296 | bytes 23068672 | tf_op jit(solution)/shard_map/pallas_call | solution.py:79
  139.8 1.6 copy.130
  141.4 37.5 %shard_map.94 = (bf16[4,2,8,128,128]{4,3,2,1,0:T(8,128)(2,1)}, f32[4,8,2,128,256]{4,3,2,1,0:T(8,128)}) custom-call(bf16[2,8,4,128,128]{4,3,2,1,0:T(8,128)(2,1)} %bitcast.148, bf16[4,8,2,128,256]{4,3,2,1,0:T(8,128)(2,1)} %pad_maximum_fusion.k_ref.v_ref, bf16[4,8,2,128,256]{4,3,2,1,0:T(8,128)(2,1)} %pad_maximum_fusion.k_ref.v_ref, ...), custom_call_target="tpu_custom_call" | custom-call | flops 10737418240 | bytes 23068672 | tf_op jit(solution)/shard_map/pallas_call | solution.py:90
  178.8 5.1 %all-to-all-start.4 = ((bf16[4,16,128,128]{3,2,1,0:T(8,128)(2,1)}), bf16[4,16,128,128]{3,2,1,0:T(8,128)(2,1)S(1)}, u32[]{:S(2)}, u32[]{:S(2)}) async-start(bf16[4,16,128,128]{3,2,1,0:T(8,128)(2,1)} %bitcast.146), calls=%async_computation.4 | async-start | bytes 4194304 | tf_op jit(solution)/shard_map/all_to_all | solution.py:307
  184.0 1.8 slice_reduce_fusion
  185.8 0.9 collective-permute-start.4
  186.8 1.3 slice_bitcast_fusion.2
  188.1 1.7 slice_bitcast_fusion.1
  190.2 1.9 collective-permute-start.2
  192.1 4.8 %collective-permute-start.3 = (bf16[2,128,256]{2,1,0:T(8,128)(2,1)S(1)}, bf16[2,128,256]{2,1,0:T(8,128)(2,1)S(1)}, u32[]{:S(2)}, u32[]{:S(2)}) collective-permute-start(bf16[2,128,256]{2,1,0:T(8,128)(2,1)S(1)} %get-tuple-element.66), channel_id=1, source_target_pairs={{4,0},{8,4},{12,8},{16,12},{20,16},{24,20},{28,24},{5,1},{9,5},{13... | collective-permute-start | bytes 393224 | tf_op jit(solution)/shard_map/ppermute | solution.py:135
  196.9 2.1 fusion.7
  199.1 0.5 copy-done.6
  199.7 1.0 fusion.4
  200.7 2.8 constant_dynamic-slice_fusion
  203.7 1.0 bitcast_dynamic-update-slice_fusion.7
  204.7 2.5 collective-permute-start.9
  207.2 0.6 collective-permute-start.10
  208.0 0.9 fusion.21
  208.9 3.7 %collective-permute-done.7 = bf16[2,2,128,256]{3,0,2,1:T(2,128)(2,1)S(1)} collective-permute-done((bf16[2,2,128,256]{3,0,2,1:T(2,128)(2,1)S(1)}, bf16[2,2,128,256]{3,0,2,1:T(2,128)(2,1)S(1)}, u32[]{:S(2)}, u32[]{:S(2)}) %collective-permute-start.7) | collective-permute-done | bytes 262176 | tf_op jit(solution)/shard_map/ppermute | solution.py:116
  212.7 0.9 bitcast_dynamic-update-slice_fusion.6
  213.9 4.3 %collective-permute-start.13 = (bf16[2,2,128,256]{3,0,2,1:T(2,128)(2,1)}, bf16[2,2,128,256]{3,0,2,1:T(2,128)(2,1)}, u32[]{:S(2)}, u32[]{:S(2)}) collective-permute-start(bf16[2,2,128,256]{3,0,2,1:T(2,128)(2,1)} %get-tuple-element.54), channel_id=1, source_target_pairs={{0,28},{4,0},{8,4},{12,8},{16,12},{20,16},{24,20},{28,24},{1,29},{... | collective-permute-start | bytes 786440 | tf_op jit(solution)/shard_map/ppermute | solution.py:116
  218.2 15.2 %all-to-all-done.4 = bf16[4,16,128,128]{3,2,1,0:T(8,128)(2,1)S(1)} async-done(((bf16[4,16,128,128]{3,2,1,0:T(8,128)(2,1)}), bf16[4,16,128,128]{3,2,1,0:T(8,128)(2,1)S(1)}, u32[]{:S(2)}, u32[]{:S(2)}) %all-to-all-start.4) | async-done | bytes 2097184 | tf_op jit(solution)/shard_map/all_to_all | solution.py:307
  233.4 4.4 %all-to-all-start.3 = ((bf16[4,16,128,128]{3,2,1,0:T(8,128)(2,1)}), bf16[4,16,128,128]{3,2,1,0:T(8,128)(2,1)}, u32[]{:S(2)}, u32[]{:S(2)}) async-start(bf16[4,16,128,128]{3,2,1,0:T(8,128)(2,1)} %bitcast.145), calls=%async_computation.3 | async-start | bytes 4194304 | tf_op jit(solution)/shard_map/all_to_all | solution.py:306
  237.8 0.9 bitcast_dynamic-update-slice_fusion.5
  238.7 0.9 bitcast_dynamic-update-slice_fusion.4
  239.6 1.8 bitcast_dynamic-update-slice_fusion.3
  241.4 1.8 bitcast_dynamic-update-slice_fusion.2
  243.3 1.8 bitcast_dynamic-update-slice_fusion.1
  245.1 1.8 bitcast_dynamic-update-slice_fusion
  246.9 7.3 %gather_fusion.2 = bf16[8,2,2,128,256]{4,1,3,2,0:T(2,128)(2,1)} fusion(bf16[8,2,2,128,256]{4,1,3,2,0:T(2,128)(2,1)} %bitcast_dynamic-update-slice_fusion, s32[1024]{0:T(1024)S(1)} %pad_clamp_fusion), kind=kCustom, calls=%fused_computation.2 | custom fusion | bytes 4194336 | tf_op jit(solution)/shard_map/jit(_take)/gather | solution.py:119
  254.7 3.5 %broadcast_select_fusion = bf16[8,2,2,128,256]{4,1,3,2,0:T(2,128)(2,1)S(1)} fusion(bf16[8,2,2,128,256]{4,1,3,2,0:T(2,128)(2,1)} %gather_fusion.2, pred[8]{0:T(512)(128)(4,1)S(1)} %compare_and_fusion.2), kind=kLoop, calls=%fused_computation.4 | loop fusion | flops 1048576 | bytes 4194312 | tf_op jit(solution)/shard_map/jit(_take)/select_n | solution.py:119
  258.1 1.3 fusion.8
  259.4 3.2 %collective-permute-done.6 = bf16[2,2,128,256]{3,2,1,0:T(8,128)(2,1)S(1)} collective-permute-done((bf16[2,2,128,256]{3,2,1,0:T(8,128)(2,1)S(1)}, bf16[2,2,128,256]{3,2,1,0:T(8,128)(2,1)S(1)}, u32[]{:S(2)}, u32[]{:S(2)}) %collective-permute-start.6) | collective-permute-done | bytes 262176 | tf_op jit(solution)/shard_map/ppermute | solution.py:152
  263.6 2.7 copy.132
  266.2 20.3 %all-to-all-done.3 = bf16[4,16,128,128]{3,2,1,0:T(8,128)(2,1)} async-done(((bf16[4,16,128,128]{3,2,1,0:T(8,128)(2,1)}), bf16[4,16,128,128]{3,2,1,0:T(8,128)(2,1)}, u32[]{:S(2)}, u32[]{:S(2)}) %all-to-all-start.3) | async-done | bytes 2097184 | tf_op jit(solution)/shard_map/all_to_all | solution.py:306
  286.5 4.3 %copy.131 = bf16[4,16,128,128]{3,1,0,2:T(8,128)(2,1)} copy(bf16[4,16,128,128]{3,2,1,0:T(8,128)(2,1)} %all-to-all-done.3) | data formatting | bytes 4194304 | tf_op jit(solution)/shard_map/all_to_all | solution.py:306
  290.8 16.5 %all_to_all.88 = bf16[4,2,128,2,128]{4,3,2,1,0:T(2,128)(2,1)S(1)} all-to-all(bf16[4,2,128,2,128]{4,3,2,1,0:T(2,128)(2,1)S(1)} %reshape.438), channel_id=1, replica_groups=mesh['seq'=8,'head'=4] {'head'}, dimensions={0} | all-to-all | bytes 1048576 | tf_op jit(solution)/shard_map/all_to_all | solution.py:312
  307.6 0.9 copy.147
  308.5 0.9 copy.148
  (86 shorter events, 5.4 us)
Async XLA Ops:
  7.2 77.6 %all-gather.2.cloned.1.call-start = ((), (), s32[]{:S(2)}) async-start(), calls=%async_computation.6 | async-start | bytes 4718592 | tf_op jit(solution)/shard_map/all_gather | solution.py:213
  8.4 21.0 %copy-start.3 = (bf16[128,64,128]{2,1,0:T(8,128)(2,1)S(1)}, bf16[128,64,128]{2,1,0:T(8,128)(2,1)}, u32[]{:S(2)}) copy-start(bf16[128,64,128]{2,1,0:T(8,128)(2,1)} %param.10) | copy-start | bytes 6291460
  32.1 3.8 %copy-start.7 = (s32[32,3]{0,1:T(4,128)S(1)}, s32[32,3]{0,1:T(4,128)}, u32[]{:S(2)}) copy-start(s32[32,3]{0,1:T(4,128)} %param.15) | copy-start | bytes 1156
  32.1 51.1 %all-to-all-start = ((bf16[64,128,128]{2,1,0:T(8,128)(2,1)}), bf16[64,128,128]{2,1,0:T(8,128)(2,1)S(1)}, u32[]{:S(2)}, u32[]{:S(2)}) async-start(bf16[64,128,128]{2,1,0:T(8,128)(2,1)} %bitcast.142), calls=%async_computation | async-start | bytes 4194304 | tf_op jit(solution)/shard_map/all_to_all | solution.py:160
  36.0 4.9 %copy-start.8 = (s32[2]{0:T(128)S(1)}, s32[2]{0:T(128)}, u32[]{:S(2)}) copy-start(s32[2]{0:T(128)} %param.14) | copy-start | bytes 28
  84.8 4.4 %copy-start = (bf16[2,512,256]{2,1,0:T(8,128)(2,1)S(1)}, bf16[2,512,256]{2,1,0:T(8,128)(2,1)}, u32[]{:S(2)}) copy-start(bf16[2,512,256]{2,1,0:T(8,128)(2,1)} %reshape.422) | copy-start | bytes 1572868
  84.8 55.1 %all-to-all-start.2 = ((bf16[64,128,128]{2,1,0:T(8,128)(2,1)}), bf16[64,128,128]{2,1,0:T(8,128)(2,1)S(1)}, u32[]{:S(2)}, u32[]{:S(2)}) async-start(bf16[64,128,128]{2,1,0:T(8,128)(2,1)} %bitcast.131), calls=%async_computation.2 | async-start | bytes 4194304 | tf_op jit(solution)/shard_map/all_to_all | solution.py:216
  89.2 7.3 %collective-permute-start = (bf16[2,128,256]{2,1,0:T(8,128)(2,1)S(1)}, bf16[2,128,256]{2,1,0:T(8,128)(2,1)S(1)}, u32[]{:S(2)}, u32[]{:S(2)}) collective-permute-start(bf16[2,128,256]{2,1,0:T(8,128)(2,1)S(1)} %get-tuple-element.73), channel_id=1, source_target_pairs={{0,4},{4,8},{8,12},{12,16},{16,20},{20,24},{24,28},{1,5},{5,9},{9,... | collective-permute-start | bytes 393224 | tf_op jit(solution)/shard_map/ppermute | solution.py:134
  91.1 7.0 %collective-permute-start.1 = (bf16[2,128,256]{2,1,0:T(8,128)(2,1)S(1)}, bf16[2,128,256]{2,1,0:T(8,128)(2,1)S(1)}, u32[]{:S(2)}, u32[]{:S(2)}) collective-permute-start(bf16[2,128,256]{2,1,0:T(8,128)(2,1)S(1)} %get-tuple-element.74), channel_id=1, source_target_pairs={{4,0},{8,4},{12,8},{16,12},{20,16},{24,20},{28,24},{5,1},{9,5},{13... | collective-permute-start | bytes 393224 | tf_op jit(solution)/shard_map/ppermute | solution.py:135
  108.8 2.3 copy-start.4
  178.8 54.5 %all-to-all-start.4 = ((bf16[4,16,128,128]{3,2,1,0:T(8,128)(2,1)}), bf16[4,16,128,128]{3,2,1,0:T(8,128)(2,1)S(1)}, u32[]{:S(2)}, u32[]{:S(2)}) async-start(bf16[4,16,128,128]{3,2,1,0:T(8,128)(2,1)} %bitcast.146), calls=%async_computation.4 | async-start | bytes 4194304 | tf_op jit(solution)/shard_map/all_to_all | solution.py:307
  185.8 22.1 %collective-permute-start.4 = (bf16[2,2,128,256]{3,2,1,0:T(8,128)(2,1)S(1)}, bf16[2,2,128,256]{3,2,1,0:T(8,128)(2,1)S(1)}, u32[]{:S(2)}, u32[]{:S(2)}) collective-permute-start(bf16[2,2,128,256]{3,2,1,0:T(8,128)(2,1)S(1)} %convert_element_type.59), channel_id=1, source_target_pairs={{0,4},{4,0},{8,12},{12,8},{16,20},{20,16},{24,28},{28,24},{1,5},{5... | collective-permute-start | bytes 786440 | tf_op jit(solution)/shard_map/ppermute | solution.py:152
  190.2 14.5 %collective-permute-start.2 = (bf16[2,128,256]{2,1,0:T(8,128)(2,1)S(1)}, bf16[2,128,256]{2,1,0:T(8,128)(2,1)S(1)}, u32[]{:S(2)}, u32[]{:S(2)}) collective-permute-start(bf16[2,128,256]{2,1,0:T(8,128)(2,1)S(1)} %get-tuple-element.65), channel_id=1, source_target_pairs={{0,4},{4,8},{8,12},{12,16},{16,20},{20,24},{24,28},{1,5},{5,9},{9,... | collective-permute-start | bytes 393224 | tf_op jit(solution)/shard_map/ppermute | solution.py:134
  192.1 15.1 %collective-permute-start.3 = (bf16[2,128,256]{2,1,0:T(8,128)(2,1)S(1)}, bf16[2,128,256]{2,1,0:T(8,128)(2,1)S(1)}, u32[]{:S(2)}, u32[]{:S(2)}) collective-permute-start(bf16[2,128,256]{2,1,0:T(8,128)(2,1)S(1)} %get-tuple-element.66), channel_id=1, source_target_pairs={{4,0},{8,4},{12,8},{16,12},{20,16},{24,20},{28,24},{5,1},{9,5},{13... | collective-permute-start | bytes 393224 | tf_op jit(solution)/shard_map/ppermute | solution.py:135
  199.0 0.7 copy-start.6
  203.6 9.0 %collective-permute-start.7 = (bf16[2,2,128,256]{3,0,2,1:T(2,128)(2,1)S(1)}, bf16[2,2,128,256]{3,0,2,1:T(2,128)(2,1)S(1)}, u32[]{:S(2)}, u32[]{:S(2)}) collective-permute-start(bf16[2,2,128,256]{3,0,2,1:T(2,128)(2,1)S(1)} %get-tuple-element.60), channel_id=1, source_target_pairs={{0,4},{4,8},{8,12},{12,16},{16,20},{20,24},{24,28},{28,0},{1,5},{5... | collective-permute-start | bytes 786440 | tf_op jit(solution)/shard_map/ppermute | solution.py:116
  203.6 10.2 %collective-permute-start.8 = (bf16[2,2,128,256]{3,0,2,1:T(2,128)(2,1)S(1)}, bf16[2,2,128,256]{3,0,2,1:T(2,128)(2,1)S(1)}, u32[]{:S(2)}, u32[]{:S(2)}) collective-permute-start(bf16[2,2,128,256]{3,0,2,1:T(2,128)(2,1)S(1)} %get-tuple-element.59), channel_id=1, source_target_pairs={{0,8},{4,12},{8,16},{12,20},{16,24},{20,28},{24,0},{28,4},{1,9},{5... | collective-permute-start | bytes 786440 | tf_op jit(solution)/shard_map/ppermute | solution.py:116
  204.7 34.0 %collective-permute-start.9 = (bf16[2,2,128,256]{3,0,2,1:T(2,128)(2,1)}, bf16[2,2,128,256]{3,0,2,1:T(2,128)(2,1)S(1)}, u32[]{:S(2)}, u32[]{:S(2)}) collective-permute-start(bf16[2,2,128,256]{3,0,2,1:T(2,128)(2,1)} %get-tuple-element.58), channel_id=1, source_target_pairs={{0,12},{4,16},{8,20},{12,24},{16,28},{20,0},{24,4},{28,8},{1,13},{... | collective-permute-start | bytes 786440 | tf_op jit(solution)/shard_map/ppermute | solution.py:116
  207.2 32.4 %collective-permute-start.10 = (bf16[2,2,128,256]{3,0,2,1:T(2,128)(2,1)}, bf16[2,2,128,256]{3,0,2,1:T(2,128)(2,1)}, u32[]{:S(2)}, u32[]{:S(2)}) collective-permute-start(bf16[2,2,128,256]{3,0,2,1:T(2,128)(2,1)} %get-tuple-element.57), channel_id=1, source_target_pairs={{0,16},{4,20},{8,24},{12,28},{16,0},{20,4},{24,8},{28,12},{1,17},{... | collective-permute-start | bytes 786440 | tf_op jit(solution)/shard_map/ppermute | solution.py:116
  207.9 6.0 %copy-start.1 = (f32[4,2,128,256]{3,2,1,0:T(8,128)}, f32[4,2,128,256]{3,2,1,0:T(8,128)S(1)}, u32[]{:S(2)}) copy-start(f32[4,2,128,256]{3,2,1,0:T(8,128)S(1)} %fusion.22) | copy-start | bytes 3145732
  207.9 33.5 %collective-permute-start.11 = (bf16[2,2,128,256]{3,0,2,1:T(2,128)(2,1)}, bf16[2,2,128,256]{3,0,2,1:T(2,128)(2,1)}, u32[]{:S(2)}, u32[]{:S(2)}) collective-permute-start(bf16[2,2,128,256]{3,0,2,1:T(2,128)(2,1)} %get-tuple-element.56), channel_id=1, source_target_pairs={{0,20},{4,24},{8,28},{12,0},{16,4},{20,8},{24,12},{28,16},{1,21},{... | collective-permute-start | bytes 786440 | tf_op jit(solution)/shard_map/ppermute | solution.py:116
  212.6 30.7 %collective-permute-start.12 = (bf16[2,2,128,256]{3,0,2,1:T(2,128)(2,1)}, bf16[2,2,128,256]{3,0,2,1:T(2,128)(2,1)}, u32[]{:S(2)}, u32[]{:S(2)}) collective-permute-start(bf16[2,2,128,256]{3,0,2,1:T(2,128)(2,1)} %get-tuple-element.55), channel_id=1, source_target_pairs={{0,24},{4,28},{8,0},{12,4},{16,8},{20,12},{24,16},{28,20},{1,25},{... | collective-permute-start | bytes 786440 | tf_op jit(solution)/shard_map/ppermute | solution.py:116
  213.9 31.3 %collective-permute-start.13 = (bf16[2,2,128,256]{3,0,2,1:T(2,128)(2,1)}, bf16[2,2,128,256]{3,0,2,1:T(2,128)(2,1)}, u32[]{:S(2)}, u32[]{:S(2)}) collective-permute-start(bf16[2,2,128,256]{3,0,2,1:T(2,128)(2,1)} %get-tuple-element.54), channel_id=1, source_target_pairs={{0,28},{4,0},{8,4},{12,8},{16,12},{20,16},{24,20},{28,24},{1,29},{... | collective-permute-start | bytes 786440 | tf_op jit(solution)/shard_map/ppermute | solution.py:116
  233.4 53.1 %all-to-all-start.3 = ((bf16[4,16,128,128]{3,2,1,0:T(8,128)(2,1)}), bf16[4,16,128,128]{3,2,1,0:T(8,128)(2,1)}, u32[]{:S(2)}, u32[]{:S(2)}) async-start(bf16[4,16,128,128]{3,2,1,0:T(8,128)(2,1)} %bitcast.145), calls=%async_computation.3 | async-start | bytes 4194304 | tf_op jit(solution)/shard_map/all_to_all | solution.py:306
  238.7 15.6 %collective-permute-start.5 = (bf16[2,2,128,256]{3,2,1,0:T(8,128)(2,1)}, bf16[2,2,128,256]{3,2,1,0:T(8,128)(2,1)S(1)}, u32[]{:S(2)}, u32[]{:S(2)}) collective-permute-start(bf16[2,2,128,256]{3,2,1,0:T(8,128)(2,1)} %fusion.21), channel_id=1, source_target_pairs={{0,8},{4,12},{8,0},{12,4},{16,24},{20,28},{24,16},{28,20},{1,9},{5... | collective-permute-start | bytes 786440 | tf_op jit(solution)/shard_map/ppermute | solution.py:152
  254.4 8.3 %collective-permute-start.6 = (bf16[2,2,128,256]{3,2,1,0:T(8,128)(2,1)S(1)}, bf16[2,2,128,256]{3,2,1,0:T(8,128)(2,1)S(1)}, u32[]{:S(2)}, u32[]{:S(2)}) collective-permute-start(bf16[2,2,128,256]{3,2,1,0:T(8,128)(2,1)S(1)} %fusion.25), channel_id=1, source_target_pairs={{0,16},{4,20},{8,24},{12,28},{16,0},{20,4},{24,8},{28,12},{1,17},{... | collective-permute-start | bytes 786440 | tf_op jit(solution)/shard_map/ppermute | solution.py:152
  258.1 4.7 %copy-start.5 = (f32[2,4]{1,0:T(2,128)S(1)}, f32[2,4]{1,0:T(2,128)}, u32[]{:S(2)}) copy-start(f32[2,4]{1,0:T(2,128)} %and_convert_fusion) | copy-start | bytes 100
  259.4 3.6 %copy-start.2 = (f32[4,2,128,256]{3,2,1,0:T(8,128)S(1)}, f32[4,2,128,256]{3,2,1,0:T(8,128)}, u32[]{:S(2)}) copy-start(f32[4,2,128,256]{3,2,1,0:T(8,128)} %copy-done.1) | copy-start | bytes 3145732
Sparse Core Ops, SparseCore 0:
  29.5 35.4 all-gather.1

commit v13 on v12

--- a/solution.py
+++ b/solution.py
@@ -35,14 +35,14 @@
     v = v_ref[...].reshape(-1, width)
     p_low = softmax_rows(q, k, bias_ref[...], scale).astype(jnp.bfloat16)
     o_low = jnp.dot(p_low, v, preferred_element_type=jnp.float32).astype(jnp.bfloat16)
-    out_ref[...] = o_low.reshape(out_ref.shape)
+    store_rows(out_ref, o_low, out_ref.shape[1] // width, width)
 
 
 def backward_kernel(q_ref, k_ref, v_ref, do_ref, o_ref, bias_ref, dq_ref, grad_ref, *, scale):
     width = k_ref.shape[-1]
     q = q_ref[...].reshape(-1, width)
     do = do_ref[...].reshape(-1, width)
-    o_low = o_ref[...].reshape(-1, width)
+    o_low = rows_of(o_ref, o_ref.shape[1] // width, width)
     k = k_ref[...].reshape(-1, width)
     v = v_ref[...].reshape(-1, width)
     rows_by_cols = (((1,), (1,)), ((), ()))
@@ -53,7 +53,7 @@
     dp = lax.dot_general(do, v, rows_by_cols, preferred_element_type=jnp.float32)
     ds_low = (p * (dp - delta)).astype(jnp.bfloat16)
     dq = jnp.dot(ds_low, k, preferred_element_type=jnp.float32) * scale
-    dq_ref[...] = dq.astype(jnp.bfloat16).reshape(dq_ref.shape)
+    store_rows(dq_ref, dq.astype(jnp.bfloat16), dq_ref.shape[1] // width, width)
     dk = lax.dot_general(ds_low, q, over_rows, preferred_element_type=jnp.float32) * scale
     dv = lax.dot_general(p_low, do, over_rows, preferred_element_type=jnp.float32)
     grad_ref[:, 0] = dk.reshape(grad_ref.shape[0], -1, width)
@@ -65,8 +65,8 @@
     tile_count = tiles.shape[1]
     rows_width = group * head_width
     q_spec = pl.BlockSpec((None, group, None, tokens, head_width), lambda j, h: (h, 0, j, 0, 0))
-    o_spec = pl.BlockSpec((None, None, group, tokens, head_width), lambda j, h: (j, h, 0, 0, 0))
-    o_shape = jax.ShapeDtypeStruct((blocks, heads_kv, group, tokens, head_width), jnp.bfloat16)
+    o_spec = pl.BlockSpec((None, tokens, rows_width), lambda j, h: (j, 0, h))
+    o_shape = jax.ShapeDtypeStruct((blocks, tokens, heads_kv * rows_width), jnp.bfloat16)
     k_spec = pl.BlockSpec((None, tile_count, None, tokens, head_width), lambda j, h: (j, 0, 0, 0, h))
     v_spec = pl.BlockSpec((None, tile_count, None, tokens, head_width), lambda j, h: (j, 0, 1, 0, h))
     b_spec = pl.BlockSpec((None, 1, bias.shape[-1]), lambda j, h: (j, 0, 0))
@@ -299,19 +299,19 @@
         preferred_element_type=jnp.float32,
     )
     kv_grad = interior.transpose(1, 0, 2, 3).reshape(2, shard_len, kv_width).astype(jnp.bfloat16)
-    out_all = out_q.reshape(blocks, heads_q, BLOCK_TOKENS, head_width)
-    query_grad_all = grad_q.reshape(blocks, heads_q, BLOCK_TOKENS, head_width)
+    out_all = out_q
+    query_grad_all = grad_q
     key_grad_all = kv_grad[0].reshape(shard_len, heads_kv, head_width)
     value_grad_all = kv_grad[1].reshape(shard_len, heads_kv, head_width)
-    out_back = lax.all_to_all(out_all, "head", split_axis=0, concat_axis=1, tiled=True)
-    query_back = lax.all_to_all(query_grad_all, "head", split_axis=0, concat_axis=1, tiled=True)
+    out_back = lax.all_to_all(out_all, "head", split_axis=0, concat_axis=2, tiled=True)
+    query_back = lax.all_to_all(query_grad_all, "head", split_axis=0, concat_axis=2, tiled=True)
     kv_blocks = interior.astype(jnp.bfloat16).reshape(
         blocks, 2, BLOCK_TOKENS, heads_kv, head_width
     )
     (out_back, query_back), kv_blocks = lax.optimization_barrier(((out_back, query_back), kv_blocks))
     kv_back = lax.all_to_all(kv_blocks, "head", split_axis=0, concat_axis=3, tiled=True)[0]
-    out_back = out_back.reshape(-1, BLOCK_TOKENS, head_width).transpose(1, 0, 2)
-    query_back = query_back.reshape(-1, BLOCK_TOKENS, head_width).transpose(1, 0, 2)
+    out_back = out_back.reshape(BLOCK_TOKENS, -1, head_width)
+    query_back = query_back.reshape(BLOCK_TOKENS, -1, head_width)
     return (out_back, query_back, kv_back[0], kv_back[1])
 
 

time: 317 us -> 318 us (level)
  blocking collectives: 35.8 us -> 19.3 us
  waiting for transfers between devices: 85.1 us -> 95.1 us
  local copies, waits for them, and re-layouts: 61.1 us -> 67.6 us
    all_to_all x1 -> x0, blocking collectives: 16.5 us -> none  [per_device(): lax.all_to_all(kv_blocks, 'head', split_axis=0, concat_axis=3, tiled=True)]
    all_to_all x2 -> x3, waiting for transfers between devices: 35.5 us -> 46.3 us  [the longest x1 19.9 us: per_device(): lax.all_to_all(query_grad_all, 'head', split_axis=0, concat_axis=2, tiled...]
    unnamed x27 -> x31, local copies, waits for them, and re-layouts: 16.8 us -> 23.8 us
    ppermute x7, starting transfers between devices: 7.77 us -> 3.59 us  [exchange(): part = lax.ppermute(part, axis, pairs)]
    all_to_all x2 -> x3, starting transfers between devices: 9.49 us -> 13 us  [the longest x1 5.05 us: per_device(): lax.all_to_all(query_grad_all, 'head', split_axis=0, concat_axis=2, tiled...]
  transfers between devices with their start and end apart: 19 -> 20, of which waited for: 7 -> 7; matrix products, arithmetic and copies ran while one was open for 21% -> 23% of each run, Pallas kernels for 8% -> 8%
where the time goes in v13:
time: 318 us; the launch traced here: 317 us
  waiting for transfers between devices  95.1 us (30%)
  local copies, waits for them, and re-layouts  67.6 us (21%)
  Pallas kernels  62.8 us (20%)
  starting transfers between devices  39.9 us (13%)
  blocking collectives  19.3 us (6%)
  other arithmetic  15.1 us (5%)
  between operations  14.7 us (5%)
    all_to_all x1, waiting for transfers between devices, per_device(): lax.all_to_all(queries.transpose(1, 0, 2), 'head', split_axis=0, concat_a...  40.7 us
    pallas_call x1, Pallas kernels, attention_call(): pl.pallas_call(functools.partial(backward_kernel, scale=scale), cost_esti...  37.4 us
    pallas_call x1, Pallas kernels, attention_call(): pl.pallas_call(functools.partial(forward_kernel, scale=scale), cost_estim...  25.3 us
    unnamed x31, local copies, waits for them, and re-layouts  23.8 us
    all_to_all x1, waiting for transfers between devices, per_device(): lax.all_to_all(query_grad_all, 'head', split_axis=0, concat_axis=2, tiled...  19.9 us
    all_to_all x1, waiting for transfers between devices, per_device(): lax.all_to_all(out_all, 'head', split_axis=0, concat_axis=2, tiled=True)  19.5 us
    all_to_all x1, blocking collectives, per_device(): lax.all_to_all(jnp.stack([keys, values]), 'head', split_axis=2, concat_ax...  19.3 us
    ppermute x2, starting transfers between devices, padded(): after = lax.ppermute(leading, axis, down)  9.48 us
  transfers between devices with their start and end apart: 20, of which 7 were waited for; matrix products, arithmetic and copies ran while one was open for 23% of the time, Pallas kernels for 8%

profile of v13, /device:TPU:4, one launch (start us, length us, event | category | flops | bytes accessed | tf_op | source)
XLA Modules:
  0.0 316.9 jit_solution(4563679482017863433)
XLA Ops:
  7.2 1.1 copy_bitcast_fusion.8
  8.4 19.3 %all_to_all.99 = bf16[2,128,8,128]{3,1,0,2:T(8,128)(2,1)S(1)} all-to-all(bf16[2,128,8,128]{3,1,0,2:T(8,128)(2,1)S(1)} %pad_maximum_fusion.5), channel_id=1, replica_groups=mesh['seq'=8,'head'=4] {'head'}, dimensions={2} | all-to-all | bytes 1048576 | tf_op jit(solution)/shard_map/all_to_all | solution.py:165
  28.3 1.1 reshape.410
  29.4 2.7 copy.186
  32.1 3.7 %all-to-all-start = ((bf16[64,128,128]{2,1,0:T(8,128)(2,1)}), bf16[64,128,128]{2,1,0:T(8,128)(2,1)S(1)}, u32[]{:S(2)}, u32[]{:S(2)}) async-start(bf16[64,128,128]{2,1,0:T(8,128)(2,1)} %bitcast.143), calls=%async_computation | async-start | bytes 4194304 | tf_op jit(solution)/shard_map/all_to_all | solution.py:160
  36.0 4.4 %copy.185 = bf16[128,64,128]{2,0,1:T(8,128)(2,1)} copy(bf16[128,64,128]{2,1,0:T(8,128)(2,1)} %param.13) | data formatting | bytes 4194304 | tf_op args[3]
  41.8 0.7 and_convert_fusion
  42.5 40.7 %all-to-all-done = bf16[64,128,128]{2,1,0:T(8,128)(2,1)S(1)} async-done(((bf16[64,128,128]{2,1,0:T(8,128)(2,1)}), bf16[64,128,128]{2,1,0:T(8,128)(2,1)S(1)}, u32[]{:S(2)}, u32[]{:S(2)}) %all-to-all-start) | async-done | bytes 2097184 | tf_op jit(solution)/shard_map/all_to_all | solution.py:160
  83.2 1.6 copy.122
  84.8 3.7 %all-to-all-start.2 = ((bf16[64,128,128]{2,1,0:T(8,128)(2,1)}), bf16[64,128,128]{2,1,0:T(8,128)(2,1)S(1)}, u32[]{:S(2)}, u32[]{:S(2)}) async-start(bf16[64,128,128]{2,1,0:T(8,128)(2,1)} %bitcast.131), calls=%async_computation.2 | async-start | bytes 4194304 | tf_op jit(solution)/shard_map/all_to_all | solution.py:216
  89.2 1.9 collective-permute-start
  91.1 4.7 %collective-permute-start.1 = (bf16[2,128,256]{2,1,0:T(8,128)(2,1)S(1)}, bf16[2,128,256]{2,1,0:T(8,128)(2,1)S(1)}, u32[]{:S(2)}, u32[]{:S(2)}) collective-permute-start(bf16[2,128,256]{2,1,0:T(8,128)(2,1)S(1)} %get-tuple-element.90), channel_id=1, source_target_pairs={{4,0},{8,4},{12,8},{16,12},{20,16},{24,20},{28,24},{5,1},{9,5},{13... | collective-permute-start | bytes 393224 | tf_op jit(solution)/shard_map/ppermute | solution.py:135
  96.5 1.7 collective-permute-done.1
  98.4 0.8 copy.192
  99.2 4.0 %gather_fusion.1 = bf16[12,2,128,256]{3,2,1,0:T(8,128)(2,1)} fusion(bf16[2,32,128,256]{3,2,1,0:T(8,128)(2,1)} %bitcast.162, s32[1024]{0:T(1024)S(1)} %get-tuple-element.101), kind=kCustom, calls=%fused_computation.1 | custom fusion | bytes 3145776 | tf_op jit(solution)/shard_map/jit(_take)/gather | solution.py:218
  103.2 1.6 broadcast_select_fusion.1
  104.8 1.2 copy.187
  106.1 2.7 gather_fusion
  108.8 0.8 broadcast_select_fusion.2
  109.6 1.5 slice_bitcast_fusion.6
  111.6 2.2 pad_maximum_fusion.k_ref.v_ref
  113.8 0.7 broadcast_in_dim.79
  114.5 25.3 %shard_map.93.o_ref = bf16[4,128,2048]{2,1,0:T(8,128)(2,1)} custom-call(bf16[2,8,4,128,128]{4,3,2,1,0:T(8,128)(2,1)} %bitcast.148, bf16[4,8,2,128,256]{4,3,2,1,0:T(8,128)(2,1)} %pad_maximum_fusion.k_ref.v_ref, bf16[4,8,2,128,256]{4,3,2,1,0:T(8,128)(2,1)} %pad_maximum_fusion.k_ref.v_ref, f32[4,1,1024]{2,1,0:T(1,128)} %bitcast.167), custom_call_target="tpu_custom_call" | custom-call | flops 4294967296 | bytes 23068672 | tf_op jit(solution)/shard_map/pallas_call | solution.py:79
  139.8 1.5 copy.134
  141.4 37.4 %shard_map.94 = (bf16[4,128,2048]{2,1,0:T(8,128)(2,1)}, f32[4,8,2,128,256]{4,3,2,1,0:T(8,128)}) custom-call(bf16[2,8,4,128,128]{4,3,2,1,0:T(8,128)(2,1)} %bitcast.149, bf16[4,8,2,128,256]{4,3,2,1,0:T(8,128)(2,1)} %pad_maximum_fusion.k_ref.v_ref, bf16[4,8,2,128,256]{4,3,2,1,0:T(8,128)(2,1)} %pad_maximum_fusion.k_ref.v_ref, ...), custom_call_target="tpu_custom_call" | custom-call | flops 10737418240 | bytes 23068672 | tf_op jit(solution)/shard_map/pallas_call | solution.py:90
  178.8 5.1 %all-to-all-start.4 = ((bf16[4,128,2048]{2,1,0:T(8,128)(2,1)}), bf16[4,128,2048]{2,1,0:T(8,128)(2,1)S(1)}, u32[]{:S(2)}, u32[]{:S(2)}) async-start(bf16[4,128,2048]{2,1,0:T(8,128)(2,1)} %get-tuple-element.43), calls=%async_computation.4 | async-start | bytes 4194304 | tf_op jit(solution)/shard_map/all_to_all | solution.py:307
  184.0 1.8 slice_reduce_fusion
  185.8 0.9 collective-permute-start.4
  186.7 1.3 slice_bitcast_fusion.2
  188.0 1.7 slice_bitcast_fusion.1
  190.2 1.9 collective-permute-start.2
  192.1 4.8 %collective-permute-start.3 = (bf16[2,128,256]{2,1,0:T(8,128)(2,1)S(1)}, bf16[2,128,256]{2,1,0:T(8,128)(2,1)S(1)}, u32[]{:S(2)}, u32[]{:S(2)}) collective-permute-start(bf16[2,128,256]{2,1,0:T(8,128)(2,1)S(1)} %get-tuple-element.82), channel_id=1, source_target_pairs={{4,0},{8,4},{12,8},{16,12},{20,16},{24,20},{28,24},{5,1},{9,5},{13... | collective-permute-start | bytes 393224 | tf_op jit(solution)/shard_map/ppermute | solution.py:135
  196.9 2.1 fusion.7
  199.6 1.0 fusion.4
  200.7 2.9 constant_dynamic-slice_fusion
  203.8 1.0 bitcast_dynamic-update-slice_fusion.7
  204.8 2.5 collective-permute-start.9
  207.3 0.6 collective-permute-start.10
  208.1 0.9 fusion.21
  209.0 3.4 %collective-permute-done.7 = bf16[2,2,128,256]{3,0,2,1:T(2,128)(2,1)S(1)} collective-permute-done((bf16[2,2,128,256]{3,0,2,1:T(2,128)(2,1)S(1)}, bf16[2,2,128,256]{3,0,2,1:T(2,128)(2,1)S(1)}, u32[]{:S(2)}, u32[]{:S(2)}) %collective-permute-start.7) | collective-permute-done | bytes 262176 | tf_op jit(solution)/shard_map/ppermute | solution.py:116
  212.6 0.9 bitcast_dynamic-update-slice_fusion.6
  213.5 19.9 %all-to-all-done.4 = bf16[4,128,2048]{2,1,0:T(8,128)(2,1)S(1)} async-done(((bf16[4,128,2048]{2,1,0:T(8,128)(2,1)}), bf16[4,128,2048]{2,1,0:T(8,128)(2,1)S(1)}, u32[]{:S(2)}, u32[]{:S(2)}) %all-to-all-start.4) | async-done | bytes 2097184 | tf_op jit(solution)/shard_map/all_to_all | solution.py:307
  233.3 4.4 %all-to-all-start.3 = ((bf16[4,128,2048]{2,1,0:T(8,128)(2,1)}), bf16[4,128,2048]{2,1,0:T(8,128)(2,1)}, u32[]{:S(2)}, u32[]{:S(2)}) async-start(bf16[4,128,2048]{2,1,0:T(8,128)(2,1)} %shard_map.93.o_ref), calls=%async_computation.3 | async-start | bytes 4194304 | tf_op jit(solution)/shard_map/all_to_all | solution.py:306
  237.9 0.9 bitcast_dynamic-update-slice_fusion.5
  238.8 1.5 collective-permute-start.5
  240.4 0.9 bitcast_dynamic-update-slice_fusion.4
  241.2 1.8 bitcast_dynamic-update-slice_fusion.3
  243.1 1.8 bitcast_dynamic-update-slice_fusion.2
  244.9 1.8 bitcast_dynamic-update-slice_fusion.1
  246.8 0.9 bitcast_dynamic-update-slice_fusion
  247.6 7.3 %gather_fusion.2 = bf16[8,2,2,128,256]{4,1,3,2,0:T(2,128)(2,1)} fusion(bf16[8,2,2,128,256]{4,1,3,2,0:T(2,128)(2,1)} %bitcast_dynamic-update-slice_fusion, s32[1024]{0:T(1024)S(1)} %pad_clamp_fusion), kind=kCustom, calls=%fused_computation.2 | custom fusion | bytes 4194336 | tf_op jit(solution)/shard_map/jit(_take)/gather | solution.py:119
  255.1 3.5 %broadcast_select_fusion = bf16[8,2,2,128,256]{4,1,3,2,0:T(2,128)(2,1)S(1)} fusion(bf16[8,2,2,128,256]{4,1,3,2,0:T(2,128)(2,1)} %gather_fusion.2, pred[8]{0:T(512)(128)(4,1)S(1)} %compare_and_fusion.2), kind=kLoop, calls=%fused_computation.4 | loop fusion | flops 1048576 | bytes 4194312 | tf_op jit(solution)/shard_map/jit(_take)/select_n | solution.py:119
  258.6 1.3 fusion.8
  259.9 2.9 collective-permute-done.6
  263.6 0.9 reshape.424
  264.5 2.5 copy.136
  267.0 19.5 %all-to-all-done.3 = bf16[4,128,2048]{2,1,0:T(8,128)(2,1)} async-done(((bf16[4,128,2048]{2,1,0:T(8,128)(2,1)}), bf16[4,128,2048]{2,1,0:T(8,128)(2,1)}, u32[]{:S(2)}, u32[]{:S(2)}) %all-to-all-start.3) | async-done | bytes 2097184 | tf_op jit(solution)/shard_map/all_to_all | solution.py:306
  286.5 3.9 %copy.135 = bf16[1,128,4,2048]{1,3,2,0:T(8,128)(2,1)} copy(bf16[1,128,4,2048]{3,1,2,0:T(8,128)(2,1)} %bitcast.37) | data formatting | bytes 4194304 | tf_op jit(solution)/shard_map/all_to_all | solution.py:306
  290.4 3.5 %all-to-all-start.5 = ((bf16[4,2,128,2,128]{4,3,2,1,0:T(2,128)(2,1)}), bf16[4,2,128,2,128]{4,3,2,1,0:T(2,128)(2,1)S(1)}, u32[]{:S(2)}, u32[]{:S(2)}) async-start(bf16[4,2,128,2,128]{4,3,2,1,0:T(2,128)(2,1)} %reshape.424), calls=%async_computation.5 | async-start | bytes 1048576 | tf_op jit(solution)/shard_map/all_to_all | solution.py:312
  293.9 4.3 %copy.153 = bf16[128,64,128]{2,1,0:T(8,128)(2,1)} copy(bf16[128,64,128]{0,2,1:T(8,128)(2,1)} %bitcast.145) | data formatting | bytes 4194304
  298.2 2.8 copy.154
  300.9 7.0 %all-to-all-done.5 = bf16[4,2,128,2,128]{4,3,2,1,0:T(2,128)(2,1)S(1)} async-done(((bf16[4,2,128,2,128]{4,3,2,1,0:T(2,128)(2,1)}), bf16[4,2,128,2,128]{4,3,2,1,0:T(2,128)(2,1)S(1)}, u32[]{:S(2)}, u32[]{:S(2)}) %all-to-all-start.5) | async-done | bytes 524320 | tf_op jit(solution)/shard_map/all_to_all | solution.py:312
  308.3 0.9 copy.151
  309.2 0.9 copy.152
  (91 shorter events, 7.0 us)
Async XLA Ops:
  7.2 77.6 %all-gather.2.cloned.1.call-start = ((), (), s32[]{:S(2)}) async-start(), calls=%async_computation.6 | async-start | bytes 4718592 | tf_op jit(solution)/shard_map/all_gather | solution.py:213
  8.4 21.0 %copy-start.4 = (bf16[128,64,128]{2,1,0:T(8,128)(2,1)S(1)}, bf16[128,64,128]{2,1,0:T(8,128)(2,1)}, u32[]{:S(2)}) copy-start(bf16[128,64,128]{2,1,0:T(8,128)(2,1)} %param.10) | copy-start | bytes 6291460
  32.1 3.8 %copy-start.8 = (s32[32,3]{0,1:T(4,128)S(1)}, s32[32,3]{0,1:T(4,128)}, u32[]{:S(2)}) copy-start(s32[32,3]{0,1:T(4,128)} %param.15) | copy-start | bytes 1156
  32.1 51.1 %all-to-all-start = ((bf16[64,128,128]{2,1,0:T(8,128)(2,1)}), bf16[64,128,128]{2,1,0:T(8,128)(2,1)S(1)}, u32[]{:S(2)}, u32[]{:S(2)}) async-start(bf16[64,128,128]{2,1,0:T(8,128)(2,1)} %bitcast.143), calls=%async_computation | async-start | bytes 4194304 | tf_op jit(solution)/shard_map/all_to_all | solution.py:160
  36.0 4.9 %copy-start.9 = (s32[2]{0:T(128)S(1)}, s32[2]{0:T(128)}, u32[]{:S(2)}) copy-start(s32[2]{0:T(128)} %param.14) | copy-start | bytes 28
  84.8 4.4 %copy-start = (bf16[2,512,256]{2,1,0:T(8,128)(2,1)S(1)}, bf16[2,512,256]{2,1,0:T(8,128)(2,1)}, u32[]{:S(2)}) copy-start(bf16[2,512,256]{2,1,0:T(8,128)(2,1)} %reshape.410) | copy-start | bytes 1572868
  84.8 55.0 %all-to-all-start.2 = ((bf16[64,128,128]{2,1,0:T(8,128)(2,1)}), bf16[64,128,128]{2,1,0:T(8,128)(2,1)S(1)}, u32[]{:S(2)}, u32[]{:S(2)}) async-start(bf16[64,128,128]{2,1,0:T(8,128)(2,1)} %bitcast.131), calls=%async_computation.2 | async-start | bytes 4194304 | tf_op jit(solution)/shard_map/all_to_all | solution.py:216
  89.2 7.3 %collective-permute-start = (bf16[2,128,256]{2,1,0:T(8,128)(2,1)S(1)}, bf16[2,128,256]{2,1,0:T(8,128)(2,1)S(1)}, u32[]{:S(2)}, u32[]{:S(2)}) collective-permute-start(bf16[2,128,256]{2,1,0:T(8,128)(2,1)S(1)} %get-tuple-element.89), channel_id=1, source_target_pairs={{0,4},{4,8},{8,12},{12,16},{16,20},{20,24},{24,28},{1,5},{5,9},{9,... | collective-permute-start | bytes 393224 | tf_op jit(solution)/shard_map/ppermute | solution.py:134
  91.1 7.0 %collective-permute-start.1 = (bf16[2,128,256]{2,1,0:T(8,128)(2,1)S(1)}, bf16[2,128,256]{2,1,0:T(8,128)(2,1)S(1)}, u32[]{:S(2)}, u32[]{:S(2)}) collective-permute-start(bf16[2,128,256]{2,1,0:T(8,128)(2,1)S(1)} %get-tuple-element.90), channel_id=1, source_target_pairs={{4,0},{8,4},{12,8},{16,12},{20,16},{24,20},{28,24},{5,1},{9,5},{13... | collective-permute-start | bytes 393224 | tf_op jit(solution)/shard_map/ppermute | solution.py:135
  108.8 2.3 copy-start.5
  178.8 54.5 %all-to-all-start.4 = ((bf16[4,128,2048]{2,1,0:T(8,128)(2,1)}), bf16[4,128,2048]{2,1,0:T(8,128)(2,1)S(1)}, u32[]{:S(2)}, u32[]{:S(2)}) async-start(bf16[4,128,2048]{2,1,0:T(8,128)(2,1)} %get-tuple-element.43), calls=%async_computation.4 | async-start | bytes 4194304 | tf_op jit(solution)/shard_map/all_to_all | solution.py:307
  185.8 22.2 %collective-permute-start.4 = (bf16[2,2,128,256]{3,2,1,0:T(8,128)(2,1)S(1)}, bf16[2,2,128,256]{3,2,1,0:T(8,128)(2,1)S(1)}, u32[]{:S(2)}, u32[]{:S(2)}) collective-permute-start(bf16[2,2,128,256]{3,2,1,0:T(8,128)(2,1)S(1)} %convert_element_type.59), channel_id=1, source_target_pairs={{0,4},{4,0},{8,12},{12,8},{16,20},{20,16},{24,28},{28,24},{1,5},{5... | collective-permute-start | bytes 786440 | tf_op jit(solution)/shard_map/ppermute | solution.py:152
  190.2 14.6 %collective-permute-start.2 = (bf16[2,128,256]{2,1,0:T(8,128)(2,1)S(1)}, bf16[2,128,256]{2,1,0:T(8,128)(2,1)S(1)}, u32[]{:S(2)}, u32[]{:S(2)}) collective-permute-start(bf16[2,128,256]{2,1,0:T(8,128)(2,1)S(1)} %get-tuple-element.81), channel_id=1, source_target_pairs={{0,4},{4,8},{8,12},{12,16},{16,20},{20,24},{24,28},{1,5},{5,9},{9,... | collective-permute-start | bytes 393224 | tf_op jit(solution)/shard_map/ppermute | solution.py:134
  192.1 15.2 %collective-permute-start.3 = (bf16[2,128,256]{2,1,0:T(8,128)(2,1)S(1)}, bf16[2,128,256]{2,1,0:T(8,128)(2,1)S(1)}, u32[]{:S(2)}, u32[]{:S(2)}) collective-permute-start(bf16[2,128,256]{2,1,0:T(8,128)(2,1)S(1)} %get-tuple-element.82), channel_id=1, source_target_pairs={{4,0},{8,4},{12,8},{16,12},{20,16},{24,20},{28,24},{5,1},{9,5},{13... | collective-permute-start | bytes 393224 | tf_op jit(solution)/shard_map/ppermute | solution.py:135
  199.0 0.7 copy-start.7
  203.6 8.8 %collective-permute-start.7 = (bf16[2,2,128,256]{3,0,2,1:T(2,128)(2,1)S(1)}, bf16[2,2,128,256]{3,0,2,1:T(2,128)(2,1)S(1)}, u32[]{:S(2)}, u32[]{:S(2)}) collective-permute-start(bf16[2,2,128,256]{3,0,2,1:T(2,128)(2,1)S(1)} %get-tuple-element.76), channel_id=1, source_target_pairs={{0,4},{4,8},{8,12},{12,16},{16,20},{20,24},{24,28},{28,0},{1,5},{5... | collective-permute-start | bytes 786440 | tf_op jit(solution)/shard_map/ppermute | solution.py:116
  203.7 34.1 %collective-permute-start.8 = (bf16[2,2,128,256]{3,0,2,1:T(2,128)(2,1)}, bf16[2,2,128,256]{3,0,2,1:T(2,128)(2,1)S(1)}, u32[]{:S(2)}, u32[]{:S(2)}) collective-permute-start(bf16[2,2,128,256]{3,0,2,1:T(2,128)(2,1)} %get-tuple-element.75), channel_id=1, source_target_pairs={{0,8},{4,12},{8,16},{12,20},{16,24},{20,28},{24,0},{28,4},{1,9},{5... | collective-permute-start | bytes 786440 | tf_op jit(solution)/shard_map/ppermute | solution.py:116
  204.8 34.1 %collective-permute-start.9 = (bf16[2,2,128,256]{3,0,2,1:T(2,128)(2,1)}, bf16[2,2,128,256]{3,0,2,1:T(2,128)(2,1)S(1)}, u32[]{:S(2)}, u32[]{:S(2)}) collective-permute-start(bf16[2,2,128,256]{3,0,2,1:T(2,128)(2,1)} %get-tuple-element.74), channel_id=1, source_target_pairs={{0,12},{4,16},{8,20},{12,24},{16,28},{20,0},{24,4},{28,8},{1,13},{... | collective-permute-start | bytes 786440 | tf_op jit(solution)/shard_map/ppermute | solution.py:116
  207.3 34.0 %collective-permute-start.10 = (bf16[2,2,128,256]{3,0,2,1:T(2,128)(2,1)}, bf16[2,2,128,256]{3,0,2,1:T(2,128)(2,1)}, u32[]{:S(2)}, u32[]{:S(2)}) collective-permute-start(bf16[2,2,128,256]{3,0,2,1:T(2,128)(2,1)} %get-tuple-element.73), channel_id=1, source_target_pairs={{0,16},{4,20},{8,24},{12,28},{16,0},{20,4},{24,8},{28,12},{1,17},{... | collective-permute-start | bytes 786440 | tf_op jit(solution)/shard_map/ppermute | solution.py:116
  208.0 4.6 %copy-start.2 = (f32[4,2,128,256]{3,2,1,0:T(8,128)}, f32[4,2,128,256]{3,2,1,0:T(8,128)S(1)}, u32[]{:S(2)}) copy-start(f32[4,2,128,256]{3,2,1,0:T(8,128)S(1)} %fusion.22) | copy-start | bytes 3145732
  208.0 35.1 %collective-permute-start.11 = (bf16[2,2,128,256]{3,0,2,1:T(2,128)(2,1)}, bf16[2,2,128,256]{3,0,2,1:T(2,128)(2,1)}, u32[]{:S(2)}, u32[]{:S(2)}) collective-permute-start(bf16[2,2,128,256]{3,0,2,1:T(2,128)(2,1)} %get-tuple-element.72), channel_id=1, source_target_pairs={{0,20},{4,24},{8,28},{12,0},{16,4},{20,8},{24,12},{28,16},{1,21},{... | collective-permute-start | bytes 786440 | tf_op jit(solution)/shard_map/ppermute | solution.py:116
  212.4 32.5 %collective-permute-start.12 = (bf16[2,2,128,256]{3,0,2,1:T(2,128)(2,1)}, bf16[2,2,128,256]{3,0,2,1:T(2,128)(2,1)}, u32[]{:S(2)}, u32[]{:S(2)}) collective-permute-start(bf16[2,2,128,256]{3,0,2,1:T(2,128)(2,1)} %get-tuple-element.71), channel_id=1, source_target_pairs={{0,24},{4,28},{8,0},{12,4},{16,8},{20,12},{24,16},{28,20},{1,25},{... | collective-permute-start | bytes 786440 | tf_op jit(solution)/shard_map/ppermute | solution.py:116
  233.3 53.1 %all-to-all-start.3 = ((bf16[4,128,2048]{2,1,0:T(8,128)(2,1)}), bf16[4,128,2048]{2,1,0:T(8,128)(2,1)}, u32[]{:S(2)}, u32[]{:S(2)}) async-start(bf16[4,128,2048]{2,1,0:T(8,128)(2,1)} %shard_map.93.o_ref), calls=%async_computation.3 | async-start | bytes 4194304 | tf_op jit(solution)/shard_map/all_to_all | solution.py:306
  237.8 9.0 %collective-permute-start.13 = (bf16[2,2,128,256]{3,0,2,1:T(2,128)(2,1)}, bf16[2,2,128,256]{3,0,2,1:T(2,128)(2,1)S(1)}, u32[]{:S(2)}, u32[]{:S(2)}) collective-permute-start(bf16[2,2,128,256]{3,0,2,1:T(2,128)(2,1)} %get-tuple-element.70), channel_id=1, source_target_pairs={{0,28},{4,0},{8,4},{12,8},{16,12},{20,16},{24,20},{28,24},{1,29},{... | collective-permute-start | bytes 786440 | tf_op jit(solution)/shard_map/ppermute | solution.py:116
  238.8 16.2 %collective-permute-start.5 = (bf16[2,2,128,256]{3,2,1,0:T(8,128)(2,1)}, bf16[2,2,128,256]{3,2,1,0:T(8,128)(2,1)S(1)}, u32[]{:S(2)}, u32[]{:S(2)}) collective-permute-start(bf16[2,2,128,256]{3,2,1,0:T(8,128)(2,1)} %fusion.21), channel_id=1, source_target_pairs={{0,8},{4,12},{8,0},{12,4},{16,24},{20,28},{24,16},{28,20},{1,9},{5... | collective-permute-start | bytes 786440 | tf_op jit(solution)/shard_map/ppermute | solution.py:152
  255.1 7.7 %collective-permute-start.6 = (bf16[2,2,128,256]{3,2,1,0:T(8,128)(2,1)S(1)}, bf16[2,2,128,256]{3,2,1,0:T(8,128)(2,1)S(1)}, u32[]{:S(2)}, u32[]{:S(2)}) collective-permute-start(bf16[2,2,128,256]{3,2,1,0:T(8,128)(2,1)S(1)} %fusion.25), channel_id=1, source_target_pairs={{0,16},{4,20},{8,24},{12,28},{16,0},{20,4},{24,8},{28,12},{1,17},{... | collective-permute-start | bytes 786440 | tf_op jit(solution)/shard_map/ppermute | solution.py:152
  258.6 4.3 %copy-start.6 = (f32[2,4]{1,0:T(2,128)S(1)}, f32[2,4]{1,0:T(2,128)}, u32[]{:S(2)}) copy-start(f32[2,4]{1,0:T(2,128)} %and_convert_fusion) | copy-start | bytes 100
  259.9 3.3 %copy-start.3 = (f32[4,2,128,256]{3,2,1,0:T(8,128)S(1)}, f32[4,2,128,256]{3,2,1,0:T(8,128)}, u32[]{:S(2)}) copy-start(f32[4,2,128,256]{3,2,1,0:T(8,128)} %copy-done.2) | copy-start | bytes 3145732
  290.4 17.5 %all-to-all-start.5 = ((bf16[4,2,128,2,128]{4,3,2,1,0:T(2,128)(2,1)}), bf16[4,2,128,2,128]{4,3,2,1,0:T(2,128)(2,1)S(1)}, u32[]{:S(2)}, u32[]{:S(2)}) async-start(bf16[4,2,128,2,128]{4,3,2,1,0:T(2,128)(2,1)} %reshape.424), calls=%async_computation.5 | async-start | bytes 1048576 | tf_op jit(solution)/shard_map/all_to_all | solution.py:312
  293.9 4.3 %copy-start.1 = (bf16[1,128,4,2048]{1,3,2,0:T(8,128)(2,1)S(1)}, bf16[1,128,4,2048]{1,3,2,0:T(8,128)(2,1)}, u32[]{:S(2)}) copy-start(bf16[1,128,4,2048]{1,3,2,0:T(8,128)(2,1)} %copy.136) | copy-start | bytes 6291460
Sparse Core Ops, SparseCore 0:
  29.5 35.4 all-gather.1

commit v14 on v12

--- a/solution.py
+++ b/solution.py
@@ -20,25 +20,31 @@
         ref[:, g * width:(g + 1) * width] = value[g * tokens:(g + 1) * tokens, :]
 
 
-def softmax_rows(q, k, bias, scale):
+def scores_of(q, k, bias, scale):
     rows_by_cols = (((1,), (1,)), ((), ()))
     s = lax.dot_general(q, k, rows_by_cols, preferred_element_type=jnp.float32) * scale
-    s = s + bias
-    e = jnp.exp(s - jnp.max(s, axis=1, keepdims=True))
-    return e / jnp.sum(e, axis=1, keepdims=True)
-
-
-def forward_kernel(q_ref, k_ref, v_ref, bias_ref, out_ref, *, scale):
+    return s + bias
+
+
+def forward_kernel(q_ref, k_ref, v_ref, bias_ref, out_ref, max_ref, sum_ref, *, scale):
     width = k_ref.shape[-1]
     q = q_ref[...].reshape(-1, width)
     k = k_ref[...].reshape(-1, width)
     v = v_ref[...].reshape(-1, width)
-    p_low = softmax_rows(q, k, bias_ref[...], scale).astype(jnp.bfloat16)
+    s = scores_of(q, k, bias_ref[...], scale)
+    row_max = jnp.max(s, axis=1, keepdims=True)
+    e = jnp.exp(s - row_max)
+    row_sum = jnp.sum(e, axis=1, keepdims=True)
+    max_ref[...] = row_max
+    sum_ref[...] = row_sum
+    p_low = (e / row_sum).astype(jnp.bfloat16)
     o_low = jnp.dot(p_low, v, preferred_element_type=jnp.float32).astype(jnp.bfloat16)
     out_ref[...] = o_low.reshape(out_ref.shape)
 
 
-def backward_kernel(q_ref, k_ref, v_ref, do_ref, o_ref, bias_ref, dq_ref, grad_ref, *, scale):
+def backward_kernel(
+    q_ref, k_ref, v_ref, do_ref, o_ref, bias_ref, max_ref, sum_ref, dq_ref, grad_ref, *, scale
+):
     width = k_ref.shape[-1]
     q = q_ref[...].reshape(-1, width)
     do = do_ref[...].reshape(-1, width)
@@ -47,7 +53,7 @@
     v = v_ref[...].reshape(-1, width)
     rows_by_cols = (((1,), (1,)), ((), ()))
     over_rows = (((0,), (0,)), ((), ()))
-    p = softmax_rows(q, k, bias_ref[...], scale)
+    p = jnp.exp(scores_of(q, k, bias_ref[...], scale) - max_ref[...]) / sum_ref[...]
     p_low = p.astype(jnp.bfloat16)
     delta = jnp.sum(do.astype(jnp.float32) * o_low.astype(jnp.float32), axis=1, keepdims=True)
     dp = lax.dot_general(do, v, rows_by_cols, preferred_element_type=jnp.float32)
@@ -66,6 +72,8 @@
     rows_width = group * head_width
     q_spec = pl.BlockSpec((None, group, None, tokens, head_width), lambda j, h: (h, 0, j, 0, 0))
     o_spec = pl.BlockSpec((None, None, group, tokens, head_width), lambda j, h: (j, h, 0, 0, 0))
+    r_spec = pl.BlockSpec((None, None, group * tokens, 1), lambda j, h: (j, h, 0, 0))
+    r_shape = jax.ShapeDtypeStruct((blocks, heads_kv, group * tokens, 1), jnp.float32)
     o_shape = jax.ShapeDtypeStruct((blocks, heads_kv, group, tokens, head_width), jnp.bfloat16)
     k_spec = pl.BlockSpec((None, tile_count, None, tokens, head_width), lambda j, h: (j, 0, 0, 0, h))
     v_spec = pl.BlockSpec((None, tile_count, None, tokens, head_width), lambda j, h: (j, 0, 1, 0, h))
@@ -83,9 +91,10 @@
         ),
         grid=(blocks, heads_kv),
         in_specs=[q_spec, k_spec, v_spec, b_spec],
-        out_specs=o_spec,
-        out_shape=o_shape,
+        out_specs=[o_spec, r_spec, r_spec],
+        out_shape=[o_shape, r_shape, r_shape],
     )(q, tiles, tiles, bias)
+    out, row_max, row_sum = out
     out, do = lax.optimization_barrier((out, do))
     grad_q, grads = pl.pallas_call(
         functools.partial(backward_kernel, scale=scale),
@@ -93,13 +102,13 @@
             flops=5 * matmul, transcendentals=rows * keys_n * steps, bytes_accessed=moved
         ),
         grid=(blocks, heads_kv),
-        in_specs=[q_spec, k_spec, v_spec, q_spec, o_spec, b_spec],
+        in_specs=[q_spec, k_spec, v_spec, q_spec, o_spec, b_spec, r_spec, r_spec],
         out_specs=[o_spec, g_spec],
         out_shape=[
             o_shape,
             jax.ShapeDtypeStruct(tiles.shape, jnp.float32),
         ],
-    )(q, tiles, tiles, do, out, bias)
+    )(q, tiles, tiles, do, out, bias, row_max, row_sum)
     return out, grad_q, grads
 
 

time: 317 us -> 311 us (0.981)
  Pallas kernels: 62.8 us -> 55.7 us
    pallas_call x1, Pallas kernels: 37.5 us -> 30.4 us  [attention_call(): pl.pallas_call(functools.partial(backward_kernel, scale=scale), cost_esti...]
  transfers between devices with their start and end apart: 19 -> 19, of which waited for: 7 -> 7; matrix products, arithmetic and copies ran while one was open for 21% -> 22% of each run, Pallas kernels for 8% -> 8%
where the time goes in v14:
time: 311 us; the launch traced here: 309 us
  waiting for transfers between devices  85.1 us (27%)
  local copies, waits for them, and re-layouts  61.2 us (20%)
  Pallas kernels  55.7 us (18%)
  starting transfers between devices  39.3 us (13%)
  blocking collectives  35.8 us (12%)
  other arithmetic  15.1 us (5%)
  between operations  14.6 us (5%)
    all_to_all x1, waiting for transfers between devices, per_device(): lax.all_to_all(queries.transpose(1, 0, 2), 'head', split_axis=0, concat_a...  40.8 us
    pallas_call x1, Pallas kernels, attention_call(): pl.pallas_call(functools.partial(backward_kernel, scale=scale), cost_esti...  30.4 us
    pallas_call x1, Pallas kernels, attention_call(): pl.pallas_call(functools.partial(forward_kernel, scale=scale), cost_estim...  25.3 us
    all_to_all x1, waiting for transfers between devices, per_device(): lax.all_to_all(out_all, 'head', split_axis=0, concat_axis=1, tiled=True)  20.3 us
    all_to_all x1, blocking collectives, per_device(): lax.all_to_all(jnp.stack([keys, values]), 'head', split_axis=2, concat_ax...  19.3 us
    unnamed x27, local copies, waits for them, and re-layouts  16.8 us
    all_to_all x1, blocking collectives, per_device(): lax.all_to_all(kv_blocks, 'head', split_axis=0, concat_axis=3, tiled=True)  16.5 us
    all_to_all x1, waiting for transfers between devices, per_device(): lax.all_to_all(query_grad_all, 'head', split_axis=0, concat_axis=1, tiled...  15.2 us
  transfers between devices with their start and end apart: 19, of which 7 were waited for; matrix products, arithmetic and copies ran while one was open for 22% of the time, Pallas kernels for 8%

profile of v14, /device:TPU:4, one launch (start us, length us, event | category | flops | bytes accessed | tf_op | source)
XLA Modules:
  0.0 309.3 jit_solution(9072275868928171417)
XLA Ops:
  7.2 1.1 copy_bitcast_fusion.8
  8.4 19.3 %all_to_all.87 = bf16[2,128,8,128]{3,1,0,2:T(8,128)(2,1)S(1)} all-to-all(bf16[2,128,8,128]{3,1,0,2:T(8,128)(2,1)S(1)} %pad_maximum_fusion.5), channel_id=1, replica_groups=mesh['seq'=8,'head'=4] {'head'}, dimensions={2} | all-to-all | bytes 1048576 | tf_op jit(solution)/shard_map/all_to_all | solution.py:174
  27.7 0.5 copy.182
  28.3 1.1 reshape.422
  29.4 2.7 copy.180
  32.1 3.7 %all-to-all-start = ((bf16[64,128,128]{2,1,0:T(8,128)(2,1)}), bf16[64,128,128]{2,1,0:T(8,128)(2,1)S(1)}, u32[]{:S(2)}, u32[]{:S(2)}) async-start(bf16[64,128,128]{2,1,0:T(8,128)(2,1)} %bitcast.142), calls=%async_computation | async-start | bytes 4194304 | tf_op jit(solution)/shard_map/all_to_all | solution.py:169
  36.0 4.4 %copy.179 = bf16[128,64,128]{2,0,1:T(8,128)(2,1)} copy(bf16[128,64,128]{2,1,0:T(8,128)(2,1)} %param.13) | data formatting | bytes 4194304 | tf_op args[3]
  41.3 0.5 fusion.45
  41.8 0.6 and_convert_fusion
  42.4 40.8 %all-to-all-done = bf16[64,128,128]{2,1,0:T(8,128)(2,1)S(1)} async-done(((bf16[64,128,128]{2,1,0:T(8,128)(2,1)}), bf16[64,128,128]{2,1,0:T(8,128)(2,1)S(1)}, u32[]{:S(2)}, u32[]{:S(2)}) %all-to-all-start) | async-done | bytes 2097184 | tf_op jit(solution)/shard_map/all_to_all | solution.py:169
  83.2 1.6 copy.118
  84.8 3.7 %all-to-all-start.2 = ((bf16[64,128,128]{2,1,0:T(8,128)(2,1)}), bf16[64,128,128]{2,1,0:T(8,128)(2,1)S(1)}, u32[]{:S(2)}, u32[]{:S(2)}) async-start(bf16[64,128,128]{2,1,0:T(8,128)(2,1)} %bitcast.131), calls=%async_computation.2 | async-start | bytes 4194304 | tf_op jit(solution)/shard_map/all_to_all | solution.py:225
  89.2 1.9 collective-permute-start
  91.1 4.7 %collective-permute-start.1 = (bf16[2,128,256]{2,1,0:T(8,128)(2,1)S(1)}, bf16[2,128,256]{2,1,0:T(8,128)(2,1)S(1)}, u32[]{:S(2)}, u32[]{:S(2)}) collective-permute-start(bf16[2,128,256]{2,1,0:T(8,128)(2,1)S(1)} %get-tuple-element.80), channel_id=1, source_target_pairs={{4,0},{8,4},{12,8},{16,12},{20,16},{24,20},{28,24},{5,1},{9,5},{13... | collective-permute-start | bytes 393224 | tf_op jit(solution)/shard_map/ppermute | solution.py:144
  95.8 0.5 fusion.44
  96.5 1.7 collective-permute-done.1
  98.4 0.8 copy.186
  99.2 4.0 %gather_fusion.1 = bf16[12,2,128,256]{3,2,1,0:T(8,128)(2,1)} fusion(bf16[2,32,128,256]{3,2,1,0:T(8,128)(2,1)} %bitcast.163, s32[1024]{0:T(1024)S(1)} %get-tuple-element.91), kind=kCustom, calls=%fused_computation.1 | custom fusion | bytes 3145776 | tf_op jit(solution)/shard_map/jit(_take)/gather | solution.py:227
  103.2 1.6 broadcast_select_fusion.1
  104.8 1.2 copy.181
  106.1 2.7 gather_fusion
  108.8 0.8 broadcast_select_fusion.2
  109.6 1.5 slice_bitcast_fusion.6
  111.6 2.3 pad_maximum_fusion.k_ref.v_ref
  113.8 0.7 broadcast_in_dim.79
  114.5 25.3 %shard_map.93 = (bf16[4,2,8,128,128]{4,3,2,1,0:T(8,128)(2,1)}, f32[4,2,1024,1]{3,2,1,0:T(8,128)}, f32[4,2,1024,1]{3,2,1,0:T(8,128)}) custom-call(bf16[2,8,4,128,128]{4,3,2,1,0:T(8,128)(2,1)} %bitcast.147, bf16[4,8,2,128,256]{4,3,2,1,0:T(8,128)(2,1)} %pad_maximum_fusion.k_ref.v_ref, bf16[4,8,2,128,256]{4,3,2,1,0:T(8,128)(2,1)} %pad_maximum_fusion.k_ref.v_ref, ...), custom_call_target="tpu_custom_call" | custom-call | flops 4294967296 | bytes 23068672 | tf_op jit(solution)/shard_map/pallas_call | solution.py:87
  139.8 1.7 copy.130
  141.5 30.4 %shard_map.94 = (bf16[4,2,8,128,128]{4,3,2,1,0:T(8,128)(2,1)}, f32[4,8,2,128,256]{4,3,2,1,0:T(8,128)}) custom-call(bf16[2,8,4,128,128]{4,3,2,1,0:T(8,128)(2,1)} %bitcast.148, bf16[4,8,2,128,256]{4,3,2,1,0:T(8,128)(2,1)} %pad_maximum_fusion.k_ref.v_ref, bf16[4,8,2,128,256]{4,3,2,1,0:T(8,128)(2,1)} %pad_maximum_fusion.k_ref.v_ref, ...), custom_call_target="tpu_custom_call" | custom-call | flops 10737418240 | bytes 23068672 | tf_op jit(solution)/shard_map/pallas_call | solution.py:99
  171.9 5.1 %all-to-all-start.4 = ((bf16[4,16,128,128]{3,2,1,0:T(8,128)(2,1)}), bf16[4,16,128,128]{3,2,1,0:T(8,128)(2,1)S(1)}, u32[]{:S(2)}, u32[]{:S(2)}) async-start(bf16[4,16,128,128]{3,2,1,0:T(8,128)(2,1)} %bitcast.146), calls=%async_computation.4 | async-start | bytes 4194304 | tf_op jit(solution)/shard_map/all_to_all | solution.py:316
  177.1 1.8 slice_reduce_fusion
  178.9 0.9 collective-permute-start.4
  179.8 1.3 slice_bitcast_fusion.2
  181.1 1.7 slice_bitcast_fusion.1
  183.3 1.9 collective-permute-start.2
  185.2 4.8 %collective-permute-start.3 = (bf16[2,128,256]{2,1,0:T(8,128)(2,1)S(1)}, bf16[2,128,256]{2,1,0:T(8,128)(2,1)S(1)}, u32[]{:S(2)}, u32[]{:S(2)}) collective-permute-start(bf16[2,128,256]{2,1,0:T(8,128)(2,1)S(1)} %get-tuple-element.72), channel_id=1, source_target_pairs={{4,0},{8,4},{12,8},{16,12},{20,16},{24,20},{28,24},{5,1},{9,5},{13... | collective-permute-start | bytes 393224 | tf_op jit(solution)/shard_map/ppermute | solution.py:144
  190.0 2.1 fusion.7
  192.2 0.5 copy-done.6
  192.7 1.0 fusion.4
  193.8 2.8 constant_dynamic-slice_fusion
  196.8 1.0 bitcast_dynamic-update-slice_fusion.7
  197.7 2.5 collective-permute-start.9
  200.3 0.6 collective-permute-start.10
  201.1 0.9 fusion.21
  202.0 3.6 %collective-permute-done.7 = bf16[2,2,128,256]{3,0,2,1:T(2,128)(2,1)S(1)} collective-permute-done((bf16[2,2,128,256]{3,0,2,1:T(2,128)(2,1)S(1)}, bf16[2,2,128,256]{3,0,2,1:T(2,128)(2,1)S(1)}, u32[]{:S(2)}, u32[]{:S(2)}) %collective-permute-start.7) | collective-permute-done | bytes 262176 | tf_op jit(solution)/shard_map/ppermute | solution.py:125
  205.8 0.9 bitcast_dynamic-update-slice_fusion.6
  206.9 4.3 %collective-permute-start.13 = (bf16[2,2,128,256]{3,0,2,1:T(2,128)(2,1)}, bf16[2,2,128,256]{3,0,2,1:T(2,128)(2,1)}, u32[]{:S(2)}, u32[]{:S(2)}) collective-permute-start(bf16[2,2,128,256]{3,0,2,1:T(2,128)(2,1)} %get-tuple-element.60), channel_id=1, source_target_pairs={{0,28},{4,0},{8,4},{12,8},{16,12},{20,16},{24,20},{28,24},{1,29},{... | collective-permute-start | bytes 786440 | tf_op jit(solution)/shard_map/ppermute | solution.py:125
  211.2 15.2 %all-to-all-done.4 = bf16[4,16,128,128]{3,2,1,0:T(8,128)(2,1)S(1)} async-done(((bf16[4,16,128,128]{3,2,1,0:T(8,128)(2,1)}), bf16[4,16,128,128]{3,2,1,0:T(8,128)(2,1)S(1)}, u32[]{:S(2)}, u32[]{:S(2)}) %all-to-all-start.4) | async-done | bytes 2097184 | tf_op jit(solution)/shard_map/all_to_all | solution.py:316
  226.4 4.5 %all-to-all-start.3 = ((bf16[4,16,128,128]{3,2,1,0:T(8,128)(2,1)}), bf16[4,16,128,128]{3,2,1,0:T(8,128)(2,1)}, u32[]{:S(2)}, u32[]{:S(2)}) async-start(bf16[4,16,128,128]{3,2,1,0:T(8,128)(2,1)} %bitcast.145), calls=%async_computation.3 | async-start | bytes 4194304 | tf_op jit(solution)/shard_map/all_to_all | solution.py:315
  230.9 0.9 bitcast_dynamic-update-slice_fusion.5
  231.8 0.9 bitcast_dynamic-update-slice_fusion.4
  232.7 1.8 bitcast_dynamic-update-slice_fusion.3
  234.5 1.8 bitcast_dynamic-update-slice_fusion.2
  236.3 1.8 bitcast_dynamic-update-slice_fusion.1
  238.2 1.8 bitcast_dynamic-update-slice_fusion
  240.0 7.3 %gather_fusion.2 = bf16[8,2,2,128,256]{4,1,3,2,0:T(2,128)(2,1)} fusion(bf16[8,2,2,128,256]{4,1,3,2,0:T(2,128)(2,1)} %bitcast_dynamic-update-slice_fusion, s32[1024]{0:T(1024)S(1)} %pad_clamp_fusion), kind=kCustom, calls=%fused_computation.2 | custom fusion | bytes 4194336 | tf_op jit(solution)/shard_map/jit(_take)/gather | solution.py:128
  247.7 3.5 %broadcast_select_fusion = bf16[8,2,2,128,256]{4,1,3,2,0:T(2,128)(2,1)S(1)} fusion(bf16[8,2,2,128,256]{4,1,3,2,0:T(2,128)(2,1)} %gather_fusion.2, pred[8]{0:T(512)(128)(4,1)S(1)} %compare_and_fusion.2), kind=kLoop, calls=%fused_computation.4 | loop fusion | flops 1048576 | bytes 4194312 | tf_op jit(solution)/shard_map/jit(_take)/select_n | solution.py:128
  251.2 1.3 fusion.8
  252.5 3.2 %collective-permute-done.6 = bf16[2,2,128,256]{3,2,1,0:T(8,128)(2,1)S(1)} collective-permute-done((bf16[2,2,128,256]{3,2,1,0:T(8,128)(2,1)S(1)}, bf16[2,2,128,256]{3,2,1,0:T(8,128)(2,1)S(1)}, u32[]{:S(2)}, u32[]{:S(2)}) %collective-permute-start.6) | collective-permute-done | bytes 262176 | tf_op jit(solution)/shard_map/ppermute | solution.py:161
  256.6 2.7 copy.132
  259.3 20.3 %all-to-all-done.3 = bf16[4,16,128,128]{3,2,1,0:T(8,128)(2,1)} async-done(((bf16[4,16,128,128]{3,2,1,0:T(8,128)(2,1)}), bf16[4,16,128,128]{3,2,1,0:T(8,128)(2,1)}, u32[]{:S(2)}, u32[]{:S(2)}) %all-to-all-start.3) | async-done | bytes 2097184 | tf_op jit(solution)/shard_map/all_to_all | solution.py:315
  279.6 4.3 %copy.131 = bf16[4,16,128,128]{3,1,0,2:T(8,128)(2,1)} copy(bf16[4,16,128,128]{3,2,1,0:T(8,128)(2,1)} %all-to-all-done.3) | data formatting | bytes 4194304 | tf_op jit(solution)/shard_map/all_to_all | solution.py:315
  283.8 16.5 %all_to_all.88 = bf16[4,2,128,2,128]{4,3,2,1,0:T(2,128)(2,1)S(1)} all-to-all(bf16[4,2,128,2,128]{4,3,2,1,0:T(2,128)(2,1)S(1)} %reshape.438), channel_id=1, replica_groups=mesh['seq'=8,'head'=4] {'head'}, dimensions={0} | all-to-all | bytes 1048576 | tf_op jit(solution)/shard_map/all_to_all | solution.py:321
  300.7 0.9 copy.147
  301.6 0.9 copy.148
  (86 shorter events, 5.4 us)
Async XLA Ops:
  7.2 77.6 %all-gather.2.cloned.1.call-start = ((), (), s32[]{:S(2)}) async-start(), calls=%async_computation.6 | async-start | bytes 4718592 | tf_op jit(solution)/shard_map/all_gather | solution.py:222
  8.4 21.0 %copy-start.3 = (bf16[128,64,128]{2,1,0:T(8,128)(2,1)S(1)}, bf16[128,64,128]{2,1,0:T(8,128)(2,1)}, u32[]{:S(2)}) copy-start(bf16[128,64,128]{2,1,0:T(8,128)(2,1)} %param.10) | copy-start | bytes 6291460
  32.1 3.8 %copy-start.7 = (s32[32,3]{0,1:T(4,128)S(1)}, s32[32,3]{0,1:T(4,128)}, u32[]{:S(2)}) copy-start(s32[32,3]{0,1:T(4,128)} %param.15) | copy-start | bytes 1156
  32.1 51.1 %all-to-all-start = ((bf16[64,128,128]{2,1,0:T(8,128)(2,1)}), bf16[64,128,128]{2,1,0:T(8,128)(2,1)S(1)}, u32[]{:S(2)}, u32[]{:S(2)}) async-start(bf16[64,128,128]{2,1,0:T(8,128)(2,1)} %bitcast.142), calls=%async_computation | async-start | bytes 4194304 | tf_op jit(solution)/shard_map/all_to_all | solution.py:169
  36.0 4.9 %copy-start.8 = (s32[2]{0:T(128)S(1)}, s32[2]{0:T(128)}, u32[]{:S(2)}) copy-start(s32[2]{0:T(128)} %param.14) | copy-start | bytes 28
  84.8 4.4 %copy-start = (bf16[2,512,256]{2,1,0:T(8,128)(2,1)S(1)}, bf16[2,512,256]{2,1,0:T(8,128)(2,1)}, u32[]{:S(2)}) copy-start(bf16[2,512,256]{2,1,0:T(8,128)(2,1)} %reshape.422) | copy-start | bytes 1572868
  84.8 55.0 %all-to-all-start.2 = ((bf16[64,128,128]{2,1,0:T(8,128)(2,1)}), bf16[64,128,128]{2,1,0:T(8,128)(2,1)S(1)}, u32[]{:S(2)}, u32[]{:S(2)}) async-start(bf16[64,128,128]{2,1,0:T(8,128)(2,1)} %bitcast.131), calls=%async_computation.2 | async-start | bytes 4194304 | tf_op jit(solution)/shard_map/all_to_all | solution.py:225
  89.2 7.3 %collective-permute-start = (bf16[2,128,256]{2,1,0:T(8,128)(2,1)S(1)}, bf16[2,128,256]{2,1,0:T(8,128)(2,1)S(1)}, u32[]{:S(2)}, u32[]{:S(2)}) collective-permute-start(bf16[2,128,256]{2,1,0:T(8,128)(2,1)S(1)} %get-tuple-element.79), channel_id=1, source_target_pairs={{0,4},{4,8},{8,12},{12,16},{16,20},{20,24},{24,28},{1,5},{5,9},{9,... | collective-permute-start | bytes 393224 | tf_op jit(solution)/shard_map/ppermute | solution.py:143
  91.1 7.0 %collective-permute-start.1 = (bf16[2,128,256]{2,1,0:T(8,128)(2,1)S(1)}, bf16[2,128,256]{2,1,0:T(8,128)(2,1)S(1)}, u32[]{:S(2)}, u32[]{:S(2)}) collective-permute-start(bf16[2,128,256]{2,1,0:T(8,128)(2,1)S(1)} %get-tuple-element.80), channel_id=1, source_target_pairs={{4,0},{8,4},{12,8},{16,12},{20,16},{24,20},{28,24},{5,1},{9,5},{13... | collective-permute-start | bytes 393224 | tf_op jit(solution)/shard_map/ppermute | solution.py:144
  108.8 2.3 copy-start.4
  171.9 54.5 %all-to-all-start.4 = ((bf16[4,16,128,128]{3,2,1,0:T(8,128)(2,1)}), bf16[4,16,128,128]{3,2,1,0:T(8,128)(2,1)S(1)}, u32[]{:S(2)}, u32[]{:S(2)}) async-start(bf16[4,16,128,128]{3,2,1,0:T(8,128)(2,1)} %bitcast.146), calls=%async_computation.4 | async-start | bytes 4194304 | tf_op jit(solution)/shard_map/all_to_all | solution.py:316
  178.9 22.1 %collective-permute-start.4 = (bf16[2,2,128,256]{3,2,1,0:T(8,128)(2,1)S(1)}, bf16[2,2,128,256]{3,2,1,0:T(8,128)(2,1)S(1)}, u32[]{:S(2)}, u32[]{:S(2)}) collective-permute-start(bf16[2,2,128,256]{3,2,1,0:T(8,128)(2,1)S(1)} %convert_element_type.59), channel_id=1, source_target_pairs={{0,4},{4,0},{8,12},{12,8},{16,20},{20,16},{24,28},{28,24},{1,5},{5... | collective-permute-start | bytes 786440 | tf_op jit(solution)/shard_map/ppermute | solution.py:161
  183.3 14.5 %collective-permute-start.2 = (bf16[2,128,256]{2,1,0:T(8,128)(2,1)S(1)}, bf16[2,128,256]{2,1,0:T(8,128)(2,1)S(1)}, u32[]{:S(2)}, u32[]{:S(2)}) collective-permute-start(bf16[2,128,256]{2,1,0:T(8,128)(2,1)S(1)} %get-tuple-element.71), channel_id=1, source_target_pairs={{0,4},{4,8},{8,12},{12,16},{16,20},{20,24},{24,28},{1,5},{5,9},{9,... | collective-permute-start | bytes 393224 | tf_op jit(solution)/shard_map/ppermute | solution.py:143
  185.2 15.1 %collective-permute-start.3 = (bf16[2,128,256]{2,1,0:T(8,128)(2,1)S(1)}, bf16[2,128,256]{2,1,0:T(8,128)(2,1)S(1)}, u32[]{:S(2)}, u32[]{:S(2)}) collective-permute-start(bf16[2,128,256]{2,1,0:T(8,128)(2,1)S(1)} %get-tuple-element.72), channel_id=1, source_target_pairs={{4,0},{8,4},{12,8},{16,12},{20,16},{24,20},{28,24},{5,1},{9,5},{13... | collective-permute-start | bytes 393224 | tf_op jit(solution)/shard_map/ppermute | solution.py:144
  192.1 0.7 copy-start.6
  196.6 9.0 %collective-permute-start.7 = (bf16[2,2,128,256]{3,0,2,1:T(2,128)(2,1)S(1)}, bf16[2,2,128,256]{3,0,2,1:T(2,128)(2,1)S(1)}, u32[]{:S(2)}, u32[]{:S(2)}) collective-permute-start(bf16[2,2,128,256]{3,0,2,1:T(2,128)(2,1)S(1)} %get-tuple-element.66), channel_id=1, source_target_pairs={{0,4},{4,8},{8,12},{12,16},{16,20},{20,24},{24,28},{28,0},{1,5},{5... | collective-permute-start | bytes 786440 | tf_op jit(solution)/shard_map/ppermute | solution.py:125
  196.7 10.2 %collective-permute-start.8 = (bf16[2,2,128,256]{3,0,2,1:T(2,128)(2,1)S(1)}, bf16[2,2,128,256]{3,0,2,1:T(2,128)(2,1)S(1)}, u32[]{:S(2)}, u32[]{:S(2)}) collective-permute-start(bf16[2,2,128,256]{3,0,2,1:T(2,128)(2,1)S(1)} %get-tuple-element.65), channel_id=1, source_target_pairs={{0,8},{4,12},{8,16},{12,20},{16,24},{20,28},{24,0},{28,4},{1,9},{5... | collective-permute-start | bytes 786440 | tf_op jit(solution)/shard_map/ppermute | solution.py:125
  197.7 34.0 %collective-permute-start.9 = (bf16[2,2,128,256]{3,0,2,1:T(2,128)(2,1)}, bf16[2,2,128,256]{3,0,2,1:T(2,128)(2,1)S(1)}, u32[]{:S(2)}, u32[]{:S(2)}) collective-permute-start(bf16[2,2,128,256]{3,0,2,1:T(2,128)(2,1)} %get-tuple-element.64), channel_id=1, source_target_pairs={{0,12},{4,16},{8,20},{12,24},{16,28},{20,0},{24,4},{28,8},{1,13},{... | collective-permute-start | bytes 786440 | tf_op jit(solution)/shard_map/ppermute | solution.py:125
  200.3 32.4 %collective-permute-start.10 = (bf16[2,2,128,256]{3,0,2,1:T(2,128)(2,1)}, bf16[2,2,128,256]{3,0,2,1:T(2,128)(2,1)}, u32[]{:S(2)}, u32[]{:S(2)}) collective-permute-start(bf16[2,2,128,256]{3,0,2,1:T(2,128)(2,1)} %get-tuple-element.63), channel_id=1, source_target_pairs={{0,16},{4,20},{8,24},{12,28},{16,0},{20,4},{24,8},{28,12},{1,17},{... | collective-permute-start | bytes 786440 | tf_op jit(solution)/shard_map/ppermute | solution.py:125
  201.0 6.0 %copy-start.1 = (f32[4,2,128,256]{3,2,1,0:T(8,128)}, f32[4,2,128,256]{3,2,1,0:T(8,128)S(1)}, u32[]{:S(2)}) copy-start(f32[4,2,128,256]{3,2,1,0:T(8,128)S(1)} %fusion.22) | copy-start | bytes 3145732
  201.0 33.5 %collective-permute-start.11 = (bf16[2,2,128,256]{3,0,2,1:T(2,128)(2,1)}, bf16[2,2,128,256]{3,0,2,1:T(2,128)(2,1)}, u32[]{:S(2)}, u32[]{:S(2)}) collective-permute-start(bf16[2,2,128,256]{3,0,2,1:T(2,128)(2,1)} %get-tuple-element.62), channel_id=1, source_target_pairs={{0,20},{4,24},{8,28},{12,0},{16,4},{20,8},{24,12},{28,16},{1,21},{... | collective-permute-start | bytes 786440 | tf_op jit(solution)/shard_map/ppermute | solution.py:125
  205.6 30.7 %collective-permute-start.12 = (bf16[2,2,128,256]{3,0,2,1:T(2,128)(2,1)}, bf16[2,2,128,256]{3,0,2,1:T(2,128)(2,1)}, u32[]{:S(2)}, u32[]{:S(2)}) collective-permute-start(bf16[2,2,128,256]{3,0,2,1:T(2,128)(2,1)} %get-tuple-element.61), channel_id=1, source_target_pairs={{0,24},{4,28},{8,0},{12,4},{16,8},{20,12},{24,16},{28,20},{1,25},{... | collective-permute-start | bytes 786440 | tf_op jit(solution)/shard_map/ppermute | solution.py:125
  206.9 31.3 %collective-permute-start.13 = (bf16[2,2,128,256]{3,0,2,1:T(2,128)(2,1)}, bf16[2,2,128,256]{3,0,2,1:T(2,128)(2,1)}, u32[]{:S(2)}, u32[]{:S(2)}) collective-permute-start(bf16[2,2,128,256]{3,0,2,1:T(2,128)(2,1)} %get-tuple-element.60), channel_id=1, source_target_pairs={{0,28},{4,0},{8,4},{12,8},{16,12},{20,16},{24,20},{28,24},{1,29},{... | collective-permute-start | bytes 786440 | tf_op jit(solution)/shard_map/ppermute | solution.py:125
  226.4 53.1 %all-to-all-start.3 = ((bf16[4,16,128,128]{3,2,1,0:T(8,128)(2,1)}), bf16[4,16,128,128]{3,2,1,0:T(8,128)(2,1)}, u32[]{:S(2)}, u32[]{:S(2)}) async-start(bf16[4,16,128,128]{3,2,1,0:T(8,128)(2,1)} %bitcast.145), calls=%async_computation.3 | async-start | bytes 4194304 | tf_op jit(solution)/shard_map/all_to_all | solution.py:315
  231.8 15.6 %collective-permute-start.5 = (bf16[2,2,128,256]{3,2,1,0:T(8,128)(2,1)}, bf16[2,2,128,256]{3,2,1,0:T(8,128)(2,1)S(1)}, u32[]{:S(2)}, u32[]{:S(2)}) collective-permute-start(bf16[2,2,128,256]{3,2,1,0:T(8,128)(2,1)} %fusion.21), channel_id=1, source_target_pairs={{0,8},{4,12},{8,0},{12,4},{16,24},{20,28},{24,16},{28,20},{1,9},{5... | collective-permute-start | bytes 786440 | tf_op jit(solution)/shard_map/ppermute | solution.py:161
  247.4 8.3 %collective-permute-start.6 = (bf16[2,2,128,256]{3,2,1,0:T(8,128)(2,1)S(1)}, bf16[2,2,128,256]{3,2,1,0:T(8,128)(2,1)S(1)}, u32[]{:S(2)}, u32[]{:S(2)}) collective-permute-start(bf16[2,2,128,256]{3,2,1,0:T(8,128)(2,1)S(1)} %fusion.25), channel_id=1, source_target_pairs={{0,16},{4,20},{8,24},{12,28},{16,0},{20,4},{24,8},{28,12},{1,17},{... | collective-permute-start | bytes 786440 | tf_op jit(solution)/shard_map/ppermute | solution.py:161
  251.2 4.7 %copy-start.5 = (f32[2,4]{1,0:T(2,128)S(1)}, f32[2,4]{1,0:T(2,128)}, u32[]{:S(2)}) copy-start(f32[2,4]{1,0:T(2,128)} %and_convert_fusion) | copy-start | bytes 100
  252.5 3.6 %copy-start.2 = (f32[4,2,128,256]{3,2,1,0:T(8,128)S(1)}, f32[4,2,128,256]{3,2,1,0:T(8,128)}, u32[]{:S(2)}) copy-start(f32[4,2,128,256]{3,2,1,0:T(8,128)} %copy-done.1) | copy-start | bytes 3145732
Sparse Core Ops, SparseCore 0:
  29.5 35.4 all-gather.1

commit v15 on v14

--- a/solution.py
+++ b/solution.py
@@ -37,7 +37,7 @@
     row_sum = jnp.sum(e, axis=1, keepdims=True)
     max_ref[...] = row_max
     sum_ref[...] = row_sum
-    p_low = (e / row_sum).astype(jnp.bfloat16)
+    p_low = (e * (1.0 / row_sum)).astype(jnp.bfloat16)
     o_low = jnp.dot(p_low, v, preferred_element_type=jnp.float32).astype(jnp.bfloat16)
     out_ref[...] = o_low.reshape(out_ref.shape)
 
@@ -53,7 +53,7 @@
     v = v_ref[...].reshape(-1, width)
     rows_by_cols = (((1,), (1,)), ((), ()))
     over_rows = (((0,), (0,)), ((), ()))
-    p = jnp.exp(scores_of(q, k, bias_ref[...], scale) - max_ref[...]) / sum_ref[...]
+    p = jnp.exp(scores_of(q, k, bias_ref[...], scale) - max_ref[...]) * (1.0 / sum_ref[...])
     p_low = p.astype(jnp.bfloat16)
     delta = jnp.sum(do.astype(jnp.float32) * o_low.astype(jnp.float32), axis=1, keepdims=True)
     dp = lax.dot_general(do, v, rows_by_cols, preferred_element_type=jnp.float32)

time: 311 us -> 311 us (level)
  no operation moved by 1% of the time
where the time goes in v15:
time: 311 us; the launch traced here: 309 us
  waiting for transfers between devices  85.1 us (27%)
  local copies, waits for them, and re-layouts  61.2 us (20%)
  Pallas kernels  55.9 us (18%)
  starting transfers between devices  39.3 us (13%)
  blocking collectives  35.8 us (12%)
  other arithmetic  15.1 us (5%)
  between operations  14.6 us (5%)
    all_to_all x1, waiting for transfers between devices, per_device(): lax.all_to_all(queries.transpose(1, 0, 2), 'head', split_axis=0, concat_a...  40.8 us
    pallas_call x1, Pallas kernels, attention_call(): pl.pallas_call(functools.partial(backward_kernel, scale=scale), cost_esti...  30.6 us
    pallas_call x1, Pallas kernels, attention_call(): pl.pallas_call(functools.partial(forward_kernel, scale=scale), cost_estim...  25.3 us
    all_to_all x1, waiting for transfers between devices, per_device(): lax.all_to_all(out_all, 'head', split_axis=0, concat_axis=1, tiled=True)  20.3 us
    all_to_all x1, blocking collectives, per_device(): lax.all_to_all(jnp.stack([keys, values]), 'head', split_axis=2, concat_ax...  19.3 us
    unnamed x27, local copies, waits for them, and re-layouts  16.8 us
    all_to_all x1, blocking collectives, per_device(): lax.all_to_all(kv_blocks, 'head', split_axis=0, concat_axis=3, tiled=True)  16.5 us
    all_to_all x1, waiting for transfers between devices, per_device(): lax.all_to_all(query_grad_all, 'head', split_axis=0, concat_axis=1, tiled...  15.2 us
  transfers between devices with their start and end apart: 19, of which 7 were waited for; matrix products, arithmetic and copies ran while one was open for 22% of the time, Pallas kernels for 8%

profile of v15, /device:TPU:4, one launch (start us, length us, event | category | flops | bytes accessed | tf_op | source)
XLA Modules:
  0.0 309.5 jit_solution(12445819788794698732)
XLA Ops:
  7.2 1.1 copy_bitcast_fusion.8
  8.4 19.3 %all_to_all.87 = bf16[2,128,8,128]{3,1,0,2:T(8,128)(2,1)S(1)} all-to-all(bf16[2,128,8,128]{3,1,0,2:T(8,128)(2,1)S(1)} %pad_maximum_fusion.5), channel_id=1, replica_groups=mesh['seq'=8,'head'=4] {'head'}, dimensions={2} | all-to-all | bytes 1048576 | tf_op jit(solution)/shard_map/all_to_all | solution.py:174
  27.7 0.5 copy.182
  28.3 1.1 reshape.422
  29.4 2.7 copy.180
  32.1 3.7 %all-to-all-start = ((bf16[64,128,128]{2,1,0:T(8,128)(2,1)}), bf16[64,128,128]{2,1,0:T(8,128)(2,1)S(1)}, u32[]{:S(2)}, u32[]{:S(2)}) async-start(bf16[64,128,128]{2,1,0:T(8,128)(2,1)} %bitcast.142), calls=%async_computation | async-start | bytes 4194304 | tf_op jit(solution)/shard_map/all_to_all | solution.py:169
  36.0 4.4 %copy.179 = bf16[128,64,128]{2,0,1:T(8,128)(2,1)} copy(bf16[128,64,128]{2,1,0:T(8,128)(2,1)} %param.13) | data formatting | bytes 4194304 | tf_op args[3]
  41.3 0.5 fusion.45
  41.8 0.6 and_convert_fusion
  42.4 40.8 %all-to-all-done = bf16[64,128,128]{2,1,0:T(8,128)(2,1)S(1)} async-done(((bf16[64,128,128]{2,1,0:T(8,128)(2,1)}), bf16[64,128,128]{2,1,0:T(8,128)(2,1)S(1)}, u32[]{:S(2)}, u32[]{:S(2)}) %all-to-all-start) | async-done | bytes 2097184 | tf_op jit(solution)/shard_map/all_to_all | solution.py:169
  83.2 1.6 copy.118
  84.8 3.7 %all-to-all-start.2 = ((bf16[64,128,128]{2,1,0:T(8,128)(2,1)}), bf16[64,128,128]{2,1,0:T(8,128)(2,1)S(1)}, u32[]{:S(2)}, u32[]{:S(2)}) async-start(bf16[64,128,128]{2,1,0:T(8,128)(2,1)} %bitcast.131), calls=%async_computation.2 | async-start | bytes 4194304 | tf_op jit(solution)/shard_map/all_to_all | solution.py:225
  89.2 1.9 collective-permute-start
  91.1 4.7 %collective-permute-start.1 = (bf16[2,128,256]{2,1,0:T(8,128)(2,1)S(1)}, bf16[2,128,256]{2,1,0:T(8,128)(2,1)S(1)}, u32[]{:S(2)}, u32[]{:S(2)}) collective-permute-start(bf16[2,128,256]{2,1,0:T(8,128)(2,1)S(1)} %get-tuple-element.80), channel_id=1, source_target_pairs={{4,0},{8,4},{12,8},{16,12},{20,16},{24,20},{28,24},{5,1},{9,5},{13... | collective-permute-start | bytes 393224 | tf_op jit(solution)/shard_map/ppermute | solution.py:144
  95.8 0.5 fusion.44
  96.5 1.7 collective-permute-done.1
  98.4 0.8 copy.186
  99.2 4.0 %gather_fusion.1 = bf16[12,2,128,256]{3,2,1,0:T(8,128)(2,1)} fusion(bf16[2,32,128,256]{3,2,1,0:T(8,128)(2,1)} %bitcast.163, s32[1024]{0:T(1024)S(1)} %get-tuple-element.91), kind=kCustom, calls=%fused_computation.1 | custom fusion | bytes 3145776 | tf_op jit(solution)/shard_map/jit(_take)/gather | solution.py:227
  103.2 1.6 broadcast_select_fusion.1
  104.8 1.2 copy.181
  106.1 2.7 gather_fusion
  108.8 0.8 broadcast_select_fusion.2
  109.6 1.5 slice_bitcast_fusion.6
  111.6 2.3 pad_maximum_fusion.k_ref.v_ref
  113.8 0.7 broadcast_in_dim.79
  114.5 25.3 %shard_map.93 = (bf16[4,2,8,128,128]{4,3,2,1,0:T(8,128)(2,1)}, f32[4,2,1024,1]{3,2,1,0:T(8,128)}, f32[4,2,1024,1]{3,2,1,0:T(8,128)}) custom-call(bf16[2,8,4,128,128]{4,3,2,1,0:T(8,128)(2,1)} %bitcast.147, bf16[4,8,2,128,256]{4,3,2,1,0:T(8,128)(2,1)} %pad_maximum_fusion.k_ref.v_ref, bf16[4,8,2,128,256]{4,3,2,1,0:T(8,128)(2,1)} %pad_maximum_fusion.k_ref.v_ref, ...), custom_call_target="tpu_custom_call" | custom-call | flops 4294967296 | bytes 23068672 | tf_op jit(solution)/shard_map/pallas_call | solution.py:87
  139.8 1.7 copy.130
  141.5 30.6 %shard_map.94 = (bf16[4,2,8,128,128]{4,3,2,1,0:T(8,128)(2,1)}, f32[4,8,2,128,256]{4,3,2,1,0:T(8,128)}) custom-call(bf16[2,8,4,128,128]{4,3,2,1,0:T(8,128)(2,1)} %bitcast.148, bf16[4,8,2,128,256]{4,3,2,1,0:T(8,128)(2,1)} %pad_maximum_fusion.k_ref.v_ref, bf16[4,8,2,128,256]{4,3,2,1,0:T(8,128)(2,1)} %pad_maximum_fusion.k_ref.v_ref, ...), custom_call_target="tpu_custom_call" | custom-call | flops 10737418240 | bytes 23068672 | tf_op jit(solution)/shard_map/pallas_call | solution.py:99
  172.1 5.1 %all-to-all-start.4 = ((bf16[4,16,128,128]{3,2,1,0:T(8,128)(2,1)}), bf16[4,16,128,128]{3,2,1,0:T(8,128)(2,1)S(1)}, u32[]{:S(2)}, u32[]{:S(2)}) async-start(bf16[4,16,128,128]{3,2,1,0:T(8,128)(2,1)} %bitcast.146), calls=%async_computation.4 | async-start | bytes 4194304 | tf_op jit(solution)/shard_map/all_to_all | solution.py:316
  177.3 1.8 slice_reduce_fusion
  179.1 0.9 collective-permute-start.4
  180.0 1.3 slice_bitcast_fusion.2
  181.3 1.7 slice_bitcast_fusion.1
  183.5 1.9 collective-permute-start.2
  185.4 4.8 %collective-permute-start.3 = (bf16[2,128,256]{2,1,0:T(8,128)(2,1)S(1)}, bf16[2,128,256]{2,1,0:T(8,128)(2,1)S(1)}, u32[]{:S(2)}, u32[]{:S(2)}) collective-permute-start(bf16[2,128,256]{2,1,0:T(8,128)(2,1)S(1)} %get-tuple-element.72), channel_id=1, source_target_pairs={{4,0},{8,4},{12,8},{16,12},{20,16},{24,20},{28,24},{5,1},{9,5},{13... | collective-permute-start | bytes 393224 | tf_op jit(solution)/shard_map/ppermute | solution.py:144
  190.2 2.1 fusion.7
  192.4 0.5 copy-done.6
  192.9 1.0 fusion.4
  194.0 2.8 constant_dynamic-slice_fusion
  197.0 1.0 bitcast_dynamic-update-slice_fusion.7
  197.9 2.5 collective-permute-start.9
  200.5 0.6 collective-permute-start.10
  201.3 0.9 fusion.21
  202.2 3.6 %collective-permute-done.7 = bf16[2,2,128,256]{3,0,2,1:T(2,128)(2,1)S(1)} collective-permute-done((bf16[2,2,128,256]{3,0,2,1:T(2,128)(2,1)S(1)}, bf16[2,2,128,256]{3,0,2,1:T(2,128)(2,1)S(1)}, u32[]{:S(2)}, u32[]{:S(2)}) %collective-permute-start.7) | collective-permute-done | bytes 262176 | tf_op jit(solution)/shard_map/ppermute | solution.py:125
  206.0 0.9 bitcast_dynamic-update-slice_fusion.6
  207.1 4.3 %collective-permute-start.13 = (bf16[2,2,128,256]{3,0,2,1:T(2,128)(2,1)}, bf16[2,2,128,256]{3,0,2,1:T(2,128)(2,1)}, u32[]{:S(2)}, u32[]{:S(2)}) collective-permute-start(bf16[2,2,128,256]{3,0,2,1:T(2,128)(2,1)} %get-tuple-element.60), channel_id=1, source_target_pairs={{0,28},{4,0},{8,4},{12,8},{16,12},{20,16},{24,20},{28,24},{1,29},{... | collective-permute-start | bytes 786440 | tf_op jit(solution)/shard_map/ppermute | solution.py:125
  211.4 15.2 %all-to-all-done.4 = bf16[4,16,128,128]{3,2,1,0:T(8,128)(2,1)S(1)} async-done(((bf16[4,16,128,128]{3,2,1,0:T(8,128)(2,1)}), bf16[4,16,128,128]{3,2,1,0:T(8,128)(2,1)S(1)}, u32[]{:S(2)}, u32[]{:S(2)}) %all-to-all-start.4) | async-done | bytes 2097184 | tf_op jit(solution)/shard_map/all_to_all | solution.py:316
  226.6 4.5 %all-to-all-start.3 = ((bf16[4,16,128,128]{3,2,1,0:T(8,128)(2,1)}), bf16[4,16,128,128]{3,2,1,0:T(8,128)(2,1)}, u32[]{:S(2)}, u32[]{:S(2)}) async-start(bf16[4,16,128,128]{3,2,1,0:T(8,128)(2,1)} %bitcast.145), calls=%async_computation.3 | async-start | bytes 4194304 | tf_op jit(solution)/shard_map/all_to_all | solution.py:315
  231.1 0.9 bitcast_dynamic-update-slice_fusion.5
  232.0 0.9 bitcast_dynamic-update-slice_fusion.4
  232.9 1.8 bitcast_dynamic-update-slice_fusion.3
  234.7 1.8 bitcast_dynamic-update-slice_fusion.2
  236.5 1.8 bitcast_dynamic-update-slice_fusion.1
  238.4 1.8 bitcast_dynamic-update-slice_fusion
  240.2 7.3 %gather_fusion.2 = bf16[8,2,2,128,256]{4,1,3,2,0:T(2,128)(2,1)} fusion(bf16[8,2,2,128,256]{4,1,3,2,0:T(2,128)(2,1)} %bitcast_dynamic-update-slice_fusion, s32[1024]{0:T(1024)S(1)} %pad_clamp_fusion), kind=kCustom, calls=%fused_computation.2 | custom fusion | bytes 4194336 | tf_op jit(solution)/shard_map/jit(_take)/gather | solution.py:128
  247.9 3.5 %broadcast_select_fusion = bf16[8,2,2,128,256]{4,1,3,2,0:T(2,128)(2,1)S(1)} fusion(bf16[8,2,2,128,256]{4,1,3,2,0:T(2,128)(2,1)} %gather_fusion.2, pred[8]{0:T(512)(128)(4,1)S(1)} %compare_and_fusion.2), kind=kLoop, calls=%fused_computation.4 | loop fusion | flops 1048576 | bytes 4194312 | tf_op jit(solution)/shard_map/jit(_take)/select_n | solution.py:128
  251.4 1.3 fusion.8
  252.7 3.2 %collective-permute-done.6 = bf16[2,2,128,256]{3,2,1,0:T(8,128)(2,1)S(1)} collective-permute-done((bf16[2,2,128,256]{3,2,1,0:T(8,128)(2,1)S(1)}, bf16[2,2,128,256]{3,2,1,0:T(8,128)(2,1)S(1)}, u32[]{:S(2)}, u32[]{:S(2)}) %collective-permute-start.6) | collective-permute-done | bytes 262176 | tf_op jit(solution)/shard_map/ppermute | solution.py:161
  256.8 2.7 copy.132
  259.5 20.3 %all-to-all-done.3 = bf16[4,16,128,128]{3,2,1,0:T(8,128)(2,1)} async-done(((bf16[4,16,128,128]{3,2,1,0:T(8,128)(2,1)}), bf16[4,16,128,128]{3,2,1,0:T(8,128)(2,1)}, u32[]{:S(2)}, u32[]{:S(2)}) %all-to-all-start.3) | async-done | bytes 2097184 | tf_op jit(solution)/shard_map/all_to_all | solution.py:315
  279.8 4.3 %copy.131 = bf16[4,16,128,128]{3,1,0,2:T(8,128)(2,1)} copy(bf16[4,16,128,128]{3,2,1,0:T(8,128)(2,1)} %all-to-all-done.3) | data formatting | bytes 4194304 | tf_op jit(solution)/shard_map/all_to_all | solution.py:315
  284.0 16.5 %all_to_all.88 = bf16[4,2,128,2,128]{4,3,2,1,0:T(2,128)(2,1)S(1)} all-to-all(bf16[4,2,128,2,128]{4,3,2,1,0:T(2,128)(2,1)S(1)} %reshape.438), channel_id=1, replica_groups=mesh['seq'=8,'head'=4] {'head'}, dimensions={0} | all-to-all | bytes 1048576 | tf_op jit(solution)/shard_map/all_to_all | solution.py:321
  300.9 0.9 copy.147
  301.8 0.9 copy.148
  (86 shorter events, 5.4 us)
Async XLA Ops:
  7.2 77.6 %all-gather.2.cloned.1.call-start = ((), (), s32[]{:S(2)}) async-start(), calls=%async_computation.6 | async-start | bytes 4718592 | tf_op jit(solution)/shard_map/all_gather | solution.py:222
  8.4 21.0 %copy-start.3 = (bf16[128,64,128]{2,1,0:T(8,128)(2,1)S(1)}, bf16[128,64,128]{2,1,0:T(8,128)(2,1)}, u32[]{:S(2)}) copy-start(bf16[128,64,128]{2,1,0:T(8,128)(2,1)} %param.10) | copy-start | bytes 6291460
  32.1 3.8 %copy-start.7 = (s32[32,3]{0,1:T(4,128)S(1)}, s32[32,3]{0,1:T(4,128)}, u32[]{:S(2)}) copy-start(s32[32,3]{0,1:T(4,128)} %param.15) | copy-start | bytes 1156
  32.1 51.1 %all-to-all-start = ((bf16[64,128,128]{2,1,0:T(8,128)(2,1)}), bf16[64,128,128]{2,1,0:T(8,128)(2,1)S(1)}, u32[]{:S(2)}, u32[]{:S(2)}) async-start(bf16[64,128,128]{2,1,0:T(8,128)(2,1)} %bitcast.142), calls=%async_computation | async-start | bytes 4194304 | tf_op jit(solution)/shard_map/all_to_all | solution.py:169
  36.0 4.9 %copy-start.8 = (s32[2]{0:T(128)S(1)}, s32[2]{0:T(128)}, u32[]{:S(2)}) copy-start(s32[2]{0:T(128)} %param.14) | copy-start | bytes 28
  84.8 4.4 %copy-start = (bf16[2,512,256]{2,1,0:T(8,128)(2,1)S(1)}, bf16[2,512,256]{2,1,0:T(8,128)(2,1)}, u32[]{:S(2)}) copy-start(bf16[2,512,256]{2,1,0:T(8,128)(2,1)} %reshape.422) | copy-start | bytes 1572868
  84.8 55.0 %all-to-all-start.2 = ((bf16[64,128,128]{2,1,0:T(8,128)(2,1)}), bf16[64,128,128]{2,1,0:T(8,128)(2,1)S(1)}, u32[]{:S(2)}, u32[]{:S(2)}) async-start(bf16[64,128,128]{2,1,0:T(8,128)(2,1)} %bitcast.131), calls=%async_computation.2 | async-start | bytes 4194304 | tf_op jit(solution)/shard_map/all_to_all | solution.py:225
  89.2 7.3 %collective-permute-start = (bf16[2,128,256]{2,1,0:T(8,128)(2,1)S(1)}, bf16[2,128,256]{2,1,0:T(8,128)(2,1)S(1)}, u32[]{:S(2)}, u32[]{:S(2)}) collective-permute-start(bf16[2,128,256]{2,1,0:T(8,128)(2,1)S(1)} %get-tuple-element.79), channel_id=1, source_target_pairs={{0,4},{4,8},{8,12},{12,16},{16,20},{20,24},{24,28},{1,5},{5,9},{9,... | collective-permute-start | bytes 393224 | tf_op jit(solution)/shard_map/ppermute | solution.py:143
  91.1 7.0 %collective-permute-start.1 = (bf16[2,128,256]{2,1,0:T(8,128)(2,1)S(1)}, bf16[2,128,256]{2,1,0:T(8,128)(2,1)S(1)}, u32[]{:S(2)}, u32[]{:S(2)}) collective-permute-start(bf16[2,128,256]{2,1,0:T(8,128)(2,1)S(1)} %get-tuple-element.80), channel_id=1, source_target_pairs={{4,0},{8,4},{12,8},{16,12},{20,16},{24,20},{28,24},{5,1},{9,5},{13... | collective-permute-start | bytes 393224 | tf_op jit(solution)/shard_map/ppermute | solution.py:144
  108.8 2.3 copy-start.4
  172.1 54.5 %all-to-all-start.4 = ((bf16[4,16,128,128]{3,2,1,0:T(8,128)(2,1)}), bf16[4,16,128,128]{3,2,1,0:T(8,128)(2,1)S(1)}, u32[]{:S(2)}, u32[]{:S(2)}) async-start(bf16[4,16,128,128]{3,2,1,0:T(8,128)(2,1)} %bitcast.146), calls=%async_computation.4 | async-start | bytes 4194304 | tf_op jit(solution)/shard_map/all_to_all | solution.py:316
  179.1 22.1 %collective-permute-start.4 = (bf16[2,2,128,256]{3,2,1,0:T(8,128)(2,1)S(1)}, bf16[2,2,128,256]{3,2,1,0:T(8,128)(2,1)S(1)}, u32[]{:S(2)}, u32[]{:S(2)}) collective-permute-start(bf16[2,2,128,256]{3,2,1,0:T(8,128)(2,1)S(1)} %convert_element_type.59), channel_id=1, source_target_pairs={{0,4},{4,0},{8,12},{12,8},{16,20},{20,16},{24,28},{28,24},{1,5},{5... | collective-permute-start | bytes 786440 | tf_op jit(solution)/shard_map/ppermute | solution.py:161
  183.5 14.5 %collective-permute-start.2 = (bf16[2,128,256]{2,1,0:T(8,128)(2,1)S(1)}, bf16[2,128,256]{2,1,0:T(8,128)(2,1)S(1)}, u32[]{:S(2)}, u32[]{:S(2)}) collective-permute-start(bf16[2,128,256]{2,1,0:T(8,128)(2,1)S(1)} %get-tuple-element.71), channel_id=1, source_target_pairs={{0,4},{4,8},{8,12},{12,16},{16,20},{20,24},{24,28},{1,5},{5,9},{9,... | collective-permute-start | bytes 393224 | tf_op jit(solution)/shard_map/ppermute | solution.py:143
  185.4 15.1 %collective-permute-start.3 = (bf16[2,128,256]{2,1,0:T(8,128)(2,1)S(1)}, bf16[2,128,256]{2,1,0:T(8,128)(2,1)S(1)}, u32[]{:S(2)}, u32[]{:S(2)}) collective-permute-start(bf16[2,128,256]{2,1,0:T(8,128)(2,1)S(1)} %get-tuple-element.72), channel_id=1, source_target_pairs={{4,0},{8,4},{12,8},{16,12},{20,16},{24,20},{28,24},{5,1},{9,5},{13... | collective-permute-start | bytes 393224 | tf_op jit(solution)/shard_map/ppermute | solution.py:144
  192.3 0.7 copy-start.6
  196.8 9.0 %collective-permute-start.7 = (bf16[2,2,128,256]{3,0,2,1:T(2,128)(2,1)S(1)}, bf16[2,2,128,256]{3,0,2,1:T(2,128)(2,1)S(1)}, u32[]{:S(2)}, u32[]{:S(2)}) collective-permute-start(bf16[2,2,128,256]{3,0,2,1:T(2,128)(2,1)S(1)} %get-tuple-element.66), channel_id=1, source_target_pairs={{0,4},{4,8},{8,12},{12,16},{16,20},{20,24},{24,28},{28,0},{1,5},{5... | collective-permute-start | bytes 786440 | tf_op jit(solution)/shard_map/ppermute | solution.py:125
  196.9 10.2 %collective-permute-start.8 = (bf16[2,2,128,256]{3,0,2,1:T(2,128)(2,1)S(1)}, bf16[2,2,128,256]{3,0,2,1:T(2,128)(2,1)S(1)}, u32[]{:S(2)}, u32[]{:S(2)}) collective-permute-start(bf16[2,2,128,256]{3,0,2,1:T(2,128)(2,1)S(1)} %get-tuple-element.65), channel_id=1, source_target_pairs={{0,8},{4,12},{8,16},{12,20},{16,24},{20,28},{24,0},{28,4},{1,9},{5... | collective-permute-start | bytes 786440 | tf_op jit(solution)/shard_map/ppermute | solution.py:125
  197.9 34.0 %collective-permute-start.9 = (bf16[2,2,128,256]{3,0,2,1:T(2,128)(2,1)}, bf16[2,2,128,256]{3,0,2,1:T(2,128)(2,1)S(1)}, u32[]{:S(2)}, u32[]{:S(2)}) collective-permute-start(bf16[2,2,128,256]{3,0,2,1:T(2,128)(2,1)} %get-tuple-element.64), channel_id=1, source_target_pairs={{0,12},{4,16},{8,20},{12,24},{16,28},{20,0},{24,4},{28,8},{1,13},{... | collective-permute-start | bytes 786440 | tf_op jit(solution)/shard_map/ppermute | solution.py:125
  200.5 32.4 %collective-permute-start.10 = (bf16[2,2,128,256]{3,0,2,1:T(2,128)(2,1)}, bf16[2,2,128,256]{3,0,2,1:T(2,128)(2,1)}, u32[]{:S(2)}, u32[]{:S(2)}) collective-permute-start(bf16[2,2,128,256]{3,0,2,1:T(2,128)(2,1)} %get-tuple-element.63), channel_id=1, source_target_pairs={{0,16},{4,20},{8,24},{12,28},{16,0},{20,4},{24,8},{28,12},{1,17},{... | collective-permute-start | bytes 786440 | tf_op jit(solution)/shard_map/ppermute | solution.py:125
  201.2 6.0 %copy-start.1 = (f32[4,2,128,256]{3,2,1,0:T(8,128)}, f32[4,2,128,256]{3,2,1,0:T(8,128)S(1)}, u32[]{:S(2)}) copy-start(f32[4,2,128,256]{3,2,1,0:T(8,128)S(1)} %fusion.22) | copy-start | bytes 3145732
  201.2 33.5 %collective-permute-start.11 = (bf16[2,2,128,256]{3,0,2,1:T(2,128)(2,1)}, bf16[2,2,128,256]{3,0,2,1:T(2,128)(2,1)}, u32[]{:S(2)}, u32[]{:S(2)}) collective-permute-start(bf16[2,2,128,256]{3,0,2,1:T(2,128)(2,1)} %get-tuple-element.62), channel_id=1, source_target_pairs={{0,20},{4,24},{8,28},{12,0},{16,4},{20,8},{24,12},{28,16},{1,21},{... | collective-permute-start | bytes 786440 | tf_op jit(solution)/shard_map/ppermute | solution.py:125
  205.8 30.7 %collective-permute-start.12 = (bf16[2,2,128,256]{3,0,2,1:T(2,128)(2,1)}, bf16[2,2,128,256]{3,0,2,1:T(2,128)(2,1)}, u32[]{:S(2)}, u32[]{:S(2)}) collective-permute-start(bf16[2,2,128,256]{3,0,2,1:T(2,128)(2,1)} %get-tuple-element.61), channel_id=1, source_target_pairs={{0,24},{4,28},{8,0},{12,4},{16,8},{20,12},{24,16},{28,20},{1,25},{... | collective-permute-start | bytes 786440 | tf_op jit(solution)/shard_map/ppermute | solution.py:125
  207.1 31.3 %collective-permute-start.13 = (bf16[2,2,128,256]{3,0,2,1:T(2,128)(2,1)}, bf16[2,2,128,256]{3,0,2,1:T(2,128)(2,1)}, u32[]{:S(2)}, u32[]{:S(2)}) collective-permute-start(bf16[2,2,128,256]{3,0,2,1:T(2,128)(2,1)} %get-tuple-element.60), channel_id=1, source_target_pairs={{0,28},{4,0},{8,4},{12,8},{16,12},{20,16},{24,20},{28,24},{1,29},{... | collective-permute-start | bytes 786440 | tf_op jit(solution)/shard_map/ppermute | solution.py:125
  226.6 53.1 %all-to-all-start.3 = ((bf16[4,16,128,128]{3,2,1,0:T(8,128)(2,1)}), bf16[4,16,128,128]{3,2,1,0:T(8,128)(2,1)}, u32[]{:S(2)}, u32[]{:S(2)}) async-start(bf16[4,16,128,128]{3,2,1,0:T(8,128)(2,1)} %bitcast.145), calls=%async_computation.3 | async-start | bytes 4194304 | tf_op jit(solution)/shard_map/all_to_all | solution.py:315
  232.0 15.6 %collective-permute-start.5 = (bf16[2,2,128,256]{3,2,1,0:T(8,128)(2,1)}, bf16[2,2,128,256]{3,2,1,0:T(8,128)(2,1)S(1)}, u32[]{:S(2)}, u32[]{:S(2)}) collective-permute-start(bf16[2,2,128,256]{3,2,1,0:T(8,128)(2,1)} %fusion.21), channel_id=1, source_target_pairs={{0,8},{4,12},{8,0},{12,4},{16,24},{20,28},{24,16},{28,20},{1,9},{5... | collective-permute-start | bytes 786440 | tf_op jit(solution)/shard_map/ppermute | solution.py:161
  247.6 8.3 %collective-permute-start.6 = (bf16[2,2,128,256]{3,2,1,0:T(8,128)(2,1)S(1)}, bf16[2,2,128,256]{3,2,1,0:T(8,128)(2,1)S(1)}, u32[]{:S(2)}, u32[]{:S(2)}) collective-permute-start(bf16[2,2,128,256]{3,2,1,0:T(8,128)(2,1)S(1)} %fusion.25), channel_id=1, source_target_pairs={{0,16},{4,20},{8,24},{12,28},{16,0},{20,4},{24,8},{28,12},{1,17},{... | collective-permute-start | bytes 786440 | tf_op jit(solution)/shard_map/ppermute | solution.py:161
  251.4 4.7 %copy-start.5 = (f32[2,4]{1,0:T(2,128)S(1)}, f32[2,4]{1,0:T(2,128)}, u32[]{:S(2)}) copy-start(f32[2,4]{1,0:T(2,128)} %and_convert_fusion) | copy-start | bytes 100
  252.7 3.6 %copy-start.2 = (f32[4,2,128,256]{3,2,1,0:T(8,128)S(1)}, f32[4,2,128,256]{3,2,1,0:T(8,128)}, u32[]{:S(2)}) copy-start(f32[4,2,128,256]{3,2,1,0:T(8,128)} %copy-done.1) | copy-start | bytes 3145732
Sparse Core Ops, SparseCore 0:
  29.5 35.4 all-gather.1
